TPU v7x, 256 devices: a whole 4x4x8 slice. The times are simulated.
256 devices in a mesh: tm: 16 (over z, core), head: 16 (over y, x).
Axes of the slice: x: 4, y: 4, z: 8, core: 2. Of those that a mesh axis runs over, the one named last changes fastest.
Arguments:
- frames: bfloat16 [8192, 2048], P(('tm', 'head')), may hold values from -6 to 6
- log_decay: float32 [8192, 16], P('tm', 'head'), may hold values from -2 to 0, as said below
- w_query: bfloat16 [2048, 2048], P('tm', 'head'), may hold values from -0.125 to 0.125
- w_key: bfloat16 [2048, 2048], P('tm', 'head'), may hold values from -0.125 to 0.125
- w_value: bfloat16 [2048, 2048], P('tm', 'head'), may hold values from -0.125 to 0.125
- w_gate: bfloat16 [2048, 2048], P('tm', 'head'), may hold values from -0.125 to 0.125
- w_out: bfloat16 [2048, 2048], P('head', 'tm'), may hold values from -0.125 to 0.125
Outputs:
- mixed: bfloat16 [8192, 2048], P(('tm', 'head'))
Inputs may be any that keep to these rules, and one draw needn't show every extreme that they name: `log_decay`: strictly negative.
All inputs are finite; a program needn't handle non-finite values.
Results may differ from a plain program's by a relative error of at most 0.015.
Values may be sent and summed in bfloat16 or wider, within the bound.
No kernel may reach another device: no remote copies, remote signals or barrier semaphores. Data moves between devices by JAX's collectives and lax.ppermute only.
A program may use at most 64 MiB of HBM per device.

v0:
```python
import jax
import jax.numpy as jnp
from jax import lax
from jax.sharding import PartitionSpec as P

HEAD_DIM = 128
BLOCK = 512


def carried_in(value, axis, join, neutral):
    count, mine = (lax.axis_size(axis), lax.axis_index(axis))
    pieces = jax.tree.map(lambda part: lax.all_gather(part, axis), value)
    running = jax.tree.map(
        lambda part, zero: jnp.full_like(part, 0) + jnp.asarray(zero, part.dtype), value, neutral
    )

    def lap(position, running):
        longer = join(running, jax.tree.map(lambda part: part[position], pieces))
        return jax.tree.map(lambda new, old: jnp.where(position < mine, new, old), longer, running)

    return lax.fori_loop(0, count - 1, lap, running)


def combine_states(earlier, later):
    return (earlier[0] * later[0], later[0][:, None, None] * earlier[1] + later[1])


def shards(frames, log_decay, w_query, w_key, w_value, w_gate, w_out):
    rows_query, rows_key, rows_value, rows_gate = (
        lax.all_gather(w_query, "tm", axis=0, tiled=True),
        lax.all_gather(w_key, "tm", axis=0, tiled=True),
        lax.all_gather(w_value, "tm", axis=0, tiled=True),
        lax.all_gather(w_gate, "tm", axis=0, tiled=True),
    )
    joined = jnp.concatenate([rows_query, rows_key, rows_value, rows_gate], axis=1)
    head_width = rows_query.shape[1]
    projected = jnp.dot(
        lax.all_gather(frames, "head", axis=0, tiled=True),
        joined,
        preferred_element_type=jnp.float32,
    )
    local_len = projected.shape[0]
    heads_here = head_width // HEAD_DIM
    block_count = local_len // BLOCK
    query_blocks = (
        projected[:, :head_width]
        .astype(jnp.bfloat16)
        .reshape(block_count, BLOCK, heads_here, HEAD_DIM)
    )
    key_blocks = (
        projected[:, head_width : 2 * head_width]
        .astype(jnp.bfloat16)
        .reshape(block_count, BLOCK, heads_here, HEAD_DIM)
    )
    value_blocks = (
        projected[:, 2 * head_width : 3 * head_width]
        .astype(jnp.bfloat16)
        .reshape(block_count, BLOCK, heads_here, HEAD_DIM)
    )
    gate_all = projected[:, 3 * head_width :]
    running_blocks = jnp.cumsum(log_decay.reshape(block_count, BLOCK, heads_here), axis=1)
    slice_ordinal = jnp.arange(BLOCK, dtype=jnp.int32)
    causal = slice_ordinal[:, None] >= slice_ordinal[None, :]

    def local_step(carry_state, inputs):
        query_block, key_block, value_block, running = inputs
        gaps = running.T[:, :, None] - running.T[:, None, :]
        decay = jnp.exp(jnp.where(causal[None], gaps, -jnp.inf))
        scores = jnp.einsum(
            "thd,shd->hts", query_block, key_block, preferred_element_type=jnp.float32
        )
        weights = (scores * decay).astype(jnp.bfloat16)
        intra = jnp.einsum("hts,shd->thd", weights, value_block, preferred_element_type=jnp.float32)
        scaled = (
            key_block.astype(jnp.float32) * jnp.exp(running[-1][None, :] - running)[:, :, None]
        ).astype(jnp.bfloat16)
        update = jnp.einsum("shd,she->hde", scaled, value_block, preferred_element_type=jnp.float32)
        next_state = jnp.exp(running[-1])[:, None, None] * carry_state + update
        return (next_state, (intra, carry_state))

    zero_state = jnp.zeros((heads_here, HEAD_DIM, HEAD_DIM), jnp.float32)
    local_final, (intra_all, local_starts) = lax.scan(
        local_step, zero_state, (query_blocks, key_blocks, value_blocks, running_blocks)
    )
    decay_total = jnp.exp(jnp.sum(log_decay, axis=0))
    identity = (jnp.ones_like(decay_total), jnp.zeros_like(local_final))
    prior = carried_in((decay_total, local_final), "tm", combine_states, identity)[1]
    block_logs = running_blocks[:, -1, :]
    before = jnp.cumsum(block_logs, axis=0) - block_logs
    start_states = jnp.exp(before)[:, :, None, None] * prior[None] + local_starts
    lifted = query_blocks.astype(jnp.float32) * jnp.exp(running_blocks)[..., None]
    inter = jnp.einsum("cthd,chde->cthe", lifted, start_states, precision=lax.Precision.HIGHEST)
    retained = (intra_all + inter).reshape(local_len, heads_here, HEAD_DIM)
    center = jnp.mean(retained, axis=-1, keepdims=True)
    spread = jnp.mean((retained - center) ** 2, axis=-1, keepdims=True)
    normed = (retained - center) / jnp.sqrt(spread + 1e-05)
    gated = (
        (jax.nn.silu(gate_all.reshape(local_len, heads_here, HEAD_DIM)) * normed)
        .astype(jnp.bfloat16)
        .reshape(local_len, head_width)
    )
    owned = lax.all_to_all(gated, "head", split_axis=0, concat_axis=1, tiled=True)
    rows_out = lax.all_gather(w_out, "tm", axis=1, tiled=True)
    return jnp.dot(
        owned,
        lax.all_gather(rows_out, "head", axis=0, tiled=True),
        preferred_element_type=jnp.float32,
    ).astype(jnp.bfloat16)


def solution(mesh):
    return jax.shard_map(
        shards,
        mesh=mesh,
        in_specs=(
            P(("tm", "head"), None),
            P("tm", "head"),
            P("tm", "head"),
            P("tm", "head"),
            P("tm", "head"),
            P("tm", "head"),
            P("head", "tm"),
        ),
        out_specs=P(("tm", "head"), None),
        check_vma=False,
    )
```

profile of v0, /device:TPU:6, one launch (start us, length us, event | category | flops | bytes accessed | tf_op | source)
XLA Modules:
  0.0 215.3 jit_solution(12153568489863305342)
XLA Ops:
  6.5 0.7 all-gather.5.cloned.1.call-update
  7.3 1.0 reduce-window.6
  9.3 0.6 slice.44
  11.3 21.6 %all_gather.33 = bf16[2048,128]{1,0:T(8,128)(2,1)S(1)} all-gather(bf16[128,128]{1,0:T(8,128)(2,1)} %param.11), channel_id=1, replica_groups=mesh['tm'=16,'head'=16] {'tm'}, dimensions={0}, use_global_device_ids=true | all-gather | bytes 557056 | tf_op jit(solution)/shard_map/all_gather | solution.py:30
  32.9 16.1 %all_gather.34 = bf16[2048,128]{1,0:T(8,128)(2,1)S(1)} all-gather(bf16[128,128]{1,0:T(8,128)(2,1)} %param.12), channel_id=1, replica_groups=mesh['tm'=16,'head'=16] {'tm'}, dimensions={0}, use_global_device_ids=true | all-gather | bytes 557056 | tf_op jit(solution)/shard_map/all_gather | solution.py:31
  49.1 17.4 %all_gather.35 = bf16[2048,128]{1,0:T(8,128)(2,1)S(1)} all-gather(bf16[128,128]{1,0:T(8,128)(2,1)} %param.13), channel_id=1, replica_groups=mesh['tm'=16,'head'=16] {'tm'}, dimensions={0}, use_global_device_ids=true | all-gather | bytes 557056 | tf_op jit(solution)/shard_map/all_gather | solution.py:32
  66.5 16.1 %all_gather.36 = bf16[2048,128]{1,0:T(8,128)(2,1)S(1)} all-gather(bf16[128,128]{1,0:T(8,128)(2,1)} %param.14), channel_id=1, replica_groups=mesh['tm'=16,'head'=16] {'tm'}, dimensions={0}, use_global_device_ids=true | all-gather | bytes 557056 | tf_op jit(solution)/shard_map/all_gather | solution.py:33
  82.6 2.9 %fusion.46 = (bf16[512,512]{1,0:T(8,128)(2,1)S(1)}, f32[512,512]{1,0:T(8,128)S(1)}) fusion(bf16[512,2048]{1,0:T(8,128)(2,1)} %all-gather.5.cloned.1.call-done, bf16[2048,128]{1,0:T(8,128)(2,1)S(1)} %all_gather.36, bf16[2048,128]{1,0:T(8,128)(2,1)S(1)} %all_gather.35, bf16[2048,128]{1,0:T(8,128)(2,1)S(1)} %all_gather.34, bf16[2048,128]{1,0:T(8,128)(2,1)S(1)} %all_gather.33), kind=kOutput, calls=%fused_computation.58 | convolution fusion | flops 1082392576 | bytes 5767168 | tf_op jit(solution)/shard_map/dot_general | solution.py:37
  85.5 0.8 copy-done
  86.3 1.0 convolution_add_fusion
  87.4 18.6 %all_gather.42 = bf16[128,2048]{1,0:T(8,128)(2,1)} all-gather(bf16[128,128]{1,0:T(8,128)(2,1)S(1)} %copy-done.1), channel_id=1, replica_groups=mesh['tm'=16,'head'=16] {'tm'}, dimensions={1}, use_global_device_ids=true | all-gather | bytes 557056 | tf_op jit(solution)/shard_map/all_gather | solution.py:103
  106.0 0.6 reduce_sum.27
  107.8 0.6 slice.42
  109.7 0.6 dynamic-slice
  110.3 0.7 dynamic-update-slice
  111.0 24.3 %all-reduce = f32[16]{0:T(128)S(1)} all-reduce(f32[16]{0:T(128)S(1)} %dynamic-update-slice), channel_id=1, replica_groups=mesh['tm'=16,'head'=16] {'tm'}, use_global_device_ids=true, to_apply=%add | all-reduce | flops 16 | bytes 128
  135.3 1.6 fusion.14
  136.9 31.8 %while.9 = (s32[]{:T(128)}, f32[1,128,128]{2,1,0:T(8,128)S(1)}, s32[]{:T(128)}, f32[16,1]{0,1:T(1,128)S(1)}, f32[16,1,128,128]{3,2,1,0:T(8,128)}, /*index=5*/s32[]{:T(128)}, s32[]{:T(128)}) while((s32[]{:T(128)}, f32[1,128,128]{2,1,0:T(8,128)S(1)}, s32[]{:T(128)}, f32[16,1]{0,1:T(1,128)S(1)}, f32[16,1,128,128]{3,2,1,0:T(8,128)}, ...), condition=%wide.region_4.5_spmd.clone, body=%wide.region_3.4_spmd.clone.sunk | while | flops 65540 | bytes 196733 | solution.py:21
  136.9 0.6 constant_dynamic-slice_fusion.2
  137.5 1.5 fusion.52
  139.1 0.6 constant_dynamic-slice_fusion.2
  139.6 1.5 fusion.52
  141.2 0.6 constant_dynamic-slice_fusion.2
  141.8 1.5 fusion.52
  143.9 1.5 fusion.52
  145.4 0.6 constant_dynamic-slice_fusion.2
  146.0 1.5 fusion.52
  147.5 0.6 constant_dynamic-slice_fusion.2
  148.1 1.5 fusion.52
  150.2 1.5 fusion.52
  151.8 0.6 constant_dynamic-slice_fusion.2
  152.3 1.5 fusion.52
  153.9 0.6 constant_dynamic-slice_fusion.2
  154.5 1.5 fusion.52
  156.0 0.6 constant_dynamic-slice_fusion.2
  156.6 1.5 fusion.52
  158.1 0.6 constant_dynamic-slice_fusion.2
  158.7 1.5 fusion.52
  160.2 0.6 constant_dynamic-slice_fusion.2
  160.8 1.5 fusion.52
  162.9 1.5 fusion.52
  164.4 0.6 constant_dynamic-slice_fusion.2
  165.0 1.5 fusion.52
  167.2 1.5 fusion.52
  168.7 1.4 fusion.47
  170.6 13.9 %all_to_all.19 = bf16[16,32,128]{2,1,0:T(8,128)(2,1)S(1)} all-to-all(bf16[16,32,128]{2,1,0:T(8,128)(2,1)S(1)} %bitcast.76), channel_id=1, replica_groups=mesh['tm'=16,'head'=16] {'head'}, dimensions={0} | all-to-all | bytes 262144 | tf_op jit(solution)/shard_map/all_to_all | solution.py:102
  184.5 18.7 %all-gather.7.cloned.1.call-done = bf16[2048,2048]{1,0:T(8,128)(2,1)} async-done(((bf16[128,2048]{1,0:T(8,128)(2,1)}), bf16[2048,2048]{1,0:T(8,128)(2,1)}) %all-gather.7.cloned.1.call-update) | async-done | bytes 8388624 | tf_op jit(solution)/shard_map/all_gather | solution.py:106
  203.2 5.6 %convolution_convert_fusion = bf16[32,2048]{1,0:T(8,128)(2,1)} fusion(bf16[2048,2048]{1,0:T(8,128)(2,1)} %all-gather.7.cloned.1.call-done, bf16[16,32,128]{2,1,0:T(8,128)(2,1)S(1)} %all_to_all.19), kind=kOutput, calls=%fused_computation.3 | convolution fusion | flops 268500992 | bytes 8650752 | tf_op jit(solution)/shard_map/dot_general | solution.py:104
  (32 shorter events, 4.6 us)
Async XLA Ops:
  6.5 76.1 %all-gather.5.cloned.1.call-start = ((), (), s32[]{:S(2)}) async-start(), calls=%async_computation.1 | async-start | bytes 2228224 | tf_op jit(solution)/shard_map/all_gather | solution.py:38
  7.3 129.7 %all-gather.9.cloned.1.call-start = ((), (), s32[]{:S(2)}) async-start(), calls=%async_computation.3 | async-start | bytes 1114112 | tf_op jit(solution)/shard_map/all_gather | solution.py:12
  82.6 4.7 %copy-start.1 = (bf16[128,128]{1,0:T(8,128)(2,1)S(1)}, bf16[128,128]{1,0:T(8,128)(2,1)}, u32[]{:S(2)}) copy-start(bf16[128,128]{1,0:T(8,128)(2,1)} %param.15) | copy-start | bytes 98308
  82.6 23.4 %copy-start.2 = (f32[512,1]{0,1:T(1,128)S(1)}, f32[512,1]{0,1:T(1,128)}, u32[]{:S(2)}) copy-start(f32[512,1]{0,1:T(1,128)} %param.10) | copy-start | bytes 6148
  82.6 27.1 %copy-start.3 = (u32[256]{0:T(256)S(1)}, u32[256]{0:T(256)}, u32[]{:S(2)}) copy-start(u32[256]{0:T(256)} %constant.74) | copy-start | bytes 3076
  85.5 0.8 copy-start
  87.3 115.9 %all-gather.7.cloned.1.call-start = ((), (), s32[]{:S(2)}) async-start(), calls=%async_computation.2 | async-start | bytes 8912896 | tf_op jit(solution)/shard_map/all_gather | solution.py:106
Sparse Core Ops, SparseCore 0:
  9.8 52.5 all-gather.4
  87.4 37.3 all-gather.8
  127.2 75.9 all-gather.6
where the time goes:
time: 217 us; the launch traced here: 215 us
  blocking collectives  128 us (59%)
  other arithmetic  25 us (12%)
  waiting for transfers between devices  19.5 us (9%)
  between operations  16.4 us (8%)
  local copies, waits for them, and re-layouts  13.5 us (6%)
  matrix products  12.4 us (6%)
    unnamed x1, blocking collectives  24.3 us
    select_n x15, other arithmetic, lap(): jnp.where(position < mine, new, old)  22.6 us
    all_gather x1, blocking collectives, shards(): lax.all_gather(w_query, 'tm', axis=0, tiled=True)  21.6 us
    all_gather x1, waiting for transfers between devices, shards(): lax.all_gather(rows_out, 'head', axis=0, tiled=True)  18.7 us
    all_gather x1, blocking collectives, shards(): rows_out = lax.all_gather(w_out, 'tm', axis=1, tiled=True)  18.6 us
    all_gather x1, blocking collectives, shards(): lax.all_gather(w_value, 'tm', axis=0, tiled=True)  17.4 us
    all_gather x1, blocking collectives, shards(): lax.all_gather(w_gate, 'tm', axis=0, tiled=True)  16.1 us
    all_gather x1, blocking collectives, shards(): lax.all_gather(w_key, 'tm', axis=0, tiled=True)  16.1 us
  transfers between devices with their start and end apart: 3, of which 1 were waited for; matrix products, arithmetic and copies ran while one was open for 19% of the time, Pallas kernels for 0%

commit v1 on v0

--- a/solution.py
+++ b/solution.py
@@ -5,35 +5,30 @@
 
 HEAD_DIM = 128
 BLOCK = 512
+PAD_ROWS = 8
 
 
-def carried_in(value, axis, join, neutral):
-    count, mine = (lax.axis_size(axis), lax.axis_index(axis))
-    pieces = jax.tree.map(lambda part: lax.all_gather(part, axis), value)
-    running = jax.tree.map(
-        lambda part, zero: jnp.full_like(part, 0) + jnp.asarray(zero, part.dtype), value, neutral
-    )
-
-    def lap(position, running):
-        longer = join(running, jax.tree.map(lambda part: part[position], pieces))
-        return jax.tree.map(lambda new, old: jnp.where(position < mine, new, old), longer, running)
-
-    return lax.fori_loop(0, count - 1, lap, running)
-
-
-def combine_states(earlier, later):
-    return (earlier[0] * later[0], later[0][:, None, None] * earlier[1] + later[1])
+def prior_state(local_final, log_total, axis):
+    heads_here = local_final.shape[0]
+    extra = jnp.broadcast_to(log_total[:, None, None], (heads_here, PAD_ROWS, HEAD_DIM))
+    packed = jnp.concatenate([local_final, extra], axis=1)
+    gathered = lax.all_gather(packed, axis)
+    finals = gathered[:, :, :HEAD_DIM, :]
+    totals = gathered[:, :, HEAD_DIM, 0]
+    count = gathered.shape[0]
+    mine = lax.axis_index(axis)
+    order = jnp.arange(count, dtype=jnp.int32)
+    between = (order[:, None] < order[None, :]) & (order[None, :] < mine)
+    exponent = jnp.sum(jnp.where(between[:, :, None], totals[None, :, :], 0.0), axis=1)
+    weight = jnp.where((order < mine)[:, None], jnp.exp(exponent), 0.0)
+    return jnp.sum(weight[:, :, None, None] * finals, axis=0)
 
 
 def shards(frames, log_decay, w_query, w_key, w_value, w_gate, w_out):
-    rows_query, rows_key, rows_value, rows_gate = (
-        lax.all_gather(w_query, "tm", axis=0, tiled=True),
-        lax.all_gather(w_key, "tm", axis=0, tiled=True),
-        lax.all_gather(w_value, "tm", axis=0, tiled=True),
-        lax.all_gather(w_gate, "tm", axis=0, tiled=True),
+    head_width = w_query.shape[1]
+    joined = lax.all_gather(
+        jnp.concatenate([w_query, w_key, w_value, w_gate], axis=1), "tm", axis=0, tiled=True
     )
-    joined = jnp.concatenate([rows_query, rows_key, rows_value, rows_gate], axis=1)
-    head_width = rows_query.shape[1]
     projected = jnp.dot(
         lax.all_gather(frames, "head", axis=0, tiled=True),
         joined,
@@ -82,9 +77,7 @@
     local_final, (intra_all, local_starts) = lax.scan(
         local_step, zero_state, (query_blocks, key_blocks, value_blocks, running_blocks)
     )
-    decay_total = jnp.exp(jnp.sum(log_decay, axis=0))
-    identity = (jnp.ones_like(decay_total), jnp.zeros_like(local_final))
-    prior = carried_in((decay_total, local_final), "tm", combine_states, identity)[1]
+    prior = prior_state(local_final, jnp.sum(log_decay, axis=0), "tm")
     block_logs = running_blocks[:, -1, :]
     before = jnp.cumsum(block_logs, axis=0) - block_logs
     start_states = jnp.exp(before)[:, :, None, None] * prior[None] + local_starts

time: 217 us -> 236 us (1.088)
  waiting for transfers between devices: 19.5 us -> 166 us
  blocking collectives: 128 us -> 31.8 us
  other arithmetic: 25 us -> 5.99 us
  local copies, waits for them, and re-layouts: 13.5 us -> 5.13 us
    all_gather x4 -> x0, blocking collectives: 71.3 us -> none  [the longest x1 21.6 us: shards(): lax.all_gather(w_query, 'tm', axis=0, tiled=True)]
    all_gather x1 -> x2, waiting for transfers between devices: 0.02 us -> 56.3 us  [the longest x1 41.3 us: shards(): lax.all_gather(jnp.concatenate([w_query, w_key, w_value, w_gate], axis=1)...]
    all_gather x1, waiting for transfers between devices: 0.01 us -> 48.1 us  [shards(): lax.all_gather(frames, 'head', axis=0, tiled=True)]
    all_gather x1, waiting for transfers between devices: 18.7 us -> 60.4 us  [shards(): lax.all_gather(rows_out, 'head', axis=0, tiled=True)]
    unnamed x1 -> x0, blocking collectives: 24.3 us -> none
    select_n x15 -> x1, other arithmetic: 22.6 us -> 0.01 us  [prior_state(): weight = jnp.where((order < mine)[:, None], jnp.exp(exponent), 0.0)]
    dynamic_slice x15 -> x0, local copies, waits for them, and re-layouts: 8.77 us -> none  [lap(): longer = join(running, jax.tree.map(lambda part: part[position], pieces))]
  transfers between devices with their start and end apart: 3 -> 4, of which waited for: 1 -> 4; matrix products, arithmetic and copies ran while one was open for 19% -> 5% of each run, Pallas kernels for 0% -> 0%
where the time goes in v1:
time: 236 us; the launch traced here: 235 us
  waiting for transfers between devices  166 us (70%)
  blocking collectives  31.8 us (13%)
  between operations  15.9 us (7%)
  matrix products  10.4 us (4%)
  other arithmetic  5.99 us (3%)
  local copies, waits for them, and re-layouts  5.13 us (2%)
    all_gather x1, waiting for transfers between devices, shards(): lax.all_gather(rows_out, 'head', axis=0, tiled=True)  60.4 us
    all_gather x1, waiting for transfers between devices, shards(): lax.all_gather(frames, 'head', axis=0, tiled=True)  48.1 us
    all_gather x1, waiting for transfers between devices, shards(): lax.all_gather(jnp.concatenate([w_query, w_key, w_value, w_gate], axis=1)...  41.3 us
    all_gather x1, blocking collectives, shards(): rows_out = lax.all_gather(w_out, 'tm', axis=1, tiled=True)  18.9 us
    all_gather x1, waiting for transfers between devices, prior_state(): gathered = lax.all_gather(packed, axis)  15 us
    all_to_all x1, blocking collectives, shards(): lax.all_to_all(gated, 'head', split_axis=0, concat_axis=1, tiled=True)  12.8 us
    dot_general x1, matrix products, shards(): jnp.dot(owned, lax.all_gather(rows_out, 'head', axis=0, tiled=True), pref...  5.58 us
  transfers between devices with their start and end apart: 4, of which 4 were waited for; matrix products, arithmetic and copies ran while one was open for 5% of the time, Pallas kernels for 0%

profile of v1, /device:TPU:6, one launch (start us, length us, event | category | flops | bytes accessed | tf_op | source)
XLA Modules:
  0.0 234.9 jit_solution(7422585032205424245)
XLA Ops:
  6.5 0.0 all-gather.8.cloned.1.call-start
  6.5 0.7 all-gather.8.cloned.1.call-update
  7.3 0.0 all-gather.6.cloned.1.call-start
  7.3 1.5 pad_maximum_fusion
  8.8 0.0 all-gather.6.cloned.1.call-update
  8.8 0.0 all-gather.12.cloned.1.call-start
  8.9 1.3 reduce_sum.45
  10.2 1.0 reduce-window.6
  11.1 0.7 slice.51
  11.8 0.2 slice_reduce_fusion.1
  12.0 0.2 reduce-window.9
  12.2 0.1 broadcast.153
  12.2 0.6 slice.52
  14.2 0.1 subtract_exponential_fusion
  14.3 0.0 copy-start
  14.3 48.1 %all-gather.8.cloned.1.call-done = bf16[512,2048]{1,0:T(8,128)(2,1)} async-done(((bf16[32,2048]{1,0:T(8,128)(2,1)}), bf16[512,2048]{1,0:T(8,128)(2,1)}) %all-gather.8.cloned.1.call-update) | async-done | bytes 2097168 | tf_op jit(solution)/shard_map/all_gather | solution.py:33
  62.4 41.3 %all-gather.6.cloned.1.call-done = bf16[2048,512]{1,0:T(8,128)(2,1)} async-done(((bf16[128,512]{1,0:T(8,128)(2,1)}), bf16[2048,512]{1,0:T(8,128)(2,1)}) %all-gather.6.cloned.1.call-update) | async-done | bytes 2097168 | tf_op jit(solution)/shard_map/all_gather | solution.py:29
  103.7 3.5 %fusion.35 = (bf16[512,512]{1,0:T(8,128)(2,1)S(1)}, f32[512,512]{1,0:T(8,128)S(1)}) fusion(bf16[512,2048]{1,0:T(8,128)(2,1)} %all-gather.8.cloned.1.call-done, bf16[2048,512]{1,0:T(8,128)(2,1)} %all-gather.6.cloned.1.call-done), kind=kOutput, calls=%fused_computation.55 | convolution fusion | flops 1074003968 | bytes 5767168 | tf_op jit(solution)/shard_map/dot_general | solution.py:32
  107.2 0.3 fusion.4
  107.5 1.3 concatenate.7
  108.7 0.0 all-gather.12.cloned.1.call-update
  108.8 0.0 all-gather.10.cloned.1.call-start
  108.8 0.0 copy-done
  108.8 18.9 %all_gather.22 = bf16[128,2048]{1,0:T(8,128)(2,1)} all-gather(bf16[128,128]{1,0:T(8,128)(2,1)S(1)} %copy-done), channel_id=1, replica_groups=mesh['tm'=16,'head'=16] {'tm'}, dimensions={1}, use_global_device_ids=true | all-gather | bytes 557056 | tf_op jit(solution)/shard_map/all_gather | solution.py:96
  127.8 0.0 all-gather.10.cloned.1.call-update
  127.8 0.6 slice.49
  128.4 0.6 slice.50
  130.5 0.5 fusion.2
  131.0 15.0 %all-gather.12.cloned.1.call-done = f32[16,136,128]{2,1,0:T(8,128)} async-done(((f32[1,136,128]{2,1,0:T(8,128)}), f32[16,136,128]{2,1,0:T(8,128)}) %all-gather.12.cloned.1.call-update) | async-done | bytes 1114128 | tf_op jit(solution)/shard_map/all_gather | solution.py:15
  146.0 1.0 slice_reduce_fusion
  147.1 0.1 select_reduce_fusion
  147.2 1.4 fusion.5
  148.6 0.5 fusion.36
  149.1 0.2 fusion.13
  149.3 0.2 fusion.16
  149.6 12.8 %all_to_all.19 = bf16[16,32,128]{2,1,0:T(8,128)(2,1)S(1)} all-to-all(bf16[16,32,128]{2,1,0:T(8,128)(2,1)S(1)} %bitcast.62), channel_id=1, replica_groups=mesh['tm'=16,'head'=16] {'head'}, dimensions={0} | all-to-all | bytes 262144 | tf_op jit(solution)/shard_map/all_to_all | solution.py:95
  162.4 60.4 %all-gather.10.cloned.1.call-done = bf16[2048,2048]{1,0:T(8,128)(2,1)} async-done(((bf16[128,2048]{1,0:T(8,128)(2,1)}), bf16[2048,2048]{1,0:T(8,128)(2,1)}) %all-gather.10.cloned.1.call-update) | async-done | bytes 8388624 | tf_op jit(solution)/shard_map/all_gather | solution.py:99
  222.8 5.6 %convolution_convert_fusion = bf16[32,2048]{1,0:T(8,128)(2,1)} fusion(bf16[2048,2048]{1,0:T(8,128)(2,1)} %all-gather.10.cloned.1.call-done, bf16[16,32,128]{2,1,0:T(8,128)(2,1)S(1)} %all_to_all.19), kind=kOutput, calls=%fused_computation | convolution fusion | flops 268500992 | bytes 8650752 | tf_op jit(solution)/shard_map/dot_general | solution.py:97
  (6 shorter events, 0.0 us)
Async XLA Ops:
  6.5 55.8 %all-gather.8.cloned.1.call-start = ((), (), s32[]{:S(2)}) async-start(), calls=%async_computation.2 | async-start | bytes 2228224 | tf_op jit(solution)/shard_map/all_gather | solution.py:33
  7.3 96.4 %all-gather.6.cloned.1.call-start = ((), (), s32[]{:S(2)}) async-start(), calls=%async_computation.1 | async-start | bytes 2228224 | tf_op jit(solution)/shard_map/all_gather | solution.py:29
  8.8 137.2 %all-gather.12.cloned.1.call-start = ((), (), s32[]{:S(2)}) async-start(), calls=%async_computation.4 | async-start | bytes 1183744 | tf_op jit(solution)/shard_map/all_gather | solution.py:15
  14.3 94.5 %copy-start = (bf16[128,128]{1,0:T(8,128)(2,1)S(1)}, bf16[128,128]{1,0:T(8,128)(2,1)}, u32[]{:S(2)}) copy-start(bf16[128,128]{1,0:T(8,128)(2,1)} %param.13) | copy-start | bytes 98308
  108.8 114.0 %all-gather.10.cloned.1.call-start = ((), (), s32[]{:S(2)}) async-start(), calls=%async_computation.3 | async-start | bytes 8912896 | tf_op jit(solution)/shard_map/all_gather | solution.py:99
Sparse Core Ops, SparseCore 0:
  9.8 52.5 all-gather.7
  64.2 39.4 all-gather.5
  108.9 37.0 all-gather.11
  148.3 74.4 all-gather.9

commit v2 on v1

--- a/solution.py
+++ b/solution.py
@@ -8,11 +8,17 @@
 PAD_ROWS = 8
 
 
+def gather_by_exchange(part, axis):
+    count = lax.axis_size(axis)
+    copies = jnp.broadcast_to(part[None], (count,) + part.shape)
+    return lax.all_to_all(copies, axis, 0, 0, tiled=False)
+
+
 def prior_state(local_final, log_total, axis):
     heads_here = local_final.shape[0]
     extra = jnp.broadcast_to(log_total[:, None, None], (heads_here, PAD_ROWS, HEAD_DIM))
     packed = jnp.concatenate([local_final, extra], axis=1)
-    gathered = lax.all_gather(packed, axis)
+    gathered = gather_by_exchange(packed, axis)
     finals = gathered[:, :, :HEAD_DIM, :]
     totals = gathered[:, :, HEAD_DIM, 0]
     count = gathered.shape[0]
@@ -29,8 +35,10 @@
     joined = lax.all_gather(
         jnp.concatenate([w_query, w_key, w_value, w_gate], axis=1), "tm", axis=0, tiled=True
     )
+    rows_out = lax.all_gather(w_out, "tm", axis=1, tiled=True)
+    frames_here = gather_by_exchange(frames, "head").reshape(-1, frames.shape[1])
     projected = jnp.dot(
-        lax.all_gather(frames, "head", axis=0, tiled=True),
+        frames_here,
         joined,
         preferred_element_type=jnp.float32,
     )
@@ -92,13 +100,12 @@
         .astype(jnp.bfloat16)
         .reshape(local_len, head_width)
     )
-    owned = lax.all_to_all(gated, "head", split_axis=0, concat_axis=1, tiled=True)
-    rows_out = lax.all_gather(w_out, "tm", axis=1, tiled=True)
-    return jnp.dot(
-        owned,
-        lax.all_gather(rows_out, "head", axis=0, tiled=True),
-        preferred_element_type=jnp.float32,
-    ).astype(jnp.bfloat16)
+    share = jnp.dot(gated, rows_out, preferred_element_type=jnp.float32).astype(jnp.bfloat16)
+    owners = lax.axis_size("head")
+    shares = lax.all_to_all(
+        share.reshape(owners, local_len // owners, share.shape[1]), "head", 0, 0, tiled=False
+    )
+    return jnp.sum(shares.astype(jnp.float32), axis=0).astype(jnp.bfloat16)
 
 
 def solution(mesh):

time: 236 us -> 148 us (0.63)
  waiting for transfers between devices: 166 us -> 29.6 us
  blocking collectives: 31.8 us -> 70.9 us
  starting transfers between devices: 0.12 us -> 12.3 us
  matrix products: 10.4 us -> 4.86 us
    all_gather x3 -> x0, waiting for transfers between devices: 123 us -> none  [the longest x1 60.4 us: shards(): lax.all_gather(rows_out, 'head', axis=0, tiled=True)]
    all_gather x1, waiting for transfers between devices: 41.3 us -> 5.39 us  [shards(): lax.all_gather(jnp.concatenate([w_query, w_key, w_value, w_gate], axis=1)...]
    all_to_all x0 -> x2, waiting for transfers between devices: none -> 24.2 us  [gather_by_exchange(): return lax.all_to_all(copies, axis, 0, 0, tiled=False)]
    all_to_all x1, blocking collectives: 12.8 us -> 33.2 us  [shards(): lax.all_to_all(share.reshape(owners, local_len // owners, share.shape[1])...]
    all_gather x1, blocking collectives: 18.9 us -> 37.7 us  [shards(): rows_out = lax.all_gather(w_out, 'tm', axis=1, tiled=True)]
    all_to_all x0 -> x2, starting transfers between devices: none -> 12.3 us  [gather_by_exchange(): return lax.all_to_all(copies, axis, 0, 0, tiled=False)]
    dot_general x2, matrix products: 9.05 us -> 3.68 us  [the longest x1 2.91 us: shards(): projected = jnp.dot(frames_here, joined, preferred_element_type=jnp.float32)]
    broadcast_in_dim x0 -> x3, local copies, waits for them, and re-layouts: none -> 4.14 us  [gather_by_exchange(): copies = jnp.broadcast_to(part[None], (count,) + part.shape)]
  transfers between devices with their start and end apart: 4 -> 3, of which waited for: 4 -> 2; matrix products, arithmetic and copies ran while one was open for 5% -> 5% of each run, Pallas kernels for 0% -> 0%
where the time goes in v2:
time: 148 us; the launch traced here: 145 us
  blocking collectives  70.9 us (48%)
  waiting for transfers between devices  29.6 us (20%)
  between operations  16.1 us (11%)
  starting transfers between devices  12.3 us (8%)
  local copies, waits for them, and re-layouts  7.03 us (5%)
  matrix products  4.86 us (3%)
  other arithmetic  4.05 us (3%)
    all_gather x1, blocking collectives, shards(): rows_out = lax.all_gather(w_out, 'tm', axis=1, tiled=True)  37.7 us
    all_to_all x1, blocking collectives, shards(): lax.all_to_all(share.reshape(owners, local_len // owners, share.shape[1])...  33.2 us
    all_to_all x2, waiting for transfers between devices, gather_by_exchange(): return lax.all_to_all(copies, axis, 0, 0, tiled=False)  24.2 us
    all_to_all x2, starting transfers between devices, gather_by_exchange(): return lax.all_to_all(copies, axis, 0, 0, tiled=False)  12.3 us
    all_gather x1, waiting for transfers between devices, shards(): lax.all_gather(jnp.concatenate([w_query, w_key, w_value, w_gate], axis=1)...  5.39 us
    broadcast_in_dim x3, local copies, waits for them, and re-layouts, gather_by_exchange(): copies = jnp.broadcast_to(part[None], (count,) + part.shape)  4.14 us
  transfers between devices with their start and end apart: 3, of which 2 were waited for; matrix products, arithmetic and copies ran while one was open for 5% of the time, Pallas kernels for 0%

profile of v2, /device:TPU:6, one launch (start us, length us, event | category | flops | bytes accessed | tf_op | source)
XLA Modules:
  0.0 144.9 jit_solution(14062614743372692566)
XLA Ops:
  6.5 0.0 all-gather.2.cloned.1.call-start
  6.5 1.5 %pad_maximum_fusion = bf16[128,512]{1,0:T(8,128)(2,1)} fusion(bf16[128,128]{1,0:T(8,128)(2,1)} %param.12, bf16[128,128]{1,0:T(8,128)(2,1)} %param.11, bf16[128,128]{1,0:T(8,128)(2,1)} %param.10, bf16[128,128]{1,0:T(8,128)(2,1)} %param.9), kind=kLoop, calls=%fused_computation.29 | loop fusion | flops 524288 | bytes 262144 | tf_op jit(solution)/shard_map/concatenate | solution.py:36
  8.0 0.0 all-gather.2.cloned.1.call-update
  8.0 2.5 %broadcast_in_dim.42 = bf16[16,32,2048]{2,1,0:T(8,128)(2,1)} broadcast(bf16[32,2048]{1,0:T(8,128)(2,1)} %param.7), dimensions={1,2} | broadcast | bytes 2228224 | tf_op jit(solution)/shard_map/broadcast_in_dim | solution.py:13
  10.5 0.0 copy-start.3
  10.5 7.6 %all-to-all-start = ((bf16[16,32,2048]{2,1,0:T(8,128)(2,1)}), bf16[16,32,2048]{2,1,0:T(8,128)(2,1)S(1)}, u32[]{:S(2)}, u32[]{:S(2)}) async-start(bf16[16,32,2048]{2,1,0:T(8,128)(2,1)} %broadcast_in_dim.42), calls=%async_computation | async-start | bytes 4194304 | tf_op jit(solution)/shard_map/all_to_all | solution.py:14
  18.0 0.0 copy-done.3
  18.1 0.6 reduce_sum.57
  18.7 0.3 reduce-window.6
  19.0 0.2 slice_reduce_fusion.1
  19.2 0.2 reduce-window.9
  19.3 0.1 broadcast.155
  19.4 0.6 slice.52
  20.0 0.7 slice.51
  22.0 0.1 subtract_exponential_fusion
  22.1 24.2 %all-to-all-done = bf16[16,32,2048]{2,1,0:T(8,128)(2,1)S(1)} async-done(((bf16[16,32,2048]{2,1,0:T(8,128)(2,1)}), bf16[16,32,2048]{2,1,0:T(8,128)(2,1)S(1)}, u32[]{:S(2)}, u32[]{:S(2)}) %all-to-all-start) | async-done | bytes 2097184 | tf_op jit(solution)/shard_map/all_to_all | solution.py:14
  46.3 5.4 %all-gather.2.cloned.1.call-done = bf16[2048,512]{1,0:T(8,128)(2,1)} async-done(((bf16[128,512]{1,0:T(8,128)(2,1)}), bf16[2048,512]{1,0:T(8,128)(2,1)}) %all-gather.2.cloned.1.call-update) | async-done | bytes 2097168 | tf_op jit(solution)/shard_map/all_gather | solution.py:35
  51.7 2.9 %fusion.38 = (bf16[512,512]{0,1:T(8,128)(2,1)S(1)}, f32[512,512]{0,1:T(8,128)S(1)}) fusion(bf16[2048,512]{1,0:T(8,128)(2,1)} %all-gather.2.cloned.1.call-done, bf16[512,2048]{1,0:T(8,128)(2,1)S(1)} %bitcast.56), kind=kOutput, calls=%fused_computation.58 | convolution fusion | flops 1074003968 | bytes 5767168 | tf_op jit(solution)/shard_map/dot_general | solution.py:40
  54.6 0.0 copy-start
  54.6 0.0 copy-start.2
  54.7 0.2 fusion.4
  54.9 0.6 pad_bitcast_fusion
  55.5 0.0 copy-done
  55.5 1.1 broadcast_in_dim.47
  56.6 0.0 copy-start.1
  56.6 4.7 %all-to-all-start.1 = ((f32[16,1,136,128]{3,2,1,0:T(8,128)}), f32[16,1,136,128]{3,2,1,0:T(8,128)S(1)}, u32[]{:S(2)}, u32[]{:S(2)}) async-start(f32[16,1,136,128]{3,2,1,0:T(8,128)} %broadcast_in_dim.47), calls=%async_computation.1 | async-start | bytes 2228224 | tf_op jit(solution)/shard_map/all_to_all | solution.py:14
  61.3 0.6 slice.50
  61.9 0.6 slice.49
  63.7 0.0 copy-done.2
  63.7 37.7 %all_gather.7 = bf16[128,2048]{1,0:T(8,128)(2,1)S(1)} all-gather(bf16[128,128]{1,0:T(8,128)(2,1)S(1)} %copy-done.2), channel_id=1, replica_groups=mesh['tm'=16,'head'=16] {'tm'}, dimensions={1}, use_global_device_ids=true | all-gather | bytes 557056 | tf_op jit(solution)/shard_map/all_gather | solution.py:38
  101.4 0.0 copy-done.1
  101.5 0.6 fusion.2
  102.0 0.0 all-to-all-done.1
  102.0 0.2 slice_reduce_fusion
  102.2 0.1 select_reduce_fusion
  102.4 0.1 fusion.5
  102.5 0.4 fusion.39
  103.0 0.1 fusion.13
  103.0 0.8 convolution_convert_fusion
  103.8 33.2 %all_to_all.15 = bf16[16,32,2048]{2,1,0:T(8,128)(2,1)S(1)} all-to-all(bf16[16,32,2048]{2,1,0:T(8,128)(2,1)S(1)} %bitcast.55), channel_id=1, replica_groups=mesh['tm'=16,'head'=16] {'head'}, dimensions={0} | all-to-all | bytes 4194304 | tf_op jit(solution)/shard_map/all_to_all | solution.py:105
  137.0 1.1 reduce_sum.62
  (6 shorter events, 0.0 us)
Async XLA Ops:
  6.5 45.2 %all-gather.2.cloned.1.call-start = ((), (), s32[]{:S(2)}) async-start(), calls=%async_computation.3 | async-start | bytes 2228224 | tf_op jit(solution)/shard_map/all_gather | solution.py:35
  10.5 7.6 %copy-start.3 = (f32[512,1]{0,1:T(1,128)S(1)}, f32[512,1]{0,1:T(1,128)}, u32[]{:S(2)}) copy-start(f32[512,1]{0,1:T(1,128)} %param.8) | copy-start | bytes 6148
  10.5 35.8 %all-to-all-start = ((bf16[16,32,2048]{2,1,0:T(8,128)(2,1)}), bf16[16,32,2048]{2,1,0:T(8,128)(2,1)S(1)}, u32[]{:S(2)}, u32[]{:S(2)}) async-start(bf16[16,32,2048]{2,1,0:T(8,128)(2,1)} %broadcast_in_dim.42), calls=%async_computation | async-start | bytes 4194304 | tf_op jit(solution)/shard_map/all_to_all | solution.py:14
  54.6 0.9 copy-start
  54.6 9.1 %copy-start.2 = (bf16[128,128]{1,0:T(8,128)(2,1)S(1)}, bf16[128,128]{1,0:T(8,128)(2,1)}, u32[]{:S(2)}) copy-start(bf16[128,128]{1,0:T(8,128)(2,1)} %param.13) | copy-start | bytes 98308
  56.6 44.9 %copy-start.1 = (bf16[512,512]{0,1:T(8,128)(2,1)S(1)}, bf16[512,512]{0,1:T(8,128)(2,1)}, u32[]{:S(2)}) copy-start(bf16[512,512]{0,1:T(8,128)(2,1)} %copy-done) | copy-start | bytes 1572868
  56.6 45.5 %all-to-all-start.1 = ((f32[16,1,136,128]{3,2,1,0:T(8,128)}), f32[16,1,136,128]{3,2,1,0:T(8,128)S(1)}, u32[]{:S(2)}, u32[]{:S(2)}) async-start(f32[16,1,136,128]{3,2,1,0:T(8,128)} %broadcast_in_dim.47), calls=%async_computation.1 | async-start | bytes 2228224 | tf_op jit(solution)/shard_map/all_to_all | solution.py:14
Sparse Core Ops, SparseCore 0:
  9.2 42.4 all-gather.1

commit v3 on v2

--- a/solution.py
+++ b/solution.py
@@ -32,10 +32,11 @@
 
 def shards(frames, log_decay, w_query, w_key, w_value, w_gate, w_out):
     head_width = w_query.shape[1]
-    joined = lax.all_gather(
-        jnp.concatenate([w_query, w_key, w_value, w_gate], axis=1), "tm", axis=0, tiled=True
+    stacked = lax.all_gather(
+        jnp.concatenate([w_query, w_key, w_value, w_gate, w_out], axis=1), "tm", axis=0, tiled=True
     )
-    rows_out = lax.all_gather(w_out, "tm", axis=1, tiled=True)
+    joined = stacked[:, : 4 * head_width]
+    out_blocks = stacked[:, 4 * head_width :].reshape(-1, head_width, w_out.shape[1])
     frames_here = gather_by_exchange(frames, "head").reshape(-1, frames.shape[1])
     projected = jnp.dot(
         frames_here,
@@ -100,7 +101,11 @@
         .astype(jnp.bfloat16)
         .reshape(local_len, head_width)
     )
-    share = jnp.dot(gated, rows_out, preferred_element_type=jnp.float32).astype(jnp.bfloat16)
+    share = (
+        jnp.einsum("fr,krc->fkc", gated, out_blocks, preferred_element_type=jnp.float32)
+        .astype(jnp.bfloat16)
+        .reshape(local_len, -1)
+    )
     owners = lax.axis_size("head")
     shares = lax.all_to_all(
         share.reshape(owners, local_len // owners, share.shape[1]), "head", 0, 0, tiled=False

time: 148 us -> 145 us (0.980)
  the two profiles are of different devices: /device:TPU:6 before, /device:TPU:1 now
where the time goes in v3:
time: 145 us; the launch traced here: 144 us
  waiting for transfers between devices  55.8 us (38%)
  blocking collectives  33.2 us (23%)
  between operations  16.1 us (11%)
  local copies, waits for them, and re-layouts  15.2 us (10%)
  starting transfers between devices  14.2 us (10%)
  matrix products  6.82 us (5%)
  other arithmetic  2.53 us (2%)
    all_to_all x2, waiting for transfers between devices, gather_by_exchange(): return lax.all_to_all(copies, axis, 0, 0, tiled=False)  51.6 us
    all_to_all x1, blocking collectives, shards(): lax.all_to_all(share.reshape(owners, local_len // owners, share.shape[1])...  33.2 us
    all_to_all x2, starting transfers between devices, gather_by_exchange(): return lax.all_to_all(copies, axis, 0, 0, tiled=False)  14.2 us
    all_gather x1, waiting for transfers between devices, shards(): lax.all_gather(jnp.concatenate([w_query, w_key, w_value, w_gate, w_out],...  4.15 us
    broadcast_in_dim x3, local copies, waits for them, and re-layouts, gather_by_exchange(): copies = jnp.broadcast_to(part[None], (count,) + part.shape)  4.11 us
    unnamed x10, local copies, waits for them, and re-layouts  3.77 us
  transfers between devices with their start and end apart: 3, of which 3 were waited for; matrix products, arithmetic and copies ran while one was open for 6% of the time, Pallas kernels for 0%

profile of v3, /device:TPU:1, one launch (start us, length us, event | category | flops | bytes accessed | tf_op | source)
XLA Modules:
  0.0 143.9 jit_solution(17075771565899021291)
XLA Ops:
  6.5 0.0 all-gather.2.cloned.1.call-start
  6.5 0.8 constant_dynamic-update-slice_fusion.4
  7.3 0.8 constant_dynamic-update-slice_fusion.3
  8.1 0.8 constant_dynamic-update-slice_fusion.2
  8.8 0.8 constant_dynamic-update-slice_fusion.1
  9.6 0.8 constant_dynamic-update-slice_fusion
  10.4 0.0 copy-start
  10.4 0.7 copy-done
  11.1 0.0 all-gather.2.cloned.1.call-update
  11.1 2.5 %broadcast_in_dim.42 = bf16[16,32,2048]{2,1,0:T(8,128)(2,1)} broadcast(bf16[32,2048]{1,0:T(8,128)(2,1)} %param.7), dimensions={1,2} | broadcast | bytes 2228224 | tf_op jit(solution)/shard_map/broadcast_in_dim | solution.py:13
  13.5 0.0 copy-start.2
  13.5 7.7 %all-to-all-start = ((bf16[16,32,2048]{2,1,0:T(8,128)(2,1)}), bf16[16,32,2048]{2,1,0:T(8,128)(2,1)S(1)}, u32[]{:S(2)}, u32[]{:S(2)}) async-start(bf16[16,32,2048]{2,1,0:T(8,128)(2,1)} %broadcast_in_dim.42), calls=%async_computation | async-start | bytes 4194304 | tf_op jit(solution)/shard_map/all_to_all | solution.py:14
  21.3 0.0 copy-done.2
  21.3 0.6 reduce_sum.57
  21.9 0.3 reduce-window.6
  22.2 0.2 slice_reduce_fusion.1
  22.4 0.2 reduce-window.9
  22.5 0.1 broadcast.155
  22.6 0.6 slice.61
  23.3 0.6 slice.60
  25.2 0.1 subtract_exponential_fusion
  25.3 26.5 %all-to-all-done = bf16[16,32,2048]{2,1,0:T(8,128)(2,1)S(1)} async-done(((bf16[16,32,2048]{2,1,0:T(8,128)(2,1)}), bf16[16,32,2048]{2,1,0:T(8,128)(2,1)S(1)}, u32[]{:S(2)}, u32[]{:S(2)}) %all-to-all-start) | async-done | bytes 2097184 | tf_op jit(solution)/shard_map/all_to_all | solution.py:14
  51.8 4.2 %all-gather.2.cloned.1.call-done = bf16[2048,640]{1,0:T(8,128)(2,1)} async-done(((bf16[128,640]{1,0:T(8,128)(2,1)}), bf16[2048,640]{1,0:T(8,128)(2,1)}) %all-gather.2.cloned.1.call-update) | async-done | bytes 2621456 | tf_op jit(solution)/shard_map/all_gather | solution.py:35
  55.9 2.9 %fusion.43 = (bf16[512,512]{0,1:T(8,128)(2,1)S(1)}, f32[512,512]{0,1:T(8,128)S(1)}) fusion(bf16[512,2048]{1,0:T(8,128)(2,1)S(1)} %bitcast.59, bf16[2048,640]{1,0:T(8,128)(2,1)} %all-gather.2.cloned.1.call-done), kind=kOutput, calls=%fused_computation.64 | convolution fusion | flops 1074003968 | bytes 5767168 | tf_op jit(solution)/shard_map/dot_general | solution.py:41
  58.8 0.0 copy-start.1
  58.8 0.2 fusion.9
  59.0 0.6 pad_bitcast_fusion
  59.6 0.0 copy-done.1
  59.6 1.1 broadcast_in_dim.47
  60.7 6.4 %all-to-all-start.1 = ((f32[16,1,136,128]{3,2,1,0:T(8,128)}), f32[16,1,136,128]{3,2,1,0:T(8,128)S(1)}, u32[]{:S(2)}, u32[]{:S(2)}) async-start(f32[16,1,136,128]{3,2,1,0:T(8,128)} %broadcast_in_dim.47), calls=%async_computation.1 | async-start | bytes 2228224 | tf_op jit(solution)/shard_map/all_to_all | solution.py:14
  67.1 0.6 slice.59
  67.7 0.6 slice.58
  69.6 0.0 slice-start
  69.6 1.6 %fusion.7 = f32[1,512,1,128]{1,3,2,0:T(8,128)S(1)} fusion(f32[512]{0:T(512)S(1)} %get-tuple-element.22, bf16[512,512]{0,1:T(8,128)(2,1)} %copy-done.1), kind=kOutput, calls=%fused_computation.8 | convolution fusion | flops 135528448 | bytes 659456 | tf_op jit(solution)/shard_map/while/body/eval_jaxpr/hts,shd->thd/dot_general | solution.py:77
  71.2 25.2 %all-to-all-done.1 = f32[16,1,136,128]{3,2,1,0:T(8,128)S(1)} async-done(((f32[16,1,136,128]{3,2,1,0:T(8,128)}), f32[16,1,136,128]{3,2,1,0:T(8,128)S(1)}, u32[]{:S(2)}, u32[]{:S(2)}) %all-to-all-start.1) | async-done | bytes 1114144 | tf_op jit(solution)/shard_map/all_to_all | solution.py:14
  96.4 0.2 slice_reduce_fusion
  96.6 0.1 select_reduce_fusion
  96.7 0.1 fusion.10
  96.9 1.3 fusion.44
  98.2 0.1 fusion.18
  98.3 0.0 slice-done
  98.3 0.8 convolution_convert_fusion
  99.1 1.4 copy.16
  100.4 2.3 %reshape_reshape.3 = bf16[16,32,2048]{2,1,0:T(8,128)(2,1)} reshape(bf16[512,16,128]{2,1,0:T(8,128)(2,1)S(1)} %copy.16) | data formatting | bytes 4194304 | tf_op jit(solution)/shard_map/reshape;reshape | solution.py:111
  102.7 33.2 %all_to_all.15 = bf16[16,32,2048]{2,1,0:T(8,128)(2,1)S(1)} all-to-all(bf16[16,32,2048]{2,1,0:T(8,128)(2,1)} %reshape_reshape.3), channel_id=1, replica_groups=mesh['tm'=16,'head'=16] {'head'}, dimensions={0} | all-to-all | bytes 4194304 | tf_op jit(solution)/shard_map/all_to_all | solution.py:110
  136.0 1.1 reduce_sum.62
  (6 shorter events, 0.0 us)
Async XLA Ops:
  6.5 49.4 %all-gather.2.cloned.1.call-start = ((), (), s32[]{:S(2)}) async-start(), calls=%async_computation.3 | async-start | bytes 2785280 | tf_op jit(solution)/shard_map/all_gather | solution.py:35
  10.4 0.7 copy-start
  13.5 7.7 %copy-start.2 = (f32[512,1]{0,1:T(1,128)S(1)}, f32[512,1]{0,1:T(1,128)}, u32[]{:S(2)}) copy-start(f32[512,1]{0,1:T(1,128)} %param.8) | copy-start | bytes 6148
  13.5 38.2 %all-to-all-start = ((bf16[16,32,2048]{2,1,0:T(8,128)(2,1)}), bf16[16,32,2048]{2,1,0:T(8,128)(2,1)S(1)}, u32[]{:S(2)}, u32[]{:S(2)}) async-start(bf16[16,32,2048]{2,1,0:T(8,128)(2,1)} %broadcast_in_dim.42), calls=%async_computation | async-start | bytes 4194304 | tf_op jit(solution)/shard_map/all_to_all | solution.py:14
  58.8 0.8 copy-start.1
  60.7 35.7 %all-to-all-start.1 = ((f32[16,1,136,128]{3,2,1,0:T(8,128)}), f32[16,1,136,128]{3,2,1,0:T(8,128)S(1)}, u32[]{:S(2)}, u32[]{:S(2)}) async-start(f32[16,1,136,128]{3,2,1,0:T(8,128)} %broadcast_in_dim.47), calls=%async_computation.1 | async-start | bytes 2228224 | tf_op jit(solution)/shard_map/all_to_all | solution.py:14
  69.6 28.7 %slice-start = ((bf16[2048,640]{1,0:T(8,128)(2,1)}), bf16[2048,128]{1,0:T(8,128)(2,1)S(1)}, s32[]{:S(2)}) async-start(bf16[2048,640]{1,0:T(8,128)(2,1)} %all-gather.2.cloned.1.call-done), calls=%async_computation.4 | async-start | bytes 1048576 | tf_op jit(solution)/shard_map/slice | solution.py:39
Sparse Core Ops, SparseCore 0:
  11.2 44.6 all-gather.1

commit v4 on v3

--- a/solution.py
+++ b/solution.py
@@ -101,16 +101,32 @@
         .astype(jnp.bfloat16)
         .reshape(local_len, head_width)
     )
-    share = (
-        jnp.einsum("fr,krc->fkc", gated, out_blocks, preferred_element_type=jnp.float32)
-        .astype(jnp.bfloat16)
-        .reshape(local_len, -1)
-    )
-    owners = lax.axis_size("head")
-    shares = lax.all_to_all(
-        share.reshape(owners, local_len // owners, share.shape[1]), "head", 0, 0, tiled=False
-    )
-    return jnp.sum(shares.astype(jnp.float32), axis=0).astype(jnp.bfloat16)
+    heads = lax.axis_size("head")
+    side = int(round(heads ** 0.5))
+    me = lax.axis_index("head")
+    row, col = me // side, me % side
+    rows_mine = out_blocks
+    by_owner = gated.reshape(side, side, local_len // heads, head_width)
+    pieces = [lax.dynamic_index_in_dim(by_owner, col, axis=1, keepdims=False)]
+    weights_in = [rows_mine]
+    for shift in range(1, side):
+        across = [(h, (h // side) * side + (h % side + shift) % side) for h in range(heads)]
+        piece = lax.dynamic_index_in_dim(by_owner, (col + shift) % side, axis=1, keepdims=False)
+        pieces.append(lax.ppermute(piece, "head", across))
+        weights_in.append(lax.ppermute(rows_mine, "head", across))
+    partial = jnp.einsum(
+        "syfr,skrc->yfkc",
+        jnp.stack(pieces),
+        jnp.stack(weights_in),
+        preferred_element_type=jnp.float32,
+    ).astype(jnp.bfloat16)
+    partial = partial.reshape(side, local_len // heads, -1)
+    total = lax.dynamic_index_in_dim(partial, row, axis=0, keepdims=False).astype(jnp.float32)
+    for shift in range(1, side):
+        down = [(h, ((h // side + shift) % side) * side + h % side) for h in range(heads)]
+        piece = lax.dynamic_index_in_dim(partial, (row + shift) % side, axis=0, keepdims=False)
+        total = total + lax.ppermute(piece, "head", down).astype(jnp.float32)
+    return total.astype(jnp.bfloat16)
 
 
 def solution(mesh):

time: 145 us -> 123 us (0.85)
  the two profiles are of different devices: /device:TPU:1 before, /device:TPU:6 now
where the time goes in v4:
time: 123 us; the launch traced here: 122 us
  waiting for transfers between devices  59.4 us (48%)
  starting transfers between devices  24.9 us (20%)
  between operations  16.3 us (13%)
  local copies, waits for them, and re-layouts  12.7 us (10%)
  matrix products  6 us (5%)
  other arithmetic  2.61 us (2%)
    all_to_all x2, waiting for transfers between devices, gather_by_exchange(): return lax.all_to_all(copies, axis, 0, 0, tiled=False)  44.3 us
    all_to_all x2, starting transfers between devices, gather_by_exchange(): return lax.all_to_all(copies, axis, 0, 0, tiled=False)  11.8 us
    ppermute x3, starting transfers between devices, shards(): total = total + lax.ppermute(piece, 'head', down).astype(jnp.float32)  5.44 us
    all_gather x1, waiting for transfers between devices, shards(): lax.all_gather(jnp.concatenate([w_query, w_key, w_value, w_gate, w_out],...  5.13 us
    ppermute x3, waiting for transfers between devices, shards(): pieces.append(lax.ppermute(piece, 'head', across))  5.13 us
    ppermute x3, waiting for transfers between devices, shards(): total = total + lax.ppermute(piece, 'head', down).astype(jnp.float32)  4.75 us
    broadcast_in_dim x3, local copies, waits for them, and re-layouts, gather_by_exchange(): copies = jnp.broadcast_to(part[None], (count,) + part.shape)  4.11 us
    ppermute x3, starting transfers between devices, shards(): weights_in.append(lax.ppermute(rows_mine, 'head', across))  3.83 us
  transfers between devices with their start and end apart: 12, of which 9 were waited for; matrix products, arithmetic and copies ran while one was open for 8% of the time, Pallas kernels for 0%

profile of v4, /device:TPU:6, one launch (start us, length us, event | category | flops | bytes accessed | tf_op | source)
XLA Modules:
  0.0 121.9 jit_solution(12966053454798614143)
XLA Ops:
  6.5 0.8 constant_dynamic-update-slice_fusion.4
  7.3 0.8 constant_dynamic-update-slice_fusion.3
  8.1 0.8 constant_dynamic-update-slice_fusion.2
  8.8 0.8 constant_dynamic-update-slice_fusion.1
  9.6 0.8 constant_dynamic-update-slice_fusion
  10.4 0.7 copy-done
  11.1 2.5 %broadcast_in_dim.42 = bf16[16,32,2048]{2,1,0:T(8,128)(2,1)} broadcast(bf16[32,2048]{1,0:T(8,128)(2,1)} %param.7), dimensions={1,2} | broadcast | bytes 2228224 | tf_op jit(solution)/shard_map/broadcast_in_dim | solution.py:13
  13.5 7.6 %all-to-all-start = ((bf16[16,32,2048]{2,1,0:T(8,128)(2,1)}), bf16[16,32,2048]{2,1,0:T(8,128)(2,1)S(1)}, u32[]{:S(2)}, u32[]{:S(2)}) async-start(bf16[16,32,2048]{2,1,0:T(8,128)(2,1)} %broadcast_in_dim.42), calls=%async_computation | async-start | bytes 4194304 | tf_op jit(solution)/shard_map/all_to_all | solution.py:14
  21.1 0.6 reduce_sum.45
  21.7 0.3 reduce-window.6
  22.0 0.2 slice_reduce_fusion.1
  22.2 0.2 reduce-window.9
  22.4 0.6 slice.61
  23.1 0.6 slice.60
  25.1 24.3 %all-to-all-done = bf16[16,32,2048]{2,1,0:T(8,128)(2,1)S(1)} async-done(((bf16[16,32,2048]{2,1,0:T(8,128)(2,1)}), bf16[16,32,2048]{2,1,0:T(8,128)(2,1)S(1)}, u32[]{:S(2)}, u32[]{:S(2)}) %all-to-all-start) | async-done | bytes 2097184 | tf_op jit(solution)/shard_map/all_to_all | solution.py:14
  49.4 5.1 %all-gather.2.cloned.1.call-done = bf16[2048,640]{1,0:T(8,128)(2,1)} async-done(((bf16[128,640]{1,0:T(8,128)(2,1)}), bf16[2048,640]{1,0:T(8,128)(2,1)}) %all-gather.2.cloned.1.call-update) | async-done | bytes 2621456 | tf_op jit(solution)/shard_map/all_gather | solution.py:35
  54.5 2.8 %fusion.58 = (bf16[512,512]{1,0:T(8,128)(2,1)S(1)}, f32[512,512]{1,0:T(8,128)S(1)}) fusion(bf16[512,2048]{1,0:T(8,128)(2,1)S(1)} %bitcast.107, bf16[2048,640]{1,0:T(8,128)(2,1)} %all-gather.2.cloned.1.call-done), kind=kOutput, calls=%fused_computation.90 | convolution fusion | flops 1074003968 | bytes 5767168 | tf_op jit(solution)/shard_map/dot_general | solution.py:41
  57.4 0.3 fusion.19
  57.7 0.6 pad_bitcast_fusion
  58.3 1.1 broadcast_in_dim.47
  59.4 4.3 %all-to-all-start.1 = ((f32[16,1,136,128]{3,2,1,0:T(8,128)}), f32[16,1,136,128]{3,2,1,0:T(8,128)S(1)}, u32[]{:S(2)}, u32[]{:S(2)}) async-start(f32[16,1,136,128]{3,2,1,0:T(8,128)} %broadcast_in_dim.47), calls=%async_computation.1 | async-start | bytes 2228224 | tf_op jit(solution)/shard_map/all_to_all | solution.py:14
  63.7 0.6 slice.59
  64.3 0.6 slice.58
  66.1 1.1 slice.64
  67.2 2.9 %collective-permute-start.3 = (bf16[16,128,128]{2,1,0:T(8,128)(2,1)S(1)}, bf16[16,128,128]{2,1,0:T(8,128)(2,1)}, u32[]{:S(2)}, u32[]{:S(2)}) collective-permute-start(bf16[16,128,128]{2,1,0:T(8,128)(2,1)S(1)} %bitcast.111), channel_id=1, source_target_pairs={{0,1},{1,2},{2,3},{3,0},{4,5},{5,6},{6,7},{7,4},{8,9},{9,10},{10,1... | collective-permute-start | bytes 1572872 | tf_op jit(solution)/shard_map/ppermute | solution.py:116
  70.1 0.1 collective-permute-start.4
  70.2 0.8 collective-permute-start.5
  71.1 0.5 fusion.17
  71.6 20.1 %all-to-all-done.1 = f32[16,1,136,128]{3,2,1,0:T(8,128)S(1)} async-done(((f32[16,1,136,128]{3,2,1,0:T(8,128)}), f32[16,1,136,128]{3,2,1,0:T(8,128)S(1)}, u32[]{:S(2)}, u32[]{:S(2)}) %all-to-all-start.1) | async-done | bytes 1114144 | tf_op jit(solution)/shard_map/all_to_all | solution.py:14
  91.7 0.2 slice_reduce_fusion
  92.0 0.1 fusion.20
  92.1 0.5 fusion.59
  92.7 0.2 fusion.31
  92.9 0.2 fusion.34
  93.2 2.9 %collective-permute-start = (bf16[4,32,128]{2,1,0:T(8,128)(2,1)S(1)}, bf16[4,32,128]{2,1,0:T(8,128)(2,1)S(1)}, u32[]{:S(2)}, u32[]{:S(2)}) collective-permute-start(bf16[4,32,128]{2,1,0:T(8,128)(2,1)S(1)} %get-tuple-element.40), channel_id=1, source_target_pairs={{0,1},{1,2},{2,3},{3,0},{4,5},{5,6},{6,7},{7,4},{8,9},{9,10},{10,1... | collective-permute-start | bytes 98312 | tf_op jit(solution)/shard_map/ppermute | solution.py:115
  96.0 0.1 collective-permute-start.1
  96.2 0.8 collective-permute-start.2
  97.0 0.6 collective-permute-done
  97.6 3.9 %collective-permute-done.1 = bf16[4,32,128]{2,1,0:T(8,128)(2,1)S(1)} collective-permute-done((bf16[4,32,128]{2,1,0:T(8,128)(2,1)S(1)}, bf16[4,32,128]{2,1,0:T(8,128)(2,1)S(1)}, u32[]{:S(2)}, u32[]{:S(2)}) %collective-permute-start.1) | collective-permute-done | bytes 32800 | tf_op jit(solution)/shard_map/ppermute | solution.py:115
  101.6 0.6 collective-permute-done.2
  102.1 1.8 %fusion.15 = bf16[4,16,4,8,128]{4,3,2,1,0:T(8,128)(2,1)S(1)} fusion(bf16[1,16,128,128]{3,2,0,1:T(8,128)(2,1)} %bitcast.38, bf16[1,16,128,128]{3,2,0,1:T(8,128)(2,1)} %bitcast.37, bf16[1,16,128,128]{3,2,0,1:T(8,128)(2,1)} %bitcast.35, bf16[1,16,128,128]{3,2,0,1:T(8,128)(2,1)S(1)} %bitcast.114, bf16[1,4,32,128]{3,2,0,1:T(8,128)(2,1)S(1)} %bitcast.123, ...), kind=kOutput, calls=%fused_computation.15 | convolution fusion | flops 277610496 | bytes 2752512 | tf_op jit(solution)/shard_map/syfr,skrc->yfkc/dot_general | solution.py:117
  104.1 1.0 collective-permute-start.6
  105.2 2.7 %collective-permute-start.7 = (bf16[32,2048]{1,0:T(8,128)(2,1)S(1)}, bf16[32,2048]{1,0:T(8,128)(2,1)S(1)}, u32[]{:S(2)}, u32[]{:S(2)}) collective-permute-start(bf16[32,2048]{1,0:T(8,128)(2,1)S(1)} %get-tuple-element.25), channel_id=1, source_target_pairs={{0,8},{1,9},{2,10},{3,11},{4,12},{5,13},{6,14},{7,15},{8,0},{9,1},... | collective-permute-start | bytes 393224 | tf_op jit(solution)/shard_map/ppermute | solution.py:128
  107.8 1.7 %collective-permute-start.8 = (bf16[32,2048]{1,0:T(8,128)(2,1)S(1)}, bf16[32,2048]{1,0:T(8,128)(2,1)S(1)}, u32[]{:S(2)}, u32[]{:S(2)}) collective-permute-start(bf16[32,2048]{1,0:T(8,128)(2,1)S(1)} %get-tuple-element.24), channel_id=1, source_target_pairs={{0,12},{1,13},{2,14},{3,15},{4,0},{5,1},{6,2},{7,3},{8,4},{9,5},{1... | collective-permute-start | bytes 393224 | tf_op jit(solution)/shard_map/ppermute | solution.py:128
  109.6 1.8 %collective-permute-done.6 = bf16[32,2048]{1,0:T(8,128)(2,1)S(1)} collective-permute-done((bf16[32,2048]{1,0:T(8,128)(2,1)S(1)}, bf16[32,2048]{1,0:T(8,128)(2,1)S(1)}, u32[]{:S(2)}, u32[]{:S(2)}) %collective-permute-start.6) | collective-permute-done | bytes 131104 | tf_op jit(solution)/shard_map/ppermute | solution.py:128
  111.4 2.8 %collective-permute-done.7 = bf16[32,2048]{1,0:T(8,128)(2,1)S(1)} collective-permute-done((bf16[32,2048]{1,0:T(8,128)(2,1)S(1)}, bf16[32,2048]{1,0:T(8,128)(2,1)S(1)}, u32[]{:S(2)}, u32[]{:S(2)}) %collective-permute-start.7) | collective-permute-done | bytes 131104 | tf_op jit(solution)/shard_map/ppermute | solution.py:128
  114.1 0.2 collective-permute-done.8
  114.3 0.7 fusion.29
  (24 shorter events, 0.5 us)
Async XLA Ops:
  6.5 48.0 %all-gather.2.cloned.1.call-start = ((), (), s32[]{:S(2)}) async-start(), calls=%async_computation.2 | async-start | bytes 2785280 | tf_op jit(solution)/shard_map/all_gather | solution.py:35
  10.4 0.7 copy-start
  13.5 7.6 %copy-start.3 = (f32[512,1]{0,1:T(1,128)S(1)}, f32[512,1]{0,1:T(1,128)}, u32[]{:S(2)}) copy-start(f32[512,1]{0,1:T(1,128)} %param.8) | copy-start | bytes 6148
  13.5 35.8 %all-to-all-start = ((bf16[16,32,2048]{2,1,0:T(8,128)(2,1)}), bf16[16,32,2048]{2,1,0:T(8,128)(2,1)S(1)}, u32[]{:S(2)}, u32[]{:S(2)}) async-start(bf16[16,32,2048]{2,1,0:T(8,128)(2,1)} %broadcast_in_dim.42), calls=%async_computation | async-start | bytes 4194304 | tf_op jit(solution)/shard_map/all_to_all | solution.py:14
  57.4 0.9 copy-start.1
  59.4 11.7 %copy-start.2 = (bf16[512,512]{1,0:T(8,128)(2,1)S(1)}, bf16[512,512]{1,0:T(8,128)(2,1)}, u32[]{:S(2)}) copy-start(bf16[512,512]{1,0:T(8,128)(2,1)} %copy-done.1) | copy-start | bytes 1572868
  59.4 32.3 %all-to-all-start.1 = ((f32[16,1,136,128]{3,2,1,0:T(8,128)}), f32[16,1,136,128]{3,2,1,0:T(8,128)S(1)}, u32[]{:S(2)}, u32[]{:S(2)}) async-start(f32[16,1,136,128]{3,2,1,0:T(8,128)} %broadcast_in_dim.47), calls=%async_computation.1 | async-start | bytes 2228224 | tf_op jit(solution)/shard_map/all_to_all | solution.py:14
  67.2 29.0 %collective-permute-start.3 = (bf16[16,128,128]{2,1,0:T(8,128)(2,1)S(1)}, bf16[16,128,128]{2,1,0:T(8,128)(2,1)}, u32[]{:S(2)}, u32[]{:S(2)}) collective-permute-start(bf16[16,128,128]{2,1,0:T(8,128)(2,1)S(1)} %bitcast.111), channel_id=1, source_target_pairs={{0,1},{1,2},{2,3},{3,0},{4,5},{5,6},{6,7},{7,4},{8,9},{9,10},{10,1... | collective-permute-start | bytes 1572872 | tf_op jit(solution)/shard_map/ppermute | solution.py:116
  70.1 26.9 %collective-permute-start.4 = (bf16[16,128,128]{2,1,0:T(8,128)(2,1)S(1)}, bf16[16,128,128]{2,1,0:T(8,128)(2,1)}, u32[]{:S(2)}, u32[]{:S(2)}) collective-permute-start(bf16[16,128,128]{2,1,0:T(8,128)(2,1)S(1)} %bitcast.112), channel_id=1, source_target_pairs={{0,2},{1,3},{2,0},{3,1},{4,6},{5,7},{6,4},{7,5},{8,10},{9,11},{10,... | collective-permute-start | bytes 1572872 | tf_op jit(solution)/shard_map/ppermute | solution.py:116
  70.2 26.8 %collective-permute-start.5 = (bf16[16,128,128]{2,1,0:T(8,128)(2,1)S(1)}, bf16[16,128,128]{2,1,0:T(8,128)(2,1)}, u32[]{:S(2)}, u32[]{:S(2)}) collective-permute-start(bf16[16,128,128]{2,1,0:T(8,128)(2,1)S(1)} %bitcast.113), channel_id=1, source_target_pairs={{0,3},{1,0},{2,1},{3,2},{4,7},{5,4},{6,5},{7,6},{8,11},{9,8},{10,9... | collective-permute-start | bytes 1572872 | tf_op jit(solution)/shard_map/ppermute | solution.py:116
  93.2 4.5 %collective-permute-start = (bf16[4,32,128]{2,1,0:T(8,128)(2,1)S(1)}, bf16[4,32,128]{2,1,0:T(8,128)(2,1)S(1)}, u32[]{:S(2)}, u32[]{:S(2)}) collective-permute-start(bf16[4,32,128]{2,1,0:T(8,128)(2,1)S(1)} %get-tuple-element.40), channel_id=1, source_target_pairs={{0,1},{1,2},{2,3},{3,0},{4,5},{5,6},{6,7},{7,4},{8,9},{9,10},{10,1... | collective-permute-start | bytes 98312 | tf_op jit(solution)/shard_map/ppermute | solution.py:115
  96.0 5.5 %collective-permute-start.1 = (bf16[4,32,128]{2,1,0:T(8,128)(2,1)S(1)}, bf16[4,32,128]{2,1,0:T(8,128)(2,1)S(1)}, u32[]{:S(2)}, u32[]{:S(2)}) collective-permute-start(bf16[4,32,128]{2,1,0:T(8,128)(2,1)S(1)} %get-tuple-element.38), channel_id=1, source_target_pairs={{0,2},{1,3},{2,0},{3,1},{4,6},{5,7},{6,4},{7,5},{8,10},{9,11},{10,... | collective-permute-start | bytes 98312 | tf_op jit(solution)/shard_map/ppermute | solution.py:115
  96.2 6.0 %collective-permute-start.2 = (bf16[4,32,128]{2,1,0:T(8,128)(2,1)S(1)}, bf16[4,32,128]{2,1,0:T(8,128)(2,1)S(1)}, u32[]{:S(2)}, u32[]{:S(2)}) collective-permute-start(bf16[4,32,128]{2,1,0:T(8,128)(2,1)S(1)} %get-tuple-element.36), channel_id=1, source_target_pairs={{0,3},{1,0},{2,1},{3,2},{4,7},{5,4},{6,5},{7,6},{8,11},{9,8},{10,9... | collective-permute-start | bytes 98312 | tf_op jit(solution)/shard_map/ppermute | solution.py:115
  104.1 7.2 %collective-permute-start.6 = (bf16[32,2048]{1,0:T(8,128)(2,1)S(1)}, bf16[32,2048]{1,0:T(8,128)(2,1)S(1)}, u32[]{:S(2)}, u32[]{:S(2)}) collective-permute-start(bf16[32,2048]{1,0:T(8,128)(2,1)S(1)} %get-tuple-element.23), channel_id=1, source_target_pairs={{0,4},{1,5},{2,6},{3,7},{4,8},{5,9},{6,10},{7,11},{8,12},{9,13},{1... | collective-permute-start | bytes 393224 | tf_op jit(solution)/shard_map/ppermute | solution.py:128
  105.2 9.0 %collective-permute-start.7 = (bf16[32,2048]{1,0:T(8,128)(2,1)S(1)}, bf16[32,2048]{1,0:T(8,128)(2,1)S(1)}, u32[]{:S(2)}, u32[]{:S(2)}) collective-permute-start(bf16[32,2048]{1,0:T(8,128)(2,1)S(1)} %get-tuple-element.25), channel_id=1, source_target_pairs={{0,8},{1,9},{2,10},{3,11},{4,12},{5,13},{6,14},{7,15},{8,0},{9,1},... | collective-permute-start | bytes 393224 | tf_op jit(solution)/shard_map/ppermute | solution.py:128
  107.8 6.5 %collective-permute-start.8 = (bf16[32,2048]{1,0:T(8,128)(2,1)S(1)}, bf16[32,2048]{1,0:T(8,128)(2,1)S(1)}, u32[]{:S(2)}, u32[]{:S(2)}) collective-permute-start(bf16[32,2048]{1,0:T(8,128)(2,1)S(1)} %get-tuple-element.24), channel_id=1, source_target_pairs={{0,12},{1,13},{2,14},{3,15},{4,0},{5,1},{6,2},{7,3},{8,4},{9,5},{1... | collective-permute-start | bytes 393224 | tf_op jit(solution)/shard_map/ppermute | solution.py:128
Sparse Core Ops, SparseCore 0:
  11.2 43.2 all-gather.1

commit v5 on v4

--- a/solution.py
+++ b/solution.py
@@ -16,11 +16,22 @@
 
 def prior_state(local_final, log_total, axis):
     heads_here = local_final.shape[0]
-    extra = jnp.broadcast_to(log_total[:, None, None], (heads_here, PAD_ROWS, HEAD_DIM))
-    packed = jnp.concatenate([local_final, extra], axis=1)
+    high = log_total.astype(jnp.bfloat16)
+    low = (log_total - high.astype(jnp.float32)).astype(jnp.bfloat16)
+    extra = jnp.concatenate(
+        [
+            jnp.broadcast_to(high[:, None, None], (heads_here, 1, HEAD_DIM)),
+            jnp.broadcast_to(low[:, None, None], (heads_here, 1, HEAD_DIM)),
+            jnp.zeros((heads_here, PAD_ROWS - 2, HEAD_DIM), jnp.bfloat16),
+        ],
+        axis=1,
+    )
+    packed = jnp.concatenate([local_final.astype(jnp.bfloat16), extra], axis=1)
     gathered = gather_by_exchange(packed, axis)
-    finals = gathered[:, :, :HEAD_DIM, :]
-    totals = gathered[:, :, HEAD_DIM, 0]
+    finals = gathered[:, :, :HEAD_DIM, :].astype(jnp.float32)
+    totals = gathered[:, :, HEAD_DIM, 0].astype(jnp.float32) + gathered[:, :, HEAD_DIM + 1, 0].astype(
+        jnp.float32
+    )
     count = gathered.shape[0]
     mine = lax.axis_index(axis)
     order = jnp.arange(count, dtype=jnp.int32)

time: 123 us -> 120 us (0.976)
  starting transfers between devices: 24.9 us -> 21.9 us
  waiting for transfers between devices: 59.4 us -> 56.9 us
    all_to_all x2, waiting for transfers between devices: 44.3 us -> 31.5 us  [gather_by_exchange(): return lax.all_to_all(copies, axis, 0, 0, tiled=False)]
    ppermute x3, waiting for transfers between devices: 0.01 us -> 12.3 us  [shards(): weights_in.append(lax.ppermute(rows_mine, 'head', across))]
    ppermute x3, waiting for transfers between devices: 5.13 us -> 2.87 us  [shards(): pieces.append(lax.ppermute(piece, 'head', across))]
    ppermute x3, starting transfers between devices: 5.44 us -> 3.4 us  [shards(): total = total + lax.ppermute(piece, 'head', down).astype(jnp.float32)]
    broadcast_in_dim x3 -> x2, local copies, waits for them, and re-layouts: 4.11 us -> 3.36 us  [gather_by_exchange(): copies = jnp.broadcast_to(part[None], (count,) + part.shape)]
where the time goes in v5:
time: 120 us; the launch traced here: 118 us
  waiting for transfers between devices  56.9 us (47%)
  starting transfers between devices  21.9 us (18%)
  between operations  17.4 us (14%)
  local copies, waits for them, and re-layouts  12.8 us (11%)
  matrix products  6.02 us (5%)
  other arithmetic  2.97 us (2%)
    all_to_all x2, waiting for transfers between devices, gather_by_exchange(): return lax.all_to_all(copies, axis, 0, 0, tiled=False)  31.5 us
    ppermute x3, waiting for transfers between devices, shards(): weights_in.append(lax.ppermute(rows_mine, 'head', across))  12.3 us
    all_to_all x2, starting transfers between devices, gather_by_exchange(): return lax.all_to_all(copies, axis, 0, 0, tiled=False)  11.7 us
    ppermute x3, waiting for transfers between devices, shards(): total = total + lax.ppermute(piece, 'head', down).astype(jnp.float32)  5.17 us
    all_gather x1, waiting for transfers between devices, shards(): lax.all_gather(jnp.concatenate([w_query, w_key, w_value, w_gate, w_out],...  5.11 us
    unnamed x12, local copies, waits for them, and re-layouts  4.53 us
    ppermute x3, starting transfers between devices, shards(): weights_in.append(lax.ppermute(rows_mine, 'head', across))  3.83 us
    ppermute x3, starting transfers between devices, shards(): total = total + lax.ppermute(piece, 'head', down).astype(jnp.float32)  3.4 us
  transfers between devices with their start and end apart: 12, of which 9 were waited for; matrix products, arithmetic and copies ran while one was open for 8% of the time, Pallas kernels for 0%

profile of v5, /device:TPU:6, one launch (start us, length us, event | category | flops | bytes accessed | tf_op | source)
XLA Modules:
  0.0 118.1 jit_solution(17337953536917006933)
XLA Ops:
  6.5 0.8 constant_dynamic-update-slice_fusion.4
  7.3 0.8 constant_dynamic-update-slice_fusion.3
  8.1 0.8 constant_dynamic-update-slice_fusion.2
  8.8 0.8 constant_dynamic-update-slice_fusion.1
  9.6 0.8 constant_dynamic-update-slice_fusion
  10.4 0.7 copy-done
  11.1 2.5 %broadcast_in_dim.51 = bf16[16,32,2048]{2,1,0:T(8,128)(2,1)} broadcast(bf16[32,2048]{1,0:T(8,128)(2,1)} %param.7), dimensions={1,2} | broadcast | bytes 2228224 | tf_op jit(solution)/shard_map/broadcast_in_dim | solution.py:13
  13.5 7.6 %all-to-all-start = ((bf16[16,32,2048]{2,1,0:T(8,128)(2,1)}), bf16[16,32,2048]{2,1,0:T(8,128)(2,1)S(1)}, u32[]{:S(2)}, u32[]{:S(2)}) async-start(bf16[16,32,2048]{2,1,0:T(8,128)(2,1)} %broadcast_in_dim.51), calls=%async_computation | async-start | bytes 4194304 | tf_op jit(solution)/shard_map/all_to_all | solution.py:14
  21.1 0.6 reduce_sum.47
  21.7 0.3 reduce-window.6
  22.0 0.2 slice_reduce_fusion
  22.2 0.2 reduce-window.9
  22.4 0.6 slice.65
  23.1 0.6 slice.64
  26.4 23.0 %all-to-all-done = bf16[16,32,2048]{2,1,0:T(8,128)(2,1)S(1)} async-done(((bf16[16,32,2048]{2,1,0:T(8,128)(2,1)}), bf16[16,32,2048]{2,1,0:T(8,128)(2,1)S(1)}, u32[]{:S(2)}, u32[]{:S(2)}) %all-to-all-start) | async-done | bytes 2097184 | tf_op jit(solution)/shard_map/all_to_all | solution.py:14
  49.4 5.1 %all-gather.2.cloned.1.call-done = bf16[2048,640]{1,0:T(8,128)(2,1)} async-done(((bf16[128,640]{1,0:T(8,128)(2,1)}), bf16[2048,640]{1,0:T(8,128)(2,1)}) %all-gather.2.cloned.1.call-update) | async-done | bytes 2621456 | tf_op jit(solution)/shard_map/all_gather | solution.py:46
  54.5 2.8 %fusion.60 = (bf16[512,512]{1,0:T(8,128)(2,1)S(1)}, f32[512,512]{1,0:T(8,128)S(1)}) fusion(bf16[512,2048]{1,0:T(8,128)(2,1)S(1)} %bitcast.110, bf16[2048,640]{1,0:T(8,128)(2,1)} %all-gather.2.cloned.1.call-done), kind=kOutput, calls=%fused_computation.93 | convolution fusion | flops 1074003968 | bytes 5767168 | tf_op jit(solution)/shard_map/dot_general | solution.py:52
  57.3 0.8 copy-done.1
  58.1 0.3 fusion.20
  58.5 0.1 maximum_bitcast_fusion.10
  58.6 0.9 broadcast_in_dim.94
  59.5 4.1 %all-to-all-start.1 = ((bf16[16,1,136,128]{3,2,1,0:T(8,128)(2,1)}), bf16[16,1,136,128]{3,2,1,0:T(8,128)(2,1)S(1)}, u32[]{:S(2)}, u32[]{:S(2)}) async-start(bf16[16,1,136,128]{3,2,1,0:T(8,128)(2,1)} %broadcast_in_dim.94), calls=%async_computation.1 | async-start | bytes 1114112 | tf_op jit(solution)/shard_map/all_to_all | solution.py:14
  63.7 0.7 slice.63
  64.4 0.6 slice.62
  66.3 1.1 slice.69
  67.4 2.9 %collective-permute-start.3 = (bf16[16,128,128]{2,1,0:T(8,128)(2,1)S(1)}, bf16[16,128,128]{2,1,0:T(8,128)(2,1)}, u32[]{:S(2)}, u32[]{:S(2)}) collective-permute-start(bf16[16,128,128]{2,1,0:T(8,128)(2,1)S(1)} %bitcast.114), channel_id=1, source_target_pairs={{0,1},{1,2},{2,3},{3,0},{4,5},{5,6},{6,7},{7,4},{8,9},{9,10},{10,1... | collective-permute-start | bytes 1572872 | tf_op jit(solution)/shard_map/ppermute | solution.py:127
  70.3 0.1 collective-permute-start.4
  70.4 0.8 collective-permute-start.5
  71.2 0.5 fusion.17
  71.8 8.5 %all-to-all-done.1 = bf16[16,1,136,128]{3,2,1,0:T(8,128)(2,1)S(1)} async-done(((bf16[16,1,136,128]{3,2,1,0:T(8,128)(2,1)}), bf16[16,1,136,128]{3,2,1,0:T(8,128)(2,1)S(1)}, u32[]{:S(2)}, u32[]{:S(2)}) %all-to-all-start.1) | async-done | bytes 557088 | tf_op jit(solution)/shard_map/all_to_all | solution.py:14
  80.3 0.2 fusion.57
  80.6 0.2 multiply_reduce_fusion
  80.8 0.5 fusion.61
  81.3 0.2 fusion.31
  81.6 0.2 fusion.34
  81.8 2.9 %collective-permute-start = (bf16[4,32,128]{2,1,0:T(8,128)(2,1)S(1)}, bf16[4,32,128]{2,1,0:T(8,128)(2,1)S(1)}, u32[]{:S(2)}, u32[]{:S(2)}) collective-permute-start(bf16[4,32,128]{2,1,0:T(8,128)(2,1)S(1)} %get-tuple-element.40), channel_id=1, source_target_pairs={{0,1},{1,2},{2,3},{3,0},{4,5},{5,6},{6,7},{7,4},{8,9},{9,10},{10,1... | collective-permute-start | bytes 98312 | tf_op jit(solution)/shard_map/ppermute | solution.py:126
  84.7 0.1 collective-permute-start.1
  84.8 9.5 %collective-permute-done.3 = bf16[16,128,128]{2,1,0:T(8,128)(2,1)} collective-permute-done((bf16[16,128,128]{2,1,0:T(8,128)(2,1)S(1)}, bf16[16,128,128]{2,1,0:T(8,128)(2,1)}, u32[]{:S(2)}, u32[]{:S(2)}) %collective-permute-start.3) | collective-permute-done | bytes 524320 | tf_op jit(solution)/shard_map/ppermute | solution.py:127
  94.3 2.8 %collective-permute-done.5 = bf16[16,128,128]{2,1,0:T(8,128)(2,1)} collective-permute-done((bf16[16,128,128]{2,1,0:T(8,128)(2,1)S(1)}, bf16[16,128,128]{2,1,0:T(8,128)(2,1)}, u32[]{:S(2)}, u32[]{:S(2)}) %collective-permute-start.5) | collective-permute-done | bytes 524320 | tf_op jit(solution)/shard_map/ppermute | solution.py:127
  97.1 0.6 collective-permute-done.1
  97.7 2.3 %collective-permute-done.2 = bf16[4,32,128]{2,1,0:T(8,128)(2,1)S(1)} collective-permute-done((bf16[4,32,128]{2,1,0:T(8,128)(2,1)S(1)}, bf16[4,32,128]{2,1,0:T(8,128)(2,1)S(1)}, u32[]{:S(2)}, u32[]{:S(2)}) %collective-permute-start.2) | collective-permute-done | bytes 32800 | tf_op jit(solution)/shard_map/ppermute | solution.py:126
  99.9 1.8 %fusion.15 = bf16[4,16,4,8,128]{4,3,2,1,0:T(8,128)(2,1)S(1)} fusion(bf16[1,16,128,128]{3,2,0,1:T(8,128)(2,1)} %bitcast.41, bf16[1,16,128,128]{3,2,0,1:T(8,128)(2,1)} %bitcast.40, bf16[1,16,128,128]{3,2,0,1:T(8,128)(2,1)} %bitcast.38, bf16[1,16,128,128]{3,2,0,1:T(8,128)(2,1)S(1)} %bitcast.117, bf16[1,4,32,128]{3,2,0,1:T(8,128)(2,1)S(1)} %bitcast.126, ...), kind=kOutput, calls=%fused_computation.15 | convolution fusion | flops 277610496 | bytes 2752512 | tf_op jit(solution)/shard_map/syfr,skrc->yfkc/dot_general | solution.py:128
  101.9 0.6 collective-permute-start.6
  102.6 1.1 collective-permute-start.7
  103.6 1.7 %collective-permute-start.8 = (bf16[32,2048]{1,0:T(8,128)(2,1)S(1)}, bf16[32,2048]{1,0:T(8,128)(2,1)S(1)}, u32[]{:S(2)}, u32[]{:S(2)}) collective-permute-start(bf16[32,2048]{1,0:T(8,128)(2,1)S(1)} %get-tuple-element.24), channel_id=1, source_target_pairs={{0,12},{1,13},{2,14},{3,15},{4,0},{5,1},{6,2},{7,3},{8,4},{9,5},{1... | collective-permute-start | bytes 393224 | tf_op jit(solution)/shard_map/ppermute | solution.py:139
  105.3 4.5 %collective-permute-done.6 = bf16[32,2048]{1,0:T(8,128)(2,1)S(1)} collective-permute-done((bf16[32,2048]{1,0:T(8,128)(2,1)S(1)}, bf16[32,2048]{1,0:T(8,128)(2,1)S(1)}, u32[]{:S(2)}, u32[]{:S(2)}) %collective-permute-start.6) | collective-permute-done | bytes 131104 | tf_op jit(solution)/shard_map/ppermute | solution.py:139
  109.8 0.7 collective-permute-done.8
  110.5 0.7 fusion.29
  (28 shorter events, 0.7 us)
Async XLA Ops:
  6.5 48.0 %all-gather.2.cloned.1.call-start = ((), (), s32[]{:S(2)}) async-start(), calls=%async_computation.2 | async-start | bytes 2785280 | tf_op jit(solution)/shard_map/all_gather | solution.py:46
  10.4 0.7 copy-start
  13.5 7.6 %copy-start.3 = (f32[512,1]{0,1:T(1,128)S(1)}, f32[512,1]{0,1:T(1,128)}, u32[]{:S(2)}) copy-start(f32[512,1]{0,1:T(1,128)} %param.8) | copy-start | bytes 6148
  13.5 35.8 %all-to-all-start = ((bf16[16,32,2048]{2,1,0:T(8,128)(2,1)}), bf16[16,32,2048]{2,1,0:T(8,128)(2,1)S(1)}, u32[]{:S(2)}, u32[]{:S(2)}) async-start(bf16[16,32,2048]{2,1,0:T(8,128)(2,1)} %broadcast_in_dim.51), calls=%async_computation | async-start | bytes 4194304 | tf_op jit(solution)/shard_map/all_to_all | solution.py:14
  57.3 0.8 copy-start.1
  58.5 12.8 %copy-start.2 = (bf16[512,512]{1,0:T(8,128)(2,1)S(1)}, bf16[512,512]{1,0:T(8,128)(2,1)}, u32[]{:S(2)}) copy-start(bf16[512,512]{1,0:T(8,128)(2,1)} %copy-done.1) | copy-start | bytes 1572868
  59.5 20.8 %all-to-all-start.1 = ((bf16[16,1,136,128]{3,2,1,0:T(8,128)(2,1)}), bf16[16,1,136,128]{3,2,1,0:T(8,128)(2,1)S(1)}, u32[]{:S(2)}, u32[]{:S(2)}) async-start(bf16[16,1,136,128]{3,2,1,0:T(8,128)(2,1)} %broadcast_in_dim.94), calls=%async_computation.1 | async-start | bytes 1114112 | tf_op jit(solution)/shard_map/all_to_all | solution.py:14
  67.4 26.9 %collective-permute-start.3 = (bf16[16,128,128]{2,1,0:T(8,128)(2,1)S(1)}, bf16[16,128,128]{2,1,0:T(8,128)(2,1)}, u32[]{:S(2)}, u32[]{:S(2)}) collective-permute-start(bf16[16,128,128]{2,1,0:T(8,128)(2,1)S(1)} %bitcast.114), channel_id=1, source_target_pairs={{0,1},{1,2},{2,3},{3,0},{4,5},{5,6},{6,7},{7,4},{8,9},{9,10},{10,1... | collective-permute-start | bytes 1572872 | tf_op jit(solution)/shard_map/ppermute | solution.py:127
  70.3 24.0 %collective-permute-start.4 = (bf16[16,128,128]{2,1,0:T(8,128)(2,1)S(1)}, bf16[16,128,128]{2,1,0:T(8,128)(2,1)}, u32[]{:S(2)}, u32[]{:S(2)}) collective-permute-start(bf16[16,128,128]{2,1,0:T(8,128)(2,1)S(1)} %bitcast.115), channel_id=1, source_target_pairs={{0,2},{1,3},{2,0},{3,1},{4,6},{5,7},{6,4},{7,5},{8,10},{9,11},{10,... | collective-permute-start | bytes 1572872 | tf_op jit(solution)/shard_map/ppermute | solution.py:127
  70.4 26.7 %collective-permute-start.5 = (bf16[16,128,128]{2,1,0:T(8,128)(2,1)S(1)}, bf16[16,128,128]{2,1,0:T(8,128)(2,1)}, u32[]{:S(2)}, u32[]{:S(2)}) collective-permute-start(bf16[16,128,128]{2,1,0:T(8,128)(2,1)S(1)} %bitcast.116), channel_id=1, source_target_pairs={{0,3},{1,0},{2,1},{3,2},{4,7},{5,4},{6,5},{7,6},{8,11},{9,8},{10,9... | collective-permute-start | bytes 1572872 | tf_op jit(solution)/shard_map/ppermute | solution.py:127
  81.8 15.3 %collective-permute-start = (bf16[4,32,128]{2,1,0:T(8,128)(2,1)S(1)}, bf16[4,32,128]{2,1,0:T(8,128)(2,1)S(1)}, u32[]{:S(2)}, u32[]{:S(2)}) collective-permute-start(bf16[4,32,128]{2,1,0:T(8,128)(2,1)S(1)} %get-tuple-element.40), channel_id=1, source_target_pairs={{0,1},{1,2},{2,3},{3,0},{4,5},{5,6},{6,7},{7,4},{8,9},{9,10},{10,1... | collective-permute-start | bytes 98312 | tf_op jit(solution)/shard_map/ppermute | solution.py:126
  84.7 13.0 %collective-permute-start.1 = (bf16[4,32,128]{2,1,0:T(8,128)(2,1)S(1)}, bf16[4,32,128]{2,1,0:T(8,128)(2,1)S(1)}, u32[]{:S(2)}, u32[]{:S(2)}) collective-permute-start(bf16[4,32,128]{2,1,0:T(8,128)(2,1)S(1)} %get-tuple-element.38), channel_id=1, source_target_pairs={{0,2},{1,3},{2,0},{3,1},{4,6},{5,7},{6,4},{7,5},{8,10},{9,11},{10,... | collective-permute-start | bytes 98312 | tf_op jit(solution)/shard_map/ppermute | solution.py:126
  94.3 5.7 %collective-permute-start.2 = (bf16[4,32,128]{2,1,0:T(8,128)(2,1)S(1)}, bf16[4,32,128]{2,1,0:T(8,128)(2,1)S(1)}, u32[]{:S(2)}, u32[]{:S(2)}) collective-permute-start(bf16[4,32,128]{2,1,0:T(8,128)(2,1)S(1)} %get-tuple-element.36), channel_id=1, source_target_pairs={{0,3},{1,0},{2,1},{3,2},{4,7},{5,4},{6,5},{7,6},{8,11},{9,8},{10,9... | collective-permute-start | bytes 98312 | tf_op jit(solution)/shard_map/ppermute | solution.py:126
  101.9 7.9 %collective-permute-start.6 = (bf16[32,2048]{1,0:T(8,128)(2,1)S(1)}, bf16[32,2048]{1,0:T(8,128)(2,1)S(1)}, u32[]{:S(2)}, u32[]{:S(2)}) collective-permute-start(bf16[32,2048]{1,0:T(8,128)(2,1)S(1)} %get-tuple-element.23), channel_id=1, source_target_pairs={{0,4},{1,5},{2,6},{3,7},{4,8},{5,9},{6,10},{7,11},{8,12},{9,13},{1... | collective-permute-start | bytes 393224 | tf_op jit(solution)/shard_map/ppermute | solution.py:139
  102.6 7.3 %collective-permute-start.7 = (bf16[32,2048]{1,0:T(8,128)(2,1)S(1)}, bf16[32,2048]{1,0:T(8,128)(2,1)S(1)}, u32[]{:S(2)}, u32[]{:S(2)}) collective-permute-start(bf16[32,2048]{1,0:T(8,128)(2,1)S(1)} %get-tuple-element.25), channel_id=1, source_target_pairs={{0,8},{1,9},{2,10},{3,11},{4,12},{5,13},{6,14},{7,15},{8,0},{9,1},... | collective-permute-start | bytes 393224 | tf_op jit(solution)/shard_map/ppermute | solution.py:139
  103.6 6.9 %collective-permute-start.8 = (bf16[32,2048]{1,0:T(8,128)(2,1)S(1)}, bf16[32,2048]{1,0:T(8,128)(2,1)S(1)}, u32[]{:S(2)}, u32[]{:S(2)}) collective-permute-start(bf16[32,2048]{1,0:T(8,128)(2,1)S(1)} %get-tuple-element.24), channel_id=1, source_target_pairs={{0,12},{1,13},{2,14},{3,15},{4,0},{5,1},{6,2},{7,3},{8,4},{9,5},{1... | collective-permute-start | bytes 393224 | tf_op jit(solution)/shard_map/ppermute | solution.py:139
Sparse Core Ops, SparseCore 0:
  11.2 43.2 all-gather.1

commit v6 on v5

--- a/solution.py
+++ b/solution.py
@@ -118,13 +118,23 @@
     row, col = me // side, me % side
     rows_mine = out_blocks
     by_owner = gated.reshape(side, side, local_len // heads, head_width)
+    units = lax.axis_size("tm")
+    half = rows_mine.shape[0] // 2
+    parity = lax.axis_index("tm") % 2
+    own_half = lax.dynamic_slice_in_dim(rows_mine, parity * half, half, axis=0)
     pieces = [lax.dynamic_index_in_dim(by_owner, col, axis=1, keepdims=False)]
-    weights_in = [rows_mine]
+    fetched = []
     for shift in range(1, side):
         across = [(h, (h // side) * side + (h % side + shift) % side) for h in range(heads)]
         piece = lax.dynamic_index_in_dim(by_owner, (col + shift) % side, axis=1, keepdims=False)
         pieces.append(lax.ppermute(piece, "head", across))
-        weights_in.append(lax.ppermute(rows_mine, "head", across))
+        fetched.append(lax.ppermute(own_half, "head", across))
+    fetched = jnp.stack(fetched)
+    swapped = lax.ppermute(fetched, "tm", [(t, t ^ 1) for t in range(units)])
+    first = jnp.where(parity == 0, fetched, swapped)
+    second = jnp.where(parity == 0, swapped, fetched)
+    remote = jnp.concatenate([first, second], axis=1)
+    weights_in = [rows_mine] + [remote[s] for s in range(side - 1)]
     partial = jnp.einsum(
         "syfr,skrc->yfkc",
         jnp.stack(pieces),

time: 120 us -> 115 us (0.958)
  waiting for transfers between devices: 56.9 us -> 49.7 us
  matrix products: 6.02 us -> 7.4 us
    all_to_all x2, waiting for transfers between devices: 31.5 us -> 23 us  [gather_by_exchange(): return lax.all_to_all(copies, axis, 0, 0, tiled=False)]
    ppermute x3, starting transfers between devices: 3.4 us -> 5.21 us  [shards(): total = total + lax.ppermute(piece, 'head', down).astype(jnp.float32)]
    ppermute x3, waiting for transfers between devices: 2.87 us -> 4.5 us  [shards(): pieces.append(lax.ppermute(piece, 'head', across))]
    dot_general x1, matrix products: 1.8 us -> 0.45 us  [shards(): jnp.einsum('syfr,skrc->yfkc', jnp.stack(pieces), jnp.stack(weights_in), p...]
    unnamed x12 -> x10, local copies, waits for them, and re-layouts: 4.53 us -> 3.75 us
    ppermute x3 -> x4, waiting for transfers between devices: 12.3 us -> 12.8 us  [the longest x3 12.8 us: shards(): fetched.append(lax.ppermute(own_half, 'head', across))]
    ppermute x3 -> x4, starting transfers between devices: 3.83 us -> 3.92 us  [the longest x3 3.83 us: shards(): fetched.append(lax.ppermute(own_half, 'head', across))]
  transfers between devices with their start and end apart: 12 -> 13, of which waited for: 9 -> 10; matrix products, arithmetic and copies ran while one was open for 8% -> 11% of each run, Pallas kernels for 0% -> 0%
where the time goes in v6:
time: 115 us; the launch traced here: 114 us
  waiting for transfers between devices  49.7 us (43%)
  starting transfers between devices  22.9 us (20%)
  between operations  17.6 us (15%)
  local copies, waits for them, and re-layouts  12 us (10%)
  matrix products  7.4 us (6%)
  other arithmetic  4.12 us (4%)
    all_to_all x2, waiting for transfers between devices, gather_by_exchange(): return lax.all_to_all(copies, axis, 0, 0, tiled=False)  23 us
    ppermute x3, waiting for transfers between devices, shards(): fetched.append(lax.ppermute(own_half, 'head', across))  12.8 us
    all_to_all x2, starting transfers between devices, gather_by_exchange(): return lax.all_to_all(copies, axis, 0, 0, tiled=False)  11.7 us
    ppermute x3, starting transfers between devices, shards(): total = total + lax.ppermute(piece, 'head', down).astype(jnp.float32)  5.21 us
    all_gather x1, waiting for transfers between devices, shards(): lax.all_gather(jnp.concatenate([w_query, w_key, w_value, w_gate, w_out],...  5.11 us
    ppermute x3, waiting for transfers between devices, shards(): pieces.append(lax.ppermute(piece, 'head', across))  4.5 us
    ppermute x3, waiting for transfers between devices, shards(): total = total + lax.ppermute(piece, 'head', down).astype(jnp.float32)  4.22 us
    dot_general x1, matrix products, shards(): projected = jnp.dot(frames_here, joined, preferred_element_type=jnp.float32)  3.83 us
  transfers between devices with their start and end apart: 13, of which 10 were waited for; matrix products, arithmetic and copies ran while one was open for 11% of the time, Pallas kernels for 0%

profile of v6, /device:TPU:6, one launch (start us, length us, event | category | flops | bytes accessed | tf_op | source)
XLA Modules:
  0.0 113.7 jit_solution(16456496478118209319)
XLA Ops:
  6.5 0.8 constant_dynamic-update-slice_fusion.4
  7.3 0.8 constant_dynamic-update-slice_fusion.3
  8.1 0.8 constant_dynamic-update-slice_fusion.2
  8.8 0.8 constant_dynamic-update-slice_fusion.1
  9.6 0.8 constant_dynamic-update-slice_fusion
  10.4 0.7 copy-done
  11.1 2.5 %broadcast_in_dim.51 = bf16[16,32,2048]{2,1,0:T(8,128)(2,1)} broadcast(bf16[32,2048]{1,0:T(8,128)(2,1)} %param.7), dimensions={1,2} | broadcast | bytes 2228224 | tf_op jit(solution)/shard_map/broadcast_in_dim | solution.py:13
  13.5 7.6 %all-to-all-start = ((bf16[16,32,2048]{2,1,0:T(8,128)(2,1)}), bf16[16,32,2048]{2,1,0:T(8,128)(2,1)S(1)}, u32[]{:S(2)}, u32[]{:S(2)}) async-start(bf16[16,32,2048]{2,1,0:T(8,128)(2,1)} %broadcast_in_dim.51), calls=%async_computation | async-start | bytes 4194304 | tf_op jit(solution)/shard_map/all_to_all | solution.py:14
  21.1 0.6 reduce_sum.47
  21.7 0.3 reduce-window.6
  22.0 0.2 slice_reduce_fusion
  22.2 0.2 reduce-window.9
  22.4 0.6 slice.69
  23.1 0.6 slice.68
  26.4 23.0 %all-to-all-done = bf16[16,32,2048]{2,1,0:T(8,128)(2,1)S(1)} async-done(((bf16[16,32,2048]{2,1,0:T(8,128)(2,1)}), bf16[16,32,2048]{2,1,0:T(8,128)(2,1)S(1)}, u32[]{:S(2)}, u32[]{:S(2)}) %all-to-all-start) | async-done | bytes 2097184 | tf_op jit(solution)/shard_map/all_to_all | solution.py:14
  49.4 5.1 %all-gather.2.cloned.1.call-done = bf16[2048,640]{1,0:T(8,128)(2,1)} async-done(((bf16[128,640]{1,0:T(8,128)(2,1)}), bf16[2048,640]{1,0:T(8,128)(2,1)}) %all-gather.2.cloned.1.call-update) | async-done | bytes 2621456 | tf_op jit(solution)/shard_map/all_gather | solution.py:46
  54.5 3.8 %fusion.58 = (bf16[512,512]{1,0:T(8,128)(2,1)S(1)}, f32[512,512]{1,0:T(8,128)}) fusion(bf16[512,2048]{1,0:T(8,128)(2,1)S(1)} %bitcast.110, bf16[2048,640]{1,0:T(8,128)(2,1)} %all-gather.2.cloned.1.call-done), kind=kOutput, calls=%fused_computation.95 | convolution fusion | flops 1074003968 | bytes 5767168 | tf_op jit(solution)/shard_map/dot_general | solution.py:52
  58.3 0.3 fusion.18
  58.8 0.9 broadcast_in_dim.94
  59.7 4.1 %all-to-all-start.1 = ((bf16[16,1,136,128]{3,2,1,0:T(8,128)(2,1)}), bf16[16,1,136,128]{3,2,1,0:T(8,128)(2,1)S(1)}, u32[]{:S(2)}, u32[]{:S(2)}) async-start(bf16[16,1,136,128]{3,2,1,0:T(8,128)(2,1)} %broadcast_in_dim.94), calls=%async_computation.1 | async-start | bytes 1114112 | tf_op jit(solution)/shard_map/all_to_all | solution.py:14
  64.0 0.6 slice.67
  64.6 0.6 slice.66
  66.6 1.1 slice.73
  67.8 2.9 %collective-permute-start.3 = (bf16[8,128,128]{2,1,0:T(8,128)(2,1)S(1)}, bf16[8,128,128]{2,1,0:T(8,128)(2,1)S(1)}, u32[]{:S(2)}, u32[]{:S(2)}) collective-permute-start(bf16[8,128,128]{2,1,0:T(8,128)(2,1)S(1)} %constant_dynamic-slice_fusion), channel_id=1, source_target_pairs={{0,1},{1,2},{2,3},{3,0},{4,5},{5,6},{6,7},{7,4},{8,9},{9,10},{10,1... | collective-permute-start | bytes 786440 | tf_op jit(solution)/shard_map/ppermute | solution.py:131
  70.6 0.1 collective-permute-start.4
  70.8 0.8 collective-permute-start.5
  71.6 1.2 %fusion.15 = f32[1,512,1,128]{3,1,2,0:T(8,128)} fusion(f32[512]{0:T(512)S(1)} %get-tuple-element.22, bf16[512,512]{1,0:T(8,128)(2,1)S(1)} %get-tuple-element.43), kind=kOutput, calls=%fused_computation.16 | convolution fusion | flops 135528448 | bytes 659456 | tf_op jit(solution)/shard_map/while/body/eval_jaxpr/hts,shd->thd/dot_general | solution.py:88
  72.8 9.4 %collective-permute-done.3 = bf16[8,128,128]{2,1,0:T(8,128)(2,1)S(1)} collective-permute-done((bf16[8,128,128]{2,1,0:T(8,128)(2,1)S(1)}, bf16[8,128,128]{2,1,0:T(8,128)(2,1)S(1)}, u32[]{:S(2)}, u32[]{:S(2)}) %collective-permute-start.3) | collective-permute-done | bytes 262176 | tf_op jit(solution)/shard_map/ppermute | solution.py:131
  82.3 3.4 %collective-permute-done.5 = bf16[8,128,128]{2,1,0:T(8,128)(2,1)S(1)} collective-permute-done((bf16[8,128,128]{2,1,0:T(8,128)(2,1)S(1)}, bf16[8,128,128]{2,1,0:T(8,128)(2,1)S(1)}, u32[]{:S(2)}, u32[]{:S(2)}) %collective-permute-start.5) | collective-permute-done | bytes 262176 | tf_op jit(solution)/shard_map/ppermute | solution.py:131
  85.9 0.2 fusion.55
  86.2 0.2 multiply_reduce_fusion
  86.4 1.5 %fusion.59 = (f32[512]{0:T(512)S(1)}, f32[1,512,1,128]{3,1,2,0:T(8,128)S(1)}) fusion(f32[1,512,1,128]{3,1,2,0:T(8,128)} %fusion.15, f32[512]{0:T(512)S(1)} %exp.53, bf16[512,512]{1,0:T(8,128)(2,1)} %copy-done.1, f32[128,128]{1,0:T(8,128)S(1)} %multiply_reduce_fusion, f32[]{:T(128)} %bitcast.11), kind=kOutput, calls=%fused_computation.96 | convolution fusion | flops 100941312 | bytes 725504 | tf_op jit(solution)/shard_map/cthd,chde->cthe/dot_general | solution.py:105
  87.9 0.2 fusion.29
  88.2 1.2 %fusion.32 = bf16[512,128]{1,0:T(8,128)(2,1)S(1)} fusion(f32[1,512,1,128]{3,1,2,0:T(8,128)S(1)} %get-tuple-element.46, f32[512,512]{1,0:T(8,128)} %get-tuple-element.44, f32[512]{0:T(512)S(1)} %add_sqrt_fusion, f32[512]{0:T(512)S(1)} %broadcast_multiply_fusion), kind=kLoop, calls=%fused_computation.43 | loop fusion | flops 524288 | bytes 659456 | tf_op jit(solution)/shard_map/convert_element_type | solution.py:112
  89.4 1.0 collective-permute-start
  90.3 0.3 collective-permute-start.1
  90.6 0.8 collective-permute-start.2
  91.6 2.0 %collective-permute-done = bf16[4,32,128]{2,1,0:T(8,128)(2,1)S(1)} collective-permute-done((bf16[4,32,128]{2,1,0:T(8,128)(2,1)S(1)}, bf16[4,32,128]{2,1,0:T(8,128)(2,1)S(1)}, u32[]{:S(2)}, u32[]{:S(2)}) %collective-permute-start) | collective-permute-done | bytes 32800 | tf_op jit(solution)/shard_map/ppermute | solution.py:130
  93.6 2.2 %collective-permute-done.1 = bf16[4,32,128]{2,1,0:T(8,128)(2,1)S(1)} collective-permute-done((bf16[4,32,128]{2,1,0:T(8,128)(2,1)S(1)}, bf16[4,32,128]{2,1,0:T(8,128)(2,1)S(1)}, u32[]{:S(2)}, u32[]{:S(2)}) %collective-permute-start.1) | collective-permute-done | bytes 32800 | tf_op jit(solution)/shard_map/ppermute | solution.py:130
  95.8 0.3 collective-permute-done.2
  96.1 0.5 fusion.13
  96.7 1.1 collective-permute-start.7
  97.8 2.7 %collective-permute-start.8 = (bf16[32,2048]{1,0:T(8,128)(2,1)S(1)}, bf16[32,2048]{1,0:T(8,128)(2,1)S(1)}, u32[]{:S(2)}, u32[]{:S(2)}) collective-permute-start(bf16[32,2048]{1,0:T(8,128)(2,1)S(1)} %get-tuple-element.36), channel_id=1, source_target_pairs={{0,8},{1,9},{2,10},{3,11},{4,12},{5,13},{6,14},{7,15},{8,0},{9,1},... | collective-permute-start | bytes 393224 | tf_op jit(solution)/shard_map/ppermute | solution.py:149
  100.5 1.4 %collective-permute-start.9 = (bf16[32,2048]{1,0:T(8,128)(2,1)S(1)}, bf16[32,2048]{1,0:T(8,128)(2,1)S(1)}, u32[]{:S(2)}, u32[]{:S(2)}) collective-permute-start(bf16[32,2048]{1,0:T(8,128)(2,1)S(1)} %get-tuple-element.26), channel_id=1, source_target_pairs={{0,12},{1,13},{2,14},{3,15},{4,0},{5,1},{6,2},{7,3},{8,4},{9,5},{1... | collective-permute-start | bytes 393224 | tf_op jit(solution)/shard_map/ppermute | solution.py:149
  102.0 2.4 %collective-permute-done.7 = bf16[32,2048]{1,0:T(8,128)(2,1)S(1)} collective-permute-done((bf16[32,2048]{1,0:T(8,128)(2,1)S(1)}, bf16[32,2048]{1,0:T(8,128)(2,1)S(1)}, u32[]{:S(2)}, u32[]{:S(2)}) %collective-permute-start.7) | collective-permute-done | bytes 131104 | tf_op jit(solution)/shard_map/ppermute | solution.py:149
  104.4 1.4 %collective-permute-done.8 = bf16[32,2048]{1,0:T(8,128)(2,1)S(1)} collective-permute-done((bf16[32,2048]{1,0:T(8,128)(2,1)S(1)}, bf16[32,2048]{1,0:T(8,128)(2,1)S(1)}, u32[]{:S(2)}, u32[]{:S(2)}) %collective-permute-start.8) | collective-permute-done | bytes 131104 | tf_op jit(solution)/shard_map/ppermute | solution.py:149
  105.8 0.3 collective-permute-done.9
  106.2 0.7 fusion.27
  (31 shorter events, 1.1 us)
Async XLA Ops:
  6.5 48.0 %all-gather.2.cloned.1.call-start = ((), (), s32[]{:S(2)}) async-start(), calls=%async_computation.2 | async-start | bytes 2785280 | tf_op jit(solution)/shard_map/all_gather | solution.py:46
  10.4 0.7 copy-start
  13.5 7.6 %copy-start.2 = (f32[512,1]{0,1:T(1,128)S(1)}, f32[512,1]{0,1:T(1,128)}, u32[]{:S(2)}) copy-start(f32[512,1]{0,1:T(1,128)} %param.8) | copy-start | bytes 6148
  13.5 35.8 %all-to-all-start = ((bf16[16,32,2048]{2,1,0:T(8,128)(2,1)}), bf16[16,32,2048]{2,1,0:T(8,128)(2,1)S(1)}, u32[]{:S(2)}, u32[]{:S(2)}) async-start(bf16[16,32,2048]{2,1,0:T(8,128)(2,1)} %broadcast_in_dim.51), calls=%async_computation | async-start | bytes 4194304 | tf_op jit(solution)/shard_map/all_to_all | solution.py:14
  58.3 14.5 %copy-start.1 = (bf16[512,512]{1,0:T(8,128)(2,1)}, bf16[512,512]{1,0:T(8,128)(2,1)S(1)}, u32[]{:S(2)}) copy-start(bf16[512,512]{1,0:T(8,128)(2,1)S(1)} %get-tuple-element.43) | copy-start | bytes 1572868
  59.7 26.2 %all-to-all-start.1 = ((bf16[16,1,136,128]{3,2,1,0:T(8,128)(2,1)}), bf16[16,1,136,128]{3,2,1,0:T(8,128)(2,1)S(1)}, u32[]{:S(2)}, u32[]{:S(2)}) async-start(bf16[16,1,136,128]{3,2,1,0:T(8,128)(2,1)} %broadcast_in_dim.94), calls=%async_computation.1 | async-start | bytes 1114112 | tf_op jit(solution)/shard_map/all_to_all | solution.py:14
  67.8 14.5 %collective-permute-start.3 = (bf16[8,128,128]{2,1,0:T(8,128)(2,1)S(1)}, bf16[8,128,128]{2,1,0:T(8,128)(2,1)S(1)}, u32[]{:S(2)}, u32[]{:S(2)}) collective-permute-start(bf16[8,128,128]{2,1,0:T(8,128)(2,1)S(1)} %constant_dynamic-slice_fusion), channel_id=1, source_target_pairs={{0,1},{1,2},{2,3},{3,0},{4,5},{5,6},{6,7},{7,4},{8,9},{9,10},{10,1... | collective-permute-start | bytes 786440 | tf_op jit(solution)/shard_map/ppermute | solution.py:131
  70.6 11.7 %collective-permute-start.4 = (bf16[8,128,128]{2,1,0:T(8,128)(2,1)S(1)}, bf16[8,128,128]{2,1,0:T(8,128)(2,1)S(1)}, u32[]{:S(2)}, u32[]{:S(2)}) collective-permute-start(bf16[8,128,128]{2,1,0:T(8,128)(2,1)S(1)} %constant_dynamic-slice_fusion), channel_id=1, source_target_pairs={{0,2},{1,3},{2,0},{3,1},{4,6},{5,7},{6,4},{7,5},{8,10},{9,11},{10,... | collective-permute-start | bytes 786440 | tf_op jit(solution)/shard_map/ppermute | solution.py:131
  70.8 14.9 %collective-permute-start.5 = (bf16[8,128,128]{2,1,0:T(8,128)(2,1)S(1)}, bf16[8,128,128]{2,1,0:T(8,128)(2,1)S(1)}, u32[]{:S(2)}, u32[]{:S(2)}) collective-permute-start(bf16[8,128,128]{2,1,0:T(8,128)(2,1)S(1)} %constant_dynamic-slice_fusion), channel_id=1, source_target_pairs={{0,3},{1,0},{2,1},{3,2},{4,7},{5,4},{6,5},{7,6},{8,11},{9,8},{10,9... | collective-permute-start | bytes 786440 | tf_op jit(solution)/shard_map/ppermute | solution.py:131
  85.7 5.7 %collective-permute-start.6 = (bf16[3,8,128,128]{3,2,0,1:T(8,128)(2,1)S(1)}, bf16[3,8,128,128]{3,2,0,1:T(8,128)(2,1)S(1)}, u32[]{:S(2)}, u32[]{:S(2)}) collective-permute-start(bf16[3,8,128,128]{3,2,0,1:T(8,128)(2,1)S(1)} %pad_maximum_fusion), channel_id=1, source_target_pairs={{0,16},{16,0},{32,48},{48,32},{64,80},{80,64},{96,112},{112,96},{1... | collective-permute-start | bytes 2359304 | tf_op jit(solution)/shard_map/ppermute | solution.py:133
  89.4 4.2 %collective-permute-start = (bf16[4,32,128]{2,1,0:T(8,128)(2,1)S(1)}, bf16[4,32,128]{2,1,0:T(8,128)(2,1)S(1)}, u32[]{:S(2)}, u32[]{:S(2)}) collective-permute-start(bf16[4,32,128]{2,1,0:T(8,128)(2,1)S(1)} %get-tuple-element.42), channel_id=1, source_target_pairs={{0,1},{1,2},{2,3},{3,0},{4,5},{5,6},{6,7},{7,4},{8,9},{9,10},{10,1... | collective-permute-start | bytes 98312 | tf_op jit(solution)/shard_map/ppermute | solution.py:130
  90.3 5.4 %collective-permute-start.1 = (bf16[4,32,128]{2,1,0:T(8,128)(2,1)S(1)}, bf16[4,32,128]{2,1,0:T(8,128)(2,1)S(1)}, u32[]{:S(2)}, u32[]{:S(2)}) collective-permute-start(bf16[4,32,128]{2,1,0:T(8,128)(2,1)S(1)} %get-tuple-element.41), channel_id=1, source_target_pairs={{0,2},{1,3},{2,0},{3,1},{4,6},{5,7},{6,4},{7,5},{8,10},{9,11},{10,... | collective-permute-start | bytes 98312 | tf_op jit(solution)/shard_map/ppermute | solution.py:130
  90.6 5.5 %collective-permute-start.2 = (bf16[4,32,128]{2,1,0:T(8,128)(2,1)S(1)}, bf16[4,32,128]{2,1,0:T(8,128)(2,1)S(1)}, u32[]{:S(2)}, u32[]{:S(2)}) collective-permute-start(bf16[4,32,128]{2,1,0:T(8,128)(2,1)S(1)} %get-tuple-element.40), channel_id=1, source_target_pairs={{0,3},{1,0},{2,1},{3,2},{4,7},{5,4},{6,5},{7,6},{8,11},{9,8},{10,9... | collective-permute-start | bytes 98312 | tf_op jit(solution)/shard_map/ppermute | solution.py:130
  96.7 7.7 %collective-permute-start.7 = (bf16[32,2048]{1,0:T(8,128)(2,1)S(1)}, bf16[32,2048]{1,0:T(8,128)(2,1)S(1)}, u32[]{:S(2)}, u32[]{:S(2)}) collective-permute-start(bf16[32,2048]{1,0:T(8,128)(2,1)S(1)} %get-tuple-element.25), channel_id=1, source_target_pairs={{0,4},{1,5},{2,6},{3,7},{4,8},{5,9},{6,10},{7,11},{8,12},{9,13},{1... | collective-permute-start | bytes 393224 | tf_op jit(solution)/shard_map/ppermute | solution.py:149
  97.8 8.0 %collective-permute-start.8 = (bf16[32,2048]{1,0:T(8,128)(2,1)S(1)}, bf16[32,2048]{1,0:T(8,128)(2,1)S(1)}, u32[]{:S(2)}, u32[]{:S(2)}) collective-permute-start(bf16[32,2048]{1,0:T(8,128)(2,1)S(1)} %get-tuple-element.36), channel_id=1, source_target_pairs={{0,8},{1,9},{2,10},{3,11},{4,12},{5,13},{6,14},{7,15},{8,0},{9,1},... | collective-permute-start | bytes 393224 | tf_op jit(solution)/shard_map/ppermute | solution.py:149
  100.5 5.7 %collective-permute-start.9 = (bf16[32,2048]{1,0:T(8,128)(2,1)S(1)}, bf16[32,2048]{1,0:T(8,128)(2,1)S(1)}, u32[]{:S(2)}, u32[]{:S(2)}) collective-permute-start(bf16[32,2048]{1,0:T(8,128)(2,1)S(1)} %get-tuple-element.26), channel_id=1, source_target_pairs={{0,12},{1,13},{2,14},{3,15},{4,0},{5,1},{6,2},{7,3},{8,4},{9,5},{1... | collective-permute-start | bytes 393224 | tf_op jit(solution)/shard_map/ppermute | solution.py:149
Sparse Core Ops, SparseCore 0:
  11.2 43.2 all-gather.1

commit v7 on v6

--- a/solution.py
+++ b/solution.py
@@ -14,8 +14,8 @@
     return lax.all_to_all(copies, axis, 0, 0, tiled=False)
 
 
-def prior_state(local_final, log_total, axis):
-    heads_here = local_final.shape[0]
+def pack_state(state, log_total):
+    heads_here = state.shape[0]
     high = log_total.astype(jnp.bfloat16)
     low = (log_total - high.astype(jnp.float32)).astype(jnp.bfloat16)
     extra = jnp.concatenate(
@@ -26,19 +26,44 @@
         ],
         axis=1,
     )
-    packed = jnp.concatenate([local_final.astype(jnp.bfloat16), extra], axis=1)
-    gathered = gather_by_exchange(packed, axis)
-    finals = gathered[:, :, :HEAD_DIM, :].astype(jnp.float32)
-    totals = gathered[:, :, HEAD_DIM, 0].astype(jnp.float32) + gathered[:, :, HEAD_DIM + 1, 0].astype(
+    return jnp.concatenate([state.astype(jnp.bfloat16), extra], axis=1)
+
+
+def unpack_state(packed):
+    state = packed[..., :HEAD_DIM, :].astype(jnp.float32)
+    total = packed[..., HEAD_DIM, 0].astype(jnp.float32) + packed[..., HEAD_DIM + 1, 0].astype(
         jnp.float32
     )
-    count = gathered.shape[0]
+    return state, total
+
+
+def prior_state(local_final, log_total, axis):
+    units = lax.axis_size(axis)
+    chips = units // 2
     mine = lax.axis_index(axis)
-    order = jnp.arange(count, dtype=jnp.int32)
-    between = (order[:, None] < order[None, :]) & (order[None, :] < mine)
-    exponent = jnp.sum(jnp.where(between[:, :, None], totals[None, :, :], 0.0), axis=1)
-    weight = jnp.where((order < mine)[:, None], jnp.exp(exponent), 0.0)
-    return jnp.sum(weight[:, :, None, None] * finals, axis=0)
+    parity = mine % 2
+    chip = mine // 2
+    partner_state, partner_total = unpack_state(
+        lax.ppermute(pack_state(local_final, log_total), axis, [(t, t ^ 1) for t in range(units)])
+    )
+    first_state = jnp.where(parity == 0, local_final, partner_state)
+    first_total = jnp.where(parity == 0, log_total, partner_total)
+    second_state = jnp.where(parity == 0, partner_state, local_final)
+    second_total = jnp.where(parity == 0, partner_total, log_total)
+    chip_state = jnp.exp(second_total)[:, None, None] * first_state + second_state
+    chip_total = first_total + second_total
+    chip_packed = pack_state(chip_state, chip_total)
+    received = []
+    for shift in range(1, chips):
+        later = [(2 * z + c, 2 * (z + shift) + c) for z in range(chips - shift) for c in range(2)]
+        received.append(lax.ppermute(chip_packed, axis, later))
+    states, totals = unpack_state(jnp.stack(received))
+    shifts = jnp.arange(1, chips, dtype=jnp.int32)
+    exponent = jnp.cumsum(totals, axis=0) - totals
+    weight = jnp.where((shifts <= chip)[:, None], jnp.exp(exponent), 0.0)
+    entering = jnp.sum(weight[:, :, None, None] * states, axis=0)
+    own_first = jnp.exp(first_total)[:, None, None] * entering + first_state
+    return jnp.where(parity == 0, entering, own_first)
 
 
 def shards(frames, log_decay, w_query, w_key, w_value, w_gate, w_out):

time: 115 us -> 125 us (1.087)
  starting transfers between devices: 22.9 us -> 45.1 us
  waiting for transfers between devices: 49.7 us -> 37.1 us
  between operations: 17.6 us -> 19.9 us
    ppermute x0 -> x8, starting transfers between devices: none -> 25.4 us  [the longest x7 25.2 us: prior_state(): received.append(lax.ppermute(chip_packed, axis, later))]
    ppermute x3, waiting for transfers between devices: 12.8 us -> 0.01 us  [shards(): fetched.append(lax.ppermute(own_half, 'head', across))]
    all_to_all x2 -> x1, starting transfers between devices: 11.7 us -> 7.55 us  [gather_by_exchange(): return lax.all_to_all(copies, axis, 0, 0, tiled=False)]
    ppermute x3, starting transfers between devices: 2.11 us -> 4.94 us  [shards(): pieces.append(lax.ppermute(piece, 'head', across))]
    all_to_all x2 -> x1, waiting for transfers between devices: 23 us -> 20.7 us  [gather_by_exchange(): return lax.all_to_all(copies, axis, 0, 0, tiled=False)]
    ppermute x0 -> x8, waiting for transfers between devices: none -> 1.59 us  [the longest x7 1.58 us: prior_state(): received.append(lax.ppermute(chip_packed, axis, later))]
    broadcast_in_dim x2 -> x1, local copies, waits for them, and re-layouts: 3.35 us -> 2.49 us  [gather_by_exchange(): copies = jnp.broadcast_to(part[None], (count,) + part.shape)]
    unnamed x10 -> x16, local copies, waits for them, and re-layouts: 3.75 us -> 4.13 us
  transfers between devices with their start and end apart: 13 -> 20, of which waited for: 10 -> 9; matrix products, arithmetic and copies ran while one was open for 11% -> 9% of each run, Pallas kernels for 0% -> 0%
where the time goes in v7:
time: 125 us; the launch traced here: 124 us
  starting transfers between devices  45.1 us (36%)
  waiting for transfers between devices  37.1 us (30%)
  between operations  19.9 us (16%)
  local copies, waits for them, and re-layouts  12 us (10%)
  matrix products  6.6 us (5%)
  other arithmetic  3.16 us (3%)
    ppermute x7, starting transfers between devices, prior_state(): received.append(lax.ppermute(chip_packed, axis, later))  25.2 us
    all_to_all x1, waiting for transfers between devices, gather_by_exchange(): return lax.all_to_all(copies, axis, 0, 0, tiled=False)  20.7 us
    all_to_all x1, starting transfers between devices, gather_by_exchange(): return lax.all_to_all(copies, axis, 0, 0, tiled=False)  7.55 us
    all_gather x1, waiting for transfers between devices, shards(): lax.all_gather(jnp.concatenate([w_query, w_key, w_value, w_gate, w_out],...  5.09 us
    ppermute x3, waiting for transfers between devices, shards(): pieces.append(lax.ppermute(piece, 'head', across))  4.97 us
    ppermute x3, starting transfers between devices, shards(): pieces.append(lax.ppermute(piece, 'head', across))  4.94 us
    ppermute x3, waiting for transfers between devices, shards(): total = total + lax.ppermute(piece, 'head', down).astype(jnp.float32)  4.75 us
    unnamed x16, local copies, waits for them, and re-layouts  4.13 us
  transfers between devices with their start and end apart: 20, of which 9 were waited for; matrix products, arithmetic and copies ran while one was open for 9% of the time, Pallas kernels for 0%

profile of v7, /device:TPU:6, one launch (start us, length us, event | category | flops | bytes accessed | tf_op | source)
XLA Modules:
  0.0 123.9 jit_solution(13976907552280029197)
XLA Ops:
  6.5 0.8 constant_dynamic-update-slice_fusion.4
  7.3 0.8 constant_dynamic-update-slice_fusion.3
  8.1 0.8 constant_dynamic-update-slice_fusion.2
  8.8 0.8 constant_dynamic-update-slice_fusion.1
  9.6 0.8 constant_dynamic-update-slice_fusion
  10.4 0.7 copy-done
  11.1 2.5 %broadcast_in_dim.41 = bf16[16,32,2048]{2,1,0:T(8,128)(2,1)} broadcast(bf16[32,2048]{1,0:T(8,128)(2,1)} %param.7), dimensions={1,2} | broadcast | bytes 2228224 | tf_op jit(solution)/shard_map/broadcast_in_dim | solution.py:13
  13.6 7.6 %all-to-all-start = ((bf16[16,32,2048]{2,1,0:T(8,128)(2,1)}), bf16[16,32,2048]{2,1,0:T(8,128)(2,1)S(1)}, u32[]{:S(2)}, u32[]{:S(2)}) async-start(bf16[16,32,2048]{2,1,0:T(8,128)(2,1)} %broadcast_in_dim.41), calls=%async_computation | async-start | bytes 4194304 | tf_op jit(solution)/shard_map/all_to_all | solution.py:14
  21.1 0.7 reduce_sum.40
  21.8 0.3 reduce-window.6
  22.5 0.6 slice.81
  23.1 0.6 slice.80
  26.4 0.6 slice.79
  26.9 0.6 slice.78
  28.7 20.7 %all-to-all-done = bf16[16,32,2048]{2,1,0:T(8,128)(2,1)S(1)} async-done(((bf16[16,32,2048]{2,1,0:T(8,128)(2,1)}), bf16[16,32,2048]{2,1,0:T(8,128)(2,1)S(1)}, u32[]{:S(2)}, u32[]{:S(2)}) %all-to-all-start) | async-done | bytes 2097184 | tf_op jit(solution)/shard_map/all_to_all | solution.py:14
  49.4 5.1 %all-gather.2.cloned.1.call-done = bf16[2048,640]{1,0:T(8,128)(2,1)} async-done(((bf16[128,640]{1,0:T(8,128)(2,1)}), bf16[2048,640]{1,0:T(8,128)(2,1)}) %all-gather.2.cloned.1.call-update) | async-done | bytes 2621456 | tf_op jit(solution)/shard_map/all_gather | solution.py:71
  54.5 2.8 %fusion.66 = (bf16[512,512]{1,0:T(8,128)(2,1)S(1)}, f32[512,512]{1,0:T(8,128)S(1)}) fusion(bf16[512,2048]{1,0:T(8,128)(2,1)S(1)} %bitcast.157, bf16[2048,640]{1,0:T(8,128)(2,1)} %all-gather.2.cloned.1.call-done), kind=kOutput, calls=%fused_computation.111 | convolution fusion | flops 1074003968 | bytes 5767168 | tf_op jit(solution)/shard_map/dot_general | solution.py:77
  57.3 0.3 convolution_add_fusion
  57.8 0.3 copy-done.1
  58.1 0.3 collective-permute-start
  58.4 1.6 %fusion.15 = f32[1,512,1,128]{3,1,2,0:T(8,128)S(1)} fusion(f32[512]{0:T(512)S(1)} %get-tuple-element.22, bf16[512,512]{1,0:T(8,128)(2,1)} %copy-done.1), kind=kOutput, calls=%fused_computation.16 | convolution fusion | flops 135528448 | bytes 659456 | tf_op jit(solution)/shard_map/while/body/eval_jaxpr/hts,shd->thd/dot_general | solution.py:113
  60.0 1.1 slice.88
  61.1 0.5 fusion.65
  64.4 2.8 %collective-permute-start.1 = (bf16[1,136,128]{2,1,0:T(8,128)(2,1)S(1)}, bf16[1,136,128]{2,1,0:T(8,128)(2,1)S(1)}, u32[]{:S(2)}, u32[]{:S(2)}) collective-permute-start(bf16[1,136,128]{2,1,0:T(8,128)(2,1)S(1)} %maximum_maximum_fusion.1), channel_id=1, source_target_pairs={{0,32},{16,48},{32,64},{48,80},{64,96},{80,112},{96,128},{112,144}... | collective-permute-start | bytes 104456 | tf_op jit(solution)/shard_map/ppermute | solution.py:59
  67.2 0.6 collective-permute-start.11
  67.8 2.4 %collective-permute-start.12 = (bf16[8,128,128]{2,1,0:T(8,128)(2,1)S(1)}, bf16[8,128,128]{2,1,0:T(8,128)(2,1)S(1)}, u32[]{:S(2)}, u32[]{:S(2)}) collective-permute-start(bf16[8,128,128]{2,1,0:T(8,128)(2,1)S(1)} %constant_dynamic-slice_fusion), channel_id=1, source_target_pairs={{0,2},{1,3},{2,0},{3,1},{4,6},{5,7},{6,4},{7,5},{8,10},{9,11},{10,... | collective-permute-start | bytes 786440 | tf_op jit(solution)/shard_map/ppermute | solution.py:156
  70.2 4.2 %collective-permute-start.2 = (bf16[1,136,128]{2,1,0:T(8,128)(2,1)S(1)}, bf16[1,136,128]{2,1,0:T(8,128)(2,1)S(1)}, u32[]{:S(2)}, u32[]{:S(2)}) collective-permute-start(bf16[1,136,128]{2,1,0:T(8,128)(2,1)S(1)} %maximum_maximum_fusion.1), channel_id=1, source_target_pairs={{0,64},{16,80},{32,96},{48,112},{64,128},{80,144},{96,160},{112,17... | collective-permute-start | bytes 104456 | tf_op jit(solution)/shard_map/ppermute | solution.py:59
  74.5 4.1 %collective-permute-start.3 = (bf16[1,136,128]{2,1,0:T(8,128)(2,1)S(1)}, bf16[1,136,128]{2,1,0:T(8,128)(2,1)S(1)}, u32[]{:S(2)}, u32[]{:S(2)}) collective-permute-start(bf16[1,136,128]{2,1,0:T(8,128)(2,1)S(1)} %maximum_maximum_fusion.1), channel_id=1, source_target_pairs={{0,96},{16,112},{32,128},{48,144},{64,160},{80,176},{96,192},{112,... | collective-permute-start | bytes 104456 | tf_op jit(solution)/shard_map/ppermute | solution.py:59
  78.6 4.9 %collective-permute-start.4 = (bf16[1,136,128]{2,1,0:T(8,128)(2,1)S(1)}, bf16[1,136,128]{2,1,0:T(8,128)(2,1)S(1)}, u32[]{:S(2)}, u32[]{:S(2)}) collective-permute-start(bf16[1,136,128]{2,1,0:T(8,128)(2,1)S(1)} %maximum_maximum_fusion.1), channel_id=1, source_target_pairs={{0,128},{16,144},{32,160},{48,176},{64,192},{80,208},{96,224},{112... | collective-permute-start | bytes 104456 | tf_op jit(solution)/shard_map/ppermute | solution.py:59
  83.6 2.4 %collective-permute-start.5 = (bf16[1,136,128]{2,1,0:T(8,128)(2,1)S(1)}, bf16[1,136,128]{2,1,0:T(8,128)(2,1)S(1)}, u32[]{:S(2)}, u32[]{:S(2)}) collective-permute-start(bf16[1,136,128]{2,1,0:T(8,128)(2,1)S(1)} %maximum_maximum_fusion.1), channel_id=1, source_target_pairs={{0,160},{16,176},{32,192},{48,208},{64,224},{80,240},{1,161},{17,1... | collective-permute-start | bytes 104456 | tf_op jit(solution)/shard_map/ppermute | solution.py:59
  86.0 5.5 %collective-permute-start.6 = (bf16[1,136,128]{2,1,0:T(8,128)(2,1)S(1)}, bf16[1,136,128]{2,1,0:T(8,128)(2,1)S(1)}, u32[]{:S(2)}, u32[]{:S(2)}) collective-permute-start(bf16[1,136,128]{2,1,0:T(8,128)(2,1)S(1)} %maximum_maximum_fusion.1), channel_id=1, source_target_pairs={{0,192},{16,208},{32,224},{48,240},{1,193},{17,209},{33,225},{49,2... | collective-permute-start | bytes 104456 | tf_op jit(solution)/shard_map/ppermute | solution.py:59
  91.5 1.3 %collective-permute-start.7 = (bf16[1,136,128]{2,1,0:T(8,128)(2,1)S(1)}, bf16[1,136,128]{2,1,0:T(8,128)(2,1)S(1)}, u32[]{:S(2)}, u32[]{:S(2)}) collective-permute-start(bf16[1,136,128]{2,1,0:T(8,128)(2,1)S(1)} %maximum_maximum_fusion.1), channel_id=1, source_target_pairs={{0,224},{16,240},{1,225},{17,241},{2,226},{18,242},{3,227},{19,243... | collective-permute-start | bytes 104456 | tf_op jit(solution)/shard_map/ppermute | solution.py:59
  92.8 0.3 collective-permute-done.6
  93.1 1.3 %collective-permute-done.7 = bf16[1,136,128]{2,1,0:T(8,128)(2,1)S(1)} collective-permute-done((bf16[1,136,128]{2,1,0:T(8,128)(2,1)S(1)}, bf16[1,136,128]{2,1,0:T(8,128)(2,1)S(1)}, u32[]{:S(2)}, u32[]{:S(2)}) %collective-permute-start.7) | collective-permute-done | bytes 34848 | tf_op jit(solution)/shard_map/ppermute | solution.py:59
  94.7 1.4 %fusion.68 = (f32[512]{0:T(512)S(1)}, f32[1,512,1,128]{3,1,2,0:T(8,128)S(1)}) fusion(f32[1,512,1,128]{3,1,2,0:T(8,128)S(1)} %fusion.15, f32[512]{0:T(512)S(1)} %exp.58, bf16[512,512]{1,0:T(8,128)(2,1)} %copy-done.1, f32[128,128]{1,0:T(8,128)S(1)} %multiply_reduce_fusion, f32[128,128]{1,0:T(8,128)S(1)} %convolution_add_fusion, f32[]{:T(128)} %bitcast.34, ...), kind=kOutput, calls=%fused_computation.113 | convolution fusion | flops 101023232 | bytes 824832 | tf_op jit(solution)/shard_map/cthd,chde->cthe/dot_general | solution.py:130
  96.3 0.2 fusion.29
  96.8 3.1 %collective-permute-start.8 = (bf16[4,32,128]{2,1,0:T(8,128)(2,1)S(1)}, bf16[4,32,128]{2,1,0:T(8,128)(2,1)S(1)}, u32[]{:S(2)}, u32[]{:S(2)}) collective-permute-start(bf16[4,32,128]{2,1,0:T(8,128)(2,1)S(1)} %get-tuple-element.42), channel_id=1, source_target_pairs={{0,1},{1,2},{2,3},{3,0},{4,5},{5,6},{6,7},{7,4},{8,9},{9,10},{10,1... | collective-permute-start | bytes 98312 | tf_op jit(solution)/shard_map/ppermute | solution.py:155
  99.9 1.8 %collective-permute-start.9 = (bf16[4,32,128]{2,1,0:T(8,128)(2,1)S(1)}, bf16[4,32,128]{2,1,0:T(8,128)(2,1)S(1)}, u32[]{:S(2)}, u32[]{:S(2)}) collective-permute-start(bf16[4,32,128]{2,1,0:T(8,128)(2,1)S(1)} %get-tuple-element.41), channel_id=1, source_target_pairs={{0,2},{1,3},{2,0},{3,1},{4,6},{5,7},{6,4},{7,5},{8,10},{9,11},{10,... | collective-permute-start | bytes 98312 | tf_op jit(solution)/shard_map/ppermute | solution.py:155
  101.9 3.5 %collective-permute-done.9 = bf16[4,32,128]{2,1,0:T(8,128)(2,1)S(1)} collective-permute-done((bf16[4,32,128]{2,1,0:T(8,128)(2,1)S(1)}, bf16[4,32,128]{2,1,0:T(8,128)(2,1)S(1)}, u32[]{:S(2)}, u32[]{:S(2)}) %collective-permute-start.9) | collective-permute-done | bytes 32800 | tf_op jit(solution)/shard_map/ppermute | solution.py:155
  105.4 1.5 %collective-permute-done.10 = bf16[4,32,128]{2,1,0:T(8,128)(2,1)S(1)} collective-permute-done((bf16[4,32,128]{2,1,0:T(8,128)(2,1)S(1)}, bf16[4,32,128]{2,1,0:T(8,128)(2,1)S(1)}, u32[]{:S(2)}, u32[]{:S(2)}) %collective-permute-start.10) | collective-permute-done | bytes 32800 | tf_op jit(solution)/shard_map/ppermute | solution.py:155
  106.9 0.5 fusion.13
  107.5 0.7 collective-permute-start.15
  108.2 2.4 %collective-permute-start.16 = (bf16[32,2048]{1,0:T(8,128)(2,1)S(1)}, bf16[32,2048]{1,0:T(8,128)(2,1)S(1)}, u32[]{:S(2)}, u32[]{:S(2)}) collective-permute-start(bf16[32,2048]{1,0:T(8,128)(2,1)S(1)} %get-tuple-element.36), channel_id=1, source_target_pairs={{0,8},{1,9},{2,10},{3,11},{4,12},{5,13},{6,14},{7,15},{8,0},{9,1},... | collective-permute-start | bytes 393224 | tf_op jit(solution)/shard_map/ppermute | solution.py:174
  110.7 0.9 collective-permute-start.17
  111.6 3.0 %collective-permute-done.15 = bf16[32,2048]{1,0:T(8,128)(2,1)S(1)} collective-permute-done((bf16[32,2048]{1,0:T(8,128)(2,1)S(1)}, bf16[32,2048]{1,0:T(8,128)(2,1)S(1)}, u32[]{:S(2)}, u32[]{:S(2)}) %collective-permute-start.15) | collective-permute-done | bytes 131104 | tf_op jit(solution)/shard_map/ppermute | solution.py:174
  114.6 1.4 %collective-permute-done.16 = bf16[32,2048]{1,0:T(8,128)(2,1)S(1)} collective-permute-done((bf16[32,2048]{1,0:T(8,128)(2,1)S(1)}, bf16[32,2048]{1,0:T(8,128)(2,1)S(1)}, u32[]{:S(2)}, u32[]{:S(2)}) %collective-permute-start.16) | collective-permute-done | bytes 131104 | tf_op jit(solution)/shard_map/ppermute | solution.py:174
  116.0 0.4 collective-permute-done.17
  116.4 0.7 fusion.27
  (54 shorter events, 2.2 us)
Async XLA Ops:
  6.5 48.0 %all-gather.2.cloned.1.call-start = ((), (), s32[]{:S(2)}) async-start(), calls=%async_computation.1 | async-start | bytes 2785280 | tf_op jit(solution)/shard_map/all_gather | solution.py:71
  10.4 0.7 copy-start
  13.6 7.6 %copy-start.2 = (f32[512,1]{0,1:T(1,128)S(1)}, f32[512,1]{0,1:T(1,128)}, u32[]{:S(2)}) copy-start(f32[512,1]{0,1:T(1,128)} %param.8) | copy-start | bytes 6148
  13.6 35.8 %all-to-all-start = ((bf16[16,32,2048]{2,1,0:T(8,128)(2,1)}), bf16[16,32,2048]{2,1,0:T(8,128)(2,1)S(1)}, u32[]{:S(2)}, u32[]{:S(2)}) async-start(bf16[16,32,2048]{2,1,0:T(8,128)(2,1)} %broadcast_in_dim.41), calls=%async_computation | async-start | bytes 4194304 | tf_op jit(solution)/shard_map/all_to_all | solution.py:14
  57.3 0.8 copy-start.1
  58.1 2.9 %collective-permute-start = (bf16[1,136,128]{2,1,0:T(8,128)(2,1)S(1)}, bf16[1,136,128]{2,1,0:T(8,128)(2,1)S(1)}, u32[]{:S(2)}, u32[]{:S(2)}) collective-permute-start(bf16[1,136,128]{2,1,0:T(8,128)(2,1)S(1)} %maximum_maximum_fusion), channel_id=1, source_target_pairs={{0,16},{16,0},{32,48},{48,32},{64,80},{80,64},{96,112},{112,96},{1... | collective-permute-start | bytes 104456 | tf_op jit(solution)/shard_map/ppermute | solution.py:47
  64.4 10.1 %collective-permute-start.1 = (bf16[1,136,128]{2,1,0:T(8,128)(2,1)S(1)}, bf16[1,136,128]{2,1,0:T(8,128)(2,1)S(1)}, u32[]{:S(2)}, u32[]{:S(2)}) collective-permute-start(bf16[1,136,128]{2,1,0:T(8,128)(2,1)S(1)} %maximum_maximum_fusion.1), channel_id=1, source_target_pairs={{0,32},{16,48},{32,64},{48,80},{64,96},{80,112},{96,128},{112,144}... | collective-permute-start | bytes 104456 | tf_op jit(solution)/shard_map/ppermute | solution.py:59
  67.2 28.9 %collective-permute-start.11 = (bf16[8,128,128]{2,1,0:T(8,128)(2,1)S(1)}, bf16[8,128,128]{2,1,0:T(8,128)(2,1)S(1)}, u32[]{:S(2)}, u32[]{:S(2)}) collective-permute-start(bf16[8,128,128]{2,1,0:T(8,128)(2,1)S(1)} %constant_dynamic-slice_fusion), channel_id=1, source_target_pairs={{0,1},{1,2},{2,3},{3,0},{4,5},{5,6},{6,7},{7,4},{8,9},{9,10},{10,1... | collective-permute-start | bytes 786440 | tf_op jit(solution)/shard_map/ppermute | solution.py:156
  67.8 28.3 %collective-permute-start.12 = (bf16[8,128,128]{2,1,0:T(8,128)(2,1)S(1)}, bf16[8,128,128]{2,1,0:T(8,128)(2,1)S(1)}, u32[]{:S(2)}, u32[]{:S(2)}) collective-permute-start(bf16[8,128,128]{2,1,0:T(8,128)(2,1)S(1)} %constant_dynamic-slice_fusion), channel_id=1, source_target_pairs={{0,2},{1,3},{2,0},{3,1},{4,6},{5,7},{6,4},{7,5},{8,10},{9,11},{10,... | collective-permute-start | bytes 786440 | tf_op jit(solution)/shard_map/ppermute | solution.py:156
  70.2 25.9 %collective-permute-start.13 = (bf16[8,128,128]{2,1,0:T(8,128)(2,1)S(1)}, bf16[8,128,128]{2,1,0:T(8,128)(2,1)S(1)}, u32[]{:S(2)}, u32[]{:S(2)}) collective-permute-start(bf16[8,128,128]{2,1,0:T(8,128)(2,1)S(1)} %constant_dynamic-slice_fusion), channel_id=1, source_target_pairs={{0,3},{1,0},{2,1},{3,2},{4,7},{5,4},{6,5},{7,6},{8,11},{9,8},{10,9... | collective-permute-start | bytes 786440 | tf_op jit(solution)/shard_map/ppermute | solution.py:156
  70.2 8.4 %collective-permute-start.2 = (bf16[1,136,128]{2,1,0:T(8,128)(2,1)S(1)}, bf16[1,136,128]{2,1,0:T(8,128)(2,1)S(1)}, u32[]{:S(2)}, u32[]{:S(2)}) collective-permute-start(bf16[1,136,128]{2,1,0:T(8,128)(2,1)S(1)} %maximum_maximum_fusion.1), channel_id=1, source_target_pairs={{0,64},{16,80},{32,96},{48,112},{64,128},{80,144},{96,160},{112,17... | collective-permute-start | bytes 104456 | tf_op jit(solution)/shard_map/ppermute | solution.py:59
  74.5 9.1 %collective-permute-start.3 = (bf16[1,136,128]{2,1,0:T(8,128)(2,1)S(1)}, bf16[1,136,128]{2,1,0:T(8,128)(2,1)S(1)}, u32[]{:S(2)}, u32[]{:S(2)}) collective-permute-start(bf16[1,136,128]{2,1,0:T(8,128)(2,1)S(1)} %maximum_maximum_fusion.1), channel_id=1, source_target_pairs={{0,96},{16,112},{32,128},{48,144},{64,160},{80,176},{96,192},{112,... | collective-permute-start | bytes 104456 | tf_op jit(solution)/shard_map/ppermute | solution.py:59
  78.6 7.4 %collective-permute-start.4 = (bf16[1,136,128]{2,1,0:T(8,128)(2,1)S(1)}, bf16[1,136,128]{2,1,0:T(8,128)(2,1)S(1)}, u32[]{:S(2)}, u32[]{:S(2)}) collective-permute-start(bf16[1,136,128]{2,1,0:T(8,128)(2,1)S(1)} %maximum_maximum_fusion.1), channel_id=1, source_target_pairs={{0,128},{16,144},{32,160},{48,176},{64,192},{80,208},{96,224},{112... | collective-permute-start | bytes 104456 | tf_op jit(solution)/shard_map/ppermute | solution.py:59
  83.6 7.9 %collective-permute-start.5 = (bf16[1,136,128]{2,1,0:T(8,128)(2,1)S(1)}, bf16[1,136,128]{2,1,0:T(8,128)(2,1)S(1)}, u32[]{:S(2)}, u32[]{:S(2)}) collective-permute-start(bf16[1,136,128]{2,1,0:T(8,128)(2,1)S(1)} %maximum_maximum_fusion.1), channel_id=1, source_target_pairs={{0,160},{16,176},{32,192},{48,208},{64,224},{80,240},{1,161},{17,1... | collective-permute-start | bytes 104456 | tf_op jit(solution)/shard_map/ppermute | solution.py:59
  86.0 7.1 %collective-permute-start.6 = (bf16[1,136,128]{2,1,0:T(8,128)(2,1)S(1)}, bf16[1,136,128]{2,1,0:T(8,128)(2,1)S(1)}, u32[]{:S(2)}, u32[]{:S(2)}) collective-permute-start(bf16[1,136,128]{2,1,0:T(8,128)(2,1)S(1)} %maximum_maximum_fusion.1), channel_id=1, source_target_pairs={{0,192},{16,208},{32,224},{48,240},{1,193},{17,209},{33,225},{49,2... | collective-permute-start | bytes 104456 | tf_op jit(solution)/shard_map/ppermute | solution.py:59
  91.5 2.9 %collective-permute-start.7 = (bf16[1,136,128]{2,1,0:T(8,128)(2,1)S(1)}, bf16[1,136,128]{2,1,0:T(8,128)(2,1)S(1)}, u32[]{:S(2)}, u32[]{:S(2)}) collective-permute-start(bf16[1,136,128]{2,1,0:T(8,128)(2,1)S(1)} %maximum_maximum_fusion.1), channel_id=1, source_target_pairs={{0,224},{16,240},{1,225},{17,241},{2,226},{18,242},{3,227},{19,243... | collective-permute-start | bytes 104456 | tf_op jit(solution)/shard_map/ppermute | solution.py:59
  96.2 5.5 %collective-permute-start.14 = (bf16[3,8,128,128]{3,2,0,1:T(8,128)(2,1)S(1)}, bf16[3,8,128,128]{3,2,0,1:T(8,128)(2,1)S(1)}, u32[]{:S(2)}, u32[]{:S(2)}) collective-permute-start(bf16[3,8,128,128]{3,2,0,1:T(8,128)(2,1)S(1)} %pad_maximum_fusion), channel_id=1, source_target_pairs={{0,16},{16,0},{32,48},{48,32},{64,80},{80,64},{96,112},{112,96},{1... | collective-permute-start | bytes 2359304 | tf_op jit(solution)/shard_map/ppermute | solution.py:158
  96.8 5.1 %collective-permute-start.8 = (bf16[4,32,128]{2,1,0:T(8,128)(2,1)S(1)}, bf16[4,32,128]{2,1,0:T(8,128)(2,1)S(1)}, u32[]{:S(2)}, u32[]{:S(2)}) collective-permute-start(bf16[4,32,128]{2,1,0:T(8,128)(2,1)S(1)} %get-tuple-element.42), channel_id=1, source_target_pairs={{0,1},{1,2},{2,3},{3,0},{4,5},{5,6},{6,7},{7,4},{8,9},{9,10},{10,1... | collective-permute-start | bytes 98312 | tf_op jit(solution)/shard_map/ppermute | solution.py:155
  99.9 5.5 %collective-permute-start.9 = (bf16[4,32,128]{2,1,0:T(8,128)(2,1)S(1)}, bf16[4,32,128]{2,1,0:T(8,128)(2,1)S(1)}, u32[]{:S(2)}, u32[]{:S(2)}) collective-permute-start(bf16[4,32,128]{2,1,0:T(8,128)(2,1)S(1)} %get-tuple-element.41), channel_id=1, source_target_pairs={{0,2},{1,3},{2,0},{3,1},{4,6},{5,7},{6,4},{7,5},{8,10},{9,11},{10,... | collective-permute-start | bytes 98312 | tf_op jit(solution)/shard_map/ppermute | solution.py:155
  101.7 5.1 %collective-permute-start.10 = (bf16[4,32,128]{2,1,0:T(8,128)(2,1)S(1)}, bf16[4,32,128]{2,1,0:T(8,128)(2,1)S(1)}, u32[]{:S(2)}, u32[]{:S(2)}) collective-permute-start(bf16[4,32,128]{2,1,0:T(8,128)(2,1)S(1)} %get-tuple-element.40), channel_id=1, source_target_pairs={{0,3},{1,0},{2,1},{3,2},{4,7},{5,4},{6,5},{7,6},{8,11},{9,8},{10,9... | collective-permute-start | bytes 98312 | tf_op jit(solution)/shard_map/ppermute | solution.py:155
  107.5 7.1 %collective-permute-start.15 = (bf16[32,2048]{1,0:T(8,128)(2,1)S(1)}, bf16[32,2048]{1,0:T(8,128)(2,1)S(1)}, u32[]{:S(2)}, u32[]{:S(2)}) collective-permute-start(bf16[32,2048]{1,0:T(8,128)(2,1)S(1)} %get-tuple-element.25), channel_id=1, source_target_pairs={{0,4},{1,5},{2,6},{3,7},{4,8},{5,9},{6,10},{7,11},{8,12},{9,13},{1... | collective-permute-start | bytes 393224 | tf_op jit(solution)/shard_map/ppermute | solution.py:174
  108.2 7.8 %collective-permute-start.16 = (bf16[32,2048]{1,0:T(8,128)(2,1)S(1)}, bf16[32,2048]{1,0:T(8,128)(2,1)S(1)}, u32[]{:S(2)}, u32[]{:S(2)}) collective-permute-start(bf16[32,2048]{1,0:T(8,128)(2,1)S(1)} %get-tuple-element.36), channel_id=1, source_target_pairs={{0,8},{1,9},{2,10},{3,11},{4,12},{5,13},{6,14},{7,15},{8,0},{9,1},... | collective-permute-start | bytes 393224 | tf_op jit(solution)/shard_map/ppermute | solution.py:174
  110.7 5.7 %collective-permute-start.17 = (bf16[32,2048]{1,0:T(8,128)(2,1)S(1)}, bf16[32,2048]{1,0:T(8,128)(2,1)S(1)}, u32[]{:S(2)}, u32[]{:S(2)}) collective-permute-start(bf16[32,2048]{1,0:T(8,128)(2,1)S(1)} %get-tuple-element.26), channel_id=1, source_target_pairs={{0,12},{1,13},{2,14},{3,15},{4,0},{5,1},{6,2},{7,3},{8,4},{9,5},{1... | collective-permute-start | bytes 393224 | tf_op jit(solution)/shard_map/ppermute | solution.py:174
Sparse Core Ops, SparseCore 0:
  11.2 43.2 all-gather.1

commit v8 on v6

--- a/solution.py
+++ b/solution.py
@@ -43,9 +43,16 @@
 
 def shards(frames, log_decay, w_query, w_key, w_value, w_gate, w_out):
     head_width = w_query.shape[1]
-    stacked = lax.all_gather(
-        jnp.concatenate([w_query, w_key, w_value, w_gate, w_out], axis=1), "tm", axis=0, tiled=True
+    packed = jnp.concatenate([w_query, w_key, w_value, w_gate, w_out], axis=1)
+    units = lax.axis_size("tm")
+    parity = lax.axis_index("tm") % 2
+    same_place = [[t for t in range(units) if t % 2 == p] for p in range(2)]
+    mine = lax.all_gather(packed, "tm", axis_index_groups=same_place)
+    theirs = lax.ppermute(mine, "tm", [(t, t ^ 1) for t in range(units)])
+    by_place = jnp.stack(
+        [jnp.where(parity == 0, mine, theirs), jnp.where(parity == 0, theirs, mine)], axis=1
     )
+    stacked = by_place.reshape(-1, packed.shape[1])
     joined = stacked[:, : 4 * head_width]
     out_blocks = stacked[:, 4 * head_width :].reshape(-1, head_width, w_out.shape[1])
     frames_here = gather_by_exchange(frames, "head").reshape(-1, frames.shape[1])

time: 115 us -> 123 us (1.070)
  waiting for transfers between devices: 49.7 us -> 53.8 us
  other arithmetic: 4.12 us -> 6.11 us
    all_gather x1, waiting for transfers between devices: 5.11 us -> 32.2 us  [shards(): mine = lax.all_gather(packed, 'tm', axis_index_groups=same_place)]
    all_to_all x2, waiting for transfers between devices: 23 us -> 0.01 us  [gather_by_exchange(): return lax.all_to_all(copies, axis, 0, 0, tiled=False)]
    another operation x2 -> x4, other arithmetic: 0.49 us -> 2.32 us  [the longest x2 1.84 us: shards(): jnp.stack([jnp.where(parity == 0, mine, theirs), jnp.where(parity == 0, t...]
    unnamed x10 -> x14, local copies, waits for them, and re-layouts: 3.75 us -> 5.34 us
    ppermute x3, waiting for transfers between devices: 12.8 us -> 11.4 us  [shards(): fetched.append(lax.ppermute(own_half, 'head', across))]
  transfers between devices with their start and end apart: 13 -> 14, of which waited for: 10 -> 9; matrix products, arithmetic and copies ran while one was open for 11% -> 11% of each run, Pallas kernels for 0% -> 0%
where the time goes in v8:
time: 123 us; the launch traced here: 122 us
  waiting for transfers between devices  53.8 us (44%)
  starting transfers between devices  23.7 us (19%)
  between operations  17.7 us (14%)
  local copies, waits for them, and re-layouts  12.8 us (10%)
  matrix products  7.62 us (6%)
  other arithmetic  6.11 us (5%)
    all_gather x1, waiting for transfers between devices, shards(): mine = lax.all_gather(packed, 'tm', axis_index_groups=same_place)  32.2 us
    all_to_all x2, starting transfers between devices, gather_by_exchange(): return lax.all_to_all(copies, axis, 0, 0, tiled=False)  12.1 us
    ppermute x3, waiting for transfers between devices, shards(): fetched.append(lax.ppermute(own_half, 'head', across))  11.4 us
    ppermute x3, waiting for transfers between devices, shards(): total = total + lax.ppermute(piece, 'head', down).astype(jnp.float32)  5.42 us
    unnamed x14, local copies, waits for them, and re-layouts  5.34 us
    ppermute x3, starting transfers between devices, shards(): total = total + lax.ppermute(piece, 'head', down).astype(jnp.float32)  5.33 us
    ppermute x3, waiting for transfers between devices, shards(): pieces.append(lax.ppermute(piece, 'head', across))  4.81 us
    dot_general x1, matrix products, shards(): projected = jnp.dot(frames_here, joined, preferred_element_type=jnp.float32)  3.84 us
  transfers between devices with their start and end apart: 14, of which 9 were waited for; matrix products, arithmetic and copies ran while one was open for 11% of the time, Pallas kernels for 0%

profile of v8, /device:TPU:6, one launch (start us, length us, event | category | flops | bytes accessed | tf_op | source)
XLA Modules:
  0.0 121.8 jit_solution(4395725683671021913)
XLA Ops:
  6.5 0.8 constant_dynamic-update-slice_fusion.4
  7.3 0.8 constant_dynamic-update-slice_fusion.3
  8.1 0.8 constant_dynamic-update-slice_fusion.2
  8.8 0.8 constant_dynamic-update-slice_fusion.1
  9.6 0.8 constant_dynamic-update-slice_fusion
  10.4 0.7 copy-done.2
  11.1 2.5 %broadcast_in_dim.51 = bf16[16,32,2048]{2,1,0:T(8,128)(2,1)} broadcast(bf16[32,2048]{1,0:T(8,128)(2,1)} %param.7), dimensions={1,2} | broadcast | bytes 2228224 | tf_op jit(solution)/shard_map/broadcast_in_dim | solution.py:13
  13.5 7.6 %all-to-all-start = ((bf16[16,32,2048]{2,1,0:T(8,128)(2,1)}), bf16[16,32,2048]{2,1,0:T(8,128)(2,1)}, u32[]{:S(2)}, u32[]{:S(2)}) async-start(bf16[16,32,2048]{2,1,0:T(8,128)(2,1)} %broadcast_in_dim.51), calls=%async_computation | async-start | bytes 4194304 | tf_op jit(solution)/shard_map/all_to_all | solution.py:14
  21.1 32.2 %all-gather.3.cloned.1.call-done = bf16[1024,640]{1,0:T(8,128)(2,1)} async-done(((bf16[128,640]{1,0:T(8,128)(2,1)}), bf16[1024,640]{1,0:T(8,128)(2,1)}) %all-gather.3.cloned.1.call-update) | async-done | bytes 1310736 | tf_op jit(solution)/shard_map/all_gather | solution.py:50
  53.3 0.7 reduce_sum.47
  54.0 0.3 reduce-window.6
  54.3 0.2 slice_reduce_fusion
  54.5 0.2 reduce-window.9
  54.8 0.6 slice.69
  55.3 0.6 slice.68
  58.8 1.6 %select_bitcast_fusion.1 = (bf16[8,1,128,640]{3,2,0,1:T(8,128)(2,1)S(1)}, bf16[8,1,128,640]{3,2,0,1:T(8,128)(2,1)S(1)}) fusion(bf16[8,128,640]{2,1,0:T(8,128)(2,1)} %bitcast.121, bf16[8,128,640]{2,1,0:T(8,128)(2,1)S(1)} %collective-permute-done, pred[]{:T(512)S(6)} %eq.16), kind=kLoop, calls=%fused_computation.13 | loop fusion | flops 1310720 | bytes 5242881 | tf_op jit(solution)/shard_map/stack | solution.py:52
  60.4 0.3 pad_maximum_fusion
  60.7 0.3 copy.31
  61.0 3.8 %fusion.58 = (bf16[512,512]{1,0:T(8,128)(2,1)S(1)}, f32[512,512]{1,0:T(8,128)}) fusion(bf16[512,2048]{1,0:T(8,128)(2,1)} %bitcast.4, bf16[2048,640]{1,0:T(8,128)(2,1)S(1)} %bitcast.116), kind=kOutput, calls=%fused_computation.98 | convolution fusion | flops 1074003968 | bytes 5767168 | tf_op jit(solution)/shard_map/dot_general | solution.py:59
  64.8 0.8 copy-done.3
  65.6 0.3 fusion.18
  66.1 0.9 broadcast_in_dim.94
  66.9 4.5 %all-to-all-start.1 = ((bf16[16,1,136,128]{3,2,1,0:T(8,128)(2,1)}), bf16[16,1,136,128]{3,2,1,0:T(8,128)(2,1)S(1)}, u32[]{:S(2)}, u32[]{:S(2)}) async-start(bf16[16,1,136,128]{3,2,1,0:T(8,128)(2,1)} %broadcast_in_dim.94), calls=%async_computation.1 | async-start | bytes 1114112 | tf_op jit(solution)/shard_map/all_to_all | solution.py:14
  71.6 0.6 slice.67
  72.2 0.6 slice.66
  74.2 0.8 copy-done
  75.1 0.6 collective-permute-start.4
  75.7 2.4 %collective-permute-start.5 = (bf16[8,128,128]{2,1,0:T(8,128)(2,1)S(1)}, bf16[8,128,128]{2,1,0:T(8,128)(2,1)S(1)}, u32[]{:S(2)}, u32[]{:S(2)}) collective-permute-start(bf16[8,128,128]{2,1,0:T(8,128)(2,1)S(1)} %constant_dynamic-slice_fusion), channel_id=1, source_target_pairs={{0,2},{1,3},{2,0},{3,1},{4,6},{5,7},{6,4},{7,5},{8,10},{9,11},{10,... | collective-permute-start | bytes 786440 | tf_op jit(solution)/shard_map/ppermute | solution.py:138
  78.1 1.6 %fusion.15 = f32[1,512,1,128]{3,1,2,0:T(8,128)S(1)} fusion(f32[512]{0:T(512)S(1)} %get-tuple-element.22, bf16[512,512]{1,0:T(8,128)(2,1)} %copy-done.3), kind=kOutput, calls=%fused_computation.19 | convolution fusion | flops 135528448 | bytes 659456 | tf_op jit(solution)/shard_map/while/body/eval_jaxpr/hts,shd->thd/dot_general | solution.py:95
  79.6 4.6 %collective-permute-done.4 = bf16[8,128,128]{2,1,0:T(8,128)(2,1)S(1)} collective-permute-done((bf16[8,128,128]{2,1,0:T(8,128)(2,1)S(1)}, bf16[8,128,128]{2,1,0:T(8,128)(2,1)S(1)}, u32[]{:S(2)}, u32[]{:S(2)}) %collective-permute-start.4) | collective-permute-done | bytes 262176 | tf_op jit(solution)/shard_map/ppermute | solution.py:138
  84.3 2.1 %collective-permute-done.5 = bf16[8,128,128]{2,1,0:T(8,128)(2,1)S(1)} collective-permute-done((bf16[8,128,128]{2,1,0:T(8,128)(2,1)S(1)}, bf16[8,128,128]{2,1,0:T(8,128)(2,1)S(1)}, u32[]{:S(2)}, u32[]{:S(2)}) %collective-permute-start.5) | collective-permute-done | bytes 262176 | tf_op jit(solution)/shard_map/ppermute | solution.py:138
  86.4 4.6 %collective-permute-done.6 = bf16[8,128,128]{2,1,0:T(8,128)(2,1)S(1)} collective-permute-done((bf16[8,128,128]{2,1,0:T(8,128)(2,1)S(1)}, bf16[8,128,128]{2,1,0:T(8,128)(2,1)S(1)}, u32[]{:S(2)}, u32[]{:S(2)}) %collective-permute-start.6) | collective-permute-done | bytes 262176 | tf_op jit(solution)/shard_map/ppermute | solution.py:138
  91.2 0.2 fusion.55
  91.7 1.4 %fusion.59 = (f32[512]{0:T(512)S(1)}, f32[1,512,1,128]{3,1,2,0:T(8,128)S(1)}) fusion(f32[1,512,1,128]{3,1,2,0:T(8,128)S(1)} %fusion.15, f32[512]{0:T(512)S(1)} %exp.53, bf16[512,512]{1,0:T(8,128)(2,1)} %copy-done.3, f32[128,128]{1,0:T(8,128)S(1)} %multiply_reduce_fusion, f32[]{:T(128)} %bitcast.15), kind=kOutput, calls=%fused_computation.99 | convolution fusion | flops 100941312 | bytes 725504 | tf_op jit(solution)/shard_map/cthd,chde->cthe/dot_general | solution.py:112
  93.1 0.2 fusion.29
  93.4 1.2 fusion.32
  94.7 1.0 collective-permute-start.1
  95.6 2.1 %collective-permute-start.2 = (bf16[4,32,128]{2,1,0:T(8,128)(2,1)S(1)}, bf16[4,32,128]{2,1,0:T(8,128)(2,1)S(1)}, u32[]{:S(2)}, u32[]{:S(2)}) collective-permute-start(bf16[4,32,128]{2,1,0:T(8,128)(2,1)S(1)} %get-tuple-element.43), channel_id=1, source_target_pairs={{0,2},{1,3},{2,0},{3,1},{4,6},{5,7},{6,4},{7,5},{8,10},{9,11},{10,... | collective-permute-start | bytes 98312 | tf_op jit(solution)/shard_map/ppermute | solution.py:137
  97.7 0.2 collective-permute-start.3
  98.0 0.6 collective-permute-done.1
  98.6 2.4 %collective-permute-done.2 = bf16[4,32,128]{2,1,0:T(8,128)(2,1)S(1)} collective-permute-done((bf16[4,32,128]{2,1,0:T(8,128)(2,1)S(1)}, bf16[4,32,128]{2,1,0:T(8,128)(2,1)S(1)}, u32[]{:S(2)}, u32[]{:S(2)}) %collective-permute-start.2) | collective-permute-done | bytes 32800 | tf_op jit(solution)/shard_map/ppermute | solution.py:137
  101.1 1.8 %collective-permute-done.3 = bf16[4,32,128]{2,1,0:T(8,128)(2,1)S(1)} collective-permute-done((bf16[4,32,128]{2,1,0:T(8,128)(2,1)S(1)}, bf16[4,32,128]{2,1,0:T(8,128)(2,1)S(1)}, u32[]{:S(2)}, u32[]{:S(2)}) %collective-permute-start.3) | collective-permute-done | bytes 32800 | tf_op jit(solution)/shard_map/ppermute | solution.py:137
  102.8 0.5 fusion.13
  103.5 2.8 %collective-permute-start.10 = (bf16[32,2048]{1,0:T(8,128)(2,1)S(1)}, bf16[32,2048]{1,0:T(8,128)(2,1)S(1)}, u32[]{:S(2)}, u32[]{:S(2)}) collective-permute-start(bf16[32,2048]{1,0:T(8,128)(2,1)S(1)} %get-tuple-element.38), channel_id=1, source_target_pairs={{0,12},{1,13},{2,14},{3,15},{4,0},{5,1},{6,2},{7,3},{8,4},{9,5},{1... | collective-permute-start | bytes 393224 | tf_op jit(solution)/shard_map/ppermute | solution.py:156
  106.3 2.5 %collective-permute-start.9 = (bf16[32,2048]{1,0:T(8,128)(2,1)S(1)}, bf16[32,2048]{1,0:T(8,128)(2,1)S(1)}, u32[]{:S(2)}, u32[]{:S(2)}) collective-permute-start(bf16[32,2048]{1,0:T(8,128)(2,1)S(1)} %get-tuple-element.40), channel_id=1, source_target_pairs={{0,8},{1,9},{2,10},{3,11},{4,12},{5,13},{6,14},{7,15},{8,0},{9,1},... | collective-permute-start | bytes 393224 | tf_op jit(solution)/shard_map/ppermute | solution.py:156
  108.8 1.4 %collective-permute-done.10 = bf16[32,2048]{1,0:T(8,128)(2,1)S(1)} collective-permute-done((bf16[32,2048]{1,0:T(8,128)(2,1)S(1)}, bf16[32,2048]{1,0:T(8,128)(2,1)S(1)}, u32[]{:S(2)}, u32[]{:S(2)}) %collective-permute-start.10) | collective-permute-done | bytes 131104 | tf_op jit(solution)/shard_map/ppermute | solution.py:156
  110.2 4.0 %collective-permute-done.8 = bf16[32,2048]{1,0:T(8,128)(2,1)S(1)} collective-permute-done((bf16[32,2048]{1,0:T(8,128)(2,1)S(1)}, bf16[32,2048]{1,0:T(8,128)(2,1)S(1)}, u32[]{:S(2)}, u32[]{:S(2)}) %collective-permute-start.8) | collective-permute-done | bytes 131104 | tf_op jit(solution)/shard_map/ppermute | solution.py:156
  114.2 0.7 fusion.27
  (40 shorter events, 1.4 us)
Async XLA Ops:
  6.5 46.8 %all-gather.3.cloned.1.call-start = ((), (), s32[]{:S(2)}) async-start(), calls=%async_computation.2 | async-start | bytes 1474560 | tf_op jit(solution)/shard_map/all_gather | solution.py:50
  10.4 0.7 copy-start.2
  13.5 39.8 %copy-start.4 = (f32[512,1]{0,1:T(1,128)S(1)}, f32[512,1]{0,1:T(1,128)}, u32[]{:S(2)}) copy-start(f32[512,1]{0,1:T(1,128)} %param.8) | copy-start | bytes 6148
  13.5 47.4 %all-to-all-start = ((bf16[16,32,2048]{2,1,0:T(8,128)(2,1)}), bf16[16,32,2048]{2,1,0:T(8,128)(2,1)}, u32[]{:S(2)}, u32[]{:S(2)}) async-start(bf16[16,32,2048]{2,1,0:T(8,128)(2,1)} %broadcast_in_dim.51), calls=%async_computation | async-start | bytes 4194304 | tf_op jit(solution)/shard_map/all_to_all | solution.py:14
  53.3 5.5 %collective-permute-start = (bf16[8,128,640]{2,1,0:T(8,128)(2,1)}, bf16[8,128,640]{2,1,0:T(8,128)(2,1)S(1)}, u32[]{:S(2)}, u32[]{:S(2)}) collective-permute-start(bf16[8,128,640]{2,1,0:T(8,128)(2,1)} %bitcast.120), channel_id=1, source_target_pairs={{0,16},{16,0},{32,48},{48,32},{64,80},{80,64},{96,112},{112,96},{1... | collective-permute-start | bytes 3932168 | tf_op jit(solution)/shard_map/ppermute | solution.py:51
  64.8 0.8 copy-start.3
  66.9 24.3 %all-to-all-start.1 = ((bf16[16,1,136,128]{3,2,1,0:T(8,128)(2,1)}), bf16[16,1,136,128]{3,2,1,0:T(8,128)(2,1)S(1)}, u32[]{:S(2)}, u32[]{:S(2)}) async-start(bf16[16,1,136,128]{3,2,1,0:T(8,128)(2,1)} %broadcast_in_dim.94), calls=%async_computation.1 | async-start | bytes 1114112 | tf_op jit(solution)/shard_map/all_to_all | solution.py:14
  74.2 0.8 copy-start
  75.1 9.2 %collective-permute-start.4 = (bf16[8,128,128]{2,1,0:T(8,128)(2,1)S(1)}, bf16[8,128,128]{2,1,0:T(8,128)(2,1)S(1)}, u32[]{:S(2)}, u32[]{:S(2)}) collective-permute-start(bf16[8,128,128]{2,1,0:T(8,128)(2,1)S(1)} %constant_dynamic-slice_fusion), channel_id=1, source_target_pairs={{0,1},{1,2},{2,3},{3,0},{4,5},{5,6},{6,7},{7,4},{8,9},{9,10},{10,1... | collective-permute-start | bytes 786440 | tf_op jit(solution)/shard_map/ppermute | solution.py:138
  75.7 10.7 %collective-permute-start.5 = (bf16[8,128,128]{2,1,0:T(8,128)(2,1)S(1)}, bf16[8,128,128]{2,1,0:T(8,128)(2,1)S(1)}, u32[]{:S(2)}, u32[]{:S(2)}) collective-permute-start(bf16[8,128,128]{2,1,0:T(8,128)(2,1)S(1)} %constant_dynamic-slice_fusion), channel_id=1, source_target_pairs={{0,2},{1,3},{2,0},{3,1},{4,6},{5,7},{6,4},{7,5},{8,10},{9,11},{10,... | collective-permute-start | bytes 786440 | tf_op jit(solution)/shard_map/ppermute | solution.py:138
  78.1 13.0 %collective-permute-start.6 = (bf16[8,128,128]{2,1,0:T(8,128)(2,1)S(1)}, bf16[8,128,128]{2,1,0:T(8,128)(2,1)S(1)}, u32[]{:S(2)}, u32[]{:S(2)}) collective-permute-start(bf16[8,128,128]{2,1,0:T(8,128)(2,1)S(1)} %constant_dynamic-slice_fusion), channel_id=1, source_target_pairs={{0,3},{1,0},{2,1},{3,2},{4,7},{5,4},{6,5},{7,6},{8,11},{9,8},{10,9... | collective-permute-start | bytes 786440 | tf_op jit(solution)/shard_map/ppermute | solution.py:138
  91.1 6.8 %collective-permute-start.7 = (bf16[3,8,128,128]{3,2,0,1:T(8,128)(2,1)S(1)}, bf16[3,8,128,128]{3,2,0,1:T(8,128)(2,1)S(1)}, u32[]{:S(2)}, u32[]{:S(2)}) collective-permute-start(bf16[3,8,128,128]{3,2,0,1:T(8,128)(2,1)S(1)} %pad_maximum_fusion.1), channel_id=1, source_target_pairs={{0,16},{16,0},{32,48},{48,32},{64,80},{80,64},{96,112},{112,96},{1... | collective-permute-start | bytes 2359304 | tf_op jit(solution)/shard_map/ppermute | solution.py:140
  93.4 9.5 %copy-start.1 = (bf16[2048,128]{1,0:T(8,128)(2,1)S(1)}, bf16[2048,128]{1,0:T(8,128)(2,1)}, u32[]{:S(2)}) copy-start(bf16[2048,128]{1,0:T(8,128)(2,1)} %copy-done) | copy-start | bytes 1572868
  94.7 4.0 %collective-permute-start.1 = (bf16[4,32,128]{2,1,0:T(8,128)(2,1)S(1)}, bf16[4,32,128]{2,1,0:T(8,128)(2,1)S(1)}, u32[]{:S(2)}, u32[]{:S(2)}) collective-permute-start(bf16[4,32,128]{2,1,0:T(8,128)(2,1)S(1)} %get-tuple-element.44), channel_id=1, source_target_pairs={{0,1},{1,2},{2,3},{3,0},{4,5},{5,6},{6,7},{7,4},{8,9},{9,10},{10,1... | collective-permute-start | bytes 98312 | tf_op jit(solution)/shard_map/ppermute | solution.py:137
  95.6 5.4 %collective-permute-start.2 = (bf16[4,32,128]{2,1,0:T(8,128)(2,1)S(1)}, bf16[4,32,128]{2,1,0:T(8,128)(2,1)S(1)}, u32[]{:S(2)}, u32[]{:S(2)}) collective-permute-start(bf16[4,32,128]{2,1,0:T(8,128)(2,1)S(1)} %get-tuple-element.43), channel_id=1, source_target_pairs={{0,2},{1,3},{2,0},{3,1},{4,6},{5,7},{6,4},{7,5},{8,10},{9,11},{10,... | collective-permute-start | bytes 98312 | tf_op jit(solution)/shard_map/ppermute | solution.py:137
  97.7 5.1 %collective-permute-start.3 = (bf16[4,32,128]{2,1,0:T(8,128)(2,1)S(1)}, bf16[4,32,128]{2,1,0:T(8,128)(2,1)S(1)}, u32[]{:S(2)}, u32[]{:S(2)}) collective-permute-start(bf16[4,32,128]{2,1,0:T(8,128)(2,1)S(1)} %get-tuple-element.42), channel_id=1, source_target_pairs={{0,3},{1,0},{2,1},{3,2},{4,7},{5,4},{6,5},{7,6},{8,11},{9,8},{10,9... | collective-permute-start | bytes 98312 | tf_op jit(solution)/shard_map/ppermute | solution.py:137
  103.5 6.7 %collective-permute-start.10 = (bf16[32,2048]{1,0:T(8,128)(2,1)S(1)}, bf16[32,2048]{1,0:T(8,128)(2,1)S(1)}, u32[]{:S(2)}, u32[]{:S(2)}) collective-permute-start(bf16[32,2048]{1,0:T(8,128)(2,1)S(1)} %get-tuple-element.38), channel_id=1, source_target_pairs={{0,12},{1,13},{2,14},{3,15},{4,0},{5,1},{6,2},{7,3},{8,4},{9,5},{1... | collective-permute-start | bytes 393224 | tf_op jit(solution)/shard_map/ppermute | solution.py:156
  106.3 7.9 %collective-permute-start.8 = (bf16[32,2048]{1,0:T(8,128)(2,1)S(1)}, bf16[32,2048]{1,0:T(8,128)(2,1)S(1)}, u32[]{:S(2)}, u32[]{:S(2)}) collective-permute-start(bf16[32,2048]{1,0:T(8,128)(2,1)S(1)} %get-tuple-element.36), channel_id=1, source_target_pairs={{0,4},{1,5},{2,6},{3,7},{4,8},{5,9},{6,10},{7,11},{8,12},{9,13},{1... | collective-permute-start | bytes 393224 | tf_op jit(solution)/shard_map/ppermute | solution.py:156
  106.3 7.9 %collective-permute-start.9 = (bf16[32,2048]{1,0:T(8,128)(2,1)S(1)}, bf16[32,2048]{1,0:T(8,128)(2,1)S(1)}, u32[]{:S(2)}, u32[]{:S(2)}) collective-permute-start(bf16[32,2048]{1,0:T(8,128)(2,1)S(1)} %get-tuple-element.40), channel_id=1, source_target_pairs={{0,8},{1,9},{2,10},{3,11},{4,12},{5,13},{6,14},{7,15},{8,0},{9,1},... | collective-permute-start | bytes 393224 | tf_op jit(solution)/shard_map/ppermute | solution.py:156
Sparse Core Ops, SparseCore 0:
  11.2 42.0 all-gather.2

commit v9 on v6

--- a/solution.py
+++ b/solution.py
@@ -14,31 +14,38 @@
     return lax.all_to_all(copies, axis, 0, 0, tiled=False)
 
 
+def fold_in(earlier, later):
+    return (earlier[0] + later[0], jnp.exp(later[0])[:, None, None] * earlier[1] + later[1])
+
+
+def shift_along(value, axis, pairs):
+    heads_here = value[1].shape[0]
+    extra = jnp.broadcast_to(value[0][:, None, None], (heads_here, PAD_ROWS, HEAD_DIM))
+    moved = lax.ppermute(jnp.concatenate([value[1], extra], axis=1), axis, pairs)
+    return (moved[:, HEAD_DIM, 0], moved[:, :HEAD_DIM, :])
+
+
 def prior_state(local_final, log_total, axis):
-    heads_here = local_final.shape[0]
-    high = log_total.astype(jnp.bfloat16)
-    low = (log_total - high.astype(jnp.float32)).astype(jnp.bfloat16)
-    extra = jnp.concatenate(
-        [
-            jnp.broadcast_to(high[:, None, None], (heads_here, 1, HEAD_DIM)),
-            jnp.broadcast_to(low[:, None, None], (heads_here, 1, HEAD_DIM)),
-            jnp.zeros((heads_here, PAD_ROWS - 2, HEAD_DIM), jnp.bfloat16),
-        ],
-        axis=1,
-    )
-    packed = jnp.concatenate([local_final.astype(jnp.bfloat16), extra], axis=1)
-    gathered = gather_by_exchange(packed, axis)
-    finals = gathered[:, :, :HEAD_DIM, :].astype(jnp.float32)
-    totals = gathered[:, :, HEAD_DIM, 0].astype(jnp.float32) + gathered[:, :, HEAD_DIM + 1, 0].astype(
-        jnp.float32
-    )
-    count = gathered.shape[0]
-    mine = lax.axis_index(axis)
-    order = jnp.arange(count, dtype=jnp.int32)
-    between = (order[:, None] < order[None, :]) & (order[None, :] < mine)
-    exponent = jnp.sum(jnp.where(between[:, :, None], totals[None, :, :], 0.0), axis=1)
-    weight = jnp.where((order < mine)[:, None], jnp.exp(exponent), 0.0)
-    return jnp.sum(weight[:, :, None, None] * finals, axis=0)
+    units = lax.axis_size(axis)
+    chips = units // 2
+    parity = lax.axis_index(axis) % 2
+    own = (log_total, local_final)
+    partner = shift_along(own, axis, [(t, t ^ 1) for t in range(units)])
+    first = jax.tree.map(lambda a, b: jnp.where(parity == 0, a, b), own, partner)
+    second = jax.tree.map(lambda a, b: jnp.where(parity == 0, b, a), own, partner)
+    chip_total = fold_in(first, second)
+
+    def from_chips_back(value, gap):
+        pairs = [(2 * z + c, 2 * (z + gap) + c) for z in range(chips - gap) for c in range(2)]
+        return shift_along(value, axis, pairs)
+
+    entering = fold_in(from_chips_back(chip_total, 2), from_chips_back(chip_total, 1))
+    gap = 2
+    while gap < chips:
+        entering = fold_in(from_chips_back(entering, gap), entering)
+        gap *= 2
+    with_first = fold_in(entering, first)
+    return jnp.where(parity == 0, entering[1], with_first[1])
 
 
 def shards(frames, log_decay, w_query, w_key, w_value, w_gate, w_out):

time: 115 us -> 125 us (1.087)
  starting transfers between devices: 22.9 us -> 38.9 us
  waiting for transfers between devices: 49.7 us -> 40.3 us
  between operations: 17.6 us -> 21.5 us
  local copies, waits for them, and re-layouts: 12 us -> 13.8 us
  other arithmetic: 4.12 us -> 2.67 us
    ppermute x0 -> x5, starting transfers between devices: none -> 20 us  [shift_along(): lax.ppermute(jnp.concatenate([value[1], extra], axis=1), axis, pairs)]
    ppermute x3, waiting for transfers between devices: 12.8 us -> 0.01 us  [shards(): fetched.append(lax.ppermute(own_half, 'head', across))]
    all_to_all x2 -> x1, starting transfers between devices: 11.7 us -> 7.55 us  [gather_by_exchange(): return lax.all_to_all(copies, axis, 0, 0, tiled=False)]
    slice x0 -> x4, local copies, waits for them, and re-layouts: none -> 2.17 us  [shift_along(): return (moved[:, HEAD_DIM, 0], moved[:, :HEAD_DIM, :])]
    ppermute x0 -> x5, waiting for transfers between devices: none -> 1.95 us  [shift_along(): lax.ppermute(jnp.concatenate([value[1], extra], axis=1), axis, pairs)]
    ppermute x3, starting transfers between devices: 2.11 us -> 3.65 us  [shards(): pieces.append(lax.ppermute(piece, 'head', across))]
    all_to_all x2 -> x1, waiting for transfers between devices: 23 us -> 24.3 us  [gather_by_exchange(): return lax.all_to_all(copies, axis, 0, 0, tiled=False)]
    broadcast_in_dim x2 -> x1, local copies, waits for them, and re-layouts: 3.35 us -> 2.48 us  [gather_by_exchange(): copies = jnp.broadcast_to(part[None], (count,) + part.shape)]
  transfers between devices with their start and end apart: 13 -> 17, of which waited for: 10 -> 10; matrix products, arithmetic and copies ran while one was open for 11% -> 10% of each run, Pallas kernels for 0% -> 0%
where the time goes in v9:
time: 125 us; the launch traced here: 124 us
  waiting for transfers between devices  40.3 us (32%)
  starting transfers between devices  38.9 us (31%)
  between operations  21.5 us (17%)
  local copies, waits for them, and re-layouts  13.8 us (11%)
  matrix products  6.6 us (5%)
  other arithmetic  2.67 us (2%)
    all_to_all x1, waiting for transfers between devices, gather_by_exchange(): return lax.all_to_all(copies, axis, 0, 0, tiled=False)  24.3 us
    ppermute x5, starting transfers between devices, shift_along(): lax.ppermute(jnp.concatenate([value[1], extra], axis=1), axis, pairs)  20 us
    all_to_all x1, starting transfers between devices, gather_by_exchange(): return lax.all_to_all(copies, axis, 0, 0, tiled=False)  7.55 us
    all_gather x1, waiting for transfers between devices, shards(): lax.all_gather(jnp.concatenate([w_query, w_key, w_value, w_gate, w_out],...  5.14 us
    ppermute x3, waiting for transfers between devices, shards(): pieces.append(lax.ppermute(piece, 'head', across))  4.98 us
    ppermute x3, starting transfers between devices, shards(): total = total + lax.ppermute(piece, 'head', down).astype(jnp.float32)  4.57 us
    ppermute x3, waiting for transfers between devices, shards(): total = total + lax.ppermute(piece, 'head', down).astype(jnp.float32)  3.97 us
    unnamed x10, local copies, waits for them, and re-layouts  3.75 us
  transfers between devices with their start and end apart: 17, of which 10 were waited for; matrix products, arithmetic and copies ran while one was open for 10% of the time, Pallas kernels for 0%

profile of v9, /device:TPU:6, one launch (start us, length us, event | category | flops | bytes accessed | tf_op | source)
XLA Modules:
  0.0 123.8 jit_solution(13400169880471158166)
XLA Ops:
  6.5 0.8 constant_dynamic-update-slice_fusion.4
  7.3 0.8 constant_dynamic-update-slice_fusion.3
  8.1 0.8 constant_dynamic-update-slice_fusion.2
  8.8 0.8 constant_dynamic-update-slice_fusion.1
  9.6 0.8 constant_dynamic-update-slice_fusion
  10.4 0.7 copy-done
  11.1 2.5 %broadcast_in_dim.27 = bf16[16,32,2048]{2,1,0:T(8,128)(2,1)} broadcast(bf16[32,2048]{1,0:T(8,128)(2,1)} %param.7), dimensions={1,2} | broadcast | bytes 2228224 | tf_op jit(solution)/shard_map/broadcast_in_dim | solution.py:13
  13.6 7.6 %all-to-all-start = ((bf16[16,32,2048]{2,1,0:T(8,128)(2,1)}), bf16[16,32,2048]{2,1,0:T(8,128)(2,1)S(1)}, u32[]{:S(2)}, u32[]{:S(2)}) async-start(bf16[16,32,2048]{2,1,0:T(8,128)(2,1)} %broadcast_in_dim.27), calls=%async_computation | async-start | bytes 4194304 | tf_op jit(solution)/shard_map/all_to_all | solution.py:14
  21.1 0.7 reduce_sum.29
  21.8 0.3 reduce-window.6
  22.5 0.6 slice.93
  23.1 0.6 slice.92
  25.1 24.3 %all-to-all-done = bf16[16,32,2048]{2,1,0:T(8,128)(2,1)S(1)} async-done(((bf16[16,32,2048]{2,1,0:T(8,128)(2,1)}), bf16[16,32,2048]{2,1,0:T(8,128)(2,1)S(1)}, u32[]{:S(2)}, u32[]{:S(2)}) %all-to-all-start) | async-done | bytes 2097184 | tf_op jit(solution)/shard_map/all_to_all | solution.py:14
  49.4 5.1 %all-gather.2.cloned.1.call-done = bf16[2048,640]{1,0:T(8,128)(2,1)} async-done(((bf16[128,640]{1,0:T(8,128)(2,1)}), bf16[2048,640]{1,0:T(8,128)(2,1)}) %all-gather.2.cloned.1.call-update) | async-done | bytes 2621456 | tf_op jit(solution)/shard_map/all_gather | solution.py:53
  54.5 2.8 %fusion.64 = (bf16[512,512]{1,0:T(8,128)(2,1)S(1)}, f32[512,512]{1,0:T(8,128)S(1)}) fusion(bf16[512,2048]{1,0:T(8,128)(2,1)S(1)} %bitcast.121, bf16[2048,640]{1,0:T(8,128)(2,1)} %all-gather.2.cloned.1.call-done), kind=kOutput, calls=%fused_computation.98 | convolution fusion | flops 1074003968 | bytes 5767168 | tf_op jit(solution)/shard_map/dot_general | solution.py:59
  57.4 0.3 fusion.17
  57.7 0.6 concatenate.20
  58.4 0.3 collective-permute-start
  58.7 0.6 slice.91
  59.3 0.6 slice.90
  61.3 1.1 slice.103
  62.4 0.5 slice.94
  65.6 2.8 %collective-permute-start.1 = (f32[1,136,128]{2,1,0:T(8,128)S(1)}, f32[1,136,128]{2,1,0:T(8,128)S(1)}, u32[]{:S(2)}, u32[]{:S(2)}) collective-permute-start(f32[1,136,128]{2,1,0:T(8,128)S(1)} %concatenate.21), channel_id=1, source_target_pairs={{0,32},{16,48},{32,64},{48,80},{64,96},{80,112},{96,128},{112,144}... | collective-permute-start | bytes 208904 | tf_op jit(solution)/shard_map/ppermute | solution.py:24
  68.4 4.2 %collective-permute-start.2 = (f32[1,136,128]{2,1,0:T(8,128)S(1)}, f32[1,136,128]{2,1,0:T(8,128)S(1)}, u32[]{:S(2)}, u32[]{:S(2)}) collective-permute-start(f32[1,136,128]{2,1,0:T(8,128)S(1)} %concatenate.21), channel_id=1, source_target_pairs={{0,64},{16,80},{32,96},{48,112},{64,128},{80,144},{96,160},{112,17... | collective-permute-start | bytes 208904 | tf_op jit(solution)/shard_map/ppermute | solution.py:24
  72.6 0.6 collective-permute-start.8
  73.3 2.4 %collective-permute-start.9 = (bf16[8,128,128]{2,1,0:T(8,128)(2,1)S(1)}, bf16[8,128,128]{2,1,0:T(8,128)(2,1)S(1)}, u32[]{:S(2)}, u32[]{:S(2)}) collective-permute-start(bf16[8,128,128]{2,1,0:T(8,128)(2,1)S(1)} %constant_dynamic-slice_fusion), channel_id=1, source_target_pairs={{0,2},{1,3},{2,0},{3,1},{4,6},{5,7},{6,4},{7,5},{8,10},{9,11},{10,... | collective-permute-start | bytes 786440 | tf_op jit(solution)/shard_map/ppermute | solution.py:138
  75.6 0.6 slice.96
  76.9 0.5 slice.99
  78.6 3.8 %collective-permute-start.3 = (f32[1,136,128]{2,1,0:T(8,128)S(1)}, f32[1,136,128]{2,1,0:T(8,128)S(1)}, u32[]{:S(2)}, u32[]{:S(2)}) collective-permute-start(f32[1,136,128]{2,1,0:T(8,128)S(1)} %concatenate.22), channel_id=1, source_target_pairs={{0,64},{16,80},{32,96},{48,112},{64,128},{80,144},{96,160},{112,17... | collective-permute-start | bytes 208904 | tf_op jit(solution)/shard_map/ppermute | solution.py:24
  82.4 1.6 %fusion.15 = f32[1,512,1,128]{3,1,2,0:T(8,128)S(1)} fusion(f32[512]{0:T(512)S(1)} %get-tuple-element.22, bf16[512,512]{1,0:T(8,128)(2,1)} %copy-done.1), kind=kOutput, calls=%fused_computation.16 | convolution fusion | flops 135528448 | bytes 659456 | tf_op jit(solution)/shard_map/while/body/eval_jaxpr/hts,shd->thd/dot_general | solution.py:95
  84.1 0.2 collective-permute-done.3
  84.3 0.5 slice.100
  85.6 8.9 %collective-permute-start.4 = (f32[1,136,128]{2,1,0:T(8,128)S(1)}, f32[1,136,128]{2,1,0:T(8,128)S(1)}, u32[]{:S(2)}, u32[]{:S(2)}) collective-permute-start(f32[1,136,128]{2,1,0:T(8,128)S(1)} %concatenate.23), channel_id=1, source_target_pairs={{0,128},{16,144},{32,160},{48,176},{64,192},{80,208},{96,224},{112... | collective-permute-start | bytes 208904 | tf_op jit(solution)/shard_map/ppermute | solution.py:24
  94.7 1.7 %collective-permute-done.4 = f32[1,136,128]{2,1,0:T(8,128)S(1)} collective-permute-done((f32[1,136,128]{2,1,0:T(8,128)S(1)}, f32[1,136,128]{2,1,0:T(8,128)S(1)}, u32[]{:S(2)}, u32[]{:S(2)}) %collective-permute-start.4) | collective-permute-done | bytes 69664 | tf_op jit(solution)/shard_map/ppermute | solution.py:24
  96.4 1.4 %fusion.65 = (f32[512]{0:T(512)S(1)}, f32[1,512,1,128]{3,1,2,0:T(8,128)S(1)}) fusion(f32[1,512,1,128]{3,1,2,0:T(8,128)S(1)} %fusion.15, f32[512]{0:T(512)S(1)} %exp.66, bf16[512,512]{1,0:T(8,128)(2,1)} %copy-done.1, f32[1,128,128]{2,1,0:T(8,128)S(1)} %fusion.51, f32[1,136,128]{2,1,0:T(8,128)S(1)} %collective-permute-done.4, f32[1,128,128]{2,1,0:T(8,128)S(1)} %fusion.17, ...), kind=kOutput, calls=%fused_computation.99 | convolution fusion | flops 101039616 | bytes 923648 | tf_op jit(solution)/shard_map/cthd,chde->cthe/dot_general | solution.py:112
  97.8 0.2 fusion.28
  98.3 2.4 %collective-permute-start.5 = (bf16[4,32,128]{2,1,0:T(8,128)(2,1)S(1)}, bf16[4,32,128]{2,1,0:T(8,128)(2,1)S(1)}, u32[]{:S(2)}, u32[]{:S(2)}) collective-permute-start(bf16[4,32,128]{2,1,0:T(8,128)(2,1)S(1)} %get-tuple-element.42), channel_id=1, source_target_pairs={{0,1},{1,2},{2,3},{3,0},{4,5},{5,6},{6,7},{7,4},{8,9},{9,10},{10,1... | collective-permute-start | bytes 98312 | tf_op jit(solution)/shard_map/ppermute | solution.py:137
  100.7 1.2 collective-permute-start.6
  102.3 3.8 %collective-permute-done.6 = bf16[4,32,128]{2,1,0:T(8,128)(2,1)S(1)} collective-permute-done((bf16[4,32,128]{2,1,0:T(8,128)(2,1)S(1)}, bf16[4,32,128]{2,1,0:T(8,128)(2,1)S(1)}, u32[]{:S(2)}, u32[]{:S(2)}) %collective-permute-start.6) | collective-permute-done | bytes 32800 | tf_op jit(solution)/shard_map/ppermute | solution.py:137
  106.2 0.9 collective-permute-done.7
  107.1 0.4 fusion.13
  107.7 0.9 collective-permute-start.12
  108.6 2.7 %collective-permute-start.13 = (bf16[32,2048]{1,0:T(8,128)(2,1)S(1)}, bf16[32,2048]{1,0:T(8,128)(2,1)S(1)}, u32[]{:S(2)}, u32[]{:S(2)}) collective-permute-start(bf16[32,2048]{1,0:T(8,128)(2,1)S(1)} %get-tuple-element.36), channel_id=1, source_target_pairs={{0,8},{1,9},{2,10},{3,11},{4,12},{5,13},{6,14},{7,15},{8,0},{9,1},... | collective-permute-start | bytes 393224 | tf_op jit(solution)/shard_map/ppermute | solution.py:156
  111.3 1.0 collective-permute-start.14
  112.3 1.7 %collective-permute-done.12 = bf16[32,2048]{1,0:T(8,128)(2,1)S(1)} collective-permute-done((bf16[32,2048]{1,0:T(8,128)(2,1)S(1)}, bf16[32,2048]{1,0:T(8,128)(2,1)S(1)}, u32[]{:S(2)}, u32[]{:S(2)}) %collective-permute-start.12) | collective-permute-done | bytes 131104 | tf_op jit(solution)/shard_map/ppermute | solution.py:156
  114.0 1.7 %collective-permute-done.13 = bf16[32,2048]{1,0:T(8,128)(2,1)S(1)} collective-permute-done((bf16[32,2048]{1,0:T(8,128)(2,1)S(1)}, bf16[32,2048]{1,0:T(8,128)(2,1)S(1)}, u32[]{:S(2)}, u32[]{:S(2)}) %collective-permute-start.13) | collective-permute-done | bytes 131104 | tf_op jit(solution)/shard_map/ppermute | solution.py:156
  115.6 0.6 collective-permute-done.14
  116.3 0.7 fusion.26
  (39 shorter events, 1.6 us)
Async XLA Ops:
  6.5 48.0 %all-gather.2.cloned.1.call-start = ((), (), s32[]{:S(2)}) async-start(), calls=%async_computation.1 | async-start | bytes 2785280 | tf_op jit(solution)/shard_map/all_gather | solution.py:53
  10.4 0.7 copy-start
  13.6 7.6 %copy-start.2 = (f32[512,1]{0,1:T(1,128)S(1)}, f32[512,1]{0,1:T(1,128)}, u32[]{:S(2)}) copy-start(f32[512,1]{0,1:T(1,128)} %param.8) | copy-start | bytes 6148
  13.6 35.8 %all-to-all-start = ((bf16[16,32,2048]{2,1,0:T(8,128)(2,1)}), bf16[16,32,2048]{2,1,0:T(8,128)(2,1)S(1)}, u32[]{:S(2)}, u32[]{:S(2)}) async-start(bf16[16,32,2048]{2,1,0:T(8,128)(2,1)} %broadcast_in_dim.27), calls=%async_computation | async-start | bytes 4194304 | tf_op jit(solution)/shard_map/all_to_all | solution.py:14
  57.4 1.3 %copy-start.1 = (bf16[512,512]{1,0:T(8,128)(2,1)}, bf16[512,512]{1,0:T(8,128)(2,1)S(1)}, u32[]{:S(2)}) copy-start(bf16[512,512]{1,0:T(8,128)(2,1)S(1)} %get-tuple-element.43) | copy-start | bytes 1572868
  58.4 4.0 %collective-permute-start = (f32[1,136,128]{2,1,0:T(8,128)S(1)}, f32[1,136,128]{2,1,0:T(8,128)S(1)}, u32[]{:S(2)}, u32[]{:S(2)}) collective-permute-start(f32[1,136,128]{2,1,0:T(8,128)S(1)} %concatenate.20), channel_id=1, source_target_pairs={{0,16},{16,0},{32,48},{48,32},{64,80},{80,64},{96,112},{112,96},{1... | collective-permute-start | bytes 208904 | tf_op jit(solution)/shard_map/ppermute | solution.py:24
  65.6 10.1 %collective-permute-start.1 = (f32[1,136,128]{2,1,0:T(8,128)S(1)}, f32[1,136,128]{2,1,0:T(8,128)S(1)}, u32[]{:S(2)}, u32[]{:S(2)}) collective-permute-start(f32[1,136,128]{2,1,0:T(8,128)S(1)} %concatenate.21), channel_id=1, source_target_pairs={{0,32},{16,48},{32,64},{48,80},{64,96},{80,112},{96,128},{112,144}... | collective-permute-start | bytes 208904 | tf_op jit(solution)/shard_map/ppermute | solution.py:24
  68.4 8.5 %collective-permute-start.2 = (f32[1,136,128]{2,1,0:T(8,128)S(1)}, f32[1,136,128]{2,1,0:T(8,128)S(1)}, u32[]{:S(2)}, u32[]{:S(2)}) collective-permute-start(f32[1,136,128]{2,1,0:T(8,128)S(1)} %concatenate.21), channel_id=1, source_target_pairs={{0,64},{16,80},{32,96},{48,112},{64,128},{80,144},{96,160},{112,17... | collective-permute-start | bytes 208904 | tf_op jit(solution)/shard_map/ppermute | solution.py:24
  72.6 21.8 %collective-permute-start.8 = (bf16[8,128,128]{2,1,0:T(8,128)(2,1)S(1)}, bf16[8,128,128]{2,1,0:T(8,128)(2,1)S(1)}, u32[]{:S(2)}, u32[]{:S(2)}) collective-permute-start(bf16[8,128,128]{2,1,0:T(8,128)(2,1)S(1)} %constant_dynamic-slice_fusion), channel_id=1, source_target_pairs={{0,1},{1,2},{2,3},{3,0},{4,5},{5,6},{6,7},{7,4},{8,9},{9,10},{10,1... | collective-permute-start | bytes 786440 | tf_op jit(solution)/shard_map/ppermute | solution.py:138
  73.3 21.2 %collective-permute-start.9 = (bf16[8,128,128]{2,1,0:T(8,128)(2,1)S(1)}, bf16[8,128,128]{2,1,0:T(8,128)(2,1)S(1)}, u32[]{:S(2)}, u32[]{:S(2)}) collective-permute-start(bf16[8,128,128]{2,1,0:T(8,128)(2,1)S(1)} %constant_dynamic-slice_fusion), channel_id=1, source_target_pairs={{0,2},{1,3},{2,0},{3,1},{4,6},{5,7},{6,4},{7,5},{8,10},{9,11},{10,... | collective-permute-start | bytes 786440 | tf_op jit(solution)/shard_map/ppermute | solution.py:138
  75.6 18.9 %collective-permute-start.10 = (bf16[8,128,128]{2,1,0:T(8,128)(2,1)S(1)}, bf16[8,128,128]{2,1,0:T(8,128)(2,1)S(1)}, u32[]{:S(2)}, u32[]{:S(2)}) collective-permute-start(bf16[8,128,128]{2,1,0:T(8,128)(2,1)S(1)} %constant_dynamic-slice_fusion), channel_id=1, source_target_pairs={{0,3},{1,0},{2,1},{3,2},{4,7},{5,4},{6,5},{7,6},{8,11},{9,8},{10,9... | collective-permute-start | bytes 786440 | tf_op jit(solution)/shard_map/ppermute | solution.py:138
  78.6 5.7 %collective-permute-start.3 = (f32[1,136,128]{2,1,0:T(8,128)S(1)}, f32[1,136,128]{2,1,0:T(8,128)S(1)}, u32[]{:S(2)}, u32[]{:S(2)}) collective-permute-start(f32[1,136,128]{2,1,0:T(8,128)S(1)} %concatenate.22), channel_id=1, source_target_pairs={{0,64},{16,80},{32,96},{48,112},{64,128},{80,144},{96,160},{112,17... | collective-permute-start | bytes 208904 | tf_op jit(solution)/shard_map/ppermute | solution.py:24
  85.6 10.8 %collective-permute-start.4 = (f32[1,136,128]{2,1,0:T(8,128)S(1)}, f32[1,136,128]{2,1,0:T(8,128)S(1)}, u32[]{:S(2)}, u32[]{:S(2)}) collective-permute-start(f32[1,136,128]{2,1,0:T(8,128)S(1)} %concatenate.23), channel_id=1, source_target_pairs={{0,128},{16,144},{32,160},{48,176},{64,192},{80,208},{96,224},{112... | collective-permute-start | bytes 208904 | tf_op jit(solution)/shard_map/ppermute | solution.py:24
  94.6 7.4 %collective-permute-start.11 = (bf16[3,8,128,128]{3,2,0,1:T(8,128)(2,1)S(1)}, bf16[3,8,128,128]{3,2,0,1:T(8,128)(2,1)S(1)}, u32[]{:S(2)}, u32[]{:S(2)}) collective-permute-start(bf16[3,8,128,128]{3,2,0,1:T(8,128)(2,1)S(1)} %pad_maximum_fusion), channel_id=1, source_target_pairs={{0,16},{16,0},{32,48},{48,32},{64,80},{80,64},{96,112},{112,96},{1... | collective-permute-start | bytes 2359304 | tf_op jit(solution)/shard_map/ppermute | solution.py:140
  98.3 4.0 %collective-permute-start.5 = (bf16[4,32,128]{2,1,0:T(8,128)(2,1)S(1)}, bf16[4,32,128]{2,1,0:T(8,128)(2,1)S(1)}, u32[]{:S(2)}, u32[]{:S(2)}) collective-permute-start(bf16[4,32,128]{2,1,0:T(8,128)(2,1)S(1)} %get-tuple-element.42), channel_id=1, source_target_pairs={{0,1},{1,2},{2,3},{3,0},{4,5},{5,6},{6,7},{7,4},{8,9},{9,10},{10,1... | collective-permute-start | bytes 98312 | tf_op jit(solution)/shard_map/ppermute | solution.py:137
  100.7 5.4 %collective-permute-start.6 = (bf16[4,32,128]{2,1,0:T(8,128)(2,1)S(1)}, bf16[4,32,128]{2,1,0:T(8,128)(2,1)S(1)}, u32[]{:S(2)}, u32[]{:S(2)}) collective-permute-start(bf16[4,32,128]{2,1,0:T(8,128)(2,1)S(1)} %get-tuple-element.41), channel_id=1, source_target_pairs={{0,2},{1,3},{2,0},{3,1},{4,6},{5,7},{6,4},{7,5},{8,10},{9,11},{10,... | collective-permute-start | bytes 98312 | tf_op jit(solution)/shard_map/ppermute | solution.py:137
  102.0 5.1 %collective-permute-start.7 = (bf16[4,32,128]{2,1,0:T(8,128)(2,1)S(1)}, bf16[4,32,128]{2,1,0:T(8,128)(2,1)S(1)}, u32[]{:S(2)}, u32[]{:S(2)}) collective-permute-start(bf16[4,32,128]{2,1,0:T(8,128)(2,1)S(1)} %get-tuple-element.40), channel_id=1, source_target_pairs={{0,3},{1,0},{2,1},{3,2},{4,7},{5,4},{6,5},{7,6},{8,11},{9,8},{10,9... | collective-permute-start | bytes 98312 | tf_op jit(solution)/shard_map/ppermute | solution.py:137
  107.7 6.3 %collective-permute-start.12 = (bf16[32,2048]{1,0:T(8,128)(2,1)S(1)}, bf16[32,2048]{1,0:T(8,128)(2,1)S(1)}, u32[]{:S(2)}, u32[]{:S(2)}) collective-permute-start(bf16[32,2048]{1,0:T(8,128)(2,1)S(1)} %get-tuple-element.25), channel_id=1, source_target_pairs={{0,4},{1,5},{2,6},{3,7},{4,8},{5,9},{6,10},{7,11},{8,12},{9,13},{1... | collective-permute-start | bytes 393224 | tf_op jit(solution)/shard_map/ppermute | solution.py:156
  108.6 7.1 %collective-permute-start.13 = (bf16[32,2048]{1,0:T(8,128)(2,1)S(1)}, bf16[32,2048]{1,0:T(8,128)(2,1)S(1)}, u32[]{:S(2)}, u32[]{:S(2)}) collective-permute-start(bf16[32,2048]{1,0:T(8,128)(2,1)S(1)} %get-tuple-element.36), channel_id=1, source_target_pairs={{0,8},{1,9},{2,10},{3,11},{4,12},{5,13},{6,14},{7,15},{8,0},{9,1},... | collective-permute-start | bytes 393224 | tf_op jit(solution)/shard_map/ppermute | solution.py:156
  111.3 5.0 %collective-permute-start.14 = (bf16[32,2048]{1,0:T(8,128)(2,1)S(1)}, bf16[32,2048]{1,0:T(8,128)(2,1)S(1)}, u32[]{:S(2)}, u32[]{:S(2)}) collective-permute-start(bf16[32,2048]{1,0:T(8,128)(2,1)S(1)} %get-tuple-element.26), channel_id=1, source_target_pairs={{0,12},{1,13},{2,14},{3,15},{4,0},{5,1},{6,2},{7,3},{8,4},{9,5},{1... | collective-permute-start | bytes 393224 | tf_op jit(solution)/shard_map/ppermute | solution.py:156
Sparse Core Ops, SparseCore 0:
  11.2 43.2 all-gather.1

commit v10 on v6

--- a/solution.py
+++ b/solution.py
@@ -44,35 +44,35 @@
 def shards(frames, log_decay, w_query, w_key, w_value, w_gate, w_out):
     head_width = w_query.shape[1]
     stacked = lax.all_gather(
-        jnp.concatenate([w_query, w_key, w_value, w_gate, w_out], axis=1), "tm", axis=0, tiled=True
+        jnp.concatenate([w_key, w_value, w_query, w_gate, w_out], axis=1), "tm", axis=0, tiled=True
     )
-    joined = stacked[:, : 4 * head_width]
     out_blocks = stacked[:, 4 * head_width :].reshape(-1, head_width, w_out.shape[1])
     frames_here = gather_by_exchange(frames, "head").reshape(-1, frames.shape[1])
-    projected = jnp.dot(
-        frames_here,
-        joined,
-        preferred_element_type=jnp.float32,
+    key_value = jnp.dot(
+        frames_here, stacked[:, : 2 * head_width], preferred_element_type=jnp.float32
     )
-    local_len = projected.shape[0]
+    query_gate = jnp.dot(
+        frames_here, stacked[:, 2 * head_width : 4 * head_width], preferred_element_type=jnp.float32
+    )
+    local_len = key_value.shape[0]
     heads_here = head_width // HEAD_DIM
     block_count = local_len // BLOCK
     query_blocks = (
-        projected[:, :head_width]
+        query_gate[:, :head_width]
         .astype(jnp.bfloat16)
         .reshape(block_count, BLOCK, heads_here, HEAD_DIM)
     )
     key_blocks = (
-        projected[:, head_width : 2 * head_width]
+        key_value[:, :head_width]
         .astype(jnp.bfloat16)
         .reshape(block_count, BLOCK, heads_here, HEAD_DIM)
     )
     value_blocks = (
-        projected[:, 2 * head_width : 3 * head_width]
+        key_value[:, head_width:]
         .astype(jnp.bfloat16)
         .reshape(block_count, BLOCK, heads_here, HEAD_DIM)
     )
-    gate_all = projected[:, 3 * head_width :]
+    gate_all = query_gate[:, head_width:]
     running_blocks = jnp.cumsum(log_decay.reshape(block_count, BLOCK, heads_here), axis=1)
     slice_ordinal = jnp.arange(BLOCK, dtype=jnp.int32)
     causal = slice_ordinal[:, None] >= slice_ordinal[None, :]

time: 115 us -> 115 us (level)
  waiting for transfers between devices: 49.7 us -> 45.9 us
  other arithmetic: 4.12 us -> 5.87 us
    ppermute x3, waiting for transfers between devices: 12.8 us -> 10.1 us  [shards(): fetched.append(lax.ppermute(own_half, 'head', across))]
    dot_general x1 -> x2, matrix products: 3.83 us -> 4.74 us  [the longest x1 2.76 us: shards(): jnp.dot(frames_here, stacked[:, 2 * head_width:4 * head_width], preferred...]
  transfers between devices with their start and end apart: 13 -> 13, of which waited for: 10 -> 10; matrix products, arithmetic and copies ran while one was open for 11% -> 16% of each run, Pallas kernels for 0% -> 0%
where the time goes in v10:
time: 115 us; the launch traced here: 113 us
  waiting for transfers between devices  45.9 us (40%)
  starting transfers between devices  22.8 us (20%)
  between operations  17.6 us (15%)
  local copies, waits for them, and re-layouts  12.9 us (11%)
  matrix products  8.38 us (7%)
  other arithmetic  5.87 us (5%)
    all_to_all x2, waiting for transfers between devices, gather_by_exchange(): return lax.all_to_all(copies, axis, 0, 0, tiled=False)  23 us
    all_to_all x2, starting transfers between devices, gather_by_exchange(): return lax.all_to_all(copies, axis, 0, 0, tiled=False)  11.7 us
    ppermute x3, waiting for transfers between devices, shards(): fetched.append(lax.ppermute(own_half, 'head', across))  10.1 us
    ppermute x3, starting transfers between devices, shards(): total = total + lax.ppermute(piece, 'head', down).astype(jnp.float32)  5.2 us
    all_gather x1, waiting for transfers between devices, shards(): lax.all_gather(jnp.concatenate([w_key, w_value, w_query, w_gate, w_out],...  5.11 us
    ppermute x3, waiting for transfers between devices, shards(): total = total + lax.ppermute(piece, 'head', down).astype(jnp.float32)  4.22 us
    unnamed x10, local copies, waits for them, and re-layouts  3.75 us
    ppermute x3, starting transfers between devices, shards(): fetched.append(lax.ppermute(own_half, 'head', across))  3.65 us
  transfers between devices with their start and end apart: 13, of which 10 were waited for; matrix products, arithmetic and copies ran while one was open for 16% of the time, Pallas kernels for 0%

profile of v10, /device:TPU:6, one launch (start us, length us, event | category | flops | bytes accessed | tf_op | source)
XLA Modules:
  0.0 113.4 jit_solution(3355077317872897272)
XLA Ops:
  6.5 0.8 constant_dynamic-update-slice_fusion.4
  7.3 0.8 constant_dynamic-update-slice_fusion.3
  8.1 0.8 constant_dynamic-update-slice_fusion.2
  8.8 0.8 constant_dynamic-update-slice_fusion.1
  9.6 0.8 constant_dynamic-update-slice_fusion
  10.4 0.7 copy-done
  11.1 2.5 %broadcast_in_dim.51 = bf16[16,32,2048]{2,1,0:T(8,128)(2,1)} broadcast(bf16[32,2048]{1,0:T(8,128)(2,1)} %param.7), dimensions={1,2} | broadcast | bytes 2228224 | tf_op jit(solution)/shard_map/broadcast_in_dim | solution.py:13
  13.5 7.6 %all-to-all-start = ((bf16[16,32,2048]{2,1,0:T(8,128)(2,1)}), bf16[16,32,2048]{2,1,0:T(8,128)(2,1)S(1)}, u32[]{:S(2)}, u32[]{:S(2)}) async-start(bf16[16,32,2048]{2,1,0:T(8,128)(2,1)} %broadcast_in_dim.51), calls=%async_computation | async-start | bytes 4194304 | tf_op jit(solution)/shard_map/all_to_all | solution.py:14
  21.1 0.6 reduce_sum.47
  21.7 0.3 reduce-window.6
  22.0 0.2 slice_reduce_fusion
  22.4 0.6 slice.74
  23.1 0.6 slice.73
  26.4 23.0 %all-to-all-done = bf16[16,32,2048]{2,1,0:T(8,128)(2,1)S(1)} async-done(((bf16[16,32,2048]{2,1,0:T(8,128)(2,1)}), bf16[16,32,2048]{2,1,0:T(8,128)(2,1)S(1)}, u32[]{:S(2)}, u32[]{:S(2)}) %all-to-all-start) | async-done | bytes 2097184 | tf_op jit(solution)/shard_map/all_to_all | solution.py:14
  49.4 5.1 %all-gather.2.cloned.1.call-done = bf16[2048,640]{1,0:T(8,128)(2,1)} async-done(((bf16[128,640]{1,0:T(8,128)(2,1)}), bf16[2048,640]{1,0:T(8,128)(2,1)}) %all-gather.2.cloned.1.call-update) | async-done | bytes 2621456 | tf_op jit(solution)/shard_map/all_gather | solution.py:46
  54.5 2.0 %fusion.10 = bf16[512,256]{0,1:T(8,128)(2,1)S(1)} fusion(bf16[512,2048]{1,0:T(8,128)(2,1)S(1)} %bitcast.113, bf16[2048,640]{1,0:T(8,128)(2,1)} %all-gather.2.cloned.1.call-done), kind=kOutput, calls=%fused_computation.14 | convolution fusion | flops 537001984 | bytes 3407872 | tf_op jit(solution)/shard_map/dot_general | solution.py:51
  56.5 0.2 fusion.14
  56.8 0.9 broadcast_in_dim.94
  57.7 4.1 %all-to-all-start.1 = ((bf16[16,1,136,128]{3,2,1,0:T(8,128)(2,1)}), bf16[16,1,136,128]{3,2,1,0:T(8,128)(2,1)S(1)}, u32[]{:S(2)}, u32[]{:S(2)}) async-start(bf16[16,1,136,128]{3,2,1,0:T(8,128)(2,1)} %broadcast_in_dim.94), calls=%async_computation.1 | async-start | bytes 1114112 | tf_op jit(solution)/shard_map/all_to_all | solution.py:14
  62.0 0.7 slice.72
  62.7 0.6 slice.71
  64.7 1.1 slice.78
  65.8 0.7 constant_dynamic-slice_fusion
  66.5 2.8 %collective-permute-start.3 = (bf16[8,128,128]{2,1,0:T(8,128)(2,1)}, bf16[8,128,128]{2,1,0:T(8,128)(2,1)S(1)}, u32[]{:S(2)}, u32[]{:S(2)}) collective-permute-start(bf16[8,128,128]{2,1,0:T(8,128)(2,1)} %constant_dynamic-slice_fusion), channel_id=1, source_target_pairs={{0,1},{1,2},{2,3},{3,0},{4,5},{5,6},{6,7},{7,4},{8,9},{9,10},{10,1... | collective-permute-start | bytes 786440 | tf_op jit(solution)/shard_map/ppermute | solution.py:131
  69.4 0.7 collective-permute-start.5
  70.2 2.8 %convolution_bitcast_fusion = f32[512,256]{0,1:T(8,128)} fusion(bf16[512,2048]{1,0:T(8,128)(2,1)S(1)} %bitcast.114, bf16[2048,640]{1,0:T(8,128)(2,1)} %all-gather.2.cloned.1.call-done), kind=kOutput, calls=%fused_computation.12 | convolution fusion | flops 536870912 | bytes 3670016 | tf_op jit(solution)/shard_map/dot_general | solution.py:54
  72.9 1.6 %fusion.11 = f32[1,512,1,128]{1,3,2,0:T(8,128)S(1)} fusion(f32[512]{0:T(512)S(1)} %get-tuple-element.22, bf16[512,256]{0,1:T(8,128)(2,1)} %copy-done.2, f32[512,256]{0,1:T(8,128)} %convolution_bitcast_fusion), kind=kOutput, calls=%fused_computation.16 | convolution fusion | flops 135528448 | bytes 659456 | tf_op jit(solution)/shard_map/while/body/eval_jaxpr/hts,shd->thd/dot_general | solution.py:88
  74.5 6.7 %collective-permute-done.3 = bf16[8,128,128]{2,1,0:T(8,128)(2,1)S(1)} collective-permute-done((bf16[8,128,128]{2,1,0:T(8,128)(2,1)}, bf16[8,128,128]{2,1,0:T(8,128)(2,1)S(1)}, u32[]{:S(2)}, u32[]{:S(2)}) %collective-permute-start.3) | collective-permute-done | bytes 262176 | tf_op jit(solution)/shard_map/ppermute | solution.py:131
  81.3 3.4 %collective-permute-done.5 = bf16[8,128,128]{2,1,0:T(8,128)(2,1)} collective-permute-done((bf16[8,128,128]{2,1,0:T(8,128)(2,1)}, bf16[8,128,128]{2,1,0:T(8,128)(2,1)}, u32[]{:S(2)}, u32[]{:S(2)}) %collective-permute-start.5) | collective-permute-done | bytes 262176 | tf_op jit(solution)/shard_map/ppermute | solution.py:131
  84.7 1.1 pad_maximum_fusion
  85.9 0.2 fusion.50
  86.4 1.4 %fusion.53 = (f32[512]{0:T(512)S(1)}, f32[1,512,1,128]{1,3,2,0:T(8,128)S(1)}) fusion(f32[1,512,1,128]{1,3,2,0:T(8,128)S(1)} %fusion.11, f32[512]{0:T(512)S(1)} %exp.53, f32[512,256]{0,1:T(8,128)} %convolution_bitcast_fusion, f32[128,128]{1,0:T(8,128)S(1)} %multiply_reduce_fusion, f32[]{:T(128)} %bitcast.12), kind=kOutput, calls=%fused_computation.96 | convolution fusion | flops 100941312 | bytes 725504 | tf_op jit(solution)/shard_map/cthd,chde->cthe/dot_general | solution.py:105
  87.9 1.0 fusion.30
  89.1 1.0 collective-permute-start
  90.0 0.3 collective-permute-start.1
  90.3 0.8 collective-permute-start.2
  91.2 1.2 %broadcast_select_fusion.1 = (bf16[3,8,128,128]{3,2,0,1:T(8,128)(2,1)S(1)}, bf16[3,8,128,128]{3,2,0,1:T(8,128)(2,1)S(1)}) fusion(bf16[3,8,128,128]{3,2,0,1:T(8,128)(2,1)S(1)} %collective-permute-done.6, pred[]{:T(512)S(6)} %eq.13, bf16[1,8,128,128]{3,2,0,1:T(8,128)(2,1)} %bitcast.42, bf16[1,8,128,128]{3,2,0,1:T(8,128)(2,1)} %bitcast.41, ...), kind=kLoop, calls=%fused_computation.30 | loop fusion | flops 1572864 | bytes 3145729 | tf_op jit(solution)/shard_map/jit(_where)/select_n | solution.py:134
  92.3 0.9 collective-permute-done
  93.3 2.2 %collective-permute-done.1 = bf16[4,32,128]{2,1,0:T(8,128)(2,1)S(1)} collective-permute-done((bf16[4,32,128]{2,1,0:T(8,128)(2,1)S(1)}, bf16[4,32,128]{2,1,0:T(8,128)(2,1)S(1)}, u32[]{:S(2)}, u32[]{:S(2)}) %collective-permute-start.1) | collective-permute-done | bytes 32800 | tf_op jit(solution)/shard_map/ppermute | solution.py:130
  95.5 0.3 collective-permute-done.2
  95.8 0.5 fusion.8
  96.4 1.1 collective-permute-start.7
  97.5 2.7 %collective-permute-start.8 = (bf16[32,2048]{1,0:T(8,128)(2,1)S(1)}, bf16[32,2048]{1,0:T(8,128)(2,1)S(1)}, u32[]{:S(2)}, u32[]{:S(2)}) collective-permute-start(bf16[32,2048]{1,0:T(8,128)(2,1)S(1)} %get-tuple-element.36), channel_id=1, source_target_pairs={{0,8},{1,9},{2,10},{3,11},{4,12},{5,13},{6,14},{7,15},{8,0},{9,1},... | collective-permute-start | bytes 393224 | tf_op jit(solution)/shard_map/ppermute | solution.py:149
  100.2 1.4 %collective-permute-start.9 = (bf16[32,2048]{1,0:T(8,128)(2,1)S(1)}, bf16[32,2048]{1,0:T(8,128)(2,1)S(1)}, u32[]{:S(2)}, u32[]{:S(2)}) collective-permute-start(bf16[32,2048]{1,0:T(8,128)(2,1)S(1)} %get-tuple-element.26), channel_id=1, source_target_pairs={{0,12},{1,13},{2,14},{3,15},{4,0},{5,1},{6,2},{7,3},{8,4},{9,5},{1... | collective-permute-start | bytes 393224 | tf_op jit(solution)/shard_map/ppermute | solution.py:149
  101.6 2.5 %collective-permute-done.7 = bf16[32,2048]{1,0:T(8,128)(2,1)S(1)} collective-permute-done((bf16[32,2048]{1,0:T(8,128)(2,1)S(1)}, bf16[32,2048]{1,0:T(8,128)(2,1)S(1)}, u32[]{:S(2)}, u32[]{:S(2)}) %collective-permute-start.7) | collective-permute-done | bytes 131104 | tf_op jit(solution)/shard_map/ppermute | solution.py:149
  104.1 1.4 %collective-permute-done.8 = bf16[32,2048]{1,0:T(8,128)(2,1)S(1)} collective-permute-done((bf16[32,2048]{1,0:T(8,128)(2,1)S(1)}, bf16[32,2048]{1,0:T(8,128)(2,1)S(1)}, u32[]{:S(2)}, u32[]{:S(2)}) %collective-permute-start.8) | collective-permute-done | bytes 131104 | tf_op jit(solution)/shard_map/ppermute | solution.py:149
  105.5 0.3 collective-permute-done.9
  105.9 0.7 fusion.25
  (33 shorter events, 1.6 us)
Async XLA Ops:
  6.5 48.0 %all-gather.2.cloned.1.call-start = ((), (), s32[]{:S(2)}) async-start(), calls=%async_computation.2 | async-start | bytes 2785280 | tf_op jit(solution)/shard_map/all_gather | solution.py:46
  10.4 0.7 copy-start
  13.5 7.6 %copy-start.1 = (f32[512,1]{0,1:T(1,128)S(1)}, f32[512,1]{0,1:T(1,128)}, u32[]{:S(2)}) copy-start(f32[512,1]{0,1:T(1,128)} %param.8) | copy-start | bytes 6148
  13.5 35.8 %all-to-all-start = ((bf16[16,32,2048]{2,1,0:T(8,128)(2,1)}), bf16[16,32,2048]{2,1,0:T(8,128)(2,1)S(1)}, u32[]{:S(2)}, u32[]{:S(2)}) async-start(bf16[16,32,2048]{2,1,0:T(8,128)(2,1)} %broadcast_in_dim.51), calls=%async_computation | async-start | bytes 4194304 | tf_op jit(solution)/shard_map/all_to_all | solution.py:14
  56.5 1.2 %copy-start.2 = (bf16[512,256]{0,1:T(8,128)(2,1)}, bf16[512,256]{0,1:T(8,128)(2,1)S(1)}, u32[]{:S(2)}) copy-start(bf16[512,256]{0,1:T(8,128)(2,1)S(1)} %fusion.10) | copy-start | bytes 786436
  57.7 28.2 %all-to-all-start.1 = ((bf16[16,1,136,128]{3,2,1,0:T(8,128)(2,1)}), bf16[16,1,136,128]{3,2,1,0:T(8,128)(2,1)S(1)}, u32[]{:S(2)}, u32[]{:S(2)}) async-start(bf16[16,1,136,128]{3,2,1,0:T(8,128)(2,1)} %broadcast_in_dim.94), calls=%async_computation.1 | async-start | bytes 1114112 | tf_op jit(solution)/shard_map/all_to_all | solution.py:14
  66.5 14.8 %collective-permute-start.3 = (bf16[8,128,128]{2,1,0:T(8,128)(2,1)}, bf16[8,128,128]{2,1,0:T(8,128)(2,1)S(1)}, u32[]{:S(2)}, u32[]{:S(2)}) collective-permute-start(bf16[8,128,128]{2,1,0:T(8,128)(2,1)} %constant_dynamic-slice_fusion), channel_id=1, source_target_pairs={{0,1},{1,2},{2,3},{3,0},{4,5},{5,6},{6,7},{7,4},{8,9},{9,10},{10,1... | collective-permute-start | bytes 786440 | tf_op jit(solution)/shard_map/ppermute | solution.py:131
  69.3 12.0 %collective-permute-start.4 = (bf16[8,128,128]{2,1,0:T(8,128)(2,1)}, bf16[8,128,128]{2,1,0:T(8,128)(2,1)}, u32[]{:S(2)}, u32[]{:S(2)}) collective-permute-start(bf16[8,128,128]{2,1,0:T(8,128)(2,1)} %constant_dynamic-slice_fusion), channel_id=1, source_target_pairs={{0,2},{1,3},{2,0},{3,1},{4,6},{5,7},{6,4},{7,5},{8,10},{9,11},{10,... | collective-permute-start | bytes 786440 | tf_op jit(solution)/shard_map/ppermute | solution.py:131
  69.4 15.2 %collective-permute-start.5 = (bf16[8,128,128]{2,1,0:T(8,128)(2,1)}, bf16[8,128,128]{2,1,0:T(8,128)(2,1)}, u32[]{:S(2)}, u32[]{:S(2)}) collective-permute-start(bf16[8,128,128]{2,1,0:T(8,128)(2,1)} %constant_dynamic-slice_fusion), channel_id=1, source_target_pairs={{0,3},{1,0},{2,1},{3,2},{4,7},{5,4},{6,5},{7,6},{8,11},{9,8},{10,9... | collective-permute-start | bytes 786440 | tf_op jit(solution)/shard_map/ppermute | solution.py:131
  85.8 5.4 %collective-permute-start.6 = (bf16[3,8,128,128]{3,2,0,1:T(8,128)(2,1)S(1)}, bf16[3,8,128,128]{3,2,0,1:T(8,128)(2,1)S(1)}, u32[]{:S(2)}, u32[]{:S(2)}) collective-permute-start(bf16[3,8,128,128]{3,2,0,1:T(8,128)(2,1)S(1)} %pad_maximum_fusion), channel_id=1, source_target_pairs={{0,16},{16,0},{32,48},{48,32},{64,80},{80,64},{96,112},{112,96},{1... | collective-permute-start | bytes 2359304 | tf_op jit(solution)/shard_map/ppermute | solution.py:133
  89.1 4.2 %collective-permute-start = (bf16[4,32,128]{2,1,0:T(8,128)(2,1)S(1)}, bf16[4,32,128]{2,1,0:T(8,128)(2,1)S(1)}, u32[]{:S(2)}, u32[]{:S(2)}) collective-permute-start(bf16[4,32,128]{2,1,0:T(8,128)(2,1)S(1)} %get-tuple-element.42), channel_id=1, source_target_pairs={{0,1},{1,2},{2,3},{3,0},{4,5},{5,6},{6,7},{7,4},{8,9},{9,10},{10,1... | collective-permute-start | bytes 98312 | tf_op jit(solution)/shard_map/ppermute | solution.py:130
  90.0 5.4 %collective-permute-start.1 = (bf16[4,32,128]{2,1,0:T(8,128)(2,1)S(1)}, bf16[4,32,128]{2,1,0:T(8,128)(2,1)S(1)}, u32[]{:S(2)}, u32[]{:S(2)}) collective-permute-start(bf16[4,32,128]{2,1,0:T(8,128)(2,1)S(1)} %get-tuple-element.41), channel_id=1, source_target_pairs={{0,2},{1,3},{2,0},{3,1},{4,6},{5,7},{6,4},{7,5},{8,10},{9,11},{10,... | collective-permute-start | bytes 98312 | tf_op jit(solution)/shard_map/ppermute | solution.py:130
  90.3 5.5 %collective-permute-start.2 = (bf16[4,32,128]{2,1,0:T(8,128)(2,1)S(1)}, bf16[4,32,128]{2,1,0:T(8,128)(2,1)S(1)}, u32[]{:S(2)}, u32[]{:S(2)}) collective-permute-start(bf16[4,32,128]{2,1,0:T(8,128)(2,1)S(1)} %get-tuple-element.40), channel_id=1, source_target_pairs={{0,3},{1,0},{2,1},{3,2},{4,7},{5,4},{6,5},{7,6},{8,11},{9,8},{10,9... | collective-permute-start | bytes 98312 | tf_op jit(solution)/shard_map/ppermute | solution.py:130
  96.4 7.7 %collective-permute-start.7 = (bf16[32,2048]{1,0:T(8,128)(2,1)S(1)}, bf16[32,2048]{1,0:T(8,128)(2,1)S(1)}, u32[]{:S(2)}, u32[]{:S(2)}) collective-permute-start(bf16[32,2048]{1,0:T(8,128)(2,1)S(1)} %get-tuple-element.25), channel_id=1, source_target_pairs={{0,4},{1,5},{2,6},{3,7},{4,8},{5,9},{6,10},{7,11},{8,12},{9,13},{1... | collective-permute-start | bytes 393224 | tf_op jit(solution)/shard_map/ppermute | solution.py:149
  97.5 8.0 %collective-permute-start.8 = (bf16[32,2048]{1,0:T(8,128)(2,1)S(1)}, bf16[32,2048]{1,0:T(8,128)(2,1)S(1)}, u32[]{:S(2)}, u32[]{:S(2)}) collective-permute-start(bf16[32,2048]{1,0:T(8,128)(2,1)S(1)} %get-tuple-element.36), channel_id=1, source_target_pairs={{0,8},{1,9},{2,10},{3,11},{4,12},{5,13},{6,14},{7,15},{8,0},{9,1},... | collective-permute-start | bytes 393224 | tf_op jit(solution)/shard_map/ppermute | solution.py:149
  100.2 5.6 %collective-permute-start.9 = (bf16[32,2048]{1,0:T(8,128)(2,1)S(1)}, bf16[32,2048]{1,0:T(8,128)(2,1)S(1)}, u32[]{:S(2)}, u32[]{:S(2)}) collective-permute-start(bf16[32,2048]{1,0:T(8,128)(2,1)S(1)} %get-tuple-element.26), channel_id=1, source_target_pairs={{0,12},{1,13},{2,14},{3,15},{4,0},{5,1},{6,2},{7,3},{8,4},{9,5},{1... | collective-permute-start | bytes 393224 | tf_op jit(solution)/shard_map/ppermute | solution.py:149
Sparse Core Ops, SparseCore 0:
  11.2 43.2 all-gather.1

commit v11 on v6

--- a/solution.py
+++ b/solution.py
@@ -8,14 +8,14 @@
 PAD_ROWS = 8
 
 
-def gather_by_exchange(part, axis):
-    count = lax.axis_size(axis)
+def gather_by_exchange(part, axis, groups=None):
+    count = lax.axis_size(axis) if groups is None else len(groups[0])
     copies = jnp.broadcast_to(part[None], (count,) + part.shape)
-    return lax.all_to_all(copies, axis, 0, 0, tiled=False)
+    return lax.all_to_all(copies, axis, 0, 0, tiled=False, axis_index_groups=groups)
 
 
-def prior_state(local_final, log_total, axis):
-    heads_here = local_final.shape[0]
+def pack_state(state, log_total):
+    heads_here = state.shape[0]
     high = log_total.astype(jnp.bfloat16)
     low = (log_total - high.astype(jnp.float32)).astype(jnp.bfloat16)
     extra = jnp.concatenate(
@@ -26,19 +26,39 @@
         ],
         axis=1,
     )
-    packed = jnp.concatenate([local_final.astype(jnp.bfloat16), extra], axis=1)
-    gathered = gather_by_exchange(packed, axis)
+    return jnp.concatenate([state.astype(jnp.bfloat16), extra], axis=1)
+
+
+def prior_state(local_final, log_total, axis):
+    units = lax.axis_size(axis)
+    heads_here = local_final.shape[0]
+    parity = lax.axis_index(axis) % 2
+    chip = lax.axis_index(axis) // 2
+    extra = jnp.broadcast_to(log_total[:, None, None], (heads_here, PAD_ROWS, HEAD_DIM))
+    moved = lax.ppermute(
+        jnp.concatenate([local_final, extra], axis=1), axis, [(t, t ^ 1) for t in range(units)]
+    )
+    partner_state, partner_total = moved[:, :HEAD_DIM, :], moved[:, HEAD_DIM, 0]
+    first_state = jnp.where(parity == 0, local_final, partner_state)
+    first_total = jnp.where(parity == 0, log_total, partner_total)
+    second_state = jnp.where(parity == 0, partner_state, local_final)
+    second_total = jnp.where(parity == 0, partner_total, log_total)
+    chip_state = jnp.exp(second_total)[:, None, None] * first_state + second_state
+    chip_total = first_total + second_total
+    same_place = [[t for t in range(units) if t % 2 == p] for p in range(2)]
+    gathered = gather_by_exchange(pack_state(chip_state, chip_total), axis, same_place)
     finals = gathered[:, :, :HEAD_DIM, :].astype(jnp.float32)
     totals = gathered[:, :, HEAD_DIM, 0].astype(jnp.float32) + gathered[:, :, HEAD_DIM + 1, 0].astype(
         jnp.float32
     )
     count = gathered.shape[0]
-    mine = lax.axis_index(axis)
     order = jnp.arange(count, dtype=jnp.int32)
-    between = (order[:, None] < order[None, :]) & (order[None, :] < mine)
+    between = (order[:, None] < order[None, :]) & (order[None, :] < chip)
     exponent = jnp.sum(jnp.where(between[:, :, None], totals[None, :, :], 0.0), axis=1)
-    weight = jnp.where((order < mine)[:, None], jnp.exp(exponent), 0.0)
-    return jnp.sum(weight[:, :, None, None] * finals, axis=0)
+    weight = jnp.where((order < chip)[:, None], jnp.exp(exponent), 0.0)
+    entering = jnp.sum(weight[:, :, None, None] * finals, axis=0)
+    with_first = jnp.exp(first_total)[:, None, None] * entering + first_state
+    return jnp.where(parity == 0, entering, with_first)
 
 
 def shards(frames, log_decay, w_query, w_key, w_value, w_gate, w_out):

time: 115 us -> 119 us (1.035)
  waiting for transfers between devices: 49.7 us -> 53.2 us
    ppermute x3, waiting for transfers between devices: 4.22 us -> 6 us  [shards(): total = total + lax.ppermute(piece, 'head', down).astype(jnp.float32)]
    all_to_all x2, waiting for transfers between devices: 23 us -> 24.2 us  [gather_by_exchange(): lax.all_to_all(copies, axis, 0, 0, tiled=False, axis_index_groups=groups)]
    unnamed x10 -> x12, local copies, waits for them, and re-layouts: 3.75 us -> 3.74 us
  transfers between devices with their start and end apart: 13 -> 14, of which waited for: 10 -> 9; matrix products, arithmetic and copies ran while one was open for 11% -> 10% of each run, Pallas kernels for 0% -> 0%
where the time goes in v11:
time: 119 us; the launch traced here: 118 us
  waiting for transfers between devices  53.2 us (45%)
  starting transfers between devices  22.4 us (19%)
  between operations  18.5 us (16%)
  local copies, waits for them, and re-layouts  12.9 us (11%)
  matrix products  6.58 us (6%)
  other arithmetic  4.02 us (3%)
    all_to_all x2, waiting for transfers between devices, gather_by_exchange(): lax.all_to_all(copies, axis, 0, 0, tiled=False, axis_index_groups=groups)  24.2 us
    ppermute x3, waiting for transfers between devices, shards(): fetched.append(lax.ppermute(own_half, 'head', across))  13.3 us
    all_to_all x2, starting transfers between devices, gather_by_exchange(): lax.all_to_all(copies, axis, 0, 0, tiled=False, axis_index_groups=groups)  11.5 us
    ppermute x3, waiting for transfers between devices, shards(): total = total + lax.ppermute(piece, 'head', down).astype(jnp.float32)  6 us
    all_gather x1, waiting for transfers between devices, shards(): lax.all_gather(jnp.concatenate([w_query, w_key, w_value, w_gate, w_out],...  5.2 us
    ppermute x3, starting transfers between devices, shards(): total = total + lax.ppermute(piece, 'head', down).astype(jnp.float32)  4.6 us
    ppermute x3, waiting for transfers between devices, shards(): pieces.append(lax.ppermute(piece, 'head', across))  4.5 us
    dot_general x1, matrix products, shards(): projected = jnp.dot(frames_here, joined, preferred_element_type=jnp.float32)  3.82 us
  transfers between devices with their start and end apart: 14, of which 9 were waited for; matrix products, arithmetic and copies ran while one was open for 10% of the time, Pallas kernels for 0%

profile of v11, /device:TPU:6, one launch (start us, length us, event | category | flops | bytes accessed | tf_op | source)
XLA Modules:
  0.0 117.7 jit_solution(1481133064924455337)
XLA Ops:
  6.5 0.8 constant_dynamic-update-slice_fusion.4
  7.3 0.8 constant_dynamic-update-slice_fusion.3
  8.1 0.8 constant_dynamic-update-slice_fusion.2
  8.8 0.8 constant_dynamic-update-slice_fusion.1
  9.6 0.8 constant_dynamic-update-slice_fusion
  10.4 0.7 copy-done.1
  11.1 2.5 %broadcast_in_dim.46 = bf16[16,32,2048]{2,1,0:T(8,128)(2,1)} broadcast(bf16[32,2048]{1,0:T(8,128)(2,1)} %param.7), dimensions={1,2} | broadcast | bytes 2228224 | tf_op jit(solution)/shard_map/broadcast_in_dim | solution.py:13
  13.5 7.6 %all-to-all-start = ((bf16[16,32,2048]{2,1,0:T(8,128)(2,1)}), bf16[16,32,2048]{2,1,0:T(8,128)(2,1)S(1)}, u32[]{:S(2)}, u32[]{:S(2)}) async-start(bf16[16,32,2048]{2,1,0:T(8,128)(2,1)} %broadcast_in_dim.46), calls=%async_computation | async-start | bytes 4194304 | tf_op jit(solution)/shard_map/all_to_all | solution.py:14
  21.1 0.6 reduce_sum.49
  21.7 0.3 reduce-window.6
  22.0 0.2 slice_reduce_fusion
  22.2 0.2 reduce-window.9
  22.4 0.7 slice.77
  23.1 0.6 slice.76
  25.1 24.2 %all-to-all-done = bf16[16,32,2048]{2,1,0:T(8,128)(2,1)S(1)} async-done(((bf16[16,32,2048]{2,1,0:T(8,128)(2,1)}), bf16[16,32,2048]{2,1,0:T(8,128)(2,1)S(1)}, u32[]{:S(2)}, u32[]{:S(2)}) %all-to-all-start) | async-done | bytes 2097184 | tf_op jit(solution)/shard_map/all_to_all | solution.py:14
  49.4 5.2 %all-gather.2.cloned.1.call-done = bf16[2048,640]{1,0:T(8,128)(2,1)} async-done(((bf16[128,640]{1,0:T(8,128)(2,1)}), bf16[2048,640]{1,0:T(8,128)(2,1)}) %all-gather.2.cloned.1.call-update) | async-done | bytes 2621456 | tf_op jit(solution)/shard_map/all_gather | solution.py:66
  54.6 3.8 %fusion.62 = (bf16[512,512]{1,0:T(8,128)(2,1)S(1)}, f32[512,512]{1,0:T(8,128)}) fusion(bf16[512,2048]{1,0:T(8,128)(2,1)S(1)} %bitcast.133, bf16[2048,640]{1,0:T(8,128)(2,1)} %all-gather.2.cloned.1.call-done), kind=kOutput, calls=%fused_computation.102 | convolution fusion | flops 1074003968 | bytes 5767168 | tf_op jit(solution)/shard_map/dot_general | solution.py:72
  58.4 0.3 fusion.17
  58.7 0.5 concatenate.13
  59.3 0.3 collective-permute-start
  59.6 0.6 slice.75
  60.2 0.6 slice.74
  62.1 1.1 slice.83
  63.2 0.5 slice.78
  66.3 0.7 broadcast_in_dim.60
  67.0 3.9 %all-to-all-start.1 = ((bf16[8,1,136,128]{3,2,1,0:T(8,128)(2,1)}), bf16[8,1,136,128]{3,2,1,0:T(8,128)(2,1)S(1)}, u32[]{:S(2)}, u32[]{:S(2)}) async-start(bf16[8,1,136,128]{3,2,1,0:T(8,128)(2,1)} %broadcast_in_dim.60), calls=%async_computation.1 | async-start | bytes 557056 | tf_op jit(solution)/shard_map/all_to_all | solution.py:14
  71.0 2.8 %collective-permute-start.4 = (bf16[8,128,128]{2,1,0:T(8,128)(2,1)S(1)}, bf16[8,128,128]{2,1,0:T(8,128)(2,1)S(1)}, u32[]{:S(2)}, u32[]{:S(2)}) collective-permute-start(bf16[8,128,128]{2,1,0:T(8,128)(2,1)S(1)} %constant_dynamic-slice_fusion), channel_id=1, source_target_pairs={{0,1},{1,2},{2,3},{3,0},{4,5},{5,6},{6,7},{7,4},{8,9},{9,10},{10,1... | collective-permute-start | bytes 786440 | tf_op jit(solution)/shard_map/ppermute | solution.py:151
  73.8 0.2 collective-permute-start.5
  74.0 0.7 collective-permute-start.6
  74.7 0.5 fusion.15
  75.3 9.9 %collective-permute-done.4 = bf16[8,128,128]{2,1,0:T(8,128)(2,1)S(1)} collective-permute-done((bf16[8,128,128]{2,1,0:T(8,128)(2,1)S(1)}, bf16[8,128,128]{2,1,0:T(8,128)(2,1)S(1)}, u32[]{:S(2)}, u32[]{:S(2)}) %collective-permute-start.4) | collective-permute-done | bytes 262176 | tf_op jit(solution)/shard_map/ppermute | solution.py:151
  85.2 3.4 %collective-permute-done.6 = bf16[8,128,128]{2,1,0:T(8,128)(2,1)S(1)} collective-permute-done((bf16[8,128,128]{2,1,0:T(8,128)(2,1)S(1)}, bf16[8,128,128]{2,1,0:T(8,128)(2,1)S(1)}, u32[]{:S(2)}, u32[]{:S(2)}) %collective-permute-start.6) | collective-permute-done | bytes 262176 | tf_op jit(solution)/shard_map/ppermute | solution.py:151
  88.8 0.1 fusion.59
  89.2 1.5 %fusion.63 = (f32[512]{0:T(512)S(1)}, f32[1,512,1,128]{3,1,2,0:T(8,128)S(1)}) fusion(f32[1,512,1,128]{3,1,2,0:T(8,128)S(1)} %fusion.15, f32[512]{0:T(512)S(1)} %exp.61, bf16[512,512]{1,0:T(8,128)(2,1)} %copy-done.2, f32[128,128]{1,0:T(8,128)S(1)} %multiply_reduce_fusion, f32[1,128,128]{2,1,0:T(8,128)S(1)} %fusion.17, f32[1,136,128]{2,1,0:T(8,128)} %copy-done, ...), kind=kOutput, calls=%fused_computation.103 | convolution fusion | flops 101006848 | bytes 857600 | tf_op jit(solution)/shard_map/cthd,chde->cthe/dot_general | solution.py:125
  90.7 0.2 fusion.28
  90.9 1.2 fusion.31
  92.1 1.0 collective-permute-start.1
  93.1 0.3 collective-permute-start.2
  93.4 0.8 collective-permute-start.3
  94.3 2.0 %collective-permute-done.1 = bf16[4,32,128]{2,1,0:T(8,128)(2,1)S(1)} collective-permute-done((bf16[4,32,128]{2,1,0:T(8,128)(2,1)S(1)}, bf16[4,32,128]{2,1,0:T(8,128)(2,1)S(1)}, u32[]{:S(2)}, u32[]{:S(2)}) %collective-permute-start.1) | collective-permute-done | bytes 32800 | tf_op jit(solution)/shard_map/ppermute | solution.py:150
  96.3 2.2 %collective-permute-done.2 = bf16[4,32,128]{2,1,0:T(8,128)(2,1)S(1)} collective-permute-done((bf16[4,32,128]{2,1,0:T(8,128)(2,1)S(1)}, bf16[4,32,128]{2,1,0:T(8,128)(2,1)S(1)}, u32[]{:S(2)}, u32[]{:S(2)}) %collective-permute-start.2) | collective-permute-done | bytes 32800 | tf_op jit(solution)/shard_map/ppermute | solution.py:150
  98.5 0.3 collective-permute-done.3
  98.9 0.5 fusion.13
  99.5 2.3 %collective-permute-start.10 = (bf16[32,2048]{1,0:T(8,128)(2,1)S(1)}, bf16[32,2048]{1,0:T(8,128)(2,1)S(1)}, u32[]{:S(2)}, u32[]{:S(2)}) collective-permute-start(bf16[32,2048]{1,0:T(8,128)(2,1)S(1)} %get-tuple-element.26), channel_id=1, source_target_pairs={{0,12},{1,13},{2,14},{3,15},{4,0},{5,1},{6,2},{7,3},{8,4},{9,5},{1... | collective-permute-start | bytes 393224 | tf_op jit(solution)/shard_map/ppermute | solution.py:169
  101.8 2.3 %collective-permute-start.9 = (bf16[32,2048]{1,0:T(8,128)(2,1)S(1)}, bf16[32,2048]{1,0:T(8,128)(2,1)S(1)}, u32[]{:S(2)}, u32[]{:S(2)}) collective-permute-start(bf16[32,2048]{1,0:T(8,128)(2,1)S(1)} %get-tuple-element.36), channel_id=1, source_target_pairs={{0,8},{1,9},{2,10},{3,11},{4,12},{5,13},{6,14},{7,15},{8,0},{9,1},... | collective-permute-start | bytes 393224 | tf_op jit(solution)/shard_map/ppermute | solution.py:169
  104.1 0.4 collective-permute-done.10
  104.5 5.6 %collective-permute-done.8 = bf16[32,2048]{1,0:T(8,128)(2,1)S(1)} collective-permute-done((bf16[32,2048]{1,0:T(8,128)(2,1)S(1)}, bf16[32,2048]{1,0:T(8,128)(2,1)S(1)}, u32[]{:S(2)}, u32[]{:S(2)}) %collective-permute-start.8) | collective-permute-done | bytes 131104 | tf_op jit(solution)/shard_map/ppermute | solution.py:169
  110.1 0.7 fusion.26
  (38 shorter events, 1.3 us)
Async XLA Ops:
  6.5 48.0 %all-gather.2.cloned.1.call-start = ((), (), s32[]{:S(2)}) async-start(), calls=%async_computation.2 | async-start | bytes 2785280 | tf_op jit(solution)/shard_map/all_gather | solution.py:66
  10.4 0.7 copy-start.1
  13.5 7.6 %copy-start.3 = (f32[512,1]{0,1:T(1,128)S(1)}, f32[512,1]{0,1:T(1,128)}, u32[]{:S(2)}) copy-start(f32[512,1]{0,1:T(1,128)} %param.8) | copy-start | bytes 6148
  13.5 35.8 %all-to-all-start = ((bf16[16,32,2048]{2,1,0:T(8,128)(2,1)}), bf16[16,32,2048]{2,1,0:T(8,128)(2,1)S(1)}, u32[]{:S(2)}, u32[]{:S(2)}) async-start(bf16[16,32,2048]{2,1,0:T(8,128)(2,1)} %broadcast_in_dim.46), calls=%async_computation | async-start | bytes 4194304 | tf_op jit(solution)/shard_map/all_to_all | solution.py:14
  58.4 30.2 %copy-start.2 = (bf16[512,512]{1,0:T(8,128)(2,1)}, bf16[512,512]{1,0:T(8,128)(2,1)S(1)}, u32[]{:S(2)}) copy-start(bf16[512,512]{1,0:T(8,128)(2,1)S(1)} %get-tuple-element.43) | copy-start | bytes 1572868
  59.3 3.9 %collective-permute-start = (f32[1,136,128]{2,1,0:T(8,128)S(1)}, f32[1,136,128]{2,1,0:T(8,128)S(1)}, u32[]{:S(2)}, u32[]{:S(2)}) collective-permute-start(f32[1,136,128]{2,1,0:T(8,128)S(1)} %concatenate.13), channel_id=1, source_target_pairs={{0,16},{16,0},{32,48},{48,32},{64,80},{80,64},{96,112},{112,96},{1... | collective-permute-start | bytes 208904 | tf_op jit(solution)/shard_map/ppermute | solution.py:38
  63.2 7.7 %copy-start = (f32[1,136,128]{2,1,0:T(8,128)}, f32[1,136,128]{2,1,0:T(8,128)S(1)}, u32[]{:S(2)}) copy-start(f32[1,136,128]{2,1,0:T(8,128)S(1)} %collective-permute-done) | copy-start | bytes 208900
  67.0 21.8 %all-to-all-start.1 = ((bf16[8,1,136,128]{3,2,1,0:T(8,128)(2,1)}), bf16[8,1,136,128]{3,2,1,0:T(8,128)(2,1)S(1)}, u32[]{:S(2)}, u32[]{:S(2)}) async-start(bf16[8,1,136,128]{3,2,1,0:T(8,128)(2,1)} %broadcast_in_dim.60), calls=%async_computation.1 | async-start | bytes 557056 | tf_op jit(solution)/shard_map/all_to_all | solution.py:14
  71.0 14.2 %collective-permute-start.4 = (bf16[8,128,128]{2,1,0:T(8,128)(2,1)S(1)}, bf16[8,128,128]{2,1,0:T(8,128)(2,1)S(1)}, u32[]{:S(2)}, u32[]{:S(2)}) collective-permute-start(bf16[8,128,128]{2,1,0:T(8,128)(2,1)S(1)} %constant_dynamic-slice_fusion), channel_id=1, source_target_pairs={{0,1},{1,2},{2,3},{3,0},{4,5},{5,6},{6,7},{7,4},{8,9},{9,10},{10,1... | collective-permute-start | bytes 786440 | tf_op jit(solution)/shard_map/ppermute | solution.py:151
  73.8 11.4 %collective-permute-start.5 = (bf16[8,128,128]{2,1,0:T(8,128)(2,1)S(1)}, bf16[8,128,128]{2,1,0:T(8,128)(2,1)S(1)}, u32[]{:S(2)}, u32[]{:S(2)}) collective-permute-start(bf16[8,128,128]{2,1,0:T(8,128)(2,1)S(1)} %constant_dynamic-slice_fusion), channel_id=1, source_target_pairs={{0,2},{1,3},{2,0},{3,1},{4,6},{5,7},{6,4},{7,5},{8,10},{9,11},{10,... | collective-permute-start | bytes 786440 | tf_op jit(solution)/shard_map/ppermute | solution.py:151
  74.0 14.6 %collective-permute-start.6 = (bf16[8,128,128]{2,1,0:T(8,128)(2,1)S(1)}, bf16[8,128,128]{2,1,0:T(8,128)(2,1)S(1)}, u32[]{:S(2)}, u32[]{:S(2)}) collective-permute-start(bf16[8,128,128]{2,1,0:T(8,128)(2,1)S(1)} %constant_dynamic-slice_fusion), channel_id=1, source_target_pairs={{0,3},{1,0},{2,1},{3,2},{4,7},{5,4},{6,5},{7,6},{8,11},{9,8},{10,9... | collective-permute-start | bytes 786440 | tf_op jit(solution)/shard_map/ppermute | solution.py:151
  88.7 5.5 %collective-permute-start.7 = (bf16[3,8,128,128]{3,2,0,1:T(8,128)(2,1)S(1)}, bf16[3,8,128,128]{3,2,0,1:T(8,128)(2,1)S(1)}, u32[]{:S(2)}, u32[]{:S(2)}) collective-permute-start(bf16[3,8,128,128]{3,2,0,1:T(8,128)(2,1)S(1)} %pad_maximum_fusion), channel_id=1, source_target_pairs={{0,16},{16,0},{32,48},{48,32},{64,80},{80,64},{96,112},{112,96},{1... | collective-permute-start | bytes 2359304 | tf_op jit(solution)/shard_map/ppermute | solution.py:153
  92.1 4.2 %collective-permute-start.1 = (bf16[4,32,128]{2,1,0:T(8,128)(2,1)S(1)}, bf16[4,32,128]{2,1,0:T(8,128)(2,1)S(1)}, u32[]{:S(2)}, u32[]{:S(2)}) collective-permute-start(bf16[4,32,128]{2,1,0:T(8,128)(2,1)S(1)} %get-tuple-element.42), channel_id=1, source_target_pairs={{0,1},{1,2},{2,3},{3,0},{4,5},{5,6},{6,7},{7,4},{8,9},{9,10},{10,1... | collective-permute-start | bytes 98312 | tf_op jit(solution)/shard_map/ppermute | solution.py:150
  93.1 5.4 %collective-permute-start.2 = (bf16[4,32,128]{2,1,0:T(8,128)(2,1)S(1)}, bf16[4,32,128]{2,1,0:T(8,128)(2,1)S(1)}, u32[]{:S(2)}, u32[]{:S(2)}) collective-permute-start(bf16[4,32,128]{2,1,0:T(8,128)(2,1)S(1)} %get-tuple-element.41), channel_id=1, source_target_pairs={{0,2},{1,3},{2,0},{3,1},{4,6},{5,7},{6,4},{7,5},{8,10},{9,11},{10,... | collective-permute-start | bytes 98312 | tf_op jit(solution)/shard_map/ppermute | solution.py:150
  93.4 5.5 %collective-permute-start.3 = (bf16[4,32,128]{2,1,0:T(8,128)(2,1)S(1)}, bf16[4,32,128]{2,1,0:T(8,128)(2,1)S(1)}, u32[]{:S(2)}, u32[]{:S(2)}) collective-permute-start(bf16[4,32,128]{2,1,0:T(8,128)(2,1)S(1)} %get-tuple-element.40), channel_id=1, source_target_pairs={{0,3},{1,0},{2,1},{3,2},{4,7},{5,4},{6,5},{7,6},{8,11},{9,8},{10,9... | collective-permute-start | bytes 98312 | tf_op jit(solution)/shard_map/ppermute | solution.py:150
  99.5 5.0 %collective-permute-start.10 = (bf16[32,2048]{1,0:T(8,128)(2,1)S(1)}, bf16[32,2048]{1,0:T(8,128)(2,1)S(1)}, u32[]{:S(2)}, u32[]{:S(2)}) collective-permute-start(bf16[32,2048]{1,0:T(8,128)(2,1)S(1)} %get-tuple-element.26), channel_id=1, source_target_pairs={{0,12},{1,13},{2,14},{3,15},{4,0},{5,1},{6,2},{7,3},{8,4},{9,5},{1... | collective-permute-start | bytes 393224 | tf_op jit(solution)/shard_map/ppermute | solution.py:169
  101.8 8.3 %collective-permute-start.8 = (bf16[32,2048]{1,0:T(8,128)(2,1)S(1)}, bf16[32,2048]{1,0:T(8,128)(2,1)S(1)}, u32[]{:S(2)}, u32[]{:S(2)}) collective-permute-start(bf16[32,2048]{1,0:T(8,128)(2,1)S(1)} %get-tuple-element.25), channel_id=1, source_target_pairs={{0,4},{1,5},{2,6},{3,7},{4,8},{5,9},{6,10},{7,11},{8,12},{9,13},{1... | collective-permute-start | bytes 393224 | tf_op jit(solution)/shard_map/ppermute | solution.py:169
  101.8 8.3 %collective-permute-start.9 = (bf16[32,2048]{1,0:T(8,128)(2,1)S(1)}, bf16[32,2048]{1,0:T(8,128)(2,1)S(1)}, u32[]{:S(2)}, u32[]{:S(2)}) collective-permute-start(bf16[32,2048]{1,0:T(8,128)(2,1)S(1)} %get-tuple-element.36), channel_id=1, source_target_pairs={{0,8},{1,9},{2,10},{3,11},{4,12},{5,13},{6,14},{7,15},{8,0},{9,1},... | collective-permute-start | bytes 393224 | tf_op jit(solution)/shard_map/ppermute | solution.py:169
Sparse Core Ops, SparseCore 0:
  11.2 43.3 all-gather.1

commit v12 on v6

--- a/solution.py
+++ b/solution.py
@@ -43,9 +43,13 @@
 
 def shards(frames, log_decay, w_query, w_key, w_value, w_gate, w_out):
     head_width = w_query.shape[1]
-    stacked = lax.all_gather(
-        jnp.concatenate([w_query, w_key, w_value, w_gate, w_out], axis=1), "tm", axis=0, tiled=True
+    blocks = [w_query, w_key, w_value, w_gate, w_out]
+    width = sum(block.shape[1] for block in blocks)
+    packed = sum(
+        jnp.pad(block, ((0, 0), (start, width - start - block.shape[1])))
+        for start, block in zip(range(0, width, head_width), blocks)
     )
+    stacked = lax.all_gather(packed, "tm", axis=0, tiled=True)
     joined = stacked[:, : 4 * head_width]
     out_blocks = stacked[:, 4 * head_width :].reshape(-1, head_width, w_out.shape[1])
     frames_here = gather_by_exchange(frames, "head").reshape(-1, frames.shape[1])

time: 115 us -> 112 us (0.974)
  local copies, waits for them, and re-layouts: 12 us -> 7.53 us
  other arithmetic: 4.12 us -> 5.63 us
    unnamed x10 -> x4, local copies, waits for them, and re-layouts: 3.75 us -> 0.01 us
    add x0 -> x1, other arithmetic: none -> 1.52 us  [shards(): sum((jnp.pad(block, ((0, 0), (start, width - start - block.shape[1]))) fo...]
where the time goes in v12:
time: 112 us; the launch traced here: 111 us
  waiting for transfers between devices  49.4 us (44%)
  starting transfers between devices  23.7 us (21%)
  between operations  17.6 us (16%)
  local copies, waits for them, and re-layouts  7.53 us (7%)
  matrix products  7.4 us (7%)
  other arithmetic  5.63 us (5%)
    all_to_all x2, waiting for transfers between devices, gather_by_exchange(): return lax.all_to_all(copies, axis, 0, 0, tiled=False)  23 us
    ppermute x3, waiting for transfers between devices, shards(): fetched.append(lax.ppermute(own_half, 'head', across))  12.7 us
    all_to_all x2, starting transfers between devices, gather_by_exchange(): return lax.all_to_all(copies, axis, 0, 0, tiled=False)  11.7 us
    all_gather x1, waiting for transfers between devices, shards(): stacked = lax.all_gather(packed, 'tm', axis=0, tiled=True)  6.1 us
    ppermute x3, starting transfers between devices, shards(): total = total + lax.ppermute(piece, 'head', down).astype(jnp.float32)  5.72 us
    ppermute x3, waiting for transfers between devices, shards(): pieces.append(lax.ppermute(piece, 'head', across))  4.18 us
    dot_general x1, matrix products, shards(): projected = jnp.dot(frames_here, joined, preferred_element_type=jnp.float32)  3.83 us
    ppermute x3, waiting for transfers between devices, shards(): total = total + lax.ppermute(piece, 'head', down).astype(jnp.float32)  3.41 us
  transfers between devices with their start and end apart: 13, of which 10 were waited for; matrix products, arithmetic and copies ran while one was open for 11% of the time, Pallas kernels for 0%

profile of v12, /device:TPU:6, one launch (start us, length us, event | category | flops | bytes accessed | tf_op | source)
XLA Modules:
  0.0 111.2 jit_solution(14545666416583052198)
XLA Ops:
  6.5 1.5 %pad_add_fusion = bf16[128,640]{1,0:T(8,128)(2,1)} fusion(bf16[128,128]{1,0:T(8,128)(2,1)} %param.13, bf16[128,128]{1,0:T(8,128)(2,1)} %param.12, bf16[128,128]{1,0:T(8,128)(2,1)} %param.11, bf16[128,128]{1,0:T(8,128)(2,1)} %param.10, bf16[128,128]{1,0:T(8,128)(2,1)} %param.9), kind=kLoop, calls=%fused_computation.47 | loop fusion | flops 819200 | bytes 327680 | tf_op jit(solution)/shard_map/add | solution.py:48
  8.1 2.5 %broadcast_in_dim.51 = bf16[16,32,2048]{2,1,0:T(8,128)(2,1)} broadcast(bf16[32,2048]{1,0:T(8,128)(2,1)} %param.7), dimensions={1,2} | broadcast | bytes 2228224 | tf_op jit(solution)/shard_map/broadcast_in_dim | solution.py:13
  10.6 7.6 %all-to-all-start = ((bf16[16,32,2048]{2,1,0:T(8,128)(2,1)}), bf16[16,32,2048]{2,1,0:T(8,128)(2,1)S(1)}, u32[]{:S(2)}, u32[]{:S(2)}) async-start(bf16[16,32,2048]{2,1,0:T(8,128)(2,1)} %broadcast_in_dim.51), calls=%async_computation | async-start | bytes 4194304 | tf_op jit(solution)/shard_map/all_to_all | solution.py:14
  18.1 0.6 reduce_sum.47
  18.7 0.3 reduce-window.6
  19.0 0.2 slice_reduce_fusion
  19.2 0.2 reduce-window.9
  19.4 0.6 slice.69
  20.1 0.6 slice.68
  23.4 23.0 %all-to-all-done = bf16[16,32,2048]{2,1,0:T(8,128)(2,1)S(1)} async-done(((bf16[16,32,2048]{2,1,0:T(8,128)(2,1)}), bf16[16,32,2048]{2,1,0:T(8,128)(2,1)S(1)}, u32[]{:S(2)}, u32[]{:S(2)}) %all-to-all-start) | async-done | bytes 2097184 | tf_op jit(solution)/shard_map/all_to_all | solution.py:14
  46.4 6.1 %all-gather.2.cloned.1.call-done = bf16[2048,640]{1,0:T(8,128)(2,1)} async-done(((bf16[128,640]{1,0:T(8,128)(2,1)}), bf16[2048,640]{1,0:T(8,128)(2,1)}) %all-gather.2.cloned.1.call-update) | async-done | bytes 2621456 | tf_op jit(solution)/shard_map/all_gather | solution.py:52
  52.5 3.8 %fusion.58 = (bf16[512,512]{1,0:T(8,128)(2,1)S(1)}, f32[512,512]{1,0:T(8,128)}) fusion(bf16[512,2048]{1,0:T(8,128)(2,1)S(1)} %bitcast.110, bf16[2048,640]{1,0:T(8,128)(2,1)} %all-gather.2.cloned.1.call-done), kind=kOutput, calls=%fused_computation.91 | convolution fusion | flops 1074003968 | bytes 5767168 | tf_op jit(solution)/shard_map/dot_general | solution.py:56
  56.3 0.3 fusion.18
  56.7 0.1 maximum_bitcast_fusion.10
  56.8 0.9 broadcast_in_dim.94
  57.7 4.1 %all-to-all-start.1 = ((bf16[16,1,136,128]{3,2,1,0:T(8,128)(2,1)}), bf16[16,1,136,128]{3,2,1,0:T(8,128)(2,1)S(1)}, u32[]{:S(2)}, u32[]{:S(2)}) async-start(bf16[16,1,136,128]{3,2,1,0:T(8,128)(2,1)} %broadcast_in_dim.94), calls=%async_computation.1 | async-start | bytes 1114112 | tf_op jit(solution)/shard_map/all_to_all | solution.py:14
  62.0 0.6 slice.67
  62.6 0.6 slice.66
  64.6 1.1 slice.73
  65.7 1.9 %collective-permute-start.3 = (bf16[8,128,128]{2,1,0:T(8,128)(2,1)S(1)}, bf16[8,128,128]{2,1,0:T(8,128)(2,1)S(1)}, u32[]{:S(2)}, u32[]{:S(2)}) collective-permute-start(bf16[8,128,128]{2,1,0:T(8,128)(2,1)S(1)} %constant_dynamic-slice_fusion), channel_id=1, source_target_pairs={{0,1},{1,2},{2,3},{3,0},{4,5},{5,6},{6,7},{7,4},{8,9},{9,10},{10,1... | collective-permute-start | bytes 786440 | tf_op jit(solution)/shard_map/ppermute | solution.py:135
  67.6 1.4 %collective-permute-start.4 = (bf16[8,128,128]{2,1,0:T(8,128)(2,1)S(1)}, bf16[8,128,128]{2,1,0:T(8,128)(2,1)S(1)}, u32[]{:S(2)}, u32[]{:S(2)}) collective-permute-start(bf16[8,128,128]{2,1,0:T(8,128)(2,1)S(1)} %constant_dynamic-slice_fusion), channel_id=1, source_target_pairs={{0,2},{1,3},{2,0},{3,1},{4,6},{5,7},{6,4},{7,5},{8,10},{9,11},{10,... | collective-permute-start | bytes 786440 | tf_op jit(solution)/shard_map/ppermute | solution.py:135
  69.1 1.2 %fusion.15 = f32[1,512,1,128]{3,1,2,0:T(8,128)} fusion(f32[512]{0:T(512)S(1)} %get-tuple-element.22, bf16[512,512]{1,0:T(8,128)(2,1)S(1)} %get-tuple-element.43), kind=kOutput, calls=%fused_computation.16 | convolution fusion | flops 135528448 | bytes 659456 | tf_op jit(solution)/shard_map/while/body/eval_jaxpr/hts,shd->thd/dot_general | solution.py:92
  70.3 9.0 %collective-permute-done.3 = bf16[8,128,128]{2,1,0:T(8,128)(2,1)S(1)} collective-permute-done((bf16[8,128,128]{2,1,0:T(8,128)(2,1)S(1)}, bf16[8,128,128]{2,1,0:T(8,128)(2,1)S(1)}, u32[]{:S(2)}, u32[]{:S(2)}) %collective-permute-start.3) | collective-permute-done | bytes 262176 | tf_op jit(solution)/shard_map/ppermute | solution.py:135
  79.3 3.7 %collective-permute-done.5 = bf16[8,128,128]{2,1,0:T(8,128)(2,1)S(1)} collective-permute-done((bf16[8,128,128]{2,1,0:T(8,128)(2,1)S(1)}, bf16[8,128,128]{2,1,0:T(8,128)(2,1)S(1)}, u32[]{:S(2)}, u32[]{:S(2)}) %collective-permute-start.5) | collective-permute-done | bytes 262176 | tf_op jit(solution)/shard_map/ppermute | solution.py:135
  82.9 0.1 pad_maximum_fusion
  83.0 0.1 collective-permute-start.6
  83.1 0.2 fusion.55
  83.4 0.1 select_reduce_fusion
  83.5 0.2 multiply_reduce_fusion
  83.7 1.5 %fusion.59 = (f32[512]{0:T(512)S(1)}, f32[1,512,1,128]{3,1,2,0:T(8,128)S(1)}) fusion(f32[1,512,1,128]{3,1,2,0:T(8,128)} %fusion.15, f32[512]{0:T(512)S(1)} %exp.53, bf16[512,512]{1,0:T(8,128)(2,1)} %copy-done, f32[128,128]{1,0:T(8,128)S(1)} %multiply_reduce_fusion, f32[]{:T(128)} %bitcast.11), kind=kOutput, calls=%fused_computation.92 | convolution fusion | flops 100941312 | bytes 725504 | tf_op jit(solution)/shard_map/cthd,chde->cthe/dot_general | solution.py:109
  85.2 0.2 fusion.29
  85.5 1.2 %fusion.32 = bf16[512,128]{1,0:T(8,128)(2,1)S(1)} fusion(f32[1,512,1,128]{3,1,2,0:T(8,128)S(1)} %get-tuple-element.46, f32[512,512]{1,0:T(8,128)} %get-tuple-element.44, f32[512]{0:T(512)S(1)} %add_sqrt_fusion, f32[512]{0:T(512)S(1)} %broadcast_multiply_fusion), kind=kLoop, calls=%fused_computation.43 | loop fusion | flops 524288 | bytes 659456 | tf_op jit(solution)/shard_map/convert_element_type | solution.py:116
  86.7 0.7 collective-permute-start
  87.3 1.4 %collective-permute-start.1 = (bf16[4,32,128]{2,1,0:T(8,128)(2,1)S(1)}, bf16[4,32,128]{2,1,0:T(8,128)(2,1)S(1)}, u32[]{:S(2)}, u32[]{:S(2)}) collective-permute-start(bf16[4,32,128]{2,1,0:T(8,128)(2,1)S(1)} %get-tuple-element.41), channel_id=1, source_target_pairs={{0,2},{1,3},{2,0},{3,1},{4,6},{5,7},{6,4},{7,5},{8,10},{9,11},{10,... | collective-permute-start | bytes 98312 | tf_op jit(solution)/shard_map/ppermute | solution.py:134
  88.8 0.8 collective-permute-start.2
  89.6 0.1 broadcast_select_fusion.1
  89.7 1.2 %collective-permute-done = bf16[4,32,128]{2,1,0:T(8,128)(2,1)S(1)} collective-permute-done((bf16[4,32,128]{2,1,0:T(8,128)(2,1)S(1)}, bf16[4,32,128]{2,1,0:T(8,128)(2,1)S(1)}, u32[]{:S(2)}, u32[]{:S(2)}) %collective-permute-start) | collective-permute-done | bytes 32800 | tf_op jit(solution)/shard_map/ppermute | solution.py:134
  90.9 1.9 %collective-permute-done.1 = bf16[4,32,128]{2,1,0:T(8,128)(2,1)S(1)} collective-permute-done((bf16[4,32,128]{2,1,0:T(8,128)(2,1)S(1)}, bf16[4,32,128]{2,1,0:T(8,128)(2,1)S(1)}, u32[]{:S(2)}, u32[]{:S(2)}) %collective-permute-start.1) | collective-permute-done | bytes 32800 | tf_op jit(solution)/shard_map/ppermute | solution.py:134
  92.8 1.1 collective-permute-done.2
  93.9 0.5 fusion.13
  94.3 0.1 copy.38
  94.5 1.3 %collective-permute-start.7 = (bf16[32,2048]{1,0:T(8,128)(2,1)S(1)}, bf16[32,2048]{1,0:T(8,128)(2,1)S(1)}, u32[]{:S(2)}, u32[]{:S(2)}) collective-permute-start(bf16[32,2048]{1,0:T(8,128)(2,1)S(1)} %get-tuple-element.25), channel_id=1, source_target_pairs={{0,4},{1,5},{2,6},{3,7},{4,8},{5,9},{6,10},{7,11},{8,12},{9,13},{1... | collective-permute-start | bytes 393224 | tf_op jit(solution)/shard_map/ppermute | solution.py:153
  95.8 2.7 %collective-permute-start.8 = (bf16[32,2048]{1,0:T(8,128)(2,1)S(1)}, bf16[32,2048]{1,0:T(8,128)(2,1)S(1)}, u32[]{:S(2)}, u32[]{:S(2)}) collective-permute-start(bf16[32,2048]{1,0:T(8,128)(2,1)S(1)} %get-tuple-element.36), channel_id=1, source_target_pairs={{0,8},{1,9},{2,10},{3,11},{4,12},{5,13},{6,14},{7,15},{8,0},{9,1},... | collective-permute-start | bytes 393224 | tf_op jit(solution)/shard_map/ppermute | solution.py:153
  98.5 1.7 %collective-permute-start.9 = (bf16[32,2048]{1,0:T(8,128)(2,1)S(1)}, bf16[32,2048]{1,0:T(8,128)(2,1)S(1)}, u32[]{:S(2)}, u32[]{:S(2)}) collective-permute-start(bf16[32,2048]{1,0:T(8,128)(2,1)S(1)} %get-tuple-element.26), channel_id=1, source_target_pairs={{0,12},{1,13},{2,14},{3,15},{4,0},{5,1},{6,2},{7,3},{8,4},{9,5},{1... | collective-permute-start | bytes 393224 | tf_op jit(solution)/shard_map/ppermute | solution.py:153
  100.2 1.8 %collective-permute-done.7 = bf16[32,2048]{1,0:T(8,128)(2,1)S(1)} collective-permute-done((bf16[32,2048]{1,0:T(8,128)(2,1)S(1)}, bf16[32,2048]{1,0:T(8,128)(2,1)S(1)}, u32[]{:S(2)}, u32[]{:S(2)}) %collective-permute-start.7) | collective-permute-done | bytes 131104 | tf_op jit(solution)/shard_map/ppermute | solution.py:153
  102.1 1.4 %collective-permute-done.8 = bf16[32,2048]{1,0:T(8,128)(2,1)S(1)} collective-permute-done((bf16[32,2048]{1,0:T(8,128)(2,1)S(1)}, bf16[32,2048]{1,0:T(8,128)(2,1)S(1)}, u32[]{:S(2)}, u32[]{:S(2)}) %collective-permute-start.8) | collective-permute-done | bytes 131104 | tf_op jit(solution)/shard_map/ppermute | solution.py:153
  103.5 0.2 collective-permute-done.9
  103.6 0.7 fusion.27
  (25 shorter events, 0.5 us)
Async XLA Ops:
  6.5 46.0 %all-gather.2.cloned.1.call-start = ((), (), s32[]{:S(2)}) async-start(), calls=%async_computation.2 | async-start | bytes 2785280 | tf_op jit(solution)/shard_map/all_gather | solution.py:52
  10.5 7.6 %copy-start.1 = (f32[512,1]{0,1:T(1,128)S(1)}, f32[512,1]{0,1:T(1,128)}, u32[]{:S(2)}) copy-start(f32[512,1]{0,1:T(1,128)} %param.8) | copy-start | bytes 6148
  10.6 35.8 %all-to-all-start = ((bf16[16,32,2048]{2,1,0:T(8,128)(2,1)}), bf16[16,32,2048]{2,1,0:T(8,128)(2,1)S(1)}, u32[]{:S(2)}, u32[]{:S(2)}) async-start(bf16[16,32,2048]{2,1,0:T(8,128)(2,1)} %broadcast_in_dim.51), calls=%async_computation | async-start | bytes 4194304 | tf_op jit(solution)/shard_map/all_to_all | solution.py:14
  56.3 14.0 %copy-start = (bf16[512,512]{1,0:T(8,128)(2,1)}, bf16[512,512]{1,0:T(8,128)(2,1)S(1)}, u32[]{:S(2)}) copy-start(bf16[512,512]{1,0:T(8,128)(2,1)S(1)} %get-tuple-element.43) | copy-start | bytes 1572868
  57.7 25.5 %all-to-all-start.1 = ((bf16[16,1,136,128]{3,2,1,0:T(8,128)(2,1)}), bf16[16,1,136,128]{3,2,1,0:T(8,128)(2,1)S(1)}, u32[]{:S(2)}, u32[]{:S(2)}) async-start(bf16[16,1,136,128]{3,2,1,0:T(8,128)(2,1)} %broadcast_in_dim.94), calls=%async_computation.1 | async-start | bytes 1114112 | tf_op jit(solution)/shard_map/all_to_all | solution.py:14
  65.7 13.5 %collective-permute-start.3 = (bf16[8,128,128]{2,1,0:T(8,128)(2,1)S(1)}, bf16[8,128,128]{2,1,0:T(8,128)(2,1)S(1)}, u32[]{:S(2)}, u32[]{:S(2)}) collective-permute-start(bf16[8,128,128]{2,1,0:T(8,128)(2,1)S(1)} %constant_dynamic-slice_fusion), channel_id=1, source_target_pairs={{0,1},{1,2},{2,3},{3,0},{4,5},{5,6},{6,7},{7,4},{8,9},{9,10},{10,1... | collective-permute-start | bytes 786440 | tf_op jit(solution)/shard_map/ppermute | solution.py:135
  67.6 11.7 %collective-permute-start.4 = (bf16[8,128,128]{2,1,0:T(8,128)(2,1)S(1)}, bf16[8,128,128]{2,1,0:T(8,128)(2,1)S(1)}, u32[]{:S(2)}, u32[]{:S(2)}) collective-permute-start(bf16[8,128,128]{2,1,0:T(8,128)(2,1)S(1)} %constant_dynamic-slice_fusion), channel_id=1, source_target_pairs={{0,2},{1,3},{2,0},{3,1},{4,6},{5,7},{6,4},{7,5},{8,10},{9,11},{10,... | collective-permute-start | bytes 786440 | tf_op jit(solution)/shard_map/ppermute | solution.py:135
  69.0 13.9 %collective-permute-start.5 = (bf16[8,128,128]{2,1,0:T(8,128)(2,1)S(1)}, bf16[8,128,128]{2,1,0:T(8,128)(2,1)S(1)}, u32[]{:S(2)}, u32[]{:S(2)}) collective-permute-start(bf16[8,128,128]{2,1,0:T(8,128)(2,1)S(1)} %constant_dynamic-slice_fusion), channel_id=1, source_target_pairs={{0,3},{1,0},{2,1},{3,2},{4,7},{5,4},{6,5},{7,6},{8,11},{9,8},{10,9... | collective-permute-start | bytes 786440 | tf_op jit(solution)/shard_map/ppermute | solution.py:135
  83.0 6.5 %collective-permute-start.6 = (bf16[3,8,128,128]{3,2,0,1:T(8,128)(2,1)S(1)}, bf16[3,8,128,128]{3,2,0,1:T(8,128)(2,1)S(1)}, u32[]{:S(2)}, u32[]{:S(2)}) collective-permute-start(bf16[3,8,128,128]{3,2,0,1:T(8,128)(2,1)S(1)} %pad_maximum_fusion), channel_id=1, source_target_pairs={{0,16},{16,0},{32,48},{48,32},{64,80},{80,64},{96,112},{112,96},{1... | collective-permute-start | bytes 2359304 | tf_op jit(solution)/shard_map/ppermute | solution.py:137
  86.7 4.3 %collective-permute-start = (bf16[4,32,128]{2,1,0:T(8,128)(2,1)S(1)}, bf16[4,32,128]{2,1,0:T(8,128)(2,1)S(1)}, u32[]{:S(2)}, u32[]{:S(2)}) collective-permute-start(bf16[4,32,128]{2,1,0:T(8,128)(2,1)S(1)} %get-tuple-element.42), channel_id=1, source_target_pairs={{0,1},{1,2},{2,3},{3,0},{4,5},{5,6},{6,7},{7,4},{8,9},{9,10},{10,1... | collective-permute-start | bytes 98312 | tf_op jit(solution)/shard_map/ppermute | solution.py:134
  87.3 5.4 %collective-permute-start.1 = (bf16[4,32,128]{2,1,0:T(8,128)(2,1)S(1)}, bf16[4,32,128]{2,1,0:T(8,128)(2,1)S(1)}, u32[]{:S(2)}, u32[]{:S(2)}) collective-permute-start(bf16[4,32,128]{2,1,0:T(8,128)(2,1)S(1)} %get-tuple-element.41), channel_id=1, source_target_pairs={{0,2},{1,3},{2,0},{3,1},{4,6},{5,7},{6,4},{7,5},{8,10},{9,11},{10,... | collective-permute-start | bytes 98312 | tf_op jit(solution)/shard_map/ppermute | solution.py:134
  88.8 5.1 %collective-permute-start.2 = (bf16[4,32,128]{2,1,0:T(8,128)(2,1)S(1)}, bf16[4,32,128]{2,1,0:T(8,128)(2,1)S(1)}, u32[]{:S(2)}, u32[]{:S(2)}) collective-permute-start(bf16[4,32,128]{2,1,0:T(8,128)(2,1)S(1)} %get-tuple-element.40), channel_id=1, source_target_pairs={{0,3},{1,0},{2,1},{3,2},{4,7},{5,4},{6,5},{7,6},{8,11},{9,8},{10,9... | collective-permute-start | bytes 98312 | tf_op jit(solution)/shard_map/ppermute | solution.py:134
  94.5 7.5 %collective-permute-start.7 = (bf16[32,2048]{1,0:T(8,128)(2,1)S(1)}, bf16[32,2048]{1,0:T(8,128)(2,1)S(1)}, u32[]{:S(2)}, u32[]{:S(2)}) collective-permute-start(bf16[32,2048]{1,0:T(8,128)(2,1)S(1)} %get-tuple-element.25), channel_id=1, source_target_pairs={{0,4},{1,5},{2,6},{3,7},{4,8},{5,9},{6,10},{7,11},{8,12},{9,13},{1... | collective-permute-start | bytes 393224 | tf_op jit(solution)/shard_map/ppermute | solution.py:153
  95.8 7.7 %collective-permute-start.8 = (bf16[32,2048]{1,0:T(8,128)(2,1)S(1)}, bf16[32,2048]{1,0:T(8,128)(2,1)S(1)}, u32[]{:S(2)}, u32[]{:S(2)}) collective-permute-start(bf16[32,2048]{1,0:T(8,128)(2,1)S(1)} %get-tuple-element.36), channel_id=1, source_target_pairs={{0,8},{1,9},{2,10},{3,11},{4,12},{5,13},{6,14},{7,15},{8,0},{9,1},... | collective-permute-start | bytes 393224 | tf_op jit(solution)/shard_map/ppermute | solution.py:153
  98.5 5.1 %collective-permute-start.9 = (bf16[32,2048]{1,0:T(8,128)(2,1)S(1)}, bf16[32,2048]{1,0:T(8,128)(2,1)S(1)}, u32[]{:S(2)}, u32[]{:S(2)}) collective-permute-start(bf16[32,2048]{1,0:T(8,128)(2,1)S(1)} %get-tuple-element.26), channel_id=1, source_target_pairs={{0,12},{1,13},{2,14},{3,15},{4,0},{5,1},{6,2},{7,3},{8,4},{9,5},{1... | collective-permute-start | bytes 393224 | tf_op jit(solution)/shard_map/ppermute | solution.py:153
Sparse Core Ops, SparseCore 0:
  9.2 43.2 all-gather.1

commit v13 on v10

--- a/solution.py
+++ b/solution.py
@@ -43,9 +43,13 @@
 
 def shards(frames, log_decay, w_query, w_key, w_value, w_gate, w_out):
     head_width = w_query.shape[1]
-    stacked = lax.all_gather(
-        jnp.concatenate([w_key, w_value, w_query, w_gate, w_out], axis=1), "tm", axis=0, tiled=True
+    blocks = [w_key, w_value, w_query, w_gate, w_out]
+    width = sum(block.shape[1] for block in blocks)
+    packed = sum(
+        jnp.pad(block, ((0, 0), (start, width - start - block.shape[1])))
+        for start, block in zip(range(0, width, head_width), blocks)
     )
+    stacked = lax.all_gather(packed, "tm", axis=0, tiled=True)
     out_blocks = stacked[:, 4 * head_width :].reshape(-1, head_width, w_out.shape[1])
     frames_here = gather_by_exchange(frames, "head").reshape(-1, frames.shape[1])
     key_value = jnp.dot(

time: 115 us -> 112 us (0.974)
  local copies, waits for them, and re-layouts: 12.9 us -> 8.38 us
  other arithmetic: 5.87 us -> 7.38 us
    unnamed x10 -> x4, local copies, waits for them, and re-layouts: 3.75 us -> 0.01 us
    add x0 -> x1, other arithmetic: none -> 1.52 us  [shards(): sum((jnp.pad(block, ((0, 0), (start, width - start - block.shape[1]))) fo...]
where the time goes in v13:
time: 112 us; the launch traced here: 111 us
  waiting for transfers between devices  45.5 us (41%)
  starting transfers between devices  23.7 us (21%)
  between operations  17.6 us (16%)
  local copies, waits for them, and re-layouts  8.38 us (7%)
  matrix products  8.37 us (7%)
  other arithmetic  7.38 us (7%)
    all_to_all x2, waiting for transfers between devices, gather_by_exchange(): return lax.all_to_all(copies, axis, 0, 0, tiled=False)  23 us
    all_to_all x2, starting transfers between devices, gather_by_exchange(): return lax.all_to_all(copies, axis, 0, 0, tiled=False)  11.7 us
    ppermute x3, waiting for transfers between devices, shards(): fetched.append(lax.ppermute(own_half, 'head', across))  9.84 us
    all_gather x1, waiting for transfers between devices, shards(): stacked = lax.all_gather(packed, 'tm', axis=0, tiled=True)  6.1 us
    ppermute x3, starting transfers between devices, shards(): total = total + lax.ppermute(piece, 'head', down).astype(jnp.float32)  5.73 us
    ppermute x3, waiting for transfers between devices, shards(): total = total + lax.ppermute(piece, 'head', down).astype(jnp.float32)  3.39 us
    broadcast_in_dim x2, local copies, waits for them, and re-layouts, gather_by_exchange(): copies = jnp.broadcast_to(part[None], (count,) + part.shape)  3.36 us
    ppermute x3, starting transfers between devices, shards(): fetched.append(lax.ppermute(own_half, 'head', across))  3.22 us
  transfers between devices with their start and end apart: 13, of which 10 were waited for; matrix products, arithmetic and copies ran while one was open for 16% of the time, Pallas kernels for 0%

profile of v13, /device:TPU:6, one launch (start us, length us, event | category | flops | bytes accessed | tf_op | source)
XLA Modules:
  0.0 110.9 jit_solution(17337134863296495562)
XLA Ops:
  6.5 1.5 %pad_add_fusion = bf16[128,640]{1,0:T(8,128)(2,1)} fusion(bf16[128,128]{1,0:T(8,128)(2,1)} %param.13, bf16[128,128]{1,0:T(8,128)(2,1)} %param.12, bf16[128,128]{1,0:T(8,128)(2,1)} %param.9, bf16[128,128]{1,0:T(8,128)(2,1)} %param.11, bf16[128,128]{1,0:T(8,128)(2,1)} %param.10), kind=kLoop, calls=%fused_computation.50 | loop fusion | flops 819200 | bytes 327680 | tf_op jit(solution)/shard_map/add | solution.py:48
  8.1 2.5 %broadcast_in_dim.51 = bf16[16,32,2048]{2,1,0:T(8,128)(2,1)} broadcast(bf16[32,2048]{1,0:T(8,128)(2,1)} %param.7), dimensions={1,2} | broadcast | bytes 2228224 | tf_op jit(solution)/shard_map/broadcast_in_dim | solution.py:13
  10.6 7.6 %all-to-all-start = ((bf16[16,32,2048]{2,1,0:T(8,128)(2,1)}), bf16[16,32,2048]{2,1,0:T(8,128)(2,1)S(1)}, u32[]{:S(2)}, u32[]{:S(2)}) async-start(bf16[16,32,2048]{2,1,0:T(8,128)(2,1)} %broadcast_in_dim.51), calls=%async_computation | async-start | bytes 4194304 | tf_op jit(solution)/shard_map/all_to_all | solution.py:14
  18.1 0.6 reduce_sum.47
  18.7 0.3 reduce-window.6
  19.0 0.2 slice_reduce_fusion
  19.2 0.2 reduce-window.9
  19.4 0.6 slice.74
  20.1 0.6 slice.73
  23.4 23.0 %all-to-all-done = bf16[16,32,2048]{2,1,0:T(8,128)(2,1)S(1)} async-done(((bf16[16,32,2048]{2,1,0:T(8,128)(2,1)}), bf16[16,32,2048]{2,1,0:T(8,128)(2,1)S(1)}, u32[]{:S(2)}, u32[]{:S(2)}) %all-to-all-start) | async-done | bytes 2097184 | tf_op jit(solution)/shard_map/all_to_all | solution.py:14
  46.4 6.1 %all-gather.2.cloned.1.call-done = bf16[2048,640]{1,0:T(8,128)(2,1)} async-done(((bf16[128,640]{1,0:T(8,128)(2,1)}), bf16[2048,640]{1,0:T(8,128)(2,1)}) %all-gather.2.cloned.1.call-update) | async-done | bytes 2621456 | tf_op jit(solution)/shard_map/all_gather | solution.py:52
  52.5 2.0 %fusion.10 = bf16[512,256]{0,1:T(8,128)(2,1)S(1)} fusion(bf16[512,2048]{1,0:T(8,128)(2,1)S(1)} %bitcast.113, bf16[2048,640]{1,0:T(8,128)(2,1)} %all-gather.2.cloned.1.call-done), kind=kOutput, calls=%fused_computation.14 | convolution fusion | flops 537001984 | bytes 3407872 | tf_op jit(solution)/shard_map/dot_general | solution.py:55
  54.5 0.2 fusion.14
  54.7 0.1 maximum_bitcast_fusion.10
  54.8 0.9 broadcast_in_dim.94
  55.7 4.1 %all-to-all-start.1 = ((bf16[16,1,136,128]{3,2,1,0:T(8,128)(2,1)}), bf16[16,1,136,128]{3,2,1,0:T(8,128)(2,1)S(1)}, u32[]{:S(2)}, u32[]{:S(2)}) async-start(bf16[16,1,136,128]{3,2,1,0:T(8,128)(2,1)} %broadcast_in_dim.94), calls=%async_computation.1 | async-start | bytes 1114112 | tf_op jit(solution)/shard_map/all_to_all | solution.py:14
  60.0 0.7 slice.72
  60.7 0.6 slice.71
  62.7 1.1 slice.78
  63.8 0.7 constant_dynamic-slice_fusion
  64.5 1.8 %collective-permute-start.3 = (bf16[8,128,128]{2,1,0:T(8,128)(2,1)}, bf16[8,128,128]{2,1,0:T(8,128)(2,1)S(1)}, u32[]{:S(2)}, u32[]{:S(2)}) collective-permute-start(bf16[8,128,128]{2,1,0:T(8,128)(2,1)} %constant_dynamic-slice_fusion), channel_id=1, source_target_pairs={{0,1},{1,2},{2,3},{3,0},{4,5},{5,6},{6,7},{7,4},{8,9},{9,10},{10,1... | collective-permute-start | bytes 786440 | tf_op jit(solution)/shard_map/ppermute | solution.py:135
  66.3 1.4 %collective-permute-start.4 = (bf16[8,128,128]{2,1,0:T(8,128)(2,1)}, bf16[8,128,128]{2,1,0:T(8,128)(2,1)}, u32[]{:S(2)}, u32[]{:S(2)}) collective-permute-start(bf16[8,128,128]{2,1,0:T(8,128)(2,1)} %constant_dynamic-slice_fusion), channel_id=1, source_target_pairs={{0,2},{1,3},{2,0},{3,1},{4,6},{5,7},{6,4},{7,5},{8,10},{9,11},{10,... | collective-permute-start | bytes 786440 | tf_op jit(solution)/shard_map/ppermute | solution.py:135
  67.7 2.8 %convolution_bitcast_fusion = f32[512,256]{0,1:T(8,128)} fusion(bf16[512,2048]{1,0:T(8,128)(2,1)S(1)} %bitcast.114, bf16[2048,640]{1,0:T(8,128)(2,1)} %all-gather.2.cloned.1.call-done), kind=kOutput, calls=%fused_computation.12 | convolution fusion | flops 536870912 | bytes 3670016 | tf_op jit(solution)/shard_map/dot_general | solution.py:58
  70.5 1.6 %fusion.11 = f32[1,512,1,128]{1,3,2,0:T(8,128)S(1)} fusion(f32[512]{0:T(512)S(1)} %get-tuple-element.22, bf16[512,256]{0,1:T(8,128)(2,1)} %copy-done.1, f32[512,256]{0,1:T(8,128)} %convolution_bitcast_fusion), kind=kOutput, calls=%fused_computation.16 | convolution fusion | flops 135528448 | bytes 659456 | tf_op jit(solution)/shard_map/while/body/eval_jaxpr/hts,shd->thd/dot_general | solution.py:92
  72.1 6.2 %collective-permute-done.3 = bf16[8,128,128]{2,1,0:T(8,128)(2,1)S(1)} collective-permute-done((bf16[8,128,128]{2,1,0:T(8,128)(2,1)}, bf16[8,128,128]{2,1,0:T(8,128)(2,1)S(1)}, u32[]{:S(2)}, u32[]{:S(2)}) %collective-permute-start.3) | collective-permute-done | bytes 262176 | tf_op jit(solution)/shard_map/ppermute | solution.py:135
  78.3 3.7 %collective-permute-done.5 = bf16[8,128,128]{2,1,0:T(8,128)(2,1)} collective-permute-done((bf16[8,128,128]{2,1,0:T(8,128)(2,1)}, bf16[8,128,128]{2,1,0:T(8,128)(2,1)}, u32[]{:S(2)}, u32[]{:S(2)}) %collective-permute-start.5) | collective-permute-done | bytes 262176 | tf_op jit(solution)/shard_map/ppermute | solution.py:135
  81.9 1.1 %pad_maximum_fusion = bf16[3,8,128,128]{3,2,0,1:T(8,128)(2,1)S(1)} fusion(bf16[1,8,128,128]{3,2,0,1:T(8,128)(2,1)} %bitcast.42, bf16[1,8,128,128]{3,2,0,1:T(8,128)(2,1)} %bitcast.41, bf16[1,8,128,128]{3,2,0,1:T(8,128)(2,1)S(1)} %bitcast.119), kind=kLoop, calls=%fused_computation.28 | loop fusion | flops 786432 | bytes 1572864 | tf_op jit(solution)/shard_map/stack | solution.py:136
  83.2 0.2 fusion.50
  83.5 0.2 multiply_reduce_fusion
  83.7 1.4 %fusion.53 = (f32[512]{0:T(512)S(1)}, f32[1,512,1,128]{1,3,2,0:T(8,128)S(1)}) fusion(f32[1,512,1,128]{1,3,2,0:T(8,128)S(1)} %fusion.11, f32[512]{0:T(512)S(1)} %exp.53, f32[512,256]{0,1:T(8,128)} %convolution_bitcast_fusion, f32[128,128]{1,0:T(8,128)S(1)} %multiply_reduce_fusion, f32[]{:T(128)} %bitcast.12), kind=kOutput, calls=%fused_computation.92 | convolution fusion | flops 100941312 | bytes 725504 | tf_op jit(solution)/shard_map/cthd,chde->cthe/dot_general | solution.py:109
  85.2 1.0 fusion.30
  86.2 0.1 copy.26
  86.4 0.7 collective-permute-start
  87.0 1.4 %collective-permute-start.1 = (bf16[4,32,128]{2,1,0:T(8,128)(2,1)S(1)}, bf16[4,32,128]{2,1,0:T(8,128)(2,1)S(1)}, u32[]{:S(2)}, u32[]{:S(2)}) collective-permute-start(bf16[4,32,128]{2,1,0:T(8,128)(2,1)S(1)} %get-tuple-element.41), channel_id=1, source_target_pairs={{0,2},{1,3},{2,0},{3,1},{4,6},{5,7},{6,4},{7,5},{8,10},{9,11},{10,... | collective-permute-start | bytes 98312 | tf_op jit(solution)/shard_map/ppermute | solution.py:134
  88.5 0.8 collective-permute-start.2
  89.3 1.2 %broadcast_select_fusion.1 = (bf16[3,8,128,128]{3,2,0,1:T(8,128)(2,1)S(1)}, bf16[3,8,128,128]{3,2,0,1:T(8,128)(2,1)S(1)}) fusion(bf16[3,8,128,128]{3,2,0,1:T(8,128)(2,1)S(1)} %collective-permute-done.6, pred[]{:T(512)S(6)} %eq.13, bf16[1,8,128,128]{3,2,0,1:T(8,128)(2,1)} %bitcast.42, bf16[1,8,128,128]{3,2,0,1:T(8,128)(2,1)} %bitcast.41, ...), kind=kLoop, calls=%fused_computation.30 | loop fusion | flops 1572864 | bytes 3145729 | tf_op jit(solution)/shard_map/jit(_where)/select_n | solution.py:138
  90.4 0.2 collective-permute-done
  90.6 1.8 %collective-permute-done.1 = bf16[4,32,128]{2,1,0:T(8,128)(2,1)S(1)} collective-permute-done((bf16[4,32,128]{2,1,0:T(8,128)(2,1)S(1)}, bf16[4,32,128]{2,1,0:T(8,128)(2,1)S(1)}, u32[]{:S(2)}, u32[]{:S(2)}) %collective-permute-start.1) | collective-permute-done | bytes 32800 | tf_op jit(solution)/shard_map/ppermute | solution.py:134
  92.5 1.1 collective-permute-done.2
  93.6 0.5 fusion.8
  94.0 0.1 copy.34
  94.2 1.3 %collective-permute-start.7 = (bf16[32,2048]{1,0:T(8,128)(2,1)S(1)}, bf16[32,2048]{1,0:T(8,128)(2,1)S(1)}, u32[]{:S(2)}, u32[]{:S(2)}) collective-permute-start(bf16[32,2048]{1,0:T(8,128)(2,1)S(1)} %get-tuple-element.25), channel_id=1, source_target_pairs={{0,4},{1,5},{2,6},{3,7},{4,8},{5,9},{6,10},{7,11},{8,12},{9,13},{1... | collective-permute-start | bytes 393224 | tf_op jit(solution)/shard_map/ppermute | solution.py:153
  95.5 2.7 %collective-permute-start.8 = (bf16[32,2048]{1,0:T(8,128)(2,1)S(1)}, bf16[32,2048]{1,0:T(8,128)(2,1)S(1)}, u32[]{:S(2)}, u32[]{:S(2)}) collective-permute-start(bf16[32,2048]{1,0:T(8,128)(2,1)S(1)} %get-tuple-element.36), channel_id=1, source_target_pairs={{0,8},{1,9},{2,10},{3,11},{4,12},{5,13},{6,14},{7,15},{8,0},{9,1},... | collective-permute-start | bytes 393224 | tf_op jit(solution)/shard_map/ppermute | solution.py:153
  98.2 1.7 %collective-permute-start.9 = (bf16[32,2048]{1,0:T(8,128)(2,1)S(1)}, bf16[32,2048]{1,0:T(8,128)(2,1)S(1)}, u32[]{:S(2)}, u32[]{:S(2)}) collective-permute-start(bf16[32,2048]{1,0:T(8,128)(2,1)S(1)} %get-tuple-element.26), channel_id=1, source_target_pairs={{0,12},{1,13},{2,14},{3,15},{4,0},{5,1},{6,2},{7,3},{8,4},{9,5},{1... | collective-permute-start | bytes 393224 | tf_op jit(solution)/shard_map/ppermute | solution.py:153
  99.9 1.8 %collective-permute-done.7 = bf16[32,2048]{1,0:T(8,128)(2,1)S(1)} collective-permute-done((bf16[32,2048]{1,0:T(8,128)(2,1)S(1)}, bf16[32,2048]{1,0:T(8,128)(2,1)S(1)}, u32[]{:S(2)}, u32[]{:S(2)}) %collective-permute-start.7) | collective-permute-done | bytes 131104 | tf_op jit(solution)/shard_map/ppermute | solution.py:153
  101.8 1.4 %collective-permute-done.8 = bf16[32,2048]{1,0:T(8,128)(2,1)S(1)} collective-permute-done((bf16[32,2048]{1,0:T(8,128)(2,1)S(1)}, bf16[32,2048]{1,0:T(8,128)(2,1)S(1)}, u32[]{:S(2)}, u32[]{:S(2)}) %collective-permute-start.8) | collective-permute-done | bytes 131104 | tf_op jit(solution)/shard_map/ppermute | solution.py:153
  103.2 0.2 collective-permute-done.9
  103.3 0.7 fusion.25
  (27 shorter events, 0.7 us)
Async XLA Ops:
  6.5 46.0 %all-gather.2.cloned.1.call-start = ((), (), s32[]{:S(2)}) async-start(), calls=%async_computation.2 | async-start | bytes 2785280 | tf_op jit(solution)/shard_map/all_gather | solution.py:52
  10.5 7.6 %copy-start = (f32[512,1]{0,1:T(1,128)S(1)}, f32[512,1]{0,1:T(1,128)}, u32[]{:S(2)}) copy-start(f32[512,1]{0,1:T(1,128)} %param.8) | copy-start | bytes 6148
  10.6 35.8 %all-to-all-start = ((bf16[16,32,2048]{2,1,0:T(8,128)(2,1)}), bf16[16,32,2048]{2,1,0:T(8,128)(2,1)S(1)}, u32[]{:S(2)}, u32[]{:S(2)}) async-start(bf16[16,32,2048]{2,1,0:T(8,128)(2,1)} %broadcast_in_dim.51), calls=%async_computation | async-start | bytes 4194304 | tf_op jit(solution)/shard_map/all_to_all | solution.py:14
  54.5 1.2 %copy-start.1 = (bf16[512,256]{0,1:T(8,128)(2,1)}, bf16[512,256]{0,1:T(8,128)(2,1)S(1)}, u32[]{:S(2)}) copy-start(bf16[512,256]{0,1:T(8,128)(2,1)S(1)} %fusion.10) | copy-start | bytes 786436
  55.7 27.5 %all-to-all-start.1 = ((bf16[16,1,136,128]{3,2,1,0:T(8,128)(2,1)}), bf16[16,1,136,128]{3,2,1,0:T(8,128)(2,1)S(1)}, u32[]{:S(2)}, u32[]{:S(2)}) async-start(bf16[16,1,136,128]{3,2,1,0:T(8,128)(2,1)} %broadcast_in_dim.94), calls=%async_computation.1 | async-start | bytes 1114112 | tf_op jit(solution)/shard_map/all_to_all | solution.py:14
  64.5 13.8 %collective-permute-start.3 = (bf16[8,128,128]{2,1,0:T(8,128)(2,1)}, bf16[8,128,128]{2,1,0:T(8,128)(2,1)S(1)}, u32[]{:S(2)}, u32[]{:S(2)}) collective-permute-start(bf16[8,128,128]{2,1,0:T(8,128)(2,1)} %constant_dynamic-slice_fusion), channel_id=1, source_target_pairs={{0,1},{1,2},{2,3},{3,0},{4,5},{5,6},{6,7},{7,4},{8,9},{9,10},{10,1... | collective-permute-start | bytes 786440 | tf_op jit(solution)/shard_map/ppermute | solution.py:135
  66.3 12.0 %collective-permute-start.4 = (bf16[8,128,128]{2,1,0:T(8,128)(2,1)}, bf16[8,128,128]{2,1,0:T(8,128)(2,1)}, u32[]{:S(2)}, u32[]{:S(2)}) collective-permute-start(bf16[8,128,128]{2,1,0:T(8,128)(2,1)} %constant_dynamic-slice_fusion), channel_id=1, source_target_pairs={{0,2},{1,3},{2,0},{3,1},{4,6},{5,7},{6,4},{7,5},{8,10},{9,11},{10,... | collective-permute-start | bytes 786440 | tf_op jit(solution)/shard_map/ppermute | solution.py:135
  67.7 14.2 %collective-permute-start.5 = (bf16[8,128,128]{2,1,0:T(8,128)(2,1)}, bf16[8,128,128]{2,1,0:T(8,128)(2,1)}, u32[]{:S(2)}, u32[]{:S(2)}) collective-permute-start(bf16[8,128,128]{2,1,0:T(8,128)(2,1)} %constant_dynamic-slice_fusion), channel_id=1, source_target_pairs={{0,3},{1,0},{2,1},{3,2},{4,7},{5,4},{6,5},{7,6},{8,11},{9,8},{10,9... | collective-permute-start | bytes 786440 | tf_op jit(solution)/shard_map/ppermute | solution.py:135
  83.1 6.2 %collective-permute-start.6 = (bf16[3,8,128,128]{3,2,0,1:T(8,128)(2,1)S(1)}, bf16[3,8,128,128]{3,2,0,1:T(8,128)(2,1)S(1)}, u32[]{:S(2)}, u32[]{:S(2)}) collective-permute-start(bf16[3,8,128,128]{3,2,0,1:T(8,128)(2,1)S(1)} %pad_maximum_fusion), channel_id=1, source_target_pairs={{0,16},{16,0},{32,48},{48,32},{64,80},{80,64},{96,112},{112,96},{1... | collective-permute-start | bytes 2359304 | tf_op jit(solution)/shard_map/ppermute | solution.py:137
  86.4 4.3 %collective-permute-start = (bf16[4,32,128]{2,1,0:T(8,128)(2,1)S(1)}, bf16[4,32,128]{2,1,0:T(8,128)(2,1)S(1)}, u32[]{:S(2)}, u32[]{:S(2)}) collective-permute-start(bf16[4,32,128]{2,1,0:T(8,128)(2,1)S(1)} %get-tuple-element.42), channel_id=1, source_target_pairs={{0,1},{1,2},{2,3},{3,0},{4,5},{5,6},{6,7},{7,4},{8,9},{9,10},{10,1... | collective-permute-start | bytes 98312 | tf_op jit(solution)/shard_map/ppermute | solution.py:134
  87.0 5.4 %collective-permute-start.1 = (bf16[4,32,128]{2,1,0:T(8,128)(2,1)S(1)}, bf16[4,32,128]{2,1,0:T(8,128)(2,1)S(1)}, u32[]{:S(2)}, u32[]{:S(2)}) collective-permute-start(bf16[4,32,128]{2,1,0:T(8,128)(2,1)S(1)} %get-tuple-element.41), channel_id=1, source_target_pairs={{0,2},{1,3},{2,0},{3,1},{4,6},{5,7},{6,4},{7,5},{8,10},{9,11},{10,... | collective-permute-start | bytes 98312 | tf_op jit(solution)/shard_map/ppermute | solution.py:134
  88.5 5.1 %collective-permute-start.2 = (bf16[4,32,128]{2,1,0:T(8,128)(2,1)S(1)}, bf16[4,32,128]{2,1,0:T(8,128)(2,1)S(1)}, u32[]{:S(2)}, u32[]{:S(2)}) collective-permute-start(bf16[4,32,128]{2,1,0:T(8,128)(2,1)S(1)} %get-tuple-element.40), channel_id=1, source_target_pairs={{0,3},{1,0},{2,1},{3,2},{4,7},{5,4},{6,5},{7,6},{8,11},{9,8},{10,9... | collective-permute-start | bytes 98312 | tf_op jit(solution)/shard_map/ppermute | solution.py:134
  94.2 7.5 %collective-permute-start.7 = (bf16[32,2048]{1,0:T(8,128)(2,1)S(1)}, bf16[32,2048]{1,0:T(8,128)(2,1)S(1)}, u32[]{:S(2)}, u32[]{:S(2)}) collective-permute-start(bf16[32,2048]{1,0:T(8,128)(2,1)S(1)} %get-tuple-element.25), channel_id=1, source_target_pairs={{0,4},{1,5},{2,6},{3,7},{4,8},{5,9},{6,10},{7,11},{8,12},{9,13},{1... | collective-permute-start | bytes 393224 | tf_op jit(solution)/shard_map/ppermute | solution.py:153
  95.5 7.7 %collective-permute-start.8 = (bf16[32,2048]{1,0:T(8,128)(2,1)S(1)}, bf16[32,2048]{1,0:T(8,128)(2,1)S(1)}, u32[]{:S(2)}, u32[]{:S(2)}) collective-permute-start(bf16[32,2048]{1,0:T(8,128)(2,1)S(1)} %get-tuple-element.36), channel_id=1, source_target_pairs={{0,8},{1,9},{2,10},{3,11},{4,12},{5,13},{6,14},{7,15},{8,0},{9,1},... | collective-permute-start | bytes 393224 | tf_op jit(solution)/shard_map/ppermute | solution.py:153
  98.2 5.1 %collective-permute-start.9 = (bf16[32,2048]{1,0:T(8,128)(2,1)S(1)}, bf16[32,2048]{1,0:T(8,128)(2,1)S(1)}, u32[]{:S(2)}, u32[]{:S(2)}) collective-permute-start(bf16[32,2048]{1,0:T(8,128)(2,1)S(1)} %get-tuple-element.26), channel_id=1, source_target_pairs={{0,12},{1,13},{2,14},{3,15},{4,0},{5,1},{6,2},{7,3},{8,4},{9,5},{1... | collective-permute-start | bytes 393224 | tf_op jit(solution)/shard_map/ppermute | solution.py:153
Sparse Core Ops, SparseCore 0:
  9.2 43.2 all-gather.1

commit v14 on v12

--- a/solution.py
+++ b/solution.py
@@ -106,7 +106,12 @@
     before = jnp.cumsum(block_logs, axis=0) - block_logs
     start_states = jnp.exp(before)[:, :, None, None] * prior[None] + local_starts
     lifted = query_blocks.astype(jnp.float32) * jnp.exp(running_blocks)[..., None]
-    inter = jnp.einsum("cthd,chde->cthe", lifted, start_states, precision=lax.Precision.HIGHEST)
+    inter = jnp.einsum(
+        "cthd,chde->cthe",
+        lifted.astype(jnp.bfloat16),
+        start_states.astype(jnp.bfloat16),
+        preferred_element_type=jnp.float32,
+    )
     retained = (intra_all + inter).reshape(local_len, heads_here, HEAD_DIM)
     center = jnp.mean(retained, axis=-1, keepdims=True)
     spread = jnp.mean((retained - center) ** 2, axis=-1, keepdims=True)

time: 112 us -> 112 us (level)
  no operation moved by 1% of the time
where the time goes in v14:
time: 112 us; the launch traced here: 111 us
  waiting for transfers between devices  49.4 us (44%)
  starting transfers between devices  23.7 us (21%)
  between operations  17.6 us (16%)
  local copies, waits for them, and re-layouts  7.53 us (7%)
  matrix products  7.26 us (6%)
  other arithmetic  5.63 us (5%)
    all_to_all x2, waiting for transfers between devices, gather_by_exchange(): return lax.all_to_all(copies, axis, 0, 0, tiled=False)  23 us
    ppermute x3, waiting for transfers between devices, shards(): fetched.append(lax.ppermute(own_half, 'head', across))  12.7 us
    all_to_all x2, starting transfers between devices, gather_by_exchange(): return lax.all_to_all(copies, axis, 0, 0, tiled=False)  11.7 us
    all_gather x1, waiting for transfers between devices, shards(): stacked = lax.all_gather(packed, 'tm', axis=0, tiled=True)  6.1 us
    ppermute x3, starting transfers between devices, shards(): total = total + lax.ppermute(piece, 'head', down).astype(jnp.float32)  5.72 us
    ppermute x3, waiting for transfers between devices, shards(): pieces.append(lax.ppermute(piece, 'head', across))  4.17 us
    dot_general x1, matrix products, shards(): projected = jnp.dot(frames_here, joined, preferred_element_type=jnp.float32)  3.83 us
    ppermute x3, waiting for transfers between devices, shards(): total = total + lax.ppermute(piece, 'head', down).astype(jnp.float32)  3.4 us
  transfers between devices with their start and end apart: 13, of which 10 were waited for; matrix products, arithmetic and copies ran while one was open for 11% of the time, Pallas kernels for 0%

profile of v14, /device:TPU:6, one launch (start us, length us, event | category | flops | bytes accessed | tf_op | source)
XLA Modules:
  0.0 111.1 jit_solution(12268145365354147369)
XLA Ops:
  6.5 1.5 %pad_add_fusion = bf16[128,640]{1,0:T(8,128)(2,1)} fusion(bf16[128,128]{1,0:T(8,128)(2,1)} %param.13, bf16[128,128]{1,0:T(8,128)(2,1)} %param.12, bf16[128,128]{1,0:T(8,128)(2,1)} %param.11, bf16[128,128]{1,0:T(8,128)(2,1)} %param.10, bf16[128,128]{1,0:T(8,128)(2,1)} %param.9), kind=kLoop, calls=%fused_computation.46 | loop fusion | flops 819200 | bytes 327680 | tf_op jit(solution)/shard_map/add | solution.py:48
  8.1 2.5 %broadcast_in_dim.51 = bf16[16,32,2048]{2,1,0:T(8,128)(2,1)} broadcast(bf16[32,2048]{1,0:T(8,128)(2,1)} %param.7), dimensions={1,2} | broadcast | bytes 2228224 | tf_op jit(solution)/shard_map/broadcast_in_dim | solution.py:13
  10.6 7.6 %all-to-all-start = ((bf16[16,32,2048]{2,1,0:T(8,128)(2,1)}), bf16[16,32,2048]{2,1,0:T(8,128)(2,1)S(1)}, u32[]{:S(2)}, u32[]{:S(2)}) async-start(bf16[16,32,2048]{2,1,0:T(8,128)(2,1)} %broadcast_in_dim.51), calls=%async_computation | async-start | bytes 4194304 | tf_op jit(solution)/shard_map/all_to_all | solution.py:14
  18.1 0.6 reduce_sum.47
  18.7 0.3 reduce-window.6
  19.0 0.2 slice_reduce_fusion
  19.2 0.2 reduce-window.9
  19.4 0.6 slice.69
  20.1 0.6 slice.68
  23.4 23.0 %all-to-all-done = bf16[16,32,2048]{2,1,0:T(8,128)(2,1)S(1)} async-done(((bf16[16,32,2048]{2,1,0:T(8,128)(2,1)}), bf16[16,32,2048]{2,1,0:T(8,128)(2,1)S(1)}, u32[]{:S(2)}, u32[]{:S(2)}) %all-to-all-start) | async-done | bytes 2097184 | tf_op jit(solution)/shard_map/all_to_all | solution.py:14
  46.4 6.1 %all-gather.2.cloned.1.call-done = bf16[2048,640]{1,0:T(8,128)(2,1)} async-done(((bf16[128,640]{1,0:T(8,128)(2,1)}), bf16[2048,640]{1,0:T(8,128)(2,1)}) %all-gather.2.cloned.1.call-update) | async-done | bytes 2621456 | tf_op jit(solution)/shard_map/all_gather | solution.py:52
  52.5 3.8 %fusion.55 = (bf16[512,512]{1,0:T(8,128)(2,1)S(1)}, f32[512,512]{1,0:T(8,128)}) fusion(bf16[512,2048]{1,0:T(8,128)(2,1)S(1)} %bitcast.110, bf16[2048,640]{1,0:T(8,128)(2,1)} %all-gather.2.cloned.1.call-done), kind=kOutput, calls=%fused_computation.90 | convolution fusion | flops 1074003968 | bytes 5767168 | tf_op jit(solution)/shard_map/dot_general | solution.py:56
  56.3 0.3 fusion.18
  56.7 0.1 maximum_bitcast_fusion.10
  56.8 0.9 broadcast_in_dim.94
  57.7 4.1 %all-to-all-start.1 = ((bf16[16,1,136,128]{3,2,1,0:T(8,128)(2,1)}), bf16[16,1,136,128]{3,2,1,0:T(8,128)(2,1)S(1)}, u32[]{:S(2)}, u32[]{:S(2)}) async-start(bf16[16,1,136,128]{3,2,1,0:T(8,128)(2,1)} %broadcast_in_dim.94), calls=%async_computation.1 | async-start | bytes 1114112 | tf_op jit(solution)/shard_map/all_to_all | solution.py:14
  62.0 0.6 slice.67
  62.6 0.6 slice.66
  64.6 1.1 slice.73
  65.7 1.9 %collective-permute-start.3 = (bf16[8,128,128]{2,1,0:T(8,128)(2,1)S(1)}, bf16[8,128,128]{2,1,0:T(8,128)(2,1)S(1)}, u32[]{:S(2)}, u32[]{:S(2)}) collective-permute-start(bf16[8,128,128]{2,1,0:T(8,128)(2,1)S(1)} %constant_dynamic-slice_fusion), channel_id=1, source_target_pairs={{0,1},{1,2},{2,3},{3,0},{4,5},{5,6},{6,7},{7,4},{8,9},{9,10},{10,1... | collective-permute-start | bytes 786440 | tf_op jit(solution)/shard_map/ppermute | solution.py:140
  67.6 1.4 %collective-permute-start.4 = (bf16[8,128,128]{2,1,0:T(8,128)(2,1)S(1)}, bf16[8,128,128]{2,1,0:T(8,128)(2,1)S(1)}, u32[]{:S(2)}, u32[]{:S(2)}) collective-permute-start(bf16[8,128,128]{2,1,0:T(8,128)(2,1)S(1)} %constant_dynamic-slice_fusion), channel_id=1, source_target_pairs={{0,2},{1,3},{2,0},{3,1},{4,6},{5,7},{6,4},{7,5},{8,10},{9,11},{10,... | collective-permute-start | bytes 786440 | tf_op jit(solution)/shard_map/ppermute | solution.py:140
  69.1 1.2 %fusion.15 = f32[1,512,1,128]{3,1,2,0:T(8,128)} fusion(f32[512]{0:T(512)S(1)} %get-tuple-element.22, bf16[512,512]{1,0:T(8,128)(2,1)S(1)} %get-tuple-element.43), kind=kOutput, calls=%fused_computation.16 | convolution fusion | flops 135528448 | bytes 659456 | tf_op jit(solution)/shard_map/while/body/eval_jaxpr/hts,shd->thd/dot_general | solution.py:92
  70.3 9.0 %collective-permute-done.3 = bf16[8,128,128]{2,1,0:T(8,128)(2,1)S(1)} collective-permute-done((bf16[8,128,128]{2,1,0:T(8,128)(2,1)S(1)}, bf16[8,128,128]{2,1,0:T(8,128)(2,1)S(1)}, u32[]{:S(2)}, u32[]{:S(2)}) %collective-permute-start.3) | collective-permute-done | bytes 262176 | tf_op jit(solution)/shard_map/ppermute | solution.py:140
  79.3 3.7 %collective-permute-done.5 = bf16[8,128,128]{2,1,0:T(8,128)(2,1)S(1)} collective-permute-done((bf16[8,128,128]{2,1,0:T(8,128)(2,1)S(1)}, bf16[8,128,128]{2,1,0:T(8,128)(2,1)S(1)}, u32[]{:S(2)}, u32[]{:S(2)}) %collective-permute-start.5) | collective-permute-done | bytes 262176 | tf_op jit(solution)/shard_map/ppermute | solution.py:140
  82.9 0.1 pad_maximum_fusion
  83.0 0.1 collective-permute-start.6
  83.1 0.2 fusion.52
  83.4 0.1 select_reduce_fusion
  83.5 0.2 multiply_reduce_fusion
  83.7 1.4 %fusion.56 = (f32[512]{0:T(512)S(1)}, f32[1,512,1,128]{3,1,2,0:T(8,128)S(1)}) fusion(f32[1,512,1,128]{3,1,2,0:T(8,128)} %fusion.15, f32[128,128]{1,0:T(8,128)S(1)} %multiply_reduce_fusion, f32[]{:T(128)} %bitcast.11, f32[512]{0:T(512)S(1)} %exp.53, bf16[512,512]{1,0:T(8,128)(2,1)} %copy-done), kind=kOutput, calls=%fused_computation.91 | convolution fusion | flops 17137152 | bytes 725504 | tf_op jit(solution)/shard_map/cthd,chde->cthe/dot_general | solution.py:109
  85.1 0.2 fusion.29
  85.3 1.2 %fusion.32 = bf16[512,128]{1,0:T(8,128)(2,1)S(1)} fusion(f32[1,512,1,128]{3,1,2,0:T(8,128)S(1)} %get-tuple-element.46, f32[512,512]{1,0:T(8,128)} %get-tuple-element.44, f32[512]{0:T(512)S(1)} %add_sqrt_fusion, f32[512]{0:T(512)S(1)} %broadcast_multiply_fusion), kind=kLoop, calls=%fused_computation.43 | loop fusion | flops 524288 | bytes 659456 | tf_op jit(solution)/shard_map/convert_element_type | solution.py:121
  86.5 0.7 collective-permute-start
  87.2 1.4 %collective-permute-start.1 = (bf16[4,32,128]{2,1,0:T(8,128)(2,1)S(1)}, bf16[4,32,128]{2,1,0:T(8,128)(2,1)S(1)}, u32[]{:S(2)}, u32[]{:S(2)}) collective-permute-start(bf16[4,32,128]{2,1,0:T(8,128)(2,1)S(1)} %get-tuple-element.41), channel_id=1, source_target_pairs={{0,2},{1,3},{2,0},{3,1},{4,6},{5,7},{6,4},{7,5},{8,10},{9,11},{10,... | collective-permute-start | bytes 98312 | tf_op jit(solution)/shard_map/ppermute | solution.py:139
  88.6 0.8 collective-permute-start.2
  89.4 0.1 broadcast_select_fusion.1
  89.6 1.2 %collective-permute-done = bf16[4,32,128]{2,1,0:T(8,128)(2,1)S(1)} collective-permute-done((bf16[4,32,128]{2,1,0:T(8,128)(2,1)S(1)}, bf16[4,32,128]{2,1,0:T(8,128)(2,1)S(1)}, u32[]{:S(2)}, u32[]{:S(2)}) %collective-permute-start) | collective-permute-done | bytes 32800 | tf_op jit(solution)/shard_map/ppermute | solution.py:139
  90.8 1.8 %collective-permute-done.1 = bf16[4,32,128]{2,1,0:T(8,128)(2,1)S(1)} collective-permute-done((bf16[4,32,128]{2,1,0:T(8,128)(2,1)S(1)}, bf16[4,32,128]{2,1,0:T(8,128)(2,1)S(1)}, u32[]{:S(2)}, u32[]{:S(2)}) %collective-permute-start.1) | collective-permute-done | bytes 32800 | tf_op jit(solution)/shard_map/ppermute | solution.py:139
  92.6 1.1 collective-permute-done.2
  93.7 0.5 fusion.13
  94.2 0.1 copy.38
  94.4 1.3 %collective-permute-start.7 = (bf16[32,2048]{1,0:T(8,128)(2,1)S(1)}, bf16[32,2048]{1,0:T(8,128)(2,1)S(1)}, u32[]{:S(2)}, u32[]{:S(2)}) collective-permute-start(bf16[32,2048]{1,0:T(8,128)(2,1)S(1)} %get-tuple-element.25), channel_id=1, source_target_pairs={{0,4},{1,5},{2,6},{3,7},{4,8},{5,9},{6,10},{7,11},{8,12},{9,13},{1... | collective-permute-start | bytes 393224 | tf_op jit(solution)/shard_map/ppermute | solution.py:158
  95.6 2.7 %collective-permute-start.8 = (bf16[32,2048]{1,0:T(8,128)(2,1)S(1)}, bf16[32,2048]{1,0:T(8,128)(2,1)S(1)}, u32[]{:S(2)}, u32[]{:S(2)}) collective-permute-start(bf16[32,2048]{1,0:T(8,128)(2,1)S(1)} %get-tuple-element.36), channel_id=1, source_target_pairs={{0,8},{1,9},{2,10},{3,11},{4,12},{5,13},{6,14},{7,15},{8,0},{9,1},... | collective-permute-start | bytes 393224 | tf_op jit(solution)/shard_map/ppermute | solution.py:158
  98.4 1.7 %collective-permute-start.9 = (bf16[32,2048]{1,0:T(8,128)(2,1)S(1)}, bf16[32,2048]{1,0:T(8,128)(2,1)S(1)}, u32[]{:S(2)}, u32[]{:S(2)}) collective-permute-start(bf16[32,2048]{1,0:T(8,128)(2,1)S(1)} %get-tuple-element.26), channel_id=1, source_target_pairs={{0,12},{1,13},{2,14},{3,15},{4,0},{5,1},{6,2},{7,3},{8,4},{9,5},{1... | collective-permute-start | bytes 393224 | tf_op jit(solution)/shard_map/ppermute | solution.py:158
  100.1 1.8 %collective-permute-done.7 = bf16[32,2048]{1,0:T(8,128)(2,1)S(1)} collective-permute-done((bf16[32,2048]{1,0:T(8,128)(2,1)S(1)}, bf16[32,2048]{1,0:T(8,128)(2,1)S(1)}, u32[]{:S(2)}, u32[]{:S(2)}) %collective-permute-start.7) | collective-permute-done | bytes 131104 | tf_op jit(solution)/shard_map/ppermute | solution.py:158
  101.9 1.4 %collective-permute-done.8 = bf16[32,2048]{1,0:T(8,128)(2,1)S(1)} collective-permute-done((bf16[32,2048]{1,0:T(8,128)(2,1)S(1)}, bf16[32,2048]{1,0:T(8,128)(2,1)S(1)}, u32[]{:S(2)}, u32[]{:S(2)}) %collective-permute-start.8) | collective-permute-done | bytes 131104 | tf_op jit(solution)/shard_map/ppermute | solution.py:158
  103.3 0.2 collective-permute-done.9
  103.5 0.7 fusion.27
  (25 shorter events, 0.5 us)
Async XLA Ops:
  6.5 46.0 %all-gather.2.cloned.1.call-start = ((), (), s32[]{:S(2)}) async-start(), calls=%async_computation.2 | async-start | bytes 2785280 | tf_op jit(solution)/shard_map/all_gather | solution.py:52
  10.5 7.6 %copy-start.1 = (f32[512,1]{0,1:T(1,128)S(1)}, f32[512,1]{0,1:T(1,128)}, u32[]{:S(2)}) copy-start(f32[512,1]{0,1:T(1,128)} %param.8) | copy-start | bytes 6148
  10.6 35.8 %all-to-all-start = ((bf16[16,32,2048]{2,1,0:T(8,128)(2,1)}), bf16[16,32,2048]{2,1,0:T(8,128)(2,1)S(1)}, u32[]{:S(2)}, u32[]{:S(2)}) async-start(bf16[16,32,2048]{2,1,0:T(8,128)(2,1)} %broadcast_in_dim.51), calls=%async_computation | async-start | bytes 4194304 | tf_op jit(solution)/shard_map/all_to_all | solution.py:14
  56.3 14.0 %copy-start = (bf16[512,512]{1,0:T(8,128)(2,1)}, bf16[512,512]{1,0:T(8,128)(2,1)S(1)}, u32[]{:S(2)}) copy-start(bf16[512,512]{1,0:T(8,128)(2,1)S(1)} %get-tuple-element.43) | copy-start | bytes 1572868
  57.7 25.5 %all-to-all-start.1 = ((bf16[16,1,136,128]{3,2,1,0:T(8,128)(2,1)}), bf16[16,1,136,128]{3,2,1,0:T(8,128)(2,1)S(1)}, u32[]{:S(2)}, u32[]{:S(2)}) async-start(bf16[16,1,136,128]{3,2,1,0:T(8,128)(2,1)} %broadcast_in_dim.94), calls=%async_computation.1 | async-start | bytes 1114112 | tf_op jit(solution)/shard_map/all_to_all | solution.py:14
  65.7 13.5 %collective-permute-start.3 = (bf16[8,128,128]{2,1,0:T(8,128)(2,1)S(1)}, bf16[8,128,128]{2,1,0:T(8,128)(2,1)S(1)}, u32[]{:S(2)}, u32[]{:S(2)}) collective-permute-start(bf16[8,128,128]{2,1,0:T(8,128)(2,1)S(1)} %constant_dynamic-slice_fusion), channel_id=1, source_target_pairs={{0,1},{1,2},{2,3},{3,0},{4,5},{5,6},{6,7},{7,4},{8,9},{9,10},{10,1... | collective-permute-start | bytes 786440 | tf_op jit(solution)/shard_map/ppermute | solution.py:140
  67.6 11.7 %collective-permute-start.4 = (bf16[8,128,128]{2,1,0:T(8,128)(2,1)S(1)}, bf16[8,128,128]{2,1,0:T(8,128)(2,1)S(1)}, u32[]{:S(2)}, u32[]{:S(2)}) collective-permute-start(bf16[8,128,128]{2,1,0:T(8,128)(2,1)S(1)} %constant_dynamic-slice_fusion), channel_id=1, source_target_pairs={{0,2},{1,3},{2,0},{3,1},{4,6},{5,7},{6,4},{7,5},{8,10},{9,11},{10,... | collective-permute-start | bytes 786440 | tf_op jit(solution)/shard_map/ppermute | solution.py:140
  69.0 13.9 %collective-permute-start.5 = (bf16[8,128,128]{2,1,0:T(8,128)(2,1)S(1)}, bf16[8,128,128]{2,1,0:T(8,128)(2,1)S(1)}, u32[]{:S(2)}, u32[]{:S(2)}) collective-permute-start(bf16[8,128,128]{2,1,0:T(8,128)(2,1)S(1)} %constant_dynamic-slice_fusion), channel_id=1, source_target_pairs={{0,3},{1,0},{2,1},{3,2},{4,7},{5,4},{6,5},{7,6},{8,11},{9,8},{10,9... | collective-permute-start | bytes 786440 | tf_op jit(solution)/shard_map/ppermute | solution.py:140
  83.0 6.4 %collective-permute-start.6 = (bf16[3,8,128,128]{3,2,0,1:T(8,128)(2,1)S(1)}, bf16[3,8,128,128]{3,2,0,1:T(8,128)(2,1)S(1)}, u32[]{:S(2)}, u32[]{:S(2)}) collective-permute-start(bf16[3,8,128,128]{3,2,0,1:T(8,128)(2,1)S(1)} %pad_maximum_fusion), channel_id=1, source_target_pairs={{0,16},{16,0},{32,48},{48,32},{64,80},{80,64},{96,112},{112,96},{1... | collective-permute-start | bytes 2359304 | tf_op jit(solution)/shard_map/ppermute | solution.py:142
  86.5 4.3 %collective-permute-start = (bf16[4,32,128]{2,1,0:T(8,128)(2,1)S(1)}, bf16[4,32,128]{2,1,0:T(8,128)(2,1)S(1)}, u32[]{:S(2)}, u32[]{:S(2)}) collective-permute-start(bf16[4,32,128]{2,1,0:T(8,128)(2,1)S(1)} %get-tuple-element.42), channel_id=1, source_target_pairs={{0,1},{1,2},{2,3},{3,0},{4,5},{5,6},{6,7},{7,4},{8,9},{9,10},{10,1... | collective-permute-start | bytes 98312 | tf_op jit(solution)/shard_map/ppermute | solution.py:139
  87.2 5.4 %collective-permute-start.1 = (bf16[4,32,128]{2,1,0:T(8,128)(2,1)S(1)}, bf16[4,32,128]{2,1,0:T(8,128)(2,1)S(1)}, u32[]{:S(2)}, u32[]{:S(2)}) collective-permute-start(bf16[4,32,128]{2,1,0:T(8,128)(2,1)S(1)} %get-tuple-element.41), channel_id=1, source_target_pairs={{0,2},{1,3},{2,0},{3,1},{4,6},{5,7},{6,4},{7,5},{8,10},{9,11},{10,... | collective-permute-start | bytes 98312 | tf_op jit(solution)/shard_map/ppermute | solution.py:139
  88.6 5.1 %collective-permute-start.2 = (bf16[4,32,128]{2,1,0:T(8,128)(2,1)S(1)}, bf16[4,32,128]{2,1,0:T(8,128)(2,1)S(1)}, u32[]{:S(2)}, u32[]{:S(2)}) collective-permute-start(bf16[4,32,128]{2,1,0:T(8,128)(2,1)S(1)} %get-tuple-element.40), channel_id=1, source_target_pairs={{0,3},{1,0},{2,1},{3,2},{4,7},{5,4},{6,5},{7,6},{8,11},{9,8},{10,9... | collective-permute-start | bytes 98312 | tf_op jit(solution)/shard_map/ppermute | solution.py:139
  94.4 7.5 %collective-permute-start.7 = (bf16[32,2048]{1,0:T(8,128)(2,1)S(1)}, bf16[32,2048]{1,0:T(8,128)(2,1)S(1)}, u32[]{:S(2)}, u32[]{:S(2)}) collective-permute-start(bf16[32,2048]{1,0:T(8,128)(2,1)S(1)} %get-tuple-element.25), channel_id=1, source_target_pairs={{0,4},{1,5},{2,6},{3,7},{4,8},{5,9},{6,10},{7,11},{8,12},{9,13},{1... | collective-permute-start | bytes 393224 | tf_op jit(solution)/shard_map/ppermute | solution.py:158
  95.6 7.7 %collective-permute-start.8 = (bf16[32,2048]{1,0:T(8,128)(2,1)S(1)}, bf16[32,2048]{1,0:T(8,128)(2,1)S(1)}, u32[]{:S(2)}, u32[]{:S(2)}) collective-permute-start(bf16[32,2048]{1,0:T(8,128)(2,1)S(1)} %get-tuple-element.36), channel_id=1, source_target_pairs={{0,8},{1,9},{2,10},{3,11},{4,12},{5,13},{6,14},{7,15},{8,0},{9,1},... | collective-permute-start | bytes 393224 | tf_op jit(solution)/shard_map/ppermute | solution.py:158
  98.4 5.1 %collective-permute-start.9 = (bf16[32,2048]{1,0:T(8,128)(2,1)S(1)}, bf16[32,2048]{1,0:T(8,128)(2,1)S(1)}, u32[]{:S(2)}, u32[]{:S(2)}) collective-permute-start(bf16[32,2048]{1,0:T(8,128)(2,1)S(1)} %get-tuple-element.26), channel_id=1, source_target_pairs={{0,12},{1,13},{2,14},{3,15},{4,0},{5,1},{6,2},{7,3},{8,4},{9,5},{1... | collective-permute-start | bytes 393224 | tf_op jit(solution)/shard_map/ppermute | solution.py:158
Sparse Core Ops, SparseCore 0:
  9.2 43.2 all-gather.1

commit v15 on v12

--- a/solution.py
+++ b/solution.py
@@ -126,31 +126,31 @@
     half = rows_mine.shape[0] // 2
     parity = lax.axis_index("tm") % 2
     own_half = lax.dynamic_slice_in_dim(rows_mine, parity * half, half, axis=0)
-    pieces = [lax.dynamic_index_in_dim(by_owner, col, axis=1, keepdims=False)]
     fetched = []
     for shift in range(1, side):
         across = [(h, (h // side) * side + (h % side + shift) % side) for h in range(heads)]
-        piece = lax.dynamic_index_in_dim(by_owner, (col + shift) % side, axis=1, keepdims=False)
-        pieces.append(lax.ppermute(piece, "head", across))
         fetched.append(lax.ppermute(own_half, "head", across))
     fetched = jnp.stack(fetched)
     swapped = lax.ppermute(fetched, "tm", [(t, t ^ 1) for t in range(units)])
     first = jnp.where(parity == 0, fetched, swapped)
     second = jnp.where(parity == 0, swapped, fetched)
     remote = jnp.concatenate([first, second], axis=1)
-    weights_in = [rows_mine] + [remote[s] for s in range(side - 1)]
+    by_shift = jnp.concatenate([rows_mine[None], remote], axis=0)
+    weights_in = jnp.take(by_shift, (col - jnp.arange(side)) % side, axis=0)
+    across_ring = [[r * side + c for c in range(side)] for r in range(side)]
+    down_ring = [[r * side + c for r in range(side)] for c in range(side)]
+    pieces = lax.all_to_all(
+        jnp.swapaxes(by_owner, 0, 1), "head", 0, 0, tiled=False, axis_index_groups=across_ring
+    )
     partial = jnp.einsum(
         "syfr,skrc->yfkc",
-        jnp.stack(pieces),
-        jnp.stack(weights_in),
+        pieces,
+        weights_in,
         preferred_element_type=jnp.float32,
     ).astype(jnp.bfloat16)
     partial = partial.reshape(side, local_len // heads, -1)
-    total = lax.dynamic_index_in_dim(partial, row, axis=0, keepdims=False).astype(jnp.float32)
-    for shift in range(1, side):
-        down = [(h, ((h // side + shift) % side) * side + h % side) for h in range(heads)]
-        piece = lax.dynamic_index_in_dim(partial, (row + shift) % side, axis=0, keepdims=False)
-        total = total + lax.ppermute(piece, "head", down).astype(jnp.float32)
+    shares = lax.all_to_all(partial, "head", 0, 0, tiled=False, axis_index_groups=down_ring)
+    total = jnp.sum(shares.astype(jnp.float32), axis=0)
     return total.astype(jnp.bfloat16)
 
 

time: 112 us -> 120 us (1.071); the launches traced: 111 us -> 118 us
  blocking collectives: 0 us -> 12.2 us
  waiting for transfers between devices: 49.4 us -> 43.2 us
  starting transfers between devices: 23.7 us -> 19.6 us
  local copies, waits for them, and re-layouts: 7.53 us -> 10.3 us
  matrix products: 7.4 us -> 9.16 us
    all_to_all x0 -> x1, blocking collectives: none -> 12.2 us  [shards(): lax.all_to_all(partial, 'head', 0, 0, tiled=False, axis_index_groups=down...]
    ppermute x6 -> x0, starting transfers between devices: 8.63 us -> none  [the longest x3 5.72 us: shards(): total = total + lax.ppermute(piece, 'head', down).astype(jnp.float32)]
    ppermute x6 -> x0, waiting for transfers between devices: 7.58 us -> none  [the longest x3 4.18 us: shards(): pieces.append(lax.ppermute(piece, 'head', across))]
    all_to_all x0 -> x1, starting transfers between devices: none -> 4.5 us  [shards(): lax.all_to_all(jnp.swapaxes(by_owner, 0, 1), 'head', 0, 0, tiled=False, a...]
    gather x0 -> x1, local copies, waits for them, and re-layouts: none -> 2.17 us  [shards(): weights_in = jnp.take(by_shift, (col - jnp.arange(side)) % side, axis=0)]
    dot_general x1, matrix products: 0.45 us -> 2.21 us  [shards(): jnp.einsum('syfr,skrc->yfkc', pieces, weights_in, preferred_element_type=...]
    all_to_all x0 -> x1, waiting for transfers between devices: none -> 1.36 us  [shards(): lax.all_to_all(jnp.swapaxes(by_owner, 0, 1), 'head', 0, 0, tiled=False, a...]
  transfers between devices with their start and end apart: 13 -> 8, of which waited for: 10 -> 5; matrix products, arithmetic and copies ran while one was open for 11% -> 13% of each run, Pallas kernels for 0% -> 0%
where the time goes in v15:
time: 120 us; the launch traced here: 118 us
  waiting for transfers between devices  43.2 us (36%)
  starting transfers between devices  19.6 us (16%)
  between operations  17.4 us (14%)
  blocking collectives  12.2 us (10%)
  local copies, waits for them, and re-layouts  10.3 us (9%)
  matrix products  9.16 us (8%)
  other arithmetic  5.93 us (5%)
    all_to_all x2, waiting for transfers between devices, gather_by_exchange(): return lax.all_to_all(copies, axis, 0, 0, tiled=False)  23 us
    ppermute x3, waiting for transfers between devices, shards(): fetched.append(lax.ppermute(own_half, 'head', across))  12.7 us
    all_to_all x1, blocking collectives, shards(): lax.all_to_all(partial, 'head', 0, 0, tiled=False, axis_index_groups=down...  12.2 us
    all_to_all x2, starting transfers between devices, gather_by_exchange(): return lax.all_to_all(copies, axis, 0, 0, tiled=False)  11.7 us
    all_gather x1, waiting for transfers between devices, shards(): stacked = lax.all_gather(packed, 'tm', axis=0, tiled=True)  6.1 us
    all_to_all x1, starting transfers between devices, shards(): lax.all_to_all(jnp.swapaxes(by_owner, 0, 1), 'head', 0, 0, tiled=False, a...  4.5 us
    dot_general x1, matrix products, shards(): projected = jnp.dot(frames_here, joined, preferred_element_type=jnp.float32)  3.83 us
    broadcast_in_dim x2, local copies, waits for them, and re-layouts, gather_by_exchange(): copies = jnp.broadcast_to(part[None], (count,) + part.shape)  3.35 us
  transfers between devices with their start and end apart: 8, of which 5 were waited for; matrix products, arithmetic and copies ran while one was open for 13% of the time, Pallas kernels for 0%

profile of v15, /device:TPU:6, one launch (start us, length us, event | category | flops | bytes accessed | tf_op | source)
XLA Modules:
  0.0 117.8 jit_solution(16607261762709802675)
XLA Ops:
  6.5 1.5 %pad_add_fusion = bf16[128,640]{1,0:T(8,128)(2,1)} fusion(bf16[128,128]{1,0:T(8,128)(2,1)} %param.13, bf16[128,128]{1,0:T(8,128)(2,1)} %param.12, bf16[128,128]{1,0:T(8,128)(2,1)} %param.11, bf16[128,128]{1,0:T(8,128)(2,1)} %param.10, bf16[128,128]{1,0:T(8,128)(2,1)} %param.9), kind=kLoop, calls=%fused_computation.43 | loop fusion | flops 819200 | bytes 327680 | tf_op jit(solution)/shard_map/add | solution.py:48
  8.1 0.0 all-gather.2.cloned.1.call-update
  8.1 2.5 %broadcast_in_dim.58 = bf16[16,32,2048]{2,1,0:T(8,128)(2,1)} broadcast(bf16[32,2048]{1,0:T(8,128)(2,1)} %param.7), dimensions={1,2} | broadcast | bytes 2228224 | tf_op jit(solution)/shard_map/broadcast_in_dim | solution.py:13
  10.6 7.6 %all-to-all-start = ((bf16[16,32,2048]{2,1,0:T(8,128)(2,1)}), bf16[16,32,2048]{2,1,0:T(8,128)(2,1)S(1)}, u32[]{:S(2)}, u32[]{:S(2)}) async-start(bf16[16,32,2048]{2,1,0:T(8,128)(2,1)} %broadcast_in_dim.58), calls=%async_computation | async-start | bytes 4194304 | tf_op jit(solution)/shard_map/all_to_all | solution.py:14
  18.1 0.6 reduce_sum.59
  18.7 0.3 reduce-window.6
  19.0 0.2 slice_reduce_fusion
  19.2 0.2 reduce-window.9
  19.4 0.1 broadcast.259
  19.4 0.6 slice.67
  20.1 0.6 slice.66
  23.1 0.1 pad.33.clone
  23.2 0.1 pad.34.clone
  23.3 0.1 subtract_exponential_fusion
  23.4 23.0 %all-to-all-done = bf16[16,32,2048]{2,1,0:T(8,128)(2,1)S(1)} async-done(((bf16[16,32,2048]{2,1,0:T(8,128)(2,1)}), bf16[16,32,2048]{2,1,0:T(8,128)(2,1)S(1)}, u32[]{:S(2)}, u32[]{:S(2)}) %all-to-all-start) | async-done | bytes 2097184 | tf_op jit(solution)/shard_map/all_to_all | solution.py:14
  46.4 6.1 %all-gather.2.cloned.1.call-done = bf16[2048,640]{1,0:T(8,128)(2,1)} async-done(((bf16[128,640]{1,0:T(8,128)(2,1)}), bf16[2048,640]{1,0:T(8,128)(2,1)}) %all-gather.2.cloned.1.call-update) | async-done | bytes 2621456 | tf_op jit(solution)/shard_map/all_gather | solution.py:52
  52.5 3.8 %fusion.56 = (bf16[512,512]{1,0:T(8,128)(2,1)S(1)}, f32[512,512]{1,0:T(8,128)}) fusion(bf16[512,2048]{1,0:T(8,128)(2,1)S(1)} %bitcast.92, bf16[2048,640]{1,0:T(8,128)(2,1)} %all-gather.2.cloned.1.call-done), kind=kOutput, calls=%fused_computation.87 | convolution fusion | flops 1074003968 | bytes 5767168 | tf_op jit(solution)/shard_map/dot_general | solution.py:56
  56.3 0.3 fusion.22
  56.7 0.1 maximum_bitcast_fusion
  56.8 0.9 broadcast_in_dim.104
  57.7 4.1 %all-to-all-start.1 = ((bf16[16,1,136,128]{3,2,1,0:T(8,128)(2,1)}), bf16[16,1,136,128]{3,2,1,0:T(8,128)(2,1)S(1)}, u32[]{:S(2)}, u32[]{:S(2)}) async-start(bf16[16,1,136,128]{3,2,1,0:T(8,128)(2,1)} %broadcast_in_dim.104), calls=%async_computation.1 | async-start | bytes 1114112 | tf_op jit(solution)/shard_map/all_to_all | solution.py:14
  61.9 0.6 slice.65
  62.5 0.6 slice.64
  64.5 1.1 slice.71
  65.6 1.9 %collective-permute-start = (bf16[8,128,128]{2,1,0:T(8,128)(2,1)S(1)}, bf16[8,128,128]{2,1,0:T(8,128)(2,1)S(1)}, u32[]{:S(2)}, u32[]{:S(2)}) collective-permute-start(bf16[8,128,128]{2,1,0:T(8,128)(2,1)S(1)} %constant_dynamic-slice_fusion), channel_id=1, source_target_pairs={{0,1},{1,2},{2,3},{3,0},{4,5},{5,6},{6,7},{7,4},{8,9},{9,10},{10,1... | collective-permute-start | bytes 786440 | tf_op jit(solution)/shard_map/ppermute | solution.py:132
  67.5 1.4 %collective-permute-start.1 = (bf16[8,128,128]{2,1,0:T(8,128)(2,1)S(1)}, bf16[8,128,128]{2,1,0:T(8,128)(2,1)S(1)}, u32[]{:S(2)}, u32[]{:S(2)}) collective-permute-start(bf16[8,128,128]{2,1,0:T(8,128)(2,1)S(1)} %constant_dynamic-slice_fusion), channel_id=1, source_target_pairs={{0,2},{1,3},{2,0},{3,1},{4,6},{5,7},{6,4},{7,5},{8,10},{9,11},{10,... | collective-permute-start | bytes 786440 | tf_op jit(solution)/shard_map/ppermute | solution.py:132
  69.0 0.0 collective-permute-start.2
  69.0 1.2 %fusion.19 = f32[1,512,1,128]{3,1,2,0:T(8,128)} fusion(f32[512]{0:T(512)S(1)} %get-tuple-element.22, bf16[512,512]{1,0:T(8,128)(2,1)S(1)} %get-tuple-element.25), kind=kOutput, calls=%fused_computation.16 | convolution fusion | flops 135528448 | bytes 659456 | tf_op jit(solution)/shard_map/while/body/eval_jaxpr/hts,shd->thd/dot_general | solution.py:92
  70.2 9.1 %collective-permute-done = bf16[8,128,128]{2,1,0:T(8,128)(2,1)S(1)} collective-permute-done((bf16[8,128,128]{2,1,0:T(8,128)(2,1)S(1)}, bf16[8,128,128]{2,1,0:T(8,128)(2,1)S(1)}, u32[]{:S(2)}, u32[]{:S(2)}) %collective-permute-start) | collective-permute-done | bytes 262176 | tf_op jit(solution)/shard_map/ppermute | solution.py:132
  79.3 3.7 %collective-permute-done.2 = bf16[8,128,128]{2,1,0:T(8,128)(2,1)S(1)} collective-permute-done((bf16[8,128,128]{2,1,0:T(8,128)(2,1)S(1)}, bf16[8,128,128]{2,1,0:T(8,128)(2,1)S(1)}, u32[]{:S(2)}, u32[]{:S(2)}) %collective-permute-start.2) | collective-permute-done | bytes 262176 | tf_op jit(solution)/shard_map/ppermute | solution.py:132
  83.0 0.1 pad_maximum_fusion
  83.1 0.1 collective-permute-start.3
  83.2 0.2 fusion.51
  83.4 0.1 select_reduce_fusion
  83.5 0.2 multiply_reduce_fusion
  83.7 1.5 %fusion.57 = (f32[512]{0:T(512)S(1)}, f32[1,512,1,128]{3,1,2,0:T(8,128)S(1)}) fusion(f32[1,512,1,128]{3,1,2,0:T(8,128)} %fusion.19, f32[512]{0:T(512)S(1)} %exp.53, bf16[512,512]{1,0:T(8,128)(2,1)} %copy-done, f32[128,128]{1,0:T(8,128)S(1)} %multiply_reduce_fusion, f32[]{:T(128)} %bitcast.11), kind=kOutput, calls=%fused_computation.88 | convolution fusion | flops 100941312 | bytes 725504 | tf_op jit(solution)/shard_map/cthd,chde->cthe/dot_general | solution.py:109
  85.2 0.2 fusion.30
  85.5 1.2 fusion.33
  86.7 0.7 copy.54
  87.3 4.5 %all-to-all-start.2 = ((bf16[4,4,32,128]{3,2,1,0:T(8,128)(2,1)}), bf16[4,4,32,128]{3,2,1,0:T(8,128)(2,1)S(1)}, u32[]{:S(2)}, u32[]{:S(2)}) async-start(bf16[4,4,32,128]{3,2,1,0:T(8,128)(2,1)} %bitcast.89), calls=%async_computation.2 | async-start | bytes 262144 | tf_op jit(solution)/shard_map/all_to_all | solution.py:142
  91.8 0.1 broadcast_select_fusion.2
  92.0 0.2 maximum_maximum_fusion
  92.2 2.2 %gather_fusion = bf16[4,16,128,128]{3,2,1,0:T(8,128)(2,1)} fusion(bf16[4,16,128,128]{3,2,1,0:T(8,128)(2,1)S(1)} %maximum_maximum_fusion, s32[1024]{0:T(1024)S(1)} %pad_clamp_fusion), kind=kCustom, calls=%fused_computation | custom fusion | bytes 4194320 | tf_op jit(solution)/shard_map/jit(_take)/gather | solution.py:139
  94.4 1.4 %all-to-all-done.2 = bf16[4,4,32,128]{3,2,1,0:T(8,128)(2,1)S(1)} async-done(((bf16[4,4,32,128]{3,2,1,0:T(8,128)(2,1)}), bf16[4,4,32,128]{3,2,1,0:T(8,128)(2,1)S(1)}, u32[]{:S(2)}, u32[]{:S(2)}) %all-to-all-start.2) | async-done | bytes 131104 | tf_op jit(solution)/shard_map/all_to_all | solution.py:142
  95.7 2.2 %fusion.15 = bf16[4,16,4,8,128]{4,3,2,1,0:T(8,128)(2,1)S(1)} fusion(bf16[4,16,128,128]{3,2,1,0:T(8,128)(2,1)} %gather_fusion, pred[4]{0:T(512)(128)(4,1)S(1)} %compare_and_fusion, bf16[4,4,32,128]{3,2,1,0:T(8,128)(2,1)S(1)} %all-to-all-done.2), kind=kOutput, calls=%fused_computation.13 | convolution fusion | flops 269746176 | bytes 2752516 | tf_op jit(solution)/shard_map/syfr,skrc->yfkc/dot_general | solution.py:145
  98.0 0.1 copy.53
  98.1 12.2 %all_to_all.20 = bf16[4,32,2048]{2,1,0:T(8,128)(2,1)S(1)} all-to-all(bf16[4,32,2048]{2,1,0:T(8,128)(2,1)S(1)} %bitcast.93), channel_id=1, replica_groups={{0,4,8,12},{1,5,9,13},{2,6,10,14},{3,7,11,15},{16,20,24,28},{17,21,25,2..., dimensions={0} | all-to-all | bytes 1048576 | tf_op jit(solution)/shard_map/all_to_all | solution.py:152
  110.3 0.7 reduce_sum.65
  (20 shorter events, 0.1 us)
Async XLA Ops:
  6.5 46.0 %all-gather.2.cloned.1.call-start = ((), (), s32[]{:S(2)}) async-start(), calls=%async_computation.4 | async-start | bytes 2785280 | tf_op jit(solution)/shard_map/all_gather | solution.py:52
  10.5 7.6 %copy-start.1 = (f32[512,1]{0,1:T(1,128)S(1)}, f32[512,1]{0,1:T(1,128)}, u32[]{:S(2)}) copy-start(f32[512,1]{0,1:T(1,128)} %param.8) | copy-start | bytes 6148
  10.6 35.8 %all-to-all-start = ((bf16[16,32,2048]{2,1,0:T(8,128)(2,1)}), bf16[16,32,2048]{2,1,0:T(8,128)(2,1)S(1)}, u32[]{:S(2)}, u32[]{:S(2)}) async-start(bf16[16,32,2048]{2,1,0:T(8,128)(2,1)} %broadcast_in_dim.58), calls=%async_computation | async-start | bytes 4194304 | tf_op jit(solution)/shard_map/all_to_all | solution.py:14
  56.3 13.9 %copy-start = (bf16[512,512]{1,0:T(8,128)(2,1)}, bf16[512,512]{1,0:T(8,128)(2,1)S(1)}, u32[]{:S(2)}) copy-start(bf16[512,512]{1,0:T(8,128)(2,1)S(1)} %get-tuple-element.25) | copy-start | bytes 1572868
  57.7 25.5 %all-to-all-start.1 = ((bf16[16,1,136,128]{3,2,1,0:T(8,128)(2,1)}), bf16[16,1,136,128]{3,2,1,0:T(8,128)(2,1)S(1)}, u32[]{:S(2)}, u32[]{:S(2)}) async-start(bf16[16,1,136,128]{3,2,1,0:T(8,128)(2,1)} %broadcast_in_dim.104), calls=%async_computation.1 | async-start | bytes 1114112 | tf_op jit(solution)/shard_map/all_to_all | solution.py:14
  65.6 13.7 %collective-permute-start = (bf16[8,128,128]{2,1,0:T(8,128)(2,1)S(1)}, bf16[8,128,128]{2,1,0:T(8,128)(2,1)S(1)}, u32[]{:S(2)}, u32[]{:S(2)}) collective-permute-start(bf16[8,128,128]{2,1,0:T(8,128)(2,1)S(1)} %constant_dynamic-slice_fusion), channel_id=1, source_target_pairs={{0,1},{1,2},{2,3},{3,0},{4,5},{5,6},{6,7},{7,4},{8,9},{9,10},{10,1... | collective-permute-start | bytes 786440 | tf_op jit(solution)/shard_map/ppermute | solution.py:132
  67.5 11.7 %collective-permute-start.1 = (bf16[8,128,128]{2,1,0:T(8,128)(2,1)S(1)}, bf16[8,128,128]{2,1,0:T(8,128)(2,1)S(1)}, u32[]{:S(2)}, u32[]{:S(2)}) collective-permute-start(bf16[8,128,128]{2,1,0:T(8,128)(2,1)S(1)} %constant_dynamic-slice_fusion), channel_id=1, source_target_pairs={{0,2},{1,3},{2,0},{3,1},{4,6},{5,7},{6,4},{7,5},{8,10},{9,11},{10,... | collective-permute-start | bytes 786440 | tf_op jit(solution)/shard_map/ppermute | solution.py:132
  69.0 14.0 %collective-permute-start.2 = (bf16[8,128,128]{2,1,0:T(8,128)(2,1)S(1)}, bf16[8,128,128]{2,1,0:T(8,128)(2,1)S(1)}, u32[]{:S(2)}, u32[]{:S(2)}) collective-permute-start(bf16[8,128,128]{2,1,0:T(8,128)(2,1)S(1)} %constant_dynamic-slice_fusion), channel_id=1, source_target_pairs={{0,3},{1,0},{2,1},{3,2},{4,7},{5,4},{6,5},{7,6},{8,11},{9,8},{10,9... | collective-permute-start | bytes 786440 | tf_op jit(solution)/shard_map/ppermute | solution.py:132
  83.1 8.8 %collective-permute-start.3 = (bf16[3,8,128,128]{3,2,1,0:T(8,128)(2,1)S(1)}, bf16[3,8,128,128]{3,2,1,0:T(8,128)(2,1)S(1)}, u32[]{:S(2)}, u32[]{:S(2)}) collective-permute-start(bf16[3,8,128,128]{3,2,1,0:T(8,128)(2,1)S(1)} %pad_maximum_fusion), channel_id=1, source_target_pairs={{0,16},{16,0},{32,48},{48,32},{64,80},{80,64},{96,112},{112,96},{1... | collective-permute-start | bytes 2359304 | tf_op jit(solution)/shard_map/ppermute | solution.py:134
  87.3 8.4 %all-to-all-start.2 = ((bf16[4,4,32,128]{3,2,1,0:T(8,128)(2,1)}), bf16[4,4,32,128]{3,2,1,0:T(8,128)(2,1)S(1)}, u32[]{:S(2)}, u32[]{:S(2)}) async-start(bf16[4,4,32,128]{3,2,1,0:T(8,128)(2,1)} %bitcast.89), calls=%async_computation.2 | async-start | bytes 262144 | tf_op jit(solution)/shard_map/all_to_all | solution.py:142
Sparse Core Ops, SparseCore 0:
  9.2 43.2 all-gather.1

commit v16 on v12

--- a/solution.py
+++ b/solution.py
@@ -121,6 +121,7 @@
     me = lax.axis_index("head")
     row, col = me // side, me % side
     rows_mine = out_blocks
+    ring_order = sorted(range(1, side), key=lambda shift: -min(shift, side - shift))
     by_owner = gated.reshape(side, side, local_len // heads, head_width)
     units = lax.axis_size("tm")
     half = rows_mine.shape[0] // 2
@@ -128,7 +129,7 @@
     own_half = lax.dynamic_slice_in_dim(rows_mine, parity * half, half, axis=0)
     pieces = [lax.dynamic_index_in_dim(by_owner, col, axis=1, keepdims=False)]
     fetched = []
-    for shift in range(1, side):
+    for shift in ring_order:
         across = [(h, (h // side) * side + (h % side + shift) % side) for h in range(heads)]
         piece = lax.dynamic_index_in_dim(by_owner, (col + shift) % side, axis=1, keepdims=False)
         pieces.append(lax.ppermute(piece, "head", across))
@@ -147,7 +148,7 @@
     ).astype(jnp.bfloat16)
     partial = partial.reshape(side, local_len // heads, -1)
     total = lax.dynamic_index_in_dim(partial, row, axis=0, keepdims=False).astype(jnp.float32)
-    for shift in range(1, side):
+    for shift in ring_order:
         down = [(h, ((h // side + shift) % side) * side + h % side) for h in range(heads)]
         piece = lax.dynamic_index_in_dim(partial, (row + shift) % side, axis=0, keepdims=False)
         total = total + lax.ppermute(piece, "head", down).astype(jnp.float32)

time: 112 us -> 111 us (level)
  waiting for transfers between devices: 49.4 us -> 47.6 us
  starting transfers between devices: 23.7 us -> 25.1 us
    ppermute x3, waiting for transfers between devices: 12.7 us -> 10.5 us  [shards(): fetched.append(lax.ppermute(own_half, 'head', across))]
where the time goes in v16:
time: 111 us
  waiting for transfers between devices  47.6 us (43%)
  starting transfers between devices  25.1 us (23%)
  between operations  17.6 us (16%)
  local copies, waits for them, and re-layouts  7.53 us (7%)
  matrix products  7.4 us (7%)
  other arithmetic  5.63 us (5%)
    all_to_all x2, waiting for transfers between devices, gather_by_exchange(): return lax.all_to_all(copies, axis, 0, 0, tiled=False)  23 us
    all_to_all x2, starting transfers between devices, gather_by_exchange(): return lax.all_to_all(copies, axis, 0, 0, tiled=False)  11.7 us
    ppermute x3, waiting for transfers between devices, shards(): fetched.append(lax.ppermute(own_half, 'head', across))  10.5 us
    all_gather x1, waiting for transfers between devices, shards(): stacked = lax.all_gather(packed, 'tm', axis=0, tiled=True)  6.1 us
    ppermute x3, starting transfers between devices, shards(): total = total + lax.ppermute(piece, 'head', down).astype(jnp.float32)  5.45 us
    ppermute x3, waiting for transfers between devices, shards(): pieces.append(lax.ppermute(piece, 'head', across))  4.7 us
    ppermute x3, starting transfers between devices, shards(): pieces.append(lax.ppermute(piece, 'head', across))  3.92 us
    ppermute x3, starting transfers between devices, shards(): fetched.append(lax.ppermute(own_half, 'head', across))  3.91 us
  transfers between devices with their start and end apart: 13, of which 10 were waited for; matrix products, arithmetic and copies ran while one was open for 11% of the time, Pallas kernels for 0%

profile of v16, /device:TPU:6, one launch (start us, length us, event | category | flops | bytes accessed | tf_op | source)
XLA Modules:
  0.0 110.8 jit_solution(4983528196670437955)
XLA Ops:
  6.5 1.5 %pad_add_fusion = bf16[128,640]{1,0:T(8,128)(2,1)} fusion(bf16[128,128]{1,0:T(8,128)(2,1)} %param.13, bf16[128,128]{1,0:T(8,128)(2,1)} %param.12, bf16[128,128]{1,0:T(8,128)(2,1)} %param.11, bf16[128,128]{1,0:T(8,128)(2,1)} %param.10, bf16[128,128]{1,0:T(8,128)(2,1)} %param.9), kind=kLoop, calls=%fused_computation.47 | loop fusion | flops 819200 | bytes 327680 | tf_op jit(solution)/shard_map/add | solution.py:48
  8.1 2.5 %broadcast_in_dim.51 = bf16[16,32,2048]{2,1,0:T(8,128)(2,1)} broadcast(bf16[32,2048]{1,0:T(8,128)(2,1)} %param.7), dimensions={1,2} | broadcast | bytes 2228224 | tf_op jit(solution)/shard_map/broadcast_in_dim | solution.py:13
  10.6 7.6 %all-to-all-start = ((bf16[16,32,2048]{2,1,0:T(8,128)(2,1)}), bf16[16,32,2048]{2,1,0:T(8,128)(2,1)S(1)}, u32[]{:S(2)}, u32[]{:S(2)}) async-start(bf16[16,32,2048]{2,1,0:T(8,128)(2,1)} %broadcast_in_dim.51), calls=%async_computation | async-start | bytes 4194304 | tf_op jit(solution)/shard_map/all_to_all | solution.py:14
  18.1 0.6 reduce_sum.47
  18.7 0.3 reduce-window.6
  19.0 0.2 slice_reduce_fusion
  19.2 0.2 reduce-window.9
  19.4 0.6 slice.69
  20.1 0.6 slice.68
  23.4 23.0 %all-to-all-done = bf16[16,32,2048]{2,1,0:T(8,128)(2,1)S(1)} async-done(((bf16[16,32,2048]{2,1,0:T(8,128)(2,1)}), bf16[16,32,2048]{2,1,0:T(8,128)(2,1)S(1)}, u32[]{:S(2)}, u32[]{:S(2)}) %all-to-all-start) | async-done | bytes 2097184 | tf_op jit(solution)/shard_map/all_to_all | solution.py:14
  46.4 6.1 %all-gather.2.cloned.1.call-done = bf16[2048,640]{1,0:T(8,128)(2,1)} async-done(((bf16[128,640]{1,0:T(8,128)(2,1)}), bf16[2048,640]{1,0:T(8,128)(2,1)}) %all-gather.2.cloned.1.call-update) | async-done | bytes 2621456 | tf_op jit(solution)/shard_map/all_gather | solution.py:52
  52.5 3.8 %fusion.58 = (bf16[512,512]{1,0:T(8,128)(2,1)S(1)}, f32[512,512]{1,0:T(8,128)}) fusion(bf16[512,2048]{1,0:T(8,128)(2,1)S(1)} %bitcast.110, bf16[2048,640]{1,0:T(8,128)(2,1)} %all-gather.2.cloned.1.call-done), kind=kOutput, calls=%fused_computation.91 | convolution fusion | flops 1074003968 | bytes 5767168 | tf_op jit(solution)/shard_map/dot_general | solution.py:56
  56.3 0.3 fusion.18
  56.7 0.1 maximum_bitcast_fusion.10
  56.8 0.9 broadcast_in_dim.94
  57.7 4.1 %all-to-all-start.1 = ((bf16[16,1,136,128]{3,2,1,0:T(8,128)(2,1)}), bf16[16,1,136,128]{3,2,1,0:T(8,128)(2,1)S(1)}, u32[]{:S(2)}, u32[]{:S(2)}) async-start(bf16[16,1,136,128]{3,2,1,0:T(8,128)(2,1)} %broadcast_in_dim.94), calls=%async_computation.1 | async-start | bytes 1114112 | tf_op jit(solution)/shard_map/all_to_all | solution.py:14
  62.0 0.6 slice.67
  62.6 0.6 slice.66
  64.6 1.1 slice.73
  65.7 1.5 %collective-permute-start.3 = (bf16[8,128,128]{2,1,0:T(8,128)(2,1)S(1)}, bf16[8,128,128]{2,1,0:T(8,128)(2,1)S(1)}, u32[]{:S(2)}, u32[]{:S(2)}) collective-permute-start(bf16[8,128,128]{2,1,0:T(8,128)(2,1)S(1)} %constant_dynamic-slice_fusion), channel_id=1, source_target_pairs={{0,2},{1,3},{2,0},{3,1},{4,6},{5,7},{6,4},{7,5},{8,10},{9,11},{10,... | collective-permute-start | bytes 786440 | tf_op jit(solution)/shard_map/ppermute | solution.py:136
  67.3 2.4 %collective-permute-start.4 = (bf16[8,128,128]{2,1,0:T(8,128)(2,1)S(1)}, bf16[8,128,128]{2,1,0:T(8,128)(2,1)S(1)}, u32[]{:S(2)}, u32[]{:S(2)}) collective-permute-start(bf16[8,128,128]{2,1,0:T(8,128)(2,1)S(1)} %constant_dynamic-slice_fusion), channel_id=1, source_target_pairs={{0,1},{1,2},{2,3},{3,0},{4,5},{5,6},{6,7},{7,4},{8,9},{9,10},{10,1... | collective-permute-start | bytes 786440 | tf_op jit(solution)/shard_map/ppermute | solution.py:136
  69.7 1.2 %fusion.15 = f32[1,512,1,128]{3,1,2,0:T(8,128)} fusion(f32[512]{0:T(512)S(1)} %get-tuple-element.22, bf16[512,512]{1,0:T(8,128)(2,1)S(1)} %get-tuple-element.43), kind=kOutput, calls=%fused_computation.16 | convolution fusion | flops 135528448 | bytes 659456 | tf_op jit(solution)/shard_map/while/body/eval_jaxpr/hts,shd->thd/dot_general | solution.py:92
  70.9 5.6 %collective-permute-done.3 = bf16[8,128,128]{2,1,0:T(8,128)(2,1)S(1)} collective-permute-done((bf16[8,128,128]{2,1,0:T(8,128)(2,1)S(1)}, bf16[8,128,128]{2,1,0:T(8,128)(2,1)S(1)}, u32[]{:S(2)}, u32[]{:S(2)}) %collective-permute-start.3) | collective-permute-done | bytes 262176 | tf_op jit(solution)/shard_map/ppermute | solution.py:136
  76.5 4.1 %collective-permute-done.4 = bf16[8,128,128]{2,1,0:T(8,128)(2,1)S(1)} collective-permute-done((bf16[8,128,128]{2,1,0:T(8,128)(2,1)S(1)}, bf16[8,128,128]{2,1,0:T(8,128)(2,1)S(1)}, u32[]{:S(2)}, u32[]{:S(2)}) %collective-permute-start.4) | collective-permute-done | bytes 262176 | tf_op jit(solution)/shard_map/ppermute | solution.py:136
  80.6 0.8 collective-permute-done.5
  81.4 0.1 pad_maximum_fusion
  81.5 0.1 collective-permute-start.6
  81.6 0.2 fusion.55
  81.8 0.1 select_reduce_fusion
  82.0 0.2 multiply_reduce_fusion
  82.1 1.5 %fusion.59 = (f32[512]{0:T(512)S(1)}, f32[1,512,1,128]{3,1,2,0:T(8,128)S(1)}) fusion(f32[1,512,1,128]{3,1,2,0:T(8,128)} %fusion.15, f32[512]{0:T(512)S(1)} %exp.53, bf16[512,512]{1,0:T(8,128)(2,1)} %copy-done, f32[128,128]{1,0:T(8,128)S(1)} %multiply_reduce_fusion, f32[]{:T(128)} %bitcast.11), kind=kOutput, calls=%fused_computation.92 | convolution fusion | flops 100941312 | bytes 725504 | tf_op jit(solution)/shard_map/cthd,chde->cthe/dot_general | solution.py:109
  83.7 0.2 fusion.29
  83.9 1.2 %fusion.32 = bf16[512,128]{1,0:T(8,128)(2,1)S(1)} fusion(f32[1,512,1,128]{3,1,2,0:T(8,128)S(1)} %get-tuple-element.46, f32[512,512]{1,0:T(8,128)} %get-tuple-element.44, f32[512]{0:T(512)S(1)} %add_sqrt_fusion, f32[512]{0:T(512)S(1)} %broadcast_multiply_fusion), kind=kLoop, calls=%fused_computation.43 | loop fusion | flops 524288 | bytes 659456 | tf_op jit(solution)/shard_map/convert_element_type | solution.py:116
  85.1 1.9 %collective-permute-start = (bf16[4,32,128]{2,1,0:T(8,128)(2,1)S(1)}, bf16[4,32,128]{2,1,0:T(8,128)(2,1)S(1)}, u32[]{:S(2)}, u32[]{:S(2)}) collective-permute-start(bf16[4,32,128]{2,1,0:T(8,128)(2,1)S(1)} %get-tuple-element.42), channel_id=1, source_target_pairs={{0,2},{1,3},{2,0},{3,1},{4,6},{5,7},{6,4},{7,5},{8,10},{9,11},{10,... | collective-permute-start | bytes 98312 | tf_op jit(solution)/shard_map/ppermute | solution.py:135
  87.0 1.7 %collective-permute-start.1 = (bf16[4,32,128]{2,1,0:T(8,128)(2,1)S(1)}, bf16[4,32,128]{2,1,0:T(8,128)(2,1)S(1)}, u32[]{:S(2)}, u32[]{:S(2)}) collective-permute-start(bf16[4,32,128]{2,1,0:T(8,128)(2,1)S(1)} %get-tuple-element.41), channel_id=1, source_target_pairs={{0,1},{1,2},{2,3},{3,0},{4,5},{5,6},{6,7},{7,4},{8,9},{9,10},{10,1... | collective-permute-start | bytes 98312 | tf_op jit(solution)/shard_map/ppermute | solution.py:135
  88.8 0.3 collective-permute-start.2
  89.1 0.1 broadcast_select_fusion.1
  89.2 1.4 %collective-permute-done = bf16[4,32,128]{2,1,0:T(8,128)(2,1)S(1)} collective-permute-done((bf16[4,32,128]{2,1,0:T(8,128)(2,1)S(1)}, bf16[4,32,128]{2,1,0:T(8,128)(2,1)S(1)}, u32[]{:S(2)}, u32[]{:S(2)}) %collective-permute-start) | collective-permute-done | bytes 32800 | tf_op jit(solution)/shard_map/ppermute | solution.py:135
  90.6 0.3 collective-permute-done.1
  91.0 3.0 %collective-permute-done.2 = bf16[4,32,128]{2,1,0:T(8,128)(2,1)S(1)} collective-permute-done((bf16[4,32,128]{2,1,0:T(8,128)(2,1)S(1)}, bf16[4,32,128]{2,1,0:T(8,128)(2,1)S(1)}, u32[]{:S(2)}, u32[]{:S(2)}) %collective-permute-start.2) | collective-permute-done | bytes 32800 | tf_op jit(solution)/shard_map/ppermute | solution.py:135
  93.9 0.5 fusion.13
  94.4 0.1 copy.38
  94.5 2.2 %collective-permute-start.7 = (bf16[32,2048]{1,0:T(8,128)(2,1)S(1)}, bf16[32,2048]{1,0:T(8,128)(2,1)S(1)}, u32[]{:S(2)}, u32[]{:S(2)}) collective-permute-start(bf16[32,2048]{1,0:T(8,128)(2,1)S(1)} %get-tuple-element.25), channel_id=1, source_target_pairs={{0,8},{1,9},{2,10},{3,11},{4,12},{5,13},{6,14},{7,15},{8,0},{9,1},... | collective-permute-start | bytes 393224 | tf_op jit(solution)/shard_map/ppermute | solution.py:154
  96.8 0.6 collective-permute-start.8
  97.3 2.7 %collective-permute-start.9 = (bf16[32,2048]{1,0:T(8,128)(2,1)S(1)}, bf16[32,2048]{1,0:T(8,128)(2,1)S(1)}, u32[]{:S(2)}, u32[]{:S(2)}) collective-permute-start(bf16[32,2048]{1,0:T(8,128)(2,1)S(1)} %get-tuple-element.26), channel_id=1, source_target_pairs={{0,12},{1,13},{2,14},{3,15},{4,0},{5,1},{6,2},{7,3},{8,4},{9,5},{1... | collective-permute-start | bytes 393224 | tf_op jit(solution)/shard_map/ppermute | solution.py:154
  100.0 1.8 %collective-permute-done.7 = bf16[32,2048]{1,0:T(8,128)(2,1)S(1)} collective-permute-done((bf16[32,2048]{1,0:T(8,128)(2,1)S(1)}, bf16[32,2048]{1,0:T(8,128)(2,1)S(1)}, u32[]{:S(2)}, u32[]{:S(2)}) %collective-permute-start.7) | collective-permute-done | bytes 131104 | tf_op jit(solution)/shard_map/ppermute | solution.py:154
  101.8 1.4 %collective-permute-done.8 = bf16[32,2048]{1,0:T(8,128)(2,1)S(1)} collective-permute-done((bf16[32,2048]{1,0:T(8,128)(2,1)S(1)}, bf16[32,2048]{1,0:T(8,128)(2,1)S(1)}, u32[]{:S(2)}, u32[]{:S(2)}) %collective-permute-start.8) | collective-permute-done | bytes 131104 | tf_op jit(solution)/shard_map/ppermute | solution.py:154
  103.3 0.7 fusion.27
  (25 shorter events, 0.5 us)
Async XLA Ops:
  6.5 46.0 %all-gather.2.cloned.1.call-start = ((), (), s32[]{:S(2)}) async-start(), calls=%async_computation.2 | async-start | bytes 2785280 | tf_op jit(solution)/shard_map/all_gather | solution.py:52
  10.5 7.6 %copy-start.1 = (f32[512,1]{0,1:T(1,128)S(1)}, f32[512,1]{0,1:T(1,128)}, u32[]{:S(2)}) copy-start(f32[512,1]{0,1:T(1,128)} %param.8) | copy-start | bytes 6148
  10.6 35.8 %all-to-all-start = ((bf16[16,32,2048]{2,1,0:T(8,128)(2,1)}), bf16[16,32,2048]{2,1,0:T(8,128)(2,1)S(1)}, u32[]{:S(2)}, u32[]{:S(2)}) async-start(bf16[16,32,2048]{2,1,0:T(8,128)(2,1)} %broadcast_in_dim.51), calls=%async_computation | async-start | bytes 4194304 | tf_op jit(solution)/shard_map/all_to_all | solution.py:14
  56.3 14.6 %copy-start = (bf16[512,512]{1,0:T(8,128)(2,1)}, bf16[512,512]{1,0:T(8,128)(2,1)S(1)}, u32[]{:S(2)}) copy-start(bf16[512,512]{1,0:T(8,128)(2,1)S(1)} %get-tuple-element.43) | copy-start | bytes 1572868
  57.7 23.9 %all-to-all-start.1 = ((bf16[16,1,136,128]{3,2,1,0:T(8,128)(2,1)}), bf16[16,1,136,128]{3,2,1,0:T(8,128)(2,1)S(1)}, u32[]{:S(2)}, u32[]{:S(2)}) async-start(bf16[16,1,136,128]{3,2,1,0:T(8,128)(2,1)} %broadcast_in_dim.94), calls=%async_computation.1 | async-start | bytes 1114112 | tf_op jit(solution)/shard_map/all_to_all | solution.py:14
  65.7 10.8 %collective-permute-start.3 = (bf16[8,128,128]{2,1,0:T(8,128)(2,1)S(1)}, bf16[8,128,128]{2,1,0:T(8,128)(2,1)S(1)}, u32[]{:S(2)}, u32[]{:S(2)}) collective-permute-start(bf16[8,128,128]{2,1,0:T(8,128)(2,1)S(1)} %constant_dynamic-slice_fusion), channel_id=1, source_target_pairs={{0,2},{1,3},{2,0},{3,1},{4,6},{5,7},{6,4},{7,5},{8,10},{9,11},{10,... | collective-permute-start | bytes 786440 | tf_op jit(solution)/shard_map/ppermute | solution.py:136
  67.3 13.3 %collective-permute-start.4 = (bf16[8,128,128]{2,1,0:T(8,128)(2,1)S(1)}, bf16[8,128,128]{2,1,0:T(8,128)(2,1)S(1)}, u32[]{:S(2)}, u32[]{:S(2)}) collective-permute-start(bf16[8,128,128]{2,1,0:T(8,128)(2,1)S(1)} %constant_dynamic-slice_fusion), channel_id=1, source_target_pairs={{0,1},{1,2},{2,3},{3,0},{4,5},{5,6},{6,7},{7,4},{8,9},{9,10},{10,1... | collective-permute-start | bytes 786440 | tf_op jit(solution)/shard_map/ppermute | solution.py:136
  69.7 11.8 %collective-permute-start.5 = (bf16[8,128,128]{2,1,0:T(8,128)(2,1)S(1)}, bf16[8,128,128]{2,1,0:T(8,128)(2,1)S(1)}, u32[]{:S(2)}, u32[]{:S(2)}) collective-permute-start(bf16[8,128,128]{2,1,0:T(8,128)(2,1)S(1)} %constant_dynamic-slice_fusion), channel_id=1, source_target_pairs={{0,3},{1,0},{2,1},{3,2},{4,7},{5,4},{6,5},{7,6},{8,11},{9,8},{10,9... | collective-permute-start | bytes 786440 | tf_op jit(solution)/shard_map/ppermute | solution.py:136
  81.5 7.5 %collective-permute-start.6 = (bf16[3,8,128,128]{3,2,0,1:T(8,128)(2,1)S(1)}, bf16[3,8,128,128]{3,2,0,1:T(8,128)(2,1)S(1)}, u32[]{:S(2)}, u32[]{:S(2)}) collective-permute-start(bf16[3,8,128,128]{3,2,0,1:T(8,128)(2,1)S(1)} %pad_maximum_fusion), channel_id=1, source_target_pairs={{0,16},{16,0},{32,48},{48,32},{64,80},{80,64},{96,112},{112,96},{1... | collective-permute-start | bytes 2359304 | tf_op jit(solution)/shard_map/ppermute | solution.py:138
  85.1 5.5 %collective-permute-start = (bf16[4,32,128]{2,1,0:T(8,128)(2,1)S(1)}, bf16[4,32,128]{2,1,0:T(8,128)(2,1)S(1)}, u32[]{:S(2)}, u32[]{:S(2)}) collective-permute-start(bf16[4,32,128]{2,1,0:T(8,128)(2,1)S(1)} %get-tuple-element.42), channel_id=1, source_target_pairs={{0,2},{1,3},{2,0},{3,1},{4,6},{5,7},{6,4},{7,5},{8,10},{9,11},{10,... | collective-permute-start | bytes 98312 | tf_op jit(solution)/shard_map/ppermute | solution.py:135
  87.0 3.9 %collective-permute-start.1 = (bf16[4,32,128]{2,1,0:T(8,128)(2,1)S(1)}, bf16[4,32,128]{2,1,0:T(8,128)(2,1)S(1)}, u32[]{:S(2)}, u32[]{:S(2)}) collective-permute-start(bf16[4,32,128]{2,1,0:T(8,128)(2,1)S(1)} %get-tuple-element.41), channel_id=1, source_target_pairs={{0,1},{1,2},{2,3},{3,0},{4,5},{5,6},{6,7},{7,4},{8,9},{9,10},{10,1... | collective-permute-start | bytes 98312 | tf_op jit(solution)/shard_map/ppermute | solution.py:135
  88.8 5.1 %collective-permute-start.2 = (bf16[4,32,128]{2,1,0:T(8,128)(2,1)S(1)}, bf16[4,32,128]{2,1,0:T(8,128)(2,1)S(1)}, u32[]{:S(2)}, u32[]{:S(2)}) collective-permute-start(bf16[4,32,128]{2,1,0:T(8,128)(2,1)S(1)} %get-tuple-element.40), channel_id=1, source_target_pairs={{0,3},{1,0},{2,1},{3,2},{4,7},{5,4},{6,5},{7,6},{8,11},{9,8},{10,9... | collective-permute-start | bytes 98312 | tf_op jit(solution)/shard_map/ppermute | solution.py:135
  94.5 7.3 %collective-permute-start.7 = (bf16[32,2048]{1,0:T(8,128)(2,1)S(1)}, bf16[32,2048]{1,0:T(8,128)(2,1)S(1)}, u32[]{:S(2)}, u32[]{:S(2)}) collective-permute-start(bf16[32,2048]{1,0:T(8,128)(2,1)S(1)} %get-tuple-element.25), channel_id=1, source_target_pairs={{0,8},{1,9},{2,10},{3,11},{4,12},{5,13},{6,14},{7,15},{8,0},{9,1},... | collective-permute-start | bytes 393224 | tf_op jit(solution)/shard_map/ppermute | solution.py:154
  96.8 6.5 %collective-permute-start.8 = (bf16[32,2048]{1,0:T(8,128)(2,1)S(1)}, bf16[32,2048]{1,0:T(8,128)(2,1)S(1)}, u32[]{:S(2)}, u32[]{:S(2)}) collective-permute-start(bf16[32,2048]{1,0:T(8,128)(2,1)S(1)} %get-tuple-element.36), channel_id=1, source_target_pairs={{0,4},{1,5},{2,6},{3,7},{4,8},{5,9},{6,10},{7,11},{8,12},{9,13},{1... | collective-permute-start | bytes 393224 | tf_op jit(solution)/shard_map/ppermute | solution.py:154
  97.3 5.9 %collective-permute-start.9 = (bf16[32,2048]{1,0:T(8,128)(2,1)S(1)}, bf16[32,2048]{1,0:T(8,128)(2,1)S(1)}, u32[]{:S(2)}, u32[]{:S(2)}) collective-permute-start(bf16[32,2048]{1,0:T(8,128)(2,1)S(1)} %get-tuple-element.26), channel_id=1, source_target_pairs={{0,12},{1,13},{2,14},{3,15},{4,0},{5,1},{6,2},{7,3},{8,4},{9,5},{1... | collective-permute-start | bytes 393224 | tf_op jit(solution)/shard_map/ppermute | solution.py:154
Sparse Core Ops, SparseCore 0:
  9.2 43.2 all-gather.1

commit v17 on v16

--- a/solution.py
+++ b/solution.py
@@ -140,18 +140,26 @@
     second = jnp.where(parity == 0, swapped, fetched)
     remote = jnp.concatenate([first, second], axis=1)
     weights_in = [rows_mine] + [remote[s] for s in range(side - 1)]
-    partial = jnp.einsum(
-        "syfr,skrc->yfkc",
-        jnp.stack(pieces),
-        jnp.stack(weights_in),
-        preferred_element_type=jnp.float32,
-    ).astype(jnp.bfloat16)
-    partial = partial.reshape(side, local_len // heads, -1)
-    total = lax.dynamic_index_in_dim(partial, row, axis=0, keepdims=False).astype(jnp.float32)
+    gathered_pieces = jnp.stack(pieces)
+    gathered_rows = jnp.stack(weights_in)
+
+    def partial_for(destination):
+        rows_for = lax.dynamic_index_in_dim(gathered_pieces, destination, axis=1, keepdims=False)
+        return (
+            jnp.einsum(
+                "sfr,skrc->fkc", rows_for, gathered_rows, preferred_element_type=jnp.float32
+            )
+            .astype(jnp.bfloat16)
+            .reshape(local_len // heads, -1)
+        )
+
+    received = []
     for shift in ring_order:
         down = [(h, ((h // side + shift) % side) * side + h % side) for h in range(heads)]
-        piece = lax.dynamic_index_in_dim(partial, (row + shift) % side, axis=0, keepdims=False)
-        total = total + lax.ppermute(piece, "head", down).astype(jnp.float32)
+        received.append(lax.ppermute(partial_for((row + shift) % side), "head", down))
+    total = partial_for(row).astype(jnp.float32)
+    for piece in received:
+        total = total + piece.astype(jnp.float32)
     return total.astype(jnp.bfloat16)
 
 

time: 111 us -> 115 us (1.036); the launches traced: 111 us -> 113 us
  matrix products: 7.4 us -> 8.81 us
    dot_general x1 -> x4, matrix products: 0.45 us -> 1.86 us  [partial_for(): jnp.einsum('sfr,skrc->fkc', rows_for, gathered_rows, preferred_element_ty...]
    ppermute x3, waiting for transfers between devices: 3.28 us -> 4.67 us  [shards(): lax.ppermute(partial_for((row + shift) % side), 'head', down)]
  transfers between devices with their start and end apart: 13 -> 13, of which waited for: 10 -> 8; matrix products, arithmetic and copies ran while one was open for 11% -> 12% of each run, Pallas kernels for 0% -> 0%
where the time goes in v17:
time: 115 us; the launch traced here: 113 us
  waiting for transfers between devices  48.6 us (42%)
  starting transfers between devices  25 us (22%)
  between operations  17.6 us (15%)
  matrix products  8.81 us (8%)
  local copies, waits for them, and re-layouts  7.45 us (6%)
  other arithmetic  5.64 us (5%)
    all_to_all x2, waiting for transfers between devices, gather_by_exchange(): return lax.all_to_all(copies, axis, 0, 0, tiled=False)  23 us
    all_to_all x2, starting transfers between devices, gather_by_exchange(): return lax.all_to_all(copies, axis, 0, 0, tiled=False)  11.6 us
    ppermute x3, waiting for transfers between devices, shards(): fetched.append(lax.ppermute(own_half, 'head', across))  10.6 us
    all_gather x1, waiting for transfers between devices, shards(): stacked = lax.all_gather(packed, 'tm', axis=0, tiled=True)  6.21 us
    ppermute x3, starting transfers between devices, shards(): lax.ppermute(partial_for((row + shift) % side), 'head', down)  5.24 us
    ppermute x3, waiting for transfers between devices, shards(): lax.ppermute(partial_for((row + shift) % side), 'head', down)  4.67 us
    ppermute x3, starting transfers between devices, shards(): pieces.append(lax.ppermute(piece, 'head', across))  4.47 us
    ppermute x3, waiting for transfers between devices, shards(): pieces.append(lax.ppermute(piece, 'head', across))  4.12 us
  transfers between devices with their start and end apart: 13, of which 8 were waited for; matrix products, arithmetic and copies ran while one was open for 12% of the time, Pallas kernels for 0%

profile of v17, /device:TPU:6, one launch (start us, length us, event | category | flops | bytes accessed | tf_op | source)
XLA Modules:
  0.0 113.1 jit_solution(6115271253880934087)
XLA Ops:
  6.5 1.5 %pad_add_fusion = bf16[128,640]{1,0:T(8,128)(2,1)} fusion(bf16[128,128]{1,0:T(8,128)(2,1)} %param.13, bf16[128,128]{1,0:T(8,128)(2,1)} %param.12, bf16[128,128]{1,0:T(8,128)(2,1)} %param.11, bf16[128,128]{1,0:T(8,128)(2,1)} %param.10, bf16[128,128]{1,0:T(8,128)(2,1)} %param.9), kind=kLoop, calls=%fused_computation.51 | loop fusion | flops 819200 | bytes 327680 | tf_op jit(solution)/shard_map/add | solution.py:48
  8.1 2.5 %broadcast_in_dim.51 = bf16[16,32,2048]{2,1,0:T(8,128)(2,1)} broadcast(bf16[32,2048]{1,0:T(8,128)(2,1)} %param.7), dimensions={1,2} | broadcast | bytes 2228224 | tf_op jit(solution)/shard_map/broadcast_in_dim | solution.py:13
  10.6 7.6 %all-to-all-start = ((bf16[16,32,2048]{2,1,0:T(8,128)(2,1)}), bf16[16,32,2048]{2,1,0:T(8,128)(2,1)S(1)}, u32[]{:S(2)}, u32[]{:S(2)}) async-start(bf16[16,32,2048]{2,1,0:T(8,128)(2,1)} %broadcast_in_dim.51), calls=%async_computation | async-start | bytes 4194304 | tf_op jit(solution)/shard_map/all_to_all | solution.py:14
  18.1 0.6 reduce_sum.47
  18.7 0.3 reduce-window.6
  19.0 0.6 slice.68
  19.6 0.2 slice_reduce_fusion
  19.8 0.2 reduce-window.9
  20.0 0.6 slice.69
  23.4 23.0 %all-to-all-done = bf16[16,32,2048]{2,1,0:T(8,128)(2,1)S(1)} async-done(((bf16[16,32,2048]{2,1,0:T(8,128)(2,1)}), bf16[16,32,2048]{2,1,0:T(8,128)(2,1)S(1)}, u32[]{:S(2)}, u32[]{:S(2)}) %all-to-all-start) | async-done | bytes 2097184 | tf_op jit(solution)/shard_map/all_to_all | solution.py:14
  46.4 6.2 %all-gather.2.cloned.1.call-done = bf16[2048,640]{1,0:T(8,128)(2,1)} async-done(((bf16[128,640]{1,0:T(8,128)(2,1)}), bf16[2048,640]{1,0:T(8,128)(2,1)}) %all-gather.2.cloned.1.call-update) | async-done | bytes 2621456 | tf_op jit(solution)/shard_map/all_gather | solution.py:52
  52.6 3.8 %fusion.64 = (bf16[512,512]{1,0:T(8,128)(2,1)S(1)}, f32[512,512]{1,0:T(8,128)}) fusion(bf16[512,2048]{1,0:T(8,128)(2,1)S(1)} %bitcast.146, bf16[2048,640]{1,0:T(8,128)(2,1)} %all-gather.2.cloned.1.call-done), kind=kOutput, calls=%fused_computation.100 | convolution fusion | flops 1074003968 | bytes 5767168 | tf_op jit(solution)/shard_map/dot_general | solution.py:56
  56.4 0.3 fusion.19
  56.8 0.1 maximum_bitcast_fusion
  56.9 0.9 broadcast_in_dim.94
  57.8 4.0 %all-to-all-start.1 = ((bf16[16,1,136,128]{3,2,1,0:T(8,128)(2,1)}), bf16[16,1,136,128]{3,2,1,0:T(8,128)(2,1)S(1)}, u32[]{:S(2)}, u32[]{:S(2)}) async-start(bf16[16,1,136,128]{3,2,1,0:T(8,128)(2,1)} %broadcast_in_dim.94), calls=%async_computation.1 | async-start | bytes 1114112 | tf_op jit(solution)/shard_map/all_to_all | solution.py:14
  62.0 0.6 slice.66
  62.6 0.6 slice.67
  64.6 1.1 slice.73
  65.8 1.2 %collective-permute-start.5 = (bf16[8,128,128]{2,1,0:T(8,128)(2,1)S(1)}, bf16[8,128,128]{2,1,0:T(8,128)(2,1)S(1)}, u32[]{:S(2)}, u32[]{:S(2)}) collective-permute-start(bf16[8,128,128]{2,1,0:T(8,128)(2,1)S(1)} %constant_dynamic-slice_fusion), channel_id=1, source_target_pairs={{0,3},{1,0},{2,1},{3,2},{4,7},{5,4},{6,5},{7,6},{8,11},{9,8},{10,9... | collective-permute-start | bytes 786440 | tf_op jit(solution)/shard_map/ppermute | solution.py:136
  67.0 2.1 %collective-permute-start.4 = (bf16[8,128,128]{2,1,0:T(8,128)(2,1)S(1)}, bf16[8,128,128]{2,1,0:T(8,128)(2,1)S(1)}, u32[]{:S(2)}, u32[]{:S(2)}) collective-permute-start(bf16[8,128,128]{2,1,0:T(8,128)(2,1)S(1)} %constant_dynamic-slice_fusion), channel_id=1, source_target_pairs={{0,1},{1,2},{2,3},{3,0},{4,5},{5,6},{6,7},{7,4},{8,9},{9,10},{10,1... | collective-permute-start | bytes 786440 | tf_op jit(solution)/shard_map/ppermute | solution.py:136
  69.1 0.2 collective-permute-start.3
  69.3 1.2 %fusion.7 = f32[1,512,1,128]{3,1,2,0:T(8,128)} fusion(f32[512]{0:T(512)S(1)} %get-tuple-element.22, bf16[512,512]{1,0:T(8,128)(2,1)S(1)} %get-tuple-element.40), kind=kOutput, calls=%fused_computation.8 | convolution fusion | flops 135528448 | bytes 659456 | tf_op jit(solution)/shard_map/while/body/eval_jaxpr/hts,shd->thd/dot_general | solution.py:92
  70.6 5.6 %collective-permute-done.5 = bf16[8,128,128]{2,1,0:T(8,128)(2,1)S(1)} collective-permute-done((bf16[8,128,128]{2,1,0:T(8,128)(2,1)S(1)}, bf16[8,128,128]{2,1,0:T(8,128)(2,1)S(1)}, u32[]{:S(2)}, u32[]{:S(2)}) %collective-permute-start.5) | collective-permute-done | bytes 262176 | tf_op jit(solution)/shard_map/ppermute | solution.py:136
  76.1 4.3 %collective-permute-done.4 = bf16[8,128,128]{2,1,0:T(8,128)(2,1)S(1)} collective-permute-done((bf16[8,128,128]{2,1,0:T(8,128)(2,1)S(1)}, bf16[8,128,128]{2,1,0:T(8,128)(2,1)S(1)}, u32[]{:S(2)}, u32[]{:S(2)}) %collective-permute-start.4) | collective-permute-done | bytes 262176 | tf_op jit(solution)/shard_map/ppermute | solution.py:136
  80.4 0.7 collective-permute-done.3
  81.2 0.1 pad_maximum_fusion
  81.3 0.1 collective-permute-start.6
  81.4 0.2 fusion.58
  81.6 0.1 select_reduce_fusion
  81.7 0.2 multiply_reduce_fusion
  81.9 1.5 %fusion.65 = (f32[512]{0:T(512)S(1)}, f32[1,512,1,128]{3,1,2,0:T(8,128)S(1)}) fusion(f32[1,512,1,128]{3,1,2,0:T(8,128)} %fusion.7, f32[512]{0:T(512)S(1)} %exp.53, bf16[512,512]{1,0:T(8,128)(2,1)} %copy-done, f32[128,128]{1,0:T(8,128)S(1)} %multiply_reduce_fusion, f32[]{:T(128)} %bitcast.11), kind=kOutput, calls=%fused_computation.101 | convolution fusion | flops 100941312 | bytes 725504 | tf_op jit(solution)/shard_map/cthd,chde->cthe/dot_general | solution.py:109
  83.4 0.2 fusion.30
  83.7 1.2 %fusion.33 = bf16[512,128]{1,0:T(8,128)(2,1)S(1)} fusion(f32[1,512,1,128]{3,1,2,0:T(8,128)S(1)} %get-tuple-element.43, f32[512,512]{1,0:T(8,128)} %get-tuple-element.41, f32[512]{0:T(512)S(1)} %add_sqrt_fusion, f32[512]{0:T(512)S(1)} %broadcast_multiply_fusion), kind=kLoop, calls=%fused_computation.47 | loop fusion | flops 524288 | bytes 659456 | tf_op jit(solution)/shard_map/convert_element_type | solution.py:116
  84.9 1.2 %collective-permute-start.2 = (bf16[4,32,128]{2,1,0:T(8,128)(2,1)S(1)}, bf16[4,32,128]{2,1,0:T(8,128)(2,1)S(1)}, u32[]{:S(2)}, u32[]{:S(2)}) collective-permute-start(bf16[4,32,128]{2,1,0:T(8,128)(2,1)S(1)} %get-tuple-element.26), channel_id=1, source_target_pairs={{0,3},{1,0},{2,1},{3,2},{4,7},{5,4},{6,5},{7,6},{8,11},{9,8},{10,9... | collective-permute-start | bytes 98312 | tf_op jit(solution)/shard_map/ppermute | solution.py:135
  86.1 2.1 %collective-permute-start.1 = (bf16[4,32,128]{2,1,0:T(8,128)(2,1)S(1)}, bf16[4,32,128]{2,1,0:T(8,128)(2,1)S(1)}, u32[]{:S(2)}, u32[]{:S(2)}) collective-permute-start(bf16[4,32,128]{2,1,0:T(8,128)(2,1)S(1)} %get-tuple-element.36), channel_id=1, source_target_pairs={{0,1},{1,2},{2,3},{3,0},{4,5},{5,6},{6,7},{7,4},{8,9},{9,10},{10,1... | collective-permute-start | bytes 98312 | tf_op jit(solution)/shard_map/ppermute | solution.py:135
  88.2 1.2 %collective-permute-start = (bf16[4,32,128]{2,1,0:T(8,128)(2,1)S(1)}, bf16[4,32,128]{2,1,0:T(8,128)(2,1)S(1)}, u32[]{:S(2)}, u32[]{:S(2)}) collective-permute-start(bf16[4,32,128]{2,1,0:T(8,128)(2,1)S(1)} %get-tuple-element.38), channel_id=1, source_target_pairs={{0,2},{1,3},{2,0},{3,1},{4,6},{5,7},{6,4},{7,5},{8,10},{9,11},{10,... | collective-permute-start | bytes 98312 | tf_op jit(solution)/shard_map/ppermute | solution.py:135
  89.3 0.1 broadcast_select_fusion.1
  89.5 0.6 collective-permute-done.2
  90.1 3.5 %collective-permute-done = bf16[4,32,128]{2,1,0:T(8,128)(2,1)S(1)} collective-permute-done((bf16[4,32,128]{2,1,0:T(8,128)(2,1)S(1)}, bf16[4,32,128]{2,1,0:T(8,128)(2,1)S(1)}, u32[]{:S(2)}, u32[]{:S(2)}) %collective-permute-start) | collective-permute-done | bytes 32800 | tf_op jit(solution)/shard_map/ppermute | solution.py:135
  93.6 0.5 fusion.15
  94.1 2.8 %collective-permute-start.9 = (bf16[32,2048]{1,0:T(8,128)(2,1)S(1)}, bf16[32,2048]{1,0:T(8,128)(2,1)S(1)}, u32[]{:S(2)}, u32[]{:S(2)}) collective-permute-start(bf16[32,2048]{1,0:T(8,128)(2,1)S(1)} %bitcast.159), channel_id=1, source_target_pairs={{0,12},{1,13},{2,14},{3,15},{4,0},{5,1},{6,2},{7,3},{8,4},{9,5},{1... | collective-permute-start | bytes 393224 | tf_op jit(solution)/shard_map/ppermute | solution.py:159
  96.9 0.5 fusion.16
  97.5 0.5 fusion.17
  98.0 2.4 %collective-permute-start.7 = (bf16[32,2048]{1,0:T(8,128)(2,1)S(1)}, bf16[32,2048]{1,0:T(8,128)(2,1)S(1)}, u32[]{:S(2)}, u32[]{:S(2)}) collective-permute-start(bf16[32,2048]{1,0:T(8,128)(2,1)S(1)} %bitcast.161), channel_id=1, source_target_pairs={{0,8},{1,9},{2,10},{3,11},{4,12},{5,13},{6,14},{7,15},{8,0},{9,1},... | collective-permute-start | bytes 393224 | tf_op jit(solution)/shard_map/ppermute | solution.py:159
  100.4 0.5 fusion.11
  100.9 4.7 %collective-permute-done.8 = bf16[32,2048]{1,0:T(8,128)(2,1)S(1)} collective-permute-done((bf16[32,2048]{1,0:T(8,128)(2,1)S(1)}, bf16[32,2048]{1,0:T(8,128)(2,1)S(1)}, u32[]{:S(2)}, u32[]{:S(2)}) %collective-permute-start.8) | collective-permute-done | bytes 131104 | tf_op jit(solution)/shard_map/ppermute | solution.py:159
  105.5 0.7 fusion.28
  (30 shorter events, 0.6 us)
Async XLA Ops:
  6.5 46.1 %all-gather.2.cloned.1.call-start = ((), (), s32[]{:S(2)}) async-start(), calls=%async_computation.2 | async-start | bytes 2785280 | tf_op jit(solution)/shard_map/all_gather | solution.py:52
  10.5 7.6 %copy-start.1 = (f32[512,1]{0,1:T(1,128)S(1)}, f32[512,1]{0,1:T(1,128)}, u32[]{:S(2)}) copy-start(f32[512,1]{0,1:T(1,128)} %param.8) | copy-start | bytes 6148
  10.6 35.8 %all-to-all-start = ((bf16[16,32,2048]{2,1,0:T(8,128)(2,1)}), bf16[16,32,2048]{2,1,0:T(8,128)(2,1)S(1)}, u32[]{:S(2)}, u32[]{:S(2)}) async-start(bf16[16,32,2048]{2,1,0:T(8,128)(2,1)} %broadcast_in_dim.51), calls=%async_computation | async-start | bytes 4194304 | tf_op jit(solution)/shard_map/all_to_all | solution.py:14
  56.4 14.1 %copy-start = (bf16[512,512]{1,0:T(8,128)(2,1)}, bf16[512,512]{1,0:T(8,128)(2,1)S(1)}, u32[]{:S(2)}) copy-start(bf16[512,512]{1,0:T(8,128)(2,1)S(1)} %get-tuple-element.40) | copy-start | bytes 1572868
  57.8 23.6 %all-to-all-start.1 = ((bf16[16,1,136,128]{3,2,1,0:T(8,128)(2,1)}), bf16[16,1,136,128]{3,2,1,0:T(8,128)(2,1)S(1)}, u32[]{:S(2)}, u32[]{:S(2)}) async-start(bf16[16,1,136,128]{3,2,1,0:T(8,128)(2,1)} %broadcast_in_dim.94), calls=%async_computation.1 | async-start | bytes 1114112 | tf_op jit(solution)/shard_map/all_to_all | solution.py:14
  65.8 10.4 %collective-permute-start.5 = (bf16[8,128,128]{2,1,0:T(8,128)(2,1)S(1)}, bf16[8,128,128]{2,1,0:T(8,128)(2,1)S(1)}, u32[]{:S(2)}, u32[]{:S(2)}) collective-permute-start(bf16[8,128,128]{2,1,0:T(8,128)(2,1)S(1)} %constant_dynamic-slice_fusion), channel_id=1, source_target_pairs={{0,3},{1,0},{2,1},{3,2},{4,7},{5,4},{6,5},{7,6},{8,11},{9,8},{10,9... | collective-permute-start | bytes 786440 | tf_op jit(solution)/shard_map/ppermute | solution.py:136
  67.0 13.5 %collective-permute-start.4 = (bf16[8,128,128]{2,1,0:T(8,128)(2,1)S(1)}, bf16[8,128,128]{2,1,0:T(8,128)(2,1)S(1)}, u32[]{:S(2)}, u32[]{:S(2)}) collective-permute-start(bf16[8,128,128]{2,1,0:T(8,128)(2,1)S(1)} %constant_dynamic-slice_fusion), channel_id=1, source_target_pairs={{0,1},{1,2},{2,3},{3,0},{4,5},{5,6},{6,7},{7,4},{8,9},{9,10},{10,1... | collective-permute-start | bytes 786440 | tf_op jit(solution)/shard_map/ppermute | solution.py:136
  69.1 12.1 %collective-permute-start.3 = (bf16[8,128,128]{2,1,0:T(8,128)(2,1)S(1)}, bf16[8,128,128]{2,1,0:T(8,128)(2,1)S(1)}, u32[]{:S(2)}, u32[]{:S(2)}) collective-permute-start(bf16[8,128,128]{2,1,0:T(8,128)(2,1)S(1)} %constant_dynamic-slice_fusion), channel_id=1, source_target_pairs={{0,2},{1,3},{2,0},{3,1},{4,6},{5,7},{6,4},{7,5},{8,10},{9,11},{10,... | collective-permute-start | bytes 786440 | tf_op jit(solution)/shard_map/ppermute | solution.py:136
  81.3 8.1 %collective-permute-start.6 = (bf16[3,8,128,128]{3,2,0,1:T(8,128)(2,1)S(1)}, bf16[3,8,128,128]{3,2,0,1:T(8,128)(2,1)S(1)}, u32[]{:S(2)}, u32[]{:S(2)}) collective-permute-start(bf16[3,8,128,128]{3,2,0,1:T(8,128)(2,1)S(1)} %pad_maximum_fusion), channel_id=1, source_target_pairs={{0,16},{16,0},{32,48},{48,32},{64,80},{80,64},{96,112},{112,96},{1... | collective-permute-start | bytes 2359304 | tf_op jit(solution)/shard_map/ppermute | solution.py:138
  84.9 5.2 %collective-permute-start.2 = (bf16[4,32,128]{2,1,0:T(8,128)(2,1)S(1)}, bf16[4,32,128]{2,1,0:T(8,128)(2,1)S(1)}, u32[]{:S(2)}, u32[]{:S(2)}) collective-permute-start(bf16[4,32,128]{2,1,0:T(8,128)(2,1)S(1)} %get-tuple-element.26), channel_id=1, source_target_pairs={{0,3},{1,0},{2,1},{3,2},{4,7},{5,4},{6,5},{7,6},{8,11},{9,8},{10,9... | collective-permute-start | bytes 98312 | tf_op jit(solution)/shard_map/ppermute | solution.py:135
  86.1 4.0 %collective-permute-start.1 = (bf16[4,32,128]{2,1,0:T(8,128)(2,1)S(1)}, bf16[4,32,128]{2,1,0:T(8,128)(2,1)S(1)}, u32[]{:S(2)}, u32[]{:S(2)}) collective-permute-start(bf16[4,32,128]{2,1,0:T(8,128)(2,1)S(1)} %get-tuple-element.36), channel_id=1, source_target_pairs={{0,1},{1,2},{2,3},{3,0},{4,5},{5,6},{6,7},{7,4},{8,9},{9,10},{10,1... | collective-permute-start | bytes 98312 | tf_op jit(solution)/shard_map/ppermute | solution.py:135
  88.2 5.4 %collective-permute-start = (bf16[4,32,128]{2,1,0:T(8,128)(2,1)S(1)}, bf16[4,32,128]{2,1,0:T(8,128)(2,1)S(1)}, u32[]{:S(2)}, u32[]{:S(2)}) collective-permute-start(bf16[4,32,128]{2,1,0:T(8,128)(2,1)S(1)} %get-tuple-element.38), channel_id=1, source_target_pairs={{0,2},{1,3},{2,0},{3,1},{4,6},{5,7},{6,4},{7,5},{8,10},{9,11},{10,... | collective-permute-start | bytes 98312 | tf_op jit(solution)/shard_map/ppermute | solution.py:135
  94.1 6.7 %collective-permute-start.9 = (bf16[32,2048]{1,0:T(8,128)(2,1)S(1)}, bf16[32,2048]{1,0:T(8,128)(2,1)S(1)}, u32[]{:S(2)}, u32[]{:S(2)}) collective-permute-start(bf16[32,2048]{1,0:T(8,128)(2,1)S(1)} %bitcast.159), channel_id=1, source_target_pairs={{0,12},{1,13},{2,14},{3,15},{4,0},{5,1},{6,2},{7,3},{8,4},{9,5},{1... | collective-permute-start | bytes 393224 | tf_op jit(solution)/shard_map/ppermute | solution.py:159
  97.4 8.1 %collective-permute-start.8 = (bf16[32,2048]{1,0:T(8,128)(2,1)S(1)}, bf16[32,2048]{1,0:T(8,128)(2,1)S(1)}, u32[]{:S(2)}, u32[]{:S(2)}) collective-permute-start(bf16[32,2048]{1,0:T(8,128)(2,1)S(1)} %bitcast.160), channel_id=1, source_target_pairs={{0,4},{1,5},{2,6},{3,7},{4,8},{5,9},{6,10},{7,11},{8,12},{9,13},{1... | collective-permute-start | bytes 393224 | tf_op jit(solution)/shard_map/ppermute | solution.py:159
  98.0 7.5 %collective-permute-start.7 = (bf16[32,2048]{1,0:T(8,128)(2,1)S(1)}, bf16[32,2048]{1,0:T(8,128)(2,1)S(1)}, u32[]{:S(2)}, u32[]{:S(2)}) collective-permute-start(bf16[32,2048]{1,0:T(8,128)(2,1)S(1)} %bitcast.161), channel_id=1, source_target_pairs={{0,8},{1,9},{2,10},{3,11},{4,12},{5,13},{6,14},{7,15},{8,0},{9,1},... | collective-permute-start | bytes 393224 | tf_op jit(solution)/shard_map/ppermute | solution.py:159
Sparse Core Ops, SparseCore 0:
  9.2 43.3 all-gather.1

commit v18 on v16

--- a/solution.py
+++ b/solution.py
@@ -14,36 +14,29 @@
     return lax.all_to_all(copies, axis, 0, 0, tiled=False)
 
 
-def prior_state(local_final, log_total, axis):
-    heads_here = local_final.shape[0]
-    high = log_total.astype(jnp.bfloat16)
-    low = (log_total - high.astype(jnp.float32)).astype(jnp.bfloat16)
-    extra = jnp.concatenate(
-        [
-            jnp.broadcast_to(high[:, None, None], (heads_here, 1, HEAD_DIM)),
-            jnp.broadcast_to(low[:, None, None], (heads_here, 1, HEAD_DIM)),
-            jnp.zeros((heads_here, PAD_ROWS - 2, HEAD_DIM), jnp.bfloat16),
-        ],
-        axis=1,
-    )
-    packed = jnp.concatenate([local_final.astype(jnp.bfloat16), extra], axis=1)
-    gathered = gather_by_exchange(packed, axis)
-    finals = gathered[:, :, :HEAD_DIM, :].astype(jnp.float32)
-    totals = gathered[:, :, HEAD_DIM, 0].astype(jnp.float32) + gathered[:, :, HEAD_DIM + 1, 0].astype(
-        jnp.float32
-    )
-    count = gathered.shape[0]
+def prior_state(local_final, totals, axis):
+    count = totals.shape[0]
     mine = lax.axis_index(axis)
     order = jnp.arange(count, dtype=jnp.int32)
     between = (order[:, None] < order[None, :]) & (order[None, :] < mine)
     exponent = jnp.sum(jnp.where(between[:, :, None], totals[None, :, :], 0.0), axis=1)
     weight = jnp.where((order < mine)[:, None], jnp.exp(exponent), 0.0)
+    finals = gather_by_exchange(local_final.astype(jnp.bfloat16), axis).astype(jnp.float32)
     return jnp.sum(weight[:, :, None, None] * finals, axis=0)
 
 
 def shards(frames, log_decay, w_query, w_key, w_value, w_gate, w_out):
     head_width = w_query.shape[1]
-    blocks = [w_query, w_key, w_value, w_gate, w_out]
+    log_total = jnp.sum(log_decay, axis=0)
+    high = log_total.astype(jnp.bfloat16)
+    low = (log_total - high.astype(jnp.float32)).astype(jnp.bfloat16)
+    row_index = jnp.arange(w_query.shape[0])[:, None]
+    totals_block = jnp.where(
+        row_index == 0,
+        jnp.repeat(high, HEAD_DIM)[None, :],
+        jnp.where(row_index == 1, jnp.repeat(low, HEAD_DIM)[None, :], jnp.zeros((), jnp.bfloat16)),
+    )
+    blocks = [w_query, w_key, w_value, w_gate, w_out, totals_block]
     width = sum(block.shape[1] for block in blocks)
     packed = sum(
         jnp.pad(block, ((0, 0), (start, width - start - block.shape[1])))
@@ -51,7 +44,9 @@
     )
     stacked = lax.all_gather(packed, "tm", axis=0, tiled=True)
     joined = stacked[:, : 4 * head_width]
-    out_blocks = stacked[:, 4 * head_width :].reshape(-1, head_width, w_out.shape[1])
+    out_blocks = stacked[:, 4 * head_width : 5 * head_width].reshape(-1, head_width, w_out.shape[1])
+    totals_rows = stacked[:, 5 * head_width :].reshape(-1, w_query.shape[0], head_width // HEAD_DIM, HEAD_DIM)
+    totals = totals_rows[:, 0, :, 0].astype(jnp.float32) + totals_rows[:, 1, :, 0].astype(jnp.float32)
     frames_here = gather_by_exchange(frames, "head").reshape(-1, frames.shape[1])
     projected = jnp.dot(
         frames_here,
@@ -101,7 +96,7 @@
     local_final, (intra_all, local_starts) = lax.scan(
         local_step, zero_state, (query_blocks, key_blocks, value_blocks, running_blocks)
     )
-    prior = prior_state(local_final, jnp.sum(log_decay, axis=0), "tm")
+    prior = prior_state(local_final, totals, "tm")
     block_logs = running_blocks[:, -1, :]
     before = jnp.cumsum(block_logs, axis=0) - block_logs
     start_states = jnp.exp(before)[:, :, None, None] * prior[None] + local_starts

time: 111 us -> 119 us (1.072)
  local copies, waits for them, and re-layouts: 7.53 us -> 10.8 us
  starting transfers between devices: 25.1 us -> 26.4 us
    all_gather x1, waiting for transfers between devices: 6.1 us -> 28.5 us  [shards(): stacked = lax.all_gather(packed, 'tm', axis=0, tiled=True)]
    all_to_all x2, waiting for transfers between devices: 23 us -> 12 us  [gather_by_exchange(): return lax.all_to_all(copies, axis, 0, 0, tiled=False)]
    ppermute x3, waiting for transfers between devices: 10.5 us -> 0.01 us  [shards(): fetched.append(lax.ppermute(own_half, 'head', across))]
    slice x1 -> x2, local copies, waits for them, and re-layouts: 1.08 us -> 2.95 us  [the longest x1 2.1 us: shards(): stacked[:, 5 * head_width:]]
  transfers between devices with their start and end apart: 13 -> 13, of which waited for: 10 -> 7; matrix products, arithmetic and copies ran while one was open for 11% -> 17% of each run, Pallas kernels for 0% -> 0%
where the time goes in v18:
time: 119 us; the launch traced here: 118 us
  waiting for transfers between devices  48.6 us (41%)
  starting transfers between devices  26.4 us (22%)
  between operations  17.4 us (15%)
  local copies, waits for them, and re-layouts  10.8 us (9%)
  matrix products  8.44 us (7%)
  other arithmetic  6.13 us (5%)
    all_gather x1, waiting for transfers between devices, shards(): stacked = lax.all_gather(packed, 'tm', axis=0, tiled=True)  28.5 us
    all_to_all x2, waiting for transfers between devices, gather_by_exchange(): return lax.all_to_all(copies, axis, 0, 0, tiled=False)  12 us
    all_to_all x2, starting transfers between devices, gather_by_exchange(): return lax.all_to_all(copies, axis, 0, 0, tiled=False)  11.9 us
    ppermute x3, starting transfers between devices, shards(): total = total + lax.ppermute(piece, 'head', down).astype(jnp.float32)  6.31 us
    ppermute x3, waiting for transfers between devices, shards(): pieces.append(lax.ppermute(piece, 'head', across))  4.22 us
    ppermute x3, starting transfers between devices, shards(): pieces.append(lax.ppermute(piece, 'head', across))  4.15 us
    ppermute x3, waiting for transfers between devices, shards(): total = total + lax.ppermute(piece, 'head', down).astype(jnp.float32)  3.91 us
    dot_general x1, matrix products, shards(): projected = jnp.dot(frames_here, joined, preferred_element_type=jnp.float32)  3.83 us
  transfers between devices with their start and end apart: 13, of which 7 were waited for; matrix products, arithmetic and copies ran while one was open for 17% of the time, Pallas kernels for 0%

profile of v18, /device:TPU:6, one launch (start us, length us, event | category | flops | bytes accessed | tf_op | source)
XLA Modules:
  0.0 117.8 jit_solution(7774902896521963349)
XLA Ops:
  6.5 1.3 %reduce_sum.47 = f32[]{:T(128)} reduce(f32[512,1]{0,1:T(1,128)} %param.8, f32[]{:T(128)} %constant.123.clone.1), dimensions={0,1}, to_apply=%region_0.0 | reduce | flops 511 | bytes 2056 | tf_op jit(solution)/shard_map/reduce_sum | solution.py:30
  9.2 0.1 broadcast_select_fusion.2
  9.3 1.5 %pad_add_fusion = bf16[128,768]{1,0:T(8,128)(2,1)} fusion(bf16[128,128]{1,0:T(8,128)(2,1)S(1)} %broadcast_select_fusion.2, bf16[128,128]{1,0:T(8,128)(2,1)} %param.13, bf16[128,128]{1,0:T(8,128)(2,1)} %param.12, bf16[128,128]{1,0:T(8,128)(2,1)} %param.11, bf16[128,128]{1,0:T(8,128)(2,1)} %param.10, bf16[128,128]{1,0:T(8,128)(2,1)} %param.9), kind=kLoop, calls=%fused_computation.46 | loop fusion | flops 1179648 | bytes 393216 | tf_op jit(solution)/shard_map/add | solution.py:41
  10.8 2.5 %broadcast_in_dim.108 = bf16[16,32,2048]{2,1,0:T(8,128)(2,1)} broadcast(bf16[32,2048]{1,0:T(8,128)(2,1)} %param.7), dimensions={1,2} | broadcast | bytes 2228224 | tf_op jit(solution)/shard_map/broadcast_in_dim | solution.py:13
  13.3 7.6 %all-to-all-start = ((bf16[16,32,2048]{2,1,0:T(8,128)(2,1)}), bf16[16,32,2048]{2,1,0:T(8,128)(2,1)S(1)}, u32[]{:S(2)}, u32[]{:S(2)}) async-start(bf16[16,32,2048]{2,1,0:T(8,128)(2,1)} %broadcast_in_dim.108), calls=%async_computation | async-start | bytes 4194304 | tf_op jit(solution)/shard_map/all_to_all | solution.py:14
  20.9 0.3 reduce-window.6
  21.2 0.2 slice_reduce_fusion
  21.4 0.2 reduce-window.9
  21.6 0.6 slice.72
  22.2 0.6 slice.71
  24.1 0.6 slice.67
  24.6 0.6 slice.66
  26.5 28.5 %all-gather.2.cloned.1.call-done = bf16[2048,768]{1,0:T(8,128)(2,1)} async-done(((bf16[128,768]{1,0:T(8,128)(2,1)}), bf16[2048,768]{1,0:T(8,128)(2,1)}) %all-gather.2.cloned.1.call-update) | async-done | bytes 3145744 | tf_op jit(solution)/shard_map/all_gather | solution.py:45
  55.0 2.1 %fusion.55 = (bf16[2048,128]{1,0:T(8,128)(2,1)}, bf16[2048,128]{1,0:T(8,128)(2,1)S(1)}) fusion(bf16[2048,768]{1,0:T(8,128)(2,1)} %all-gather.2.cloned.1.call-done), kind=kLoop, calls=%fused_computation.89 | loop fusion | bytes 2097152 | tf_op jit(solution)/shard_map/slice | solution.py:48
  57.1 0.7 constant_dynamic-slice_fusion
  57.8 1.5 %collective-permute-start.3 = (bf16[8,128,128]{2,1,0:T(8,128)(2,1)}, bf16[8,128,128]{2,1,0:T(8,128)(2,1)S(1)}, u32[]{:S(2)}, u32[]{:S(2)}) collective-permute-start(bf16[8,128,128]{2,1,0:T(8,128)(2,1)} %constant_dynamic-slice_fusion), channel_id=1, source_target_pairs={{0,2},{1,3},{2,0},{3,1},{4,6},{5,7},{6,4},{7,5},{8,10},{9,11},{10,... | collective-permute-start | bytes 786440 | tf_op jit(solution)/shard_map/ppermute | solution.py:131
  59.3 2.1 %collective-permute-start.4 = (bf16[8,128,128]{2,1,0:T(8,128)(2,1)}, bf16[8,128,128]{2,1,0:T(8,128)(2,1)S(1)}, u32[]{:S(2)}, u32[]{:S(2)}) collective-permute-start(bf16[8,128,128]{2,1,0:T(8,128)(2,1)} %constant_dynamic-slice_fusion), channel_id=1, source_target_pairs={{0,1},{1,2},{2,3},{3,0},{4,5},{5,6},{6,7},{7,4},{8,9},{9,10},{10,1... | collective-permute-start | bytes 786440 | tf_op jit(solution)/shard_map/ppermute | solution.py:131
  61.3 3.8 %fusion.57 = (bf16[512,512]{1,0:T(8,128)(2,1)S(1)}, f32[512,512]{1,0:T(8,128)}) fusion(bf16[512,2048]{1,0:T(8,128)(2,1)S(1)} %bitcast.109, bf16[2048,768]{1,0:T(8,128)(2,1)} %all-gather.2.cloned.1.call-done), kind=kOutput, calls=%fused_computation.91 | convolution fusion | flops 1074003968 | bytes 5767168 | tf_op jit(solution)/shard_map/dot_general | solution.py:51
  65.2 0.8 copy-done
  66.0 0.3 fusion.17
  66.3 0.9 broadcast_in_dim.114
  67.2 4.4 %all-to-all-start.1 = ((bf16[16,1,128,128]{3,2,1,0:T(8,128)(2,1)}), bf16[16,1,128,128]{3,2,1,0:T(8,128)(2,1)S(1)}, u32[]{:S(2)}, u32[]{:S(2)}) async-start(bf16[16,1,128,128]{3,2,1,0:T(8,128)(2,1)} %broadcast_in_dim.114), calls=%async_computation.1 | async-start | bytes 1048576 | tf_op jit(solution)/shard_map/all_to_all | solution.py:14
  71.6 0.9 fusion.56
  72.5 0.1 copy.32
  72.6 0.1 copy.33
  72.7 2.3 %fusion.15 = f32[1,512,1,128]{3,1,2,0:T(8,128)} fusion(f32[512]{0:T(512)S(1)} %get-tuple-element.22, bf16[512,512]{1,0:T(8,128)(2,1)} %copy-done), kind=kOutput, calls=%fused_computation.16 | convolution fusion | flops 135528448 | bytes 659456 | tf_op jit(solution)/shard_map/while/body/eval_jaxpr/hts,shd->thd/dot_general | solution.py:87
  75.0 0.1 select_reduce_fusion
  75.2 0.5 collective-permute-start.6
  75.7 12.0 %all-to-all-done.1 = bf16[16,1,128,128]{3,2,1,0:T(8,128)(2,1)S(1)} async-done(((bf16[16,1,128,128]{3,2,1,0:T(8,128)(2,1)}), bf16[16,1,128,128]{3,2,1,0:T(8,128)(2,1)S(1)}, u32[]{:S(2)}, u32[]{:S(2)}) %all-to-all-start.1) | async-done | bytes 524320 | tf_op jit(solution)/shard_map/all_to_all | solution.py:14
  87.7 0.2 multiply_reduce_fusion
  87.8 1.5 %fusion.58 = (f32[512]{0:T(512)S(1)}, f32[1,512,1,128]{3,1,2,0:T(8,128)S(1)}) fusion(f32[1,512,1,128]{3,1,2,0:T(8,128)} %fusion.15, f32[512]{0:T(512)S(1)} %exp.53, bf16[512,512]{1,0:T(8,128)(2,1)} %copy-done, f32[128,128]{1,0:T(8,128)S(1)} %multiply_reduce_fusion, f32[]{:T(128)} %bitcast.14), kind=kOutput, calls=%fused_computation.92 | convolution fusion | flops 100941312 | bytes 725504 | tf_op jit(solution)/shard_map/cthd,chde->cthe/dot_general | solution.py:104
  89.4 0.2 fusion.28
  89.6 1.2 fusion.31
  90.8 2.1 %collective-permute-start = (bf16[4,32,128]{2,1,0:T(8,128)(2,1)S(1)}, bf16[4,32,128]{2,1,0:T(8,128)(2,1)S(1)}, u32[]{:S(2)}, u32[]{:S(2)}) collective-permute-start(bf16[4,32,128]{2,1,0:T(8,128)(2,1)S(1)} %get-tuple-element.46), channel_id=1, source_target_pairs={{0,2},{1,3},{2,0},{3,1},{4,6},{5,7},{6,4},{7,5},{8,10},{9,11},{10,... | collective-permute-start | bytes 98312 | tf_op jit(solution)/shard_map/ppermute | solution.py:130
  92.9 1.3 %collective-permute-start.1 = (bf16[4,32,128]{2,1,0:T(8,128)(2,1)S(1)}, bf16[4,32,128]{2,1,0:T(8,128)(2,1)S(1)}, u32[]{:S(2)}, u32[]{:S(2)}) collective-permute-start(bf16[4,32,128]{2,1,0:T(8,128)(2,1)S(1)} %get-tuple-element.45), channel_id=1, source_target_pairs={{0,1},{1,2},{2,3},{3,0},{4,5},{5,6},{6,7},{7,4},{8,9},{9,10},{10,1... | collective-permute-start | bytes 98312 | tf_op jit(solution)/shard_map/ppermute | solution.py:130
  94.2 0.8 collective-permute-start.2
  95.0 0.1 broadcast_select_fusion.1
  95.1 1.2 %collective-permute-done = bf16[4,32,128]{2,1,0:T(8,128)(2,1)S(1)} collective-permute-done((bf16[4,32,128]{2,1,0:T(8,128)(2,1)S(1)}, bf16[4,32,128]{2,1,0:T(8,128)(2,1)S(1)}, u32[]{:S(2)}, u32[]{:S(2)}) %collective-permute-start) | collective-permute-done | bytes 32800 | tf_op jit(solution)/shard_map/ppermute | solution.py:130
  96.3 0.9 collective-permute-done.1
  97.2 2.1 %collective-permute-done.2 = bf16[4,32,128]{2,1,0:T(8,128)(2,1)S(1)} collective-permute-done((bf16[4,32,128]{2,1,0:T(8,128)(2,1)S(1)}, bf16[4,32,128]{2,1,0:T(8,128)(2,1)S(1)}, u32[]{:S(2)}, u32[]{:S(2)}) %collective-permute-start.2) | collective-permute-done | bytes 32800 | tf_op jit(solution)/shard_map/ppermute | solution.py:130
  99.3 0.5 fusion.13
  99.8 0.1 copy.36
  100.0 3.1 %collective-permute-start.7 = (bf16[32,2048]{1,0:T(8,128)(2,1)S(1)}, bf16[32,2048]{1,0:T(8,128)(2,1)S(1)}, u32[]{:S(2)}, u32[]{:S(2)}) collective-permute-start(bf16[32,2048]{1,0:T(8,128)(2,1)S(1)} %get-tuple-element.36), channel_id=1, source_target_pairs={{0,8},{1,9},{2,10},{3,11},{4,12},{5,13},{6,14},{7,15},{8,0},{9,1},... | collective-permute-start | bytes 393224 | tf_op jit(solution)/shard_map/ppermute | solution.py:149
  103.1 0.7 collective-permute-start.8
  103.7 2.5 %collective-permute-start.9 = (bf16[32,2048]{1,0:T(8,128)(2,1)S(1)}, bf16[32,2048]{1,0:T(8,128)(2,1)S(1)}, u32[]{:S(2)}, u32[]{:S(2)}) collective-permute-start(bf16[32,2048]{1,0:T(8,128)(2,1)S(1)} %get-tuple-element.38), channel_id=1, source_target_pairs={{0,12},{1,13},{2,14},{3,15},{4,0},{5,1},{6,2},{7,3},{8,4},{9,5},{1... | collective-permute-start | bytes 393224 | tf_op jit(solution)/shard_map/ppermute | solution.py:149
  106.3 1.6 %collective-permute-done.7 = bf16[32,2048]{1,0:T(8,128)(2,1)S(1)} collective-permute-done((bf16[32,2048]{1,0:T(8,128)(2,1)S(1)}, bf16[32,2048]{1,0:T(8,128)(2,1)S(1)}, u32[]{:S(2)}, u32[]{:S(2)}) %collective-permute-start.7) | collective-permute-done | bytes 131104 | tf_op jit(solution)/shard_map/ppermute | solution.py:149
  107.9 2.3 %collective-permute-done.8 = bf16[32,2048]{1,0:T(8,128)(2,1)S(1)} collective-permute-done((bf16[32,2048]{1,0:T(8,128)(2,1)S(1)}, bf16[32,2048]{1,0:T(8,128)(2,1)S(1)}, u32[]{:S(2)}, u32[]{:S(2)}) %collective-permute-start.8) | collective-permute-done | bytes 131104 | tf_op jit(solution)/shard_map/ppermute | solution.py:149
  110.2 0.7 fusion.26
  (26 shorter events, 0.4 us)
Async XLA Ops:
  6.5 48.4 %all-gather.2.cloned.1.call-start = ((), (), s32[]{:S(2)}) async-start(), calls=%async_computation.2 | async-start | bytes 3342336 | tf_op jit(solution)/shard_map/all_gather | solution.py:45
  13.3 7.6 %copy-start.1 = (f32[512,1]{0,1:T(1,128)S(1)}, f32[512,1]{0,1:T(1,128)}, u32[]{:S(2)}) copy-start(f32[512,1]{0,1:T(1,128)} %param.8) | copy-start | bytes 6148
  13.3 48.0 %all-to-all-start = ((bf16[16,32,2048]{2,1,0:T(8,128)(2,1)}), bf16[16,32,2048]{2,1,0:T(8,128)(2,1)S(1)}, u32[]{:S(2)}, u32[]{:S(2)}) async-start(bf16[16,32,2048]{2,1,0:T(8,128)(2,1)} %broadcast_in_dim.108), calls=%async_computation | async-start | bytes 4194304 | tf_op jit(solution)/shard_map/all_to_all | solution.py:14
  57.8 17.3 %collective-permute-start.3 = (bf16[8,128,128]{2,1,0:T(8,128)(2,1)}, bf16[8,128,128]{2,1,0:T(8,128)(2,1)S(1)}, u32[]{:S(2)}, u32[]{:S(2)}) collective-permute-start(bf16[8,128,128]{2,1,0:T(8,128)(2,1)} %constant_dynamic-slice_fusion), channel_id=1, source_target_pairs={{0,2},{1,3},{2,0},{3,1},{4,6},{5,7},{6,4},{7,5},{8,10},{9,11},{10,... | collective-permute-start | bytes 786440 | tf_op jit(solution)/shard_map/ppermute | solution.py:131
  59.3 15.8 %collective-permute-start.4 = (bf16[8,128,128]{2,1,0:T(8,128)(2,1)}, bf16[8,128,128]{2,1,0:T(8,128)(2,1)S(1)}, u32[]{:S(2)}, u32[]{:S(2)}) collective-permute-start(bf16[8,128,128]{2,1,0:T(8,128)(2,1)} %constant_dynamic-slice_fusion), channel_id=1, source_target_pairs={{0,1},{1,2},{2,3},{3,0},{4,5},{5,6},{6,7},{7,4},{8,9},{9,10},{10,1... | collective-permute-start | bytes 786440 | tf_op jit(solution)/shard_map/ppermute | solution.py:131
  61.3 13.8 %collective-permute-start.5 = (bf16[8,128,128]{2,1,0:T(8,128)(2,1)}, bf16[8,128,128]{2,1,0:T(8,128)(2,1)S(1)}, u32[]{:S(2)}, u32[]{:S(2)}) collective-permute-start(bf16[8,128,128]{2,1,0:T(8,128)(2,1)} %constant_dynamic-slice_fusion), channel_id=1, source_target_pairs={{0,3},{1,0},{2,1},{3,2},{4,7},{5,4},{6,5},{7,6},{8,11},{9,8},{10,9... | collective-permute-start | bytes 786440 | tf_op jit(solution)/shard_map/ppermute | solution.py:131
  65.2 0.8 copy-start
  67.2 20.4 %all-to-all-start.1 = ((bf16[16,1,128,128]{3,2,1,0:T(8,128)(2,1)}), bf16[16,1,128,128]{3,2,1,0:T(8,128)(2,1)S(1)}, u32[]{:S(2)}, u32[]{:S(2)}) async-start(bf16[16,1,128,128]{3,2,1,0:T(8,128)(2,1)} %broadcast_in_dim.114), calls=%async_computation.1 | async-start | bytes 1048576 | tf_op jit(solution)/shard_map/all_to_all | solution.py:14
  75.2 19.8 %collective-permute-start.6 = (bf16[3,8,128,128]{3,2,0,1:T(8,128)(2,1)S(1)}, bf16[3,8,128,128]{3,2,0,1:T(8,128)(2,1)S(1)}, u32[]{:S(2)}, u32[]{:S(2)}) collective-permute-start(bf16[3,8,128,128]{3,2,0,1:T(8,128)(2,1)S(1)} %pad_maximum_fusion), channel_id=1, source_target_pairs={{0,16},{16,0},{32,48},{48,32},{64,80},{80,64},{96,112},{112,96},{1... | collective-permute-start | bytes 2359304 | tf_op jit(solution)/shard_map/ppermute | solution.py:133
  90.8 5.5 %collective-permute-start = (bf16[4,32,128]{2,1,0:T(8,128)(2,1)S(1)}, bf16[4,32,128]{2,1,0:T(8,128)(2,1)S(1)}, u32[]{:S(2)}, u32[]{:S(2)}) collective-permute-start(bf16[4,32,128]{2,1,0:T(8,128)(2,1)S(1)} %get-tuple-element.46), channel_id=1, source_target_pairs={{0,2},{1,3},{2,0},{3,1},{4,6},{5,7},{6,4},{7,5},{8,10},{9,11},{10,... | collective-permute-start | bytes 98312 | tf_op jit(solution)/shard_map/ppermute | solution.py:130
  92.9 4.3 %collective-permute-start.1 = (bf16[4,32,128]{2,1,0:T(8,128)(2,1)S(1)}, bf16[4,32,128]{2,1,0:T(8,128)(2,1)S(1)}, u32[]{:S(2)}, u32[]{:S(2)}) collective-permute-start(bf16[4,32,128]{2,1,0:T(8,128)(2,1)S(1)} %get-tuple-element.45), channel_id=1, source_target_pairs={{0,1},{1,2},{2,3},{3,0},{4,5},{5,6},{6,7},{7,4},{8,9},{9,10},{10,1... | collective-permute-start | bytes 98312 | tf_op jit(solution)/shard_map/ppermute | solution.py:130
  94.2 5.1 %collective-permute-start.2 = (bf16[4,32,128]{2,1,0:T(8,128)(2,1)S(1)}, bf16[4,32,128]{2,1,0:T(8,128)(2,1)S(1)}, u32[]{:S(2)}, u32[]{:S(2)}) collective-permute-start(bf16[4,32,128]{2,1,0:T(8,128)(2,1)S(1)} %get-tuple-element.44), channel_id=1, source_target_pairs={{0,3},{1,0},{2,1},{3,2},{4,7},{5,4},{6,5},{7,6},{8,11},{9,8},{10,9... | collective-permute-start | bytes 98312 | tf_op jit(solution)/shard_map/ppermute | solution.py:130
  100.0 7.9 %collective-permute-start.7 = (bf16[32,2048]{1,0:T(8,128)(2,1)S(1)}, bf16[32,2048]{1,0:T(8,128)(2,1)S(1)}, u32[]{:S(2)}, u32[]{:S(2)}) collective-permute-start(bf16[32,2048]{1,0:T(8,128)(2,1)S(1)} %get-tuple-element.36), channel_id=1, source_target_pairs={{0,8},{1,9},{2,10},{3,11},{4,12},{5,13},{6,14},{7,15},{8,0},{9,1},... | collective-permute-start | bytes 393224 | tf_op jit(solution)/shard_map/ppermute | solution.py:149
  103.1 7.1 %collective-permute-start.8 = (bf16[32,2048]{1,0:T(8,128)(2,1)S(1)}, bf16[32,2048]{1,0:T(8,128)(2,1)S(1)}, u32[]{:S(2)}, u32[]{:S(2)}) collective-permute-start(bf16[32,2048]{1,0:T(8,128)(2,1)S(1)} %get-tuple-element.40), channel_id=1, source_target_pairs={{0,4},{1,5},{2,6},{3,7},{4,8},{5,9},{6,10},{7,11},{8,12},{9,13},{1... | collective-permute-start | bytes 393224 | tf_op jit(solution)/shard_map/ppermute | solution.py:149
  103.7 6.5 %collective-permute-start.9 = (bf16[32,2048]{1,0:T(8,128)(2,1)S(1)}, bf16[32,2048]{1,0:T(8,128)(2,1)S(1)}, u32[]{:S(2)}, u32[]{:S(2)}) collective-permute-start(bf16[32,2048]{1,0:T(8,128)(2,1)S(1)} %get-tuple-element.38), channel_id=1, source_target_pairs={{0,12},{1,13},{2,14},{3,15},{4,0},{5,1},{6,2},{7,3},{8,4},{9,5},{1... | collective-permute-start | bytes 393224 | tf_op jit(solution)/shard_map/ppermute | solution.py:149
Sparse Core Ops, SparseCore 0:
  10.9 44.0 all-gather.1

commit v19 on v14

--- a/solution.py
+++ b/solution.py
@@ -115,7 +115,7 @@
     retained = (intra_all + inter).reshape(local_len, heads_here, HEAD_DIM)
     center = jnp.mean(retained, axis=-1, keepdims=True)
     spread = jnp.mean((retained - center) ** 2, axis=-1, keepdims=True)
-    normed = (retained - center) / jnp.sqrt(spread + 1e-05)
+    normed = (retained - center) * lax.rsqrt(spread + 1e-05)
     gated = (
         (jax.nn.silu(gate_all.reshape(local_len, heads_here, HEAD_DIM)) * normed)
         .astype(jnp.bfloat16)
@@ -126,6 +126,7 @@
     me = lax.axis_index("head")
     row, col = me // side, me % side
     rows_mine = out_blocks
+    ring_order = sorted(range(1, side), key=lambda shift: -min(shift, side - shift))
     by_owner = gated.reshape(side, side, local_len // heads, head_width)
     units = lax.axis_size("tm")
     half = rows_mine.shape[0] // 2
@@ -133,7 +134,7 @@
     own_half = lax.dynamic_slice_in_dim(rows_mine, parity * half, half, axis=0)
     pieces = [lax.dynamic_index_in_dim(by_owner, col, axis=1, keepdims=False)]
     fetched = []
-    for shift in range(1, side):
+    for shift in ring_order:
         across = [(h, (h // side) * side + (h % side + shift) % side) for h in range(heads)]
         piece = lax.dynamic_index_in_dim(by_owner, (col + shift) % side, axis=1, keepdims=False)
         pieces.append(lax.ppermute(piece, "head", across))
@@ -152,7 +153,7 @@
     ).astype(jnp.bfloat16)
     partial = partial.reshape(side, local_len // heads, -1)
     total = lax.dynamic_index_in_dim(partial, row, axis=0, keepdims=False).astype(jnp.float32)
-    for shift in range(1, side):
+    for shift in ring_order:
         down = [(h, ((h // side + shift) % side) * side + h % side) for h in range(heads)]
         piece = lax.dynamic_index_in_dim(partial, (row + shift) % side, axis=0, keepdims=False)
         total = total + lax.ppermute(piece, "head", down).astype(jnp.float32)

time: 112 us -> 111 us (level)
  waiting for transfers between devices: 49.4 us -> 47.7 us
  starting transfers between devices: 23.7 us -> 25.1 us
    ppermute x3, waiting for transfers between devices: 12.7 us -> 10.5 us  [shards(): fetched.append(lax.ppermute(own_half, 'head', across))]
where the time goes in v19:
time: 111 us
  waiting for transfers between devices  47.7 us (43%)
  starting transfers between devices  25.1 us (23%)
  between operations  17.6 us (16%)
  local copies, waits for them, and re-layouts  7.53 us (7%)
  matrix products  7.26 us (7%)
  other arithmetic  5.63 us (5%)
    all_to_all x2, waiting for transfers between devices, gather_by_exchange(): return lax.all_to_all(copies, axis, 0, 0, tiled=False)  23 us
    all_to_all x2, starting transfers between devices, gather_by_exchange(): return lax.all_to_all(copies, axis, 0, 0, tiled=False)  11.7 us
    ppermute x3, waiting for transfers between devices, shards(): fetched.append(lax.ppermute(own_half, 'head', across))  10.5 us
    all_gather x1, waiting for transfers between devices, shards(): stacked = lax.all_gather(packed, 'tm', axis=0, tiled=True)  6.1 us
    ppermute x3, starting transfers between devices, shards(): total = total + lax.ppermute(piece, 'head', down).astype(jnp.float32)  5.44 us
    ppermute x3, waiting for transfers between devices, shards(): pieces.append(lax.ppermute(piece, 'head', across))  4.71 us
    ppermute x3, starting transfers between devices, shards(): pieces.append(lax.ppermute(piece, 'head', across))  3.92 us
    ppermute x3, starting transfers between devices, shards(): fetched.append(lax.ppermute(own_half, 'head', across))  3.91 us
  transfers between devices with their start and end apart: 13, of which 10 were waited for; matrix products, arithmetic and copies ran while one was open for 11% of the time, Pallas kernels for 0%

profile of v19, /device:TPU:6, one launch (start us, length us, event | category | flops | bytes accessed | tf_op | source)
XLA Modules:
  0.0 110.7 jit_solution(15828763802035323449)
XLA Ops:
  6.5 1.5 %pad_add_fusion = bf16[128,640]{1,0:T(8,128)(2,1)} fusion(bf16[128,128]{1,0:T(8,128)(2,1)} %param.13, bf16[128,128]{1,0:T(8,128)(2,1)} %param.12, bf16[128,128]{1,0:T(8,128)(2,1)} %param.11, bf16[128,128]{1,0:T(8,128)(2,1)} %param.10, bf16[128,128]{1,0:T(8,128)(2,1)} %param.9), kind=kLoop, calls=%fused_computation.46 | loop fusion | flops 819200 | bytes 327680 | tf_op jit(solution)/shard_map/add | solution.py:48
  8.1 2.5 %broadcast_in_dim.51 = bf16[16,32,2048]{2,1,0:T(8,128)(2,1)} broadcast(bf16[32,2048]{1,0:T(8,128)(2,1)} %param.7), dimensions={1,2} | broadcast | bytes 2228224 | tf_op jit(solution)/shard_map/broadcast_in_dim | solution.py:13
  10.6 7.6 %all-to-all-start = ((bf16[16,32,2048]{2,1,0:T(8,128)(2,1)}), bf16[16,32,2048]{2,1,0:T(8,128)(2,1)S(1)}, u32[]{:S(2)}, u32[]{:S(2)}) async-start(bf16[16,32,2048]{2,1,0:T(8,128)(2,1)} %broadcast_in_dim.51), calls=%async_computation | async-start | bytes 4194304 | tf_op jit(solution)/shard_map/all_to_all | solution.py:14
  18.1 0.6 reduce_sum.47
  18.7 0.3 reduce-window.6
  19.0 0.2 slice_reduce_fusion
  19.2 0.2 reduce-window.9
  19.4 0.6 slice.69
  20.1 0.6 slice.68
  23.4 23.0 %all-to-all-done = bf16[16,32,2048]{2,1,0:T(8,128)(2,1)S(1)} async-done(((bf16[16,32,2048]{2,1,0:T(8,128)(2,1)}), bf16[16,32,2048]{2,1,0:T(8,128)(2,1)S(1)}, u32[]{:S(2)}, u32[]{:S(2)}) %all-to-all-start) | async-done | bytes 2097184 | tf_op jit(solution)/shard_map/all_to_all | solution.py:14
  46.4 6.1 %all-gather.2.cloned.1.call-done = bf16[2048,640]{1,0:T(8,128)(2,1)} async-done(((bf16[128,640]{1,0:T(8,128)(2,1)}), bf16[2048,640]{1,0:T(8,128)(2,1)}) %all-gather.2.cloned.1.call-update) | async-done | bytes 2621456 | tf_op jit(solution)/shard_map/all_gather | solution.py:52
  52.5 3.8 %fusion.55 = (bf16[512,512]{1,0:T(8,128)(2,1)S(1)}, f32[512,512]{1,0:T(8,128)}) fusion(bf16[512,2048]{1,0:T(8,128)(2,1)S(1)} %bitcast.110, bf16[2048,640]{1,0:T(8,128)(2,1)} %all-gather.2.cloned.1.call-done), kind=kOutput, calls=%fused_computation.90 | convolution fusion | flops 1074003968 | bytes 5767168 | tf_op jit(solution)/shard_map/dot_general | solution.py:56
  56.3 0.3 fusion.18
  56.7 0.1 maximum_bitcast_fusion.10
  56.8 0.9 broadcast_in_dim.94
  57.7 4.1 %all-to-all-start.1 = ((bf16[16,1,136,128]{3,2,1,0:T(8,128)(2,1)}), bf16[16,1,136,128]{3,2,1,0:T(8,128)(2,1)S(1)}, u32[]{:S(2)}, u32[]{:S(2)}) async-start(bf16[16,1,136,128]{3,2,1,0:T(8,128)(2,1)} %broadcast_in_dim.94), calls=%async_computation.1 | async-start | bytes 1114112 | tf_op jit(solution)/shard_map/all_to_all | solution.py:14
  62.0 0.6 slice.67
  62.6 0.6 slice.66
  64.6 1.1 slice.73
  65.7 1.5 %collective-permute-start.3 = (bf16[8,128,128]{2,1,0:T(8,128)(2,1)S(1)}, bf16[8,128,128]{2,1,0:T(8,128)(2,1)S(1)}, u32[]{:S(2)}, u32[]{:S(2)}) collective-permute-start(bf16[8,128,128]{2,1,0:T(8,128)(2,1)S(1)} %constant_dynamic-slice_fusion), channel_id=1, source_target_pairs={{0,2},{1,3},{2,0},{3,1},{4,6},{5,7},{6,4},{7,5},{8,10},{9,11},{10,... | collective-permute-start | bytes 786440 | tf_op jit(solution)/shard_map/ppermute | solution.py:141
  67.3 2.4 %collective-permute-start.4 = (bf16[8,128,128]{2,1,0:T(8,128)(2,1)S(1)}, bf16[8,128,128]{2,1,0:T(8,128)(2,1)S(1)}, u32[]{:S(2)}, u32[]{:S(2)}) collective-permute-start(bf16[8,128,128]{2,1,0:T(8,128)(2,1)S(1)} %constant_dynamic-slice_fusion), channel_id=1, source_target_pairs={{0,1},{1,2},{2,3},{3,0},{4,5},{5,6},{6,7},{7,4},{8,9},{9,10},{10,1... | collective-permute-start | bytes 786440 | tf_op jit(solution)/shard_map/ppermute | solution.py:141
  69.7 1.2 %fusion.15 = f32[1,512,1,128]{3,1,2,0:T(8,128)} fusion(f32[512]{0:T(512)S(1)} %get-tuple-element.22, bf16[512,512]{1,0:T(8,128)(2,1)S(1)} %get-tuple-element.43), kind=kOutput, calls=%fused_computation.16 | convolution fusion | flops 135528448 | bytes 659456 | tf_op jit(solution)/shard_map/while/body/eval_jaxpr/hts,shd->thd/dot_general | solution.py:92
  70.9 5.6 %collective-permute-done.3 = bf16[8,128,128]{2,1,0:T(8,128)(2,1)S(1)} collective-permute-done((bf16[8,128,128]{2,1,0:T(8,128)(2,1)S(1)}, bf16[8,128,128]{2,1,0:T(8,128)(2,1)S(1)}, u32[]{:S(2)}, u32[]{:S(2)}) %collective-permute-start.3) | collective-permute-done | bytes 262176 | tf_op jit(solution)/shard_map/ppermute | solution.py:141
  76.5 4.1 %collective-permute-done.4 = bf16[8,128,128]{2,1,0:T(8,128)(2,1)S(1)} collective-permute-done((bf16[8,128,128]{2,1,0:T(8,128)(2,1)S(1)}, bf16[8,128,128]{2,1,0:T(8,128)(2,1)S(1)}, u32[]{:S(2)}, u32[]{:S(2)}) %collective-permute-start.4) | collective-permute-done | bytes 262176 | tf_op jit(solution)/shard_map/ppermute | solution.py:141
  80.6 0.8 collective-permute-done.5
  81.4 0.1 pad_maximum_fusion
  81.5 0.1 collective-permute-start.6
  81.6 0.2 fusion.52
  81.8 0.1 select_reduce_fusion
  82.0 0.2 multiply_reduce_fusion
  82.1 1.4 %fusion.56 = (f32[512]{0:T(512)S(1)}, f32[1,512,1,128]{3,1,2,0:T(8,128)S(1)}) fusion(f32[1,512,1,128]{3,1,2,0:T(8,128)} %fusion.15, f32[128,128]{1,0:T(8,128)S(1)} %multiply_reduce_fusion, f32[]{:T(128)} %bitcast.11, f32[512]{0:T(512)S(1)} %exp.53, bf16[512,512]{1,0:T(8,128)(2,1)} %copy-done), kind=kOutput, calls=%fused_computation.91 | convolution fusion | flops 17137152 | bytes 725504 | tf_op jit(solution)/shard_map/cthd,chde->cthe/dot_general | solution.py:109
  83.6 0.2 fusion.29
  83.8 1.2 %fusion.32 = bf16[512,128]{1,0:T(8,128)(2,1)S(1)} fusion(f32[1,512,1,128]{3,1,2,0:T(8,128)S(1)} %get-tuple-element.46, f32[512,512]{1,0:T(8,128)} %get-tuple-element.44, f32[512]{0:T(512)S(1)} %add_rsqrt_fusion, f32[512]{0:T(512)S(1)} %broadcast_multiply_fusion), kind=kLoop, calls=%fused_computation.43 | loop fusion | flops 524288 | bytes 659456 | tf_op jit(solution)/shard_map/convert_element_type | solution.py:121
  85.0 1.9 %collective-permute-start = (bf16[4,32,128]{2,1,0:T(8,128)(2,1)S(1)}, bf16[4,32,128]{2,1,0:T(8,128)(2,1)S(1)}, u32[]{:S(2)}, u32[]{:S(2)}) collective-permute-start(bf16[4,32,128]{2,1,0:T(8,128)(2,1)S(1)} %get-tuple-element.42), channel_id=1, source_target_pairs={{0,2},{1,3},{2,0},{3,1},{4,6},{5,7},{6,4},{7,5},{8,10},{9,11},{10,... | collective-permute-start | bytes 98312 | tf_op jit(solution)/shard_map/ppermute | solution.py:140
  86.9 1.7 %collective-permute-start.1 = (bf16[4,32,128]{2,1,0:T(8,128)(2,1)S(1)}, bf16[4,32,128]{2,1,0:T(8,128)(2,1)S(1)}, u32[]{:S(2)}, u32[]{:S(2)}) collective-permute-start(bf16[4,32,128]{2,1,0:T(8,128)(2,1)S(1)} %get-tuple-element.41), channel_id=1, source_target_pairs={{0,1},{1,2},{2,3},{3,0},{4,5},{5,6},{6,7},{7,4},{8,9},{9,10},{10,1... | collective-permute-start | bytes 98312 | tf_op jit(solution)/shard_map/ppermute | solution.py:140
  88.6 0.3 collective-permute-start.2
  88.9 0.1 broadcast_select_fusion.1
  89.1 1.4 %collective-permute-done = bf16[4,32,128]{2,1,0:T(8,128)(2,1)S(1)} collective-permute-done((bf16[4,32,128]{2,1,0:T(8,128)(2,1)S(1)}, bf16[4,32,128]{2,1,0:T(8,128)(2,1)S(1)}, u32[]{:S(2)}, u32[]{:S(2)}) %collective-permute-start) | collective-permute-done | bytes 32800 | tf_op jit(solution)/shard_map/ppermute | solution.py:140
  90.5 0.3 collective-permute-done.1
  90.8 3.0 %collective-permute-done.2 = bf16[4,32,128]{2,1,0:T(8,128)(2,1)S(1)} collective-permute-done((bf16[4,32,128]{2,1,0:T(8,128)(2,1)S(1)}, bf16[4,32,128]{2,1,0:T(8,128)(2,1)S(1)}, u32[]{:S(2)}, u32[]{:S(2)}) %collective-permute-start.2) | collective-permute-done | bytes 32800 | tf_op jit(solution)/shard_map/ppermute | solution.py:140
  93.8 0.5 fusion.13
  94.2 0.1 copy.38
  94.4 2.2 %collective-permute-start.7 = (bf16[32,2048]{1,0:T(8,128)(2,1)S(1)}, bf16[32,2048]{1,0:T(8,128)(2,1)S(1)}, u32[]{:S(2)}, u32[]{:S(2)}) collective-permute-start(bf16[32,2048]{1,0:T(8,128)(2,1)S(1)} %get-tuple-element.25), channel_id=1, source_target_pairs={{0,8},{1,9},{2,10},{3,11},{4,12},{5,13},{6,14},{7,15},{8,0},{9,1},... | collective-permute-start | bytes 393224 | tf_op jit(solution)/shard_map/ppermute | solution.py:159
  96.6 0.6 collective-permute-start.8
  97.2 2.6 %collective-permute-start.9 = (bf16[32,2048]{1,0:T(8,128)(2,1)S(1)}, bf16[32,2048]{1,0:T(8,128)(2,1)S(1)}, u32[]{:S(2)}, u32[]{:S(2)}) collective-permute-start(bf16[32,2048]{1,0:T(8,128)(2,1)S(1)} %get-tuple-element.26), channel_id=1, source_target_pairs={{0,12},{1,13},{2,14},{3,15},{4,0},{5,1},{6,2},{7,3},{8,4},{9,5},{1... | collective-permute-start | bytes 393224 | tf_op jit(solution)/shard_map/ppermute | solution.py:159
  99.8 1.8 %collective-permute-done.7 = bf16[32,2048]{1,0:T(8,128)(2,1)S(1)} collective-permute-done((bf16[32,2048]{1,0:T(8,128)(2,1)S(1)}, bf16[32,2048]{1,0:T(8,128)(2,1)S(1)}, u32[]{:S(2)}, u32[]{:S(2)}) %collective-permute-start.7) | collective-permute-done | bytes 131104 | tf_op jit(solution)/shard_map/ppermute | solution.py:159
  101.7 1.4 %collective-permute-done.8 = bf16[32,2048]{1,0:T(8,128)(2,1)S(1)} collective-permute-done((bf16[32,2048]{1,0:T(8,128)(2,1)S(1)}, bf16[32,2048]{1,0:T(8,128)(2,1)S(1)}, u32[]{:S(2)}, u32[]{:S(2)}) %collective-permute-start.8) | collective-permute-done | bytes 131104 | tf_op jit(solution)/shard_map/ppermute | solution.py:159
  103.1 0.7 fusion.27
  (25 shorter events, 0.5 us)
Async XLA Ops:
  6.5 46.0 %all-gather.2.cloned.1.call-start = ((), (), s32[]{:S(2)}) async-start(), calls=%async_computation.2 | async-start | bytes 2785280 | tf_op jit(solution)/shard_map/all_gather | solution.py:52
  10.5 7.6 %copy-start.1 = (f32[512,1]{0,1:T(1,128)S(1)}, f32[512,1]{0,1:T(1,128)}, u32[]{:S(2)}) copy-start(f32[512,1]{0,1:T(1,128)} %param.8) | copy-start | bytes 6148
  10.6 35.8 %all-to-all-start = ((bf16[16,32,2048]{2,1,0:T(8,128)(2,1)}), bf16[16,32,2048]{2,1,0:T(8,128)(2,1)S(1)}, u32[]{:S(2)}, u32[]{:S(2)}) async-start(bf16[16,32,2048]{2,1,0:T(8,128)(2,1)} %broadcast_in_dim.51), calls=%async_computation | async-start | bytes 4194304 | tf_op jit(solution)/shard_map/all_to_all | solution.py:14
  56.3 14.6 %copy-start = (bf16[512,512]{1,0:T(8,128)(2,1)}, bf16[512,512]{1,0:T(8,128)(2,1)S(1)}, u32[]{:S(2)}) copy-start(bf16[512,512]{1,0:T(8,128)(2,1)S(1)} %get-tuple-element.43) | copy-start | bytes 1572868
  57.7 23.9 %all-to-all-start.1 = ((bf16[16,1,136,128]{3,2,1,0:T(8,128)(2,1)}), bf16[16,1,136,128]{3,2,1,0:T(8,128)(2,1)S(1)}, u32[]{:S(2)}, u32[]{:S(2)}) async-start(bf16[16,1,136,128]{3,2,1,0:T(8,128)(2,1)} %broadcast_in_dim.94), calls=%async_computation.1 | async-start | bytes 1114112 | tf_op jit(solution)/shard_map/all_to_all | solution.py:14
  65.7 10.8 %collective-permute-start.3 = (bf16[8,128,128]{2,1,0:T(8,128)(2,1)S(1)}, bf16[8,128,128]{2,1,0:T(8,128)(2,1)S(1)}, u32[]{:S(2)}, u32[]{:S(2)}) collective-permute-start(bf16[8,128,128]{2,1,0:T(8,128)(2,1)S(1)} %constant_dynamic-slice_fusion), channel_id=1, source_target_pairs={{0,2},{1,3},{2,0},{3,1},{4,6},{5,7},{6,4},{7,5},{8,10},{9,11},{10,... | collective-permute-start | bytes 786440 | tf_op jit(solution)/shard_map/ppermute | solution.py:141
  67.3 13.3 %collective-permute-start.4 = (bf16[8,128,128]{2,1,0:T(8,128)(2,1)S(1)}, bf16[8,128,128]{2,1,0:T(8,128)(2,1)S(1)}, u32[]{:S(2)}, u32[]{:S(2)}) collective-permute-start(bf16[8,128,128]{2,1,0:T(8,128)(2,1)S(1)} %constant_dynamic-slice_fusion), channel_id=1, source_target_pairs={{0,1},{1,2},{2,3},{3,0},{4,5},{5,6},{6,7},{7,4},{8,9},{9,10},{10,1... | collective-permute-start | bytes 786440 | tf_op jit(solution)/shard_map/ppermute | solution.py:141
  69.7 11.8 %collective-permute-start.5 = (bf16[8,128,128]{2,1,0:T(8,128)(2,1)S(1)}, bf16[8,128,128]{2,1,0:T(8,128)(2,1)S(1)}, u32[]{:S(2)}, u32[]{:S(2)}) collective-permute-start(bf16[8,128,128]{2,1,0:T(8,128)(2,1)S(1)} %constant_dynamic-slice_fusion), channel_id=1, source_target_pairs={{0,3},{1,0},{2,1},{3,2},{4,7},{5,4},{6,5},{7,6},{8,11},{9,8},{10,9... | collective-permute-start | bytes 786440 | tf_op jit(solution)/shard_map/ppermute | solution.py:141
  81.5 7.4 %collective-permute-start.6 = (bf16[3,8,128,128]{3,2,0,1:T(8,128)(2,1)S(1)}, bf16[3,8,128,128]{3,2,0,1:T(8,128)(2,1)S(1)}, u32[]{:S(2)}, u32[]{:S(2)}) collective-permute-start(bf16[3,8,128,128]{3,2,0,1:T(8,128)(2,1)S(1)} %pad_maximum_fusion), channel_id=1, source_target_pairs={{0,16},{16,0},{32,48},{48,32},{64,80},{80,64},{96,112},{112,96},{1... | collective-permute-start | bytes 2359304 | tf_op jit(solution)/shard_map/ppermute | solution.py:143
  85.0 5.5 %collective-permute-start = (bf16[4,32,128]{2,1,0:T(8,128)(2,1)S(1)}, bf16[4,32,128]{2,1,0:T(8,128)(2,1)S(1)}, u32[]{:S(2)}, u32[]{:S(2)}) collective-permute-start(bf16[4,32,128]{2,1,0:T(8,128)(2,1)S(1)} %get-tuple-element.42), channel_id=1, source_target_pairs={{0,2},{1,3},{2,0},{3,1},{4,6},{5,7},{6,4},{7,5},{8,10},{9,11},{10,... | collective-permute-start | bytes 98312 | tf_op jit(solution)/shard_map/ppermute | solution.py:140
  86.9 3.9 %collective-permute-start.1 = (bf16[4,32,128]{2,1,0:T(8,128)(2,1)S(1)}, bf16[4,32,128]{2,1,0:T(8,128)(2,1)S(1)}, u32[]{:S(2)}, u32[]{:S(2)}) collective-permute-start(bf16[4,32,128]{2,1,0:T(8,128)(2,1)S(1)} %get-tuple-element.41), channel_id=1, source_target_pairs={{0,1},{1,2},{2,3},{3,0},{4,5},{5,6},{6,7},{7,4},{8,9},{9,10},{10,1... | collective-permute-start | bytes 98312 | tf_op jit(solution)/shard_map/ppermute | solution.py:140
  88.6 5.1 %collective-permute-start.2 = (bf16[4,32,128]{2,1,0:T(8,128)(2,1)S(1)}, bf16[4,32,128]{2,1,0:T(8,128)(2,1)S(1)}, u32[]{:S(2)}, u32[]{:S(2)}) collective-permute-start(bf16[4,32,128]{2,1,0:T(8,128)(2,1)S(1)} %get-tuple-element.40), channel_id=1, source_target_pairs={{0,3},{1,0},{2,1},{3,2},{4,7},{5,4},{6,5},{7,6},{8,11},{9,8},{10,9... | collective-permute-start | bytes 98312 | tf_op jit(solution)/shard_map/ppermute | solution.py:140
  94.4 7.3 %collective-permute-start.7 = (bf16[32,2048]{1,0:T(8,128)(2,1)S(1)}, bf16[32,2048]{1,0:T(8,128)(2,1)S(1)}, u32[]{:S(2)}, u32[]{:S(2)}) collective-permute-start(bf16[32,2048]{1,0:T(8,128)(2,1)S(1)} %get-tuple-element.25), channel_id=1, source_target_pairs={{0,8},{1,9},{2,10},{3,11},{4,12},{5,13},{6,14},{7,15},{8,0},{9,1},... | collective-permute-start | bytes 393224 | tf_op jit(solution)/shard_map/ppermute | solution.py:159
  96.6 6.5 %collective-permute-start.8 = (bf16[32,2048]{1,0:T(8,128)(2,1)S(1)}, bf16[32,2048]{1,0:T(8,128)(2,1)S(1)}, u32[]{:S(2)}, u32[]{:S(2)}) collective-permute-start(bf16[32,2048]{1,0:T(8,128)(2,1)S(1)} %get-tuple-element.36), channel_id=1, source_target_pairs={{0,4},{1,5},{2,6},{3,7},{4,8},{5,9},{6,10},{7,11},{8,12},{9,13},{1... | collective-permute-start | bytes 393224 | tf_op jit(solution)/shard_map/ppermute | solution.py:159
  97.2 5.9 %collective-permute-start.9 = (bf16[32,2048]{1,0:T(8,128)(2,1)S(1)}, bf16[32,2048]{1,0:T(8,128)(2,1)S(1)}, u32[]{:S(2)}, u32[]{:S(2)}) collective-permute-start(bf16[32,2048]{1,0:T(8,128)(2,1)S(1)} %get-tuple-element.26), channel_id=1, source_target_pairs={{0,12},{1,13},{2,14},{3,15},{4,0},{5,1},{6,2},{7,3},{8,4},{9,5},{1... | collective-permute-start | bytes 393224 | tf_op jit(solution)/shard_map/ppermute | solution.py:159
Sparse Core Ops, SparseCore 0:
  9.2 43.2 all-gather.1

commit v20 on v16

--- a/solution.py
+++ b/solution.py
@@ -45,10 +45,11 @@
     head_width = w_query.shape[1]
     blocks = [w_query, w_key, w_value, w_gate, w_out]
     width = sum(block.shape[1] for block in blocks)
-    packed = sum(
-        jnp.pad(block, ((0, 0), (start, width - start - block.shape[1])))
-        for start, block in zip(range(0, width, head_width), blocks)
-    )
+    column = jnp.arange(width)[None, :]
+    packed = jnp.pad(blocks[-1], ((0, 0), (width - head_width, 0)))
+    for start, block in reversed(list(zip(range(0, width, head_width), blocks))[:-1]):
+        padded = jnp.pad(block, ((0, 0), (start, width - start - head_width)))
+        packed = jnp.where(column < start + head_width, padded, packed)
     stacked = lax.all_gather(packed, "tm", axis=0, tiled=True)
     joined = stacked[:, : 4 * head_width]
     out_blocks = stacked[:, 4 * head_width :].reshape(-1, head_width, w_out.shape[1])

time: 111 us -> 111 us (level)
    select_n x0 -> x1, other arithmetic: none -> 1.55 us  [shards(): packed = jnp.where(column < start + head_width, padded, packed)]
    add x1 -> x0, other arithmetic: 1.52 us -> none  [shards(): sum((jnp.pad(block, ((0, 0), (start, width - start - block.shape[1]))) fo...]
where the time goes in v20:
time: 111 us
  waiting for transfers between devices  47.6 us (43%)
  starting transfers between devices  24.9 us (22%)
  between operations  17.6 us (16%)
  matrix products  7.4 us (7%)
  local copies, waits for them, and re-layouts  7.38 us (7%)
  other arithmetic  5.77 us (5%)
    all_to_all x2, waiting for transfers between devices, gather_by_exchange(): return lax.all_to_all(copies, axis, 0, 0, tiled=False)  22.9 us
    all_to_all x2, starting transfers between devices, gather_by_exchange(): return lax.all_to_all(copies, axis, 0, 0, tiled=False)  11.6 us
    ppermute x3, waiting for transfers between devices, shards(): fetched.append(lax.ppermute(own_half, 'head', across))  10.5 us
    all_gather x1, waiting for transfers between devices, shards(): stacked = lax.all_gather(packed, 'tm', axis=0, tiled=True)  6.14 us
    ppermute x3, starting transfers between devices, shards(): total = total + lax.ppermute(piece, 'head', down).astype(jnp.float32)  5.39 us
    ppermute x3, waiting for transfers between devices, shards(): pieces.append(lax.ppermute(piece, 'head', across))  4.76 us
    ppermute x3, starting transfers between devices, shards(): pieces.append(lax.ppermute(piece, 'head', across))  3.92 us
    ppermute x3, starting transfers between devices, shards(): fetched.append(lax.ppermute(own_half, 'head', across))  3.91 us
  transfers between devices with their start and end apart: 13, of which 10 were waited for; matrix products, arithmetic and copies ran while one was open for 11% of the time, Pallas kernels for 0%

profile of v20, /device:TPU:6, one launch (start us, length us, event | category | flops | bytes accessed | tf_op | source)
XLA Modules:
  0.0 110.7 jit_solution(12447846987612990103)
XLA Ops:
  6.5 1.6 %select_select_fusion = bf16[128,640]{1,0:T(8,128)(2,1)} fusion(bf16[128,128]{1,0:T(8,128)(2,1)} %param.13, bf16[128,128]{1,0:T(8,128)(2,1)} %param.12, bf16[128,128]{1,0:T(8,128)(2,1)} %param.11, bf16[128,128]{1,0:T(8,128)(2,1)} %param.10, bf16[128,128]{1,0:T(8,128)(2,1)} %param.9, pred[640]{0:T(1024)(128)(4,1)S(1)} %get-tuple-element.47, ...), kind=kLoop, calls=%fused_computation.47 | loop fusion | flops 327680 | bytes 330240 | tf_op jit(solution)/shard_map/jit(_where)/select_n | solution.py:52
  8.1 2.5 %broadcast_in_dim.113 = bf16[16,32,2048]{2,1,0:T(8,128)(2,1)} broadcast(bf16[32,2048]{1,0:T(8,128)(2,1)} %param.7), dimensions={1,2} | broadcast | bytes 2228224 | tf_op jit(solution)/shard_map/broadcast_in_dim | solution.py:13
  10.6 7.6 %all-to-all-start = ((bf16[16,32,2048]{2,1,0:T(8,128)(2,1)}), bf16[16,32,2048]{2,1,0:T(8,128)(2,1)S(1)}, u32[]{:S(2)}, u32[]{:S(2)}) async-start(bf16[16,32,2048]{2,1,0:T(8,128)(2,1)} %broadcast_in_dim.113), calls=%async_computation | async-start | bytes 4194304 | tf_op jit(solution)/shard_map/all_to_all | solution.py:14
  18.2 0.7 reduce_sum.47
  18.8 0.3 reduce-window.6
  19.1 0.2 slice_reduce_fusion
  19.3 0.2 reduce-window.9
  19.6 0.6 slice.69
  20.1 0.6 slice.68
  23.6 22.9 %all-to-all-done = bf16[16,32,2048]{2,1,0:T(8,128)(2,1)S(1)} async-done(((bf16[16,32,2048]{2,1,0:T(8,128)(2,1)}), bf16[16,32,2048]{2,1,0:T(8,128)(2,1)S(1)}, u32[]{:S(2)}, u32[]{:S(2)}) %all-to-all-start) | async-done | bytes 2097184 | tf_op jit(solution)/shard_map/all_to_all | solution.py:14
  46.4 6.1 %all-gather.2.cloned.1.call-done = bf16[2048,640]{1,0:T(8,128)(2,1)} async-done(((bf16[128,640]{1,0:T(8,128)(2,1)}), bf16[2048,640]{1,0:T(8,128)(2,1)}) %all-gather.2.cloned.1.call-update) | async-done | bytes 2621456 | tf_op jit(solution)/shard_map/all_gather | solution.py:53
  52.6 3.8 %fusion.58 = (bf16[512,512]{1,0:T(8,128)(2,1)S(1)}, f32[512,512]{1,0:T(8,128)}) fusion(bf16[512,2048]{1,0:T(8,128)(2,1)S(1)} %bitcast.110, bf16[2048,640]{1,0:T(8,128)(2,1)} %all-gather.2.cloned.1.call-done), kind=kOutput, calls=%fused_computation.95 | convolution fusion | flops 1074003968 | bytes 5767168 | tf_op jit(solution)/shard_map/dot_general | solution.py:57
  56.4 0.3 fusion.18
  56.8 0.1 maximum_bitcast_fusion.10
  56.9 0.9 broadcast_in_dim.122
  57.8 4.0 %all-to-all-start.1 = ((bf16[16,1,136,128]{3,2,1,0:T(8,128)(2,1)}), bf16[16,1,136,128]{3,2,1,0:T(8,128)(2,1)S(1)}, u32[]{:S(2)}, u32[]{:S(2)}) async-start(bf16[16,1,136,128]{3,2,1,0:T(8,128)(2,1)} %broadcast_in_dim.122), calls=%async_computation.1 | async-start | bytes 1114112 | tf_op jit(solution)/shard_map/all_to_all | solution.py:14
  62.0 0.6 slice.67
  62.6 0.6 slice.66
  64.4 1.1 slice.73
  65.6 1.5 %collective-permute-start.3 = (bf16[8,128,128]{2,1,0:T(8,128)(2,1)S(1)}, bf16[8,128,128]{2,1,0:T(8,128)(2,1)S(1)}, u32[]{:S(2)}, u32[]{:S(2)}) collective-permute-start(bf16[8,128,128]{2,1,0:T(8,128)(2,1)S(1)} %constant_dynamic-slice_fusion), channel_id=1, source_target_pairs={{0,2},{1,3},{2,0},{3,1},{4,6},{5,7},{6,4},{7,5},{8,10},{9,11},{10,... | collective-permute-start | bytes 786440 | tf_op jit(solution)/shard_map/ppermute | solution.py:137
  67.1 2.4 %collective-permute-start.4 = (bf16[8,128,128]{2,1,0:T(8,128)(2,1)S(1)}, bf16[8,128,128]{2,1,0:T(8,128)(2,1)S(1)}, u32[]{:S(2)}, u32[]{:S(2)}) collective-permute-start(bf16[8,128,128]{2,1,0:T(8,128)(2,1)S(1)} %constant_dynamic-slice_fusion), channel_id=1, source_target_pairs={{0,1},{1,2},{2,3},{3,0},{4,5},{5,6},{6,7},{7,4},{8,9},{9,10},{10,1... | collective-permute-start | bytes 786440 | tf_op jit(solution)/shard_map/ppermute | solution.py:137
  69.5 1.2 %fusion.15 = f32[1,512,1,128]{3,1,2,0:T(8,128)} fusion(f32[512]{0:T(512)S(1)} %get-tuple-element.22, bf16[512,512]{1,0:T(8,128)(2,1)S(1)} %get-tuple-element.43), kind=kOutput, calls=%fused_computation.16 | convolution fusion | flops 135528448 | bytes 659456 | tf_op jit(solution)/shard_map/while/body/eval_jaxpr/hts,shd->thd/dot_general | solution.py:93
  70.7 5.6 %collective-permute-done.3 = bf16[8,128,128]{2,1,0:T(8,128)(2,1)S(1)} collective-permute-done((bf16[8,128,128]{2,1,0:T(8,128)(2,1)S(1)}, bf16[8,128,128]{2,1,0:T(8,128)(2,1)S(1)}, u32[]{:S(2)}, u32[]{:S(2)}) %collective-permute-start.3) | collective-permute-done | bytes 262176 | tf_op jit(solution)/shard_map/ppermute | solution.py:137
  76.3 4.1 %collective-permute-done.4 = bf16[8,128,128]{2,1,0:T(8,128)(2,1)S(1)} collective-permute-done((bf16[8,128,128]{2,1,0:T(8,128)(2,1)S(1)}, bf16[8,128,128]{2,1,0:T(8,128)(2,1)S(1)}, u32[]{:S(2)}, u32[]{:S(2)}) %collective-permute-start.4) | collective-permute-done | bytes 262176 | tf_op jit(solution)/shard_map/ppermute | solution.py:137
  80.5 0.8 collective-permute-done.5
  81.3 0.1 pad_maximum_fusion
  81.3 0.1 collective-permute-start.6
  81.5 0.2 fusion.55
  81.7 0.1 select_reduce_fusion
  81.8 0.2 multiply_reduce_fusion
  82.0 1.5 %fusion.59 = (f32[512]{0:T(512)S(1)}, f32[1,512,1,128]{3,1,2,0:T(8,128)S(1)}) fusion(f32[1,512,1,128]{3,1,2,0:T(8,128)} %fusion.15, f32[512]{0:T(512)S(1)} %exp.53, bf16[512,512]{1,0:T(8,128)(2,1)} %copy-done, f32[128,128]{1,0:T(8,128)S(1)} %multiply_reduce_fusion, f32[]{:T(128)} %bitcast.11), kind=kOutput, calls=%fused_computation.96 | convolution fusion | flops 100941312 | bytes 725504 | tf_op jit(solution)/shard_map/cthd,chde->cthe/dot_general | solution.py:110
  83.5 0.2 fusion.29
  83.8 1.2 %fusion.32 = bf16[512,128]{1,0:T(8,128)(2,1)S(1)} fusion(f32[1,512,1,128]{3,1,2,0:T(8,128)S(1)} %get-tuple-element.46, f32[512,512]{1,0:T(8,128)} %get-tuple-element.44, f32[512]{0:T(512)S(1)} %add_sqrt_fusion, f32[512]{0:T(512)S(1)} %broadcast_multiply_fusion), kind=kLoop, calls=%fused_computation.43 | loop fusion | flops 524288 | bytes 659456 | tf_op jit(solution)/shard_map/convert_element_type | solution.py:117
  85.0 1.9 %collective-permute-start = (bf16[4,32,128]{2,1,0:T(8,128)(2,1)S(1)}, bf16[4,32,128]{2,1,0:T(8,128)(2,1)S(1)}, u32[]{:S(2)}, u32[]{:S(2)}) collective-permute-start(bf16[4,32,128]{2,1,0:T(8,128)(2,1)S(1)} %get-tuple-element.42), channel_id=1, source_target_pairs={{0,2},{1,3},{2,0},{3,1},{4,6},{5,7},{6,4},{7,5},{8,10},{9,11},{10,... | collective-permute-start | bytes 98312 | tf_op jit(solution)/shard_map/ppermute | solution.py:136
  86.9 1.8 %collective-permute-start.1 = (bf16[4,32,128]{2,1,0:T(8,128)(2,1)S(1)}, bf16[4,32,128]{2,1,0:T(8,128)(2,1)S(1)}, u32[]{:S(2)}, u32[]{:S(2)}) collective-permute-start(bf16[4,32,128]{2,1,0:T(8,128)(2,1)S(1)} %get-tuple-element.41), channel_id=1, source_target_pairs={{0,1},{1,2},{2,3},{3,0},{4,5},{5,6},{6,7},{7,4},{8,9},{9,10},{10,1... | collective-permute-start | bytes 98312 | tf_op jit(solution)/shard_map/ppermute | solution.py:136
  88.7 0.2 collective-permute-start.2
  88.9 0.1 broadcast_select_fusion.1
  89.0 1.5 %collective-permute-done = bf16[4,32,128]{2,1,0:T(8,128)(2,1)S(1)} collective-permute-done((bf16[4,32,128]{2,1,0:T(8,128)(2,1)S(1)}, bf16[4,32,128]{2,1,0:T(8,128)(2,1)S(1)}, u32[]{:S(2)}, u32[]{:S(2)}) %collective-permute-start) | collective-permute-done | bytes 32800 | tf_op jit(solution)/shard_map/ppermute | solution.py:136
  90.5 0.3 collective-permute-done.1
  90.8 3.0 %collective-permute-done.2 = bf16[4,32,128]{2,1,0:T(8,128)(2,1)S(1)} collective-permute-done((bf16[4,32,128]{2,1,0:T(8,128)(2,1)S(1)}, bf16[4,32,128]{2,1,0:T(8,128)(2,1)S(1)}, u32[]{:S(2)}, u32[]{:S(2)}) %collective-permute-start.2) | collective-permute-done | bytes 32800 | tf_op jit(solution)/shard_map/ppermute | solution.py:136
  93.8 0.5 fusion.13
  94.2 0.1 copy.38
  94.4 2.2 %collective-permute-start.7 = (bf16[32,2048]{1,0:T(8,128)(2,1)S(1)}, bf16[32,2048]{1,0:T(8,128)(2,1)S(1)}, u32[]{:S(2)}, u32[]{:S(2)}) collective-permute-start(bf16[32,2048]{1,0:T(8,128)(2,1)S(1)} %get-tuple-element.25), channel_id=1, source_target_pairs={{0,8},{1,9},{2,10},{3,11},{4,12},{5,13},{6,14},{7,15},{8,0},{9,1},... | collective-permute-start | bytes 393224 | tf_op jit(solution)/shard_map/ppermute | solution.py:155
  96.6 0.6 collective-permute-start.8
  97.2 2.6 %collective-permute-start.9 = (bf16[32,2048]{1,0:T(8,128)(2,1)S(1)}, bf16[32,2048]{1,0:T(8,128)(2,1)S(1)}, u32[]{:S(2)}, u32[]{:S(2)}) collective-permute-start(bf16[32,2048]{1,0:T(8,128)(2,1)S(1)} %get-tuple-element.26), channel_id=1, source_target_pairs={{0,12},{1,13},{2,14},{3,15},{4,0},{5,1},{6,2},{7,3},{8,4},{9,5},{1... | collective-permute-start | bytes 393224 | tf_op jit(solution)/shard_map/ppermute | solution.py:155
  99.8 1.9 %collective-permute-done.7 = bf16[32,2048]{1,0:T(8,128)(2,1)S(1)} collective-permute-done((bf16[32,2048]{1,0:T(8,128)(2,1)S(1)}, bf16[32,2048]{1,0:T(8,128)(2,1)S(1)}, u32[]{:S(2)}, u32[]{:S(2)}) %collective-permute-start.7) | collective-permute-done | bytes 131104 | tf_op jit(solution)/shard_map/ppermute | solution.py:155
  101.7 1.4 %collective-permute-done.8 = bf16[32,2048]{1,0:T(8,128)(2,1)S(1)} collective-permute-done((bf16[32,2048]{1,0:T(8,128)(2,1)S(1)}, bf16[32,2048]{1,0:T(8,128)(2,1)S(1)}, u32[]{:S(2)}, u32[]{:S(2)}) %collective-permute-start.8) | collective-permute-done | bytes 131104 | tf_op jit(solution)/shard_map/ppermute | solution.py:155
  103.1 0.7 fusion.27
  (27 shorter events, 0.5 us)
Async XLA Ops:
  6.5 46.1 %all-gather.2.cloned.1.call-start = ((), (), s32[]{:S(2)}) async-start(), calls=%async_computation.2 | async-start | bytes 2785280 | tf_op jit(solution)/shard_map/all_gather | solution.py:53
  10.6 7.6 %copy-start.1 = (f32[512,1]{0,1:T(1,128)S(1)}, f32[512,1]{0,1:T(1,128)}, u32[]{:S(2)}) copy-start(f32[512,1]{0,1:T(1,128)} %param.8) | copy-start | bytes 6148
  10.6 35.8 %all-to-all-start = ((bf16[16,32,2048]{2,1,0:T(8,128)(2,1)}), bf16[16,32,2048]{2,1,0:T(8,128)(2,1)S(1)}, u32[]{:S(2)}, u32[]{:S(2)}) async-start(bf16[16,32,2048]{2,1,0:T(8,128)(2,1)} %broadcast_in_dim.113), calls=%async_computation | async-start | bytes 4194304 | tf_op jit(solution)/shard_map/all_to_all | solution.py:14
  56.4 14.3 %copy-start = (bf16[512,512]{1,0:T(8,128)(2,1)}, bf16[512,512]{1,0:T(8,128)(2,1)S(1)}, u32[]{:S(2)}) copy-start(bf16[512,512]{1,0:T(8,128)(2,1)S(1)} %get-tuple-element.43) | copy-start | bytes 1572868
  57.8 23.7 %all-to-all-start.1 = ((bf16[16,1,136,128]{3,2,1,0:T(8,128)(2,1)}), bf16[16,1,136,128]{3,2,1,0:T(8,128)(2,1)S(1)}, u32[]{:S(2)}, u32[]{:S(2)}) async-start(bf16[16,1,136,128]{3,2,1,0:T(8,128)(2,1)} %broadcast_in_dim.122), calls=%async_computation.1 | async-start | bytes 1114112 | tf_op jit(solution)/shard_map/all_to_all | solution.py:14
  65.6 10.8 %collective-permute-start.3 = (bf16[8,128,128]{2,1,0:T(8,128)(2,1)S(1)}, bf16[8,128,128]{2,1,0:T(8,128)(2,1)S(1)}, u32[]{:S(2)}, u32[]{:S(2)}) collective-permute-start(bf16[8,128,128]{2,1,0:T(8,128)(2,1)S(1)} %constant_dynamic-slice_fusion), channel_id=1, source_target_pairs={{0,2},{1,3},{2,0},{3,1},{4,6},{5,7},{6,4},{7,5},{8,10},{9,11},{10,... | collective-permute-start | bytes 786440 | tf_op jit(solution)/shard_map/ppermute | solution.py:137
  67.1 13.4 %collective-permute-start.4 = (bf16[8,128,128]{2,1,0:T(8,128)(2,1)S(1)}, bf16[8,128,128]{2,1,0:T(8,128)(2,1)S(1)}, u32[]{:S(2)}, u32[]{:S(2)}) collective-permute-start(bf16[8,128,128]{2,1,0:T(8,128)(2,1)S(1)} %constant_dynamic-slice_fusion), channel_id=1, source_target_pairs={{0,1},{1,2},{2,3},{3,0},{4,5},{5,6},{6,7},{7,4},{8,9},{9,10},{10,1... | collective-permute-start | bytes 786440 | tf_op jit(solution)/shard_map/ppermute | solution.py:137
  69.5 11.8 %collective-permute-start.5 = (bf16[8,128,128]{2,1,0:T(8,128)(2,1)S(1)}, bf16[8,128,128]{2,1,0:T(8,128)(2,1)S(1)}, u32[]{:S(2)}, u32[]{:S(2)}) collective-permute-start(bf16[8,128,128]{2,1,0:T(8,128)(2,1)S(1)} %constant_dynamic-slice_fusion), channel_id=1, source_target_pairs={{0,3},{1,0},{2,1},{3,2},{4,7},{5,4},{6,5},{7,6},{8,11},{9,8},{10,9... | collective-permute-start | bytes 786440 | tf_op jit(solution)/shard_map/ppermute | solution.py:137
  81.3 7.5 %collective-permute-start.6 = (bf16[3,8,128,128]{3,2,0,1:T(8,128)(2,1)S(1)}, bf16[3,8,128,128]{3,2,0,1:T(8,128)(2,1)S(1)}, u32[]{:S(2)}, u32[]{:S(2)}) collective-permute-start(bf16[3,8,128,128]{3,2,0,1:T(8,128)(2,1)S(1)} %pad_maximum_fusion), channel_id=1, source_target_pairs={{0,16},{16,0},{32,48},{48,32},{64,80},{80,64},{96,112},{112,96},{1... | collective-permute-start | bytes 2359304 | tf_op jit(solution)/shard_map/ppermute | solution.py:139
  85.0 5.5 %collective-permute-start = (bf16[4,32,128]{2,1,0:T(8,128)(2,1)S(1)}, bf16[4,32,128]{2,1,0:T(8,128)(2,1)S(1)}, u32[]{:S(2)}, u32[]{:S(2)}) collective-permute-start(bf16[4,32,128]{2,1,0:T(8,128)(2,1)S(1)} %get-tuple-element.42), channel_id=1, source_target_pairs={{0,2},{1,3},{2,0},{3,1},{4,6},{5,7},{6,4},{7,5},{8,10},{9,11},{10,... | collective-permute-start | bytes 98312 | tf_op jit(solution)/shard_map/ppermute | solution.py:136
  86.9 3.9 %collective-permute-start.1 = (bf16[4,32,128]{2,1,0:T(8,128)(2,1)S(1)}, bf16[4,32,128]{2,1,0:T(8,128)(2,1)S(1)}, u32[]{:S(2)}, u32[]{:S(2)}) collective-permute-start(bf16[4,32,128]{2,1,0:T(8,128)(2,1)S(1)} %get-tuple-element.41), channel_id=1, source_target_pairs={{0,1},{1,2},{2,3},{3,0},{4,5},{5,6},{6,7},{7,4},{8,9},{9,10},{10,1... | collective-permute-start | bytes 98312 | tf_op jit(solution)/shard_map/ppermute | solution.py:136
  88.7 5.1 %collective-permute-start.2 = (bf16[4,32,128]{2,1,0:T(8,128)(2,1)S(1)}, bf16[4,32,128]{2,1,0:T(8,128)(2,1)S(1)}, u32[]{:S(2)}, u32[]{:S(2)}) collective-permute-start(bf16[4,32,128]{2,1,0:T(8,128)(2,1)S(1)} %get-tuple-element.40), channel_id=1, source_target_pairs={{0,3},{1,0},{2,1},{3,2},{4,7},{5,4},{6,5},{7,6},{8,11},{9,8},{10,9... | collective-permute-start | bytes 98312 | tf_op jit(solution)/shard_map/ppermute | solution.py:136
  94.4 7.3 %collective-permute-start.7 = (bf16[32,2048]{1,0:T(8,128)(2,1)S(1)}, bf16[32,2048]{1,0:T(8,128)(2,1)S(1)}, u32[]{:S(2)}, u32[]{:S(2)}) collective-permute-start(bf16[32,2048]{1,0:T(8,128)(2,1)S(1)} %get-tuple-element.25), channel_id=1, source_target_pairs={{0,8},{1,9},{2,10},{3,11},{4,12},{5,13},{6,14},{7,15},{8,0},{9,1},... | collective-permute-start | bytes 393224 | tf_op jit(solution)/shard_map/ppermute | solution.py:155
  96.6 6.5 %collective-permute-start.8 = (bf16[32,2048]{1,0:T(8,128)(2,1)S(1)}, bf16[32,2048]{1,0:T(8,128)(2,1)S(1)}, u32[]{:S(2)}, u32[]{:S(2)}) collective-permute-start(bf16[32,2048]{1,0:T(8,128)(2,1)S(1)} %get-tuple-element.36), channel_id=1, source_target_pairs={{0,4},{1,5},{2,6},{3,7},{4,8},{5,9},{6,10},{7,11},{8,12},{9,13},{1... | collective-permute-start | bytes 393224 | tf_op jit(solution)/shard_map/ppermute | solution.py:155
  97.2 5.9 %collective-permute-start.9 = (bf16[32,2048]{1,0:T(8,128)(2,1)S(1)}, bf16[32,2048]{1,0:T(8,128)(2,1)S(1)}, u32[]{:S(2)}, u32[]{:S(2)}) collective-permute-start(bf16[32,2048]{1,0:T(8,128)(2,1)S(1)} %get-tuple-element.26), channel_id=1, source_target_pairs={{0,12},{1,13},{2,14},{3,15},{4,0},{5,1},{6,2},{7,3},{8,4},{9,5},{1... | collective-permute-start | bytes 393224 | tf_op jit(solution)/shard_map/ppermute | solution.py:155
Sparse Core Ops, SparseCore 0:
  9.2 43.3 all-gather.1
